TPU v7x, 32 devices: a whole 2x2x4 slice. The times are simulated.
32 devices in a mesh: section: 2 (over core), expert: 8 (over z, y), tensor: 2 (over x).
Axes of the slice: x: 2, y: 2, z: 4, core: 2. Of those that a mesh axis runs over, the one named last changes fastest.
Arguments:
- hidden_in: bfloat16 [1, 1024, 2560], P(None, 'expert', 'tensor'), may hold values from -6 to 6
- segment_ids: int32 [1, 1024], P(None, 'expert'), may hold values from -1 to 7, as said below
- prompt_lengths: int32 [1, 8], replicated, may hold values from 1 to 682, as said below
- expert_choice: int32 [2, 1, 1024, 4], P('section', None, 'expert'), may hold values from 0 to 7, all different within a row; in each aligned block of 128 rows (0 to 127, 128 to 255, ..., all dimensions but the last counted through in order) at most 80 rows name the same one
- attn_gain: float32 [2, 2560], P('section', 'tensor'), may hold values from 0.1 to 1.9
- ffn_gain: float32 [2, 2560], P('section', 'tensor'), may hold values from 0.1 to 1.9
- w_qkv: bfloat16 [2, 2560, 4, 896], P('section', 'expert', 'tensor'), may hold values from -0.125 to 0.125
- w_out: bfloat16 [2, 2560, 2560], P('section', 'expert', 'tensor'), may hold values from -0.125 to 0.125
- w_shared_in: bfloat16 [2, 2560, 2, 3072], P('section', 'expert', None, 'tensor'), may hold values from -0.125 to 0.125
- w_shared_down: bfloat16 [2, 2560, 3072], P('section', 'expert', 'tensor'), may hold values from -0.109375 to 0.109375
- router_weight: float32 [2, 2560, 8], P('section', 'tensor'), may hold values from -0.125 to 0.125
- w_in: bfloat16 [2, 8, 2560, 2, 1536], P('section', 'expert', None, None, 'tensor'), may hold values from -0.125 to 0.125
- w_down: bfloat16 [2, 8, 1536, 2560], P('section', 'expert', 'tensor'), may hold values from -0.15625 to 0.15625
Outputs:
- hidden_states: bfloat16 [2, 1, 1024, 2560], P('section', None, 'expert', 'tensor')
- kv_cache: bfloat16 [2, 1, 1024, 2, 512], P('section', None, 'expert', None, 'tensor')
Inputs may be any that keep to these rules, and one draw needn't show every extreme that they name: segment_ids agree with prompt_lengths: slot s of micro-batch m lies in prompt j where the first j lengths of m sum to at most s and the first j + 1 to more than s; slots past all 8 prompts hold -1. `prompt_lengths`: in every micro-batch exactly one prompt has 682 slots; the 8 lengths sum to at most 1024. `expert_choice`: the 4 entries of a row differ; in each aligned block of 128 rows (section, micro-batch and slot taken together in order) no expert is named by more than 80 rows.
All inputs are finite; a program needn't handle non-finite values.
Results may differ from a plain program's by a relative error of at most 0.02.
Values may be sent and summed in bfloat16 or wider, within the bound.
No kernel may reach another device: no remote copies, remote signals or barrier semaphores. Data moves between devices by JAX's collectives and lax.ppermute only.
A program may use at most 192 MiB of HBM per device.

v0:
```python
import jax
import jax.numpy as jnp
from jax import lax
from jax.sharding import PartitionSpec as P

HD = 128


NORM_EPS = 1e-05
ROPE_BASE = 500000.0


def passed_along(value, axis, steps):
    count = lax.axis_size(axis)
    leading, last = (max(0, -steps), min(count, count - steps))
    return lax.ppermute(value, axis, [(source, source + steps) for source in range(leading, last)])


def rotate_heads(values_in, positions):
    head_width = values_in.shape[-1]
    half_width = head_width // 2
    frequency = ROPE_BASE ** (-(jnp.arange(half_width, dtype=jnp.float32) * (2.0 / head_width)))
    angles = positions[:, None] * frequency[None, :]
    angles = angles.reshape((positions.shape[0],) + (1,) * (values_in.ndim - 2) + (half_width,))
    cosines = jnp.cos(angles)
    sines = jnp.sin(angles)
    first_half = values_in[..., :half_width]
    second_half = values_in[..., half_width:]
    return jnp.concatenate(
        [first_half * cosines - second_half * sines, second_half * cosines + first_half * sines],
        axis=-1,
    )


def norm_rows(values_in, gain_row, model_width):
    widened = values_in.astype(jnp.float32)
    squares = lax.psum(jnp.sum(widened * widened, axis=-1), "tensor")
    return (widened * lax.rsqrt(squares / model_width + NORM_EPS)[:, None] * gain_row).astype(
        jnp.bfloat16
    )


def expert_path(full_rows, w_in_local, w_down_local):
    sources, slot_count, model_width = full_rows.shape
    local_width = w_down_local.shape[0]
    hidden = jnp.dot(
        full_rows.reshape(sources * slot_count, model_width),
        w_in_local.reshape(model_width, 2 * local_width),
        preferred_element_type=jnp.float32,
    )
    activated = (jax.nn.silu(hidden[:, :local_width]) * hidden[:, local_width:]).astype(
        jnp.bfloat16
    )
    partial_value = jnp.dot(activated, w_down_local, preferred_element_type=jnp.float32)
    partial_value = partial_value.reshape(sources, slot_count, model_width)
    summed = lax.psum_scatter(
        partial_value.astype(jnp.bfloat16), "tensor", scatter_dimension=2, tiled=True
    )
    return lax.all_to_all(summed, "expert", split_axis=0, concat_axis=0, tiled=True)


def local(
    hidden_in,
    segment_ids,
    prompt_lengths,
    expert_choice,
    attn_gain,
    ffn_gain,
    w_qkv,
    w_out,
    w_shared_in,
    w_shared_down,
    router_weight,
    w_in,
    w_down,
):
    sections = lax.axis_size("section")
    section_id = lax.axis_index("section")
    experts_count = lax.axis_size("expert")
    expert_id = lax.axis_index("expert")
    micro_count, tokens_dev, columns = hidden_in.shape
    qkv_full, out_full, shared_in_full, shared_down_full = (
        lax.all_gather(w_qkv[0], "expert", axis=0, tiled=True),
        lax.all_gather(w_out[0], "expert", axis=0, tiled=True),
        lax.all_gather(w_shared_in[0], "expert", axis=0, tiled=True),
        lax.all_gather(w_shared_down[0], "expert", axis=0, tiled=True),
    )
    model_width, kv_local, group_cols = qkv_full.shape
    shared_local = shared_down_full.shape[1]
    head_width = HD
    group = group_cols // head_width - 2
    scale = head_width ** (-0.5)
    top_count = expert_choice.shape[-1]
    capacity = 5 * tokens_dev * top_count // (4 * experts_count)
    slot_index = expert_id * tokens_dev + jnp.arange(tokens_dev, dtype=jnp.int32)
    w_in_local = w_in[0, 0]
    w_down_local = w_down[0, 0]
    carried_rows = jnp.zeros((tokens_dev, columns), jnp.bfloat16)
    states = jnp.zeros((micro_count, tokens_dev, columns), jnp.bfloat16)
    caches = jnp.zeros((micro_count, tokens_dev, 2, kv_local * head_width), jnp.bfloat16)
    ticks = micro_count + sections - 1
    for tick_index in range(ticks):
        micro_index = jnp.clip(tick_index - section_id, 0, micro_count - 1)
        incoming = jnp.where(
            section_id == 0, hidden_in[min(tick_index, micro_count - 1)], carried_rows
        )
        active = (tick_index - section_id >= 0) & (tick_index - section_id < micro_count)
        segments = segment_ids[micro_index]
        lengths = prompt_lengths[micro_index]
        choices = expert_choice[0, micro_index]
        starts = jnp.cumsum(lengths) - lengths
        member = segments[:, None] == jnp.arange(lengths.shape[0], dtype=jnp.int32)[None, :]
        first_slot = jnp.sum(jnp.where(member, starts[None, :], 0), axis=1)
        positions = jnp.where(segments >= 0, slot_index - first_slot, 0).astype(jnp.float32)
        normed = norm_rows(incoming, attn_gain[0], model_width)
        normed_full = lax.all_gather(normed, "tensor", axis=1, tiled=True)
        projected = jnp.dot(
            normed_full, qkv_full.reshape(model_width, -1), preferred_element_type=jnp.float32
        )
        projected = projected.reshape(tokens_dev, kv_local, group + 2, head_width)
        queries = rotate_heads(projected[:, :, :group], positions).astype(jnp.bfloat16)
        key_rows = rotate_heads(projected[:, :, group], positions).astype(jnp.bfloat16)
        value_rows = projected[:, :, group + 1].astype(jnp.bfloat16)
        cache = jnp.stack(
            [key_rows.reshape(tokens_dev, -1), value_rows.reshape(tokens_dev, -1)], axis=1
        )
        kv_piece = lax.all_gather(cache.reshape(tokens_dev, -1), "expert", axis=0, tiled=True)
        seg_piece = lax.all_gather(segments, "expert", axis=0, tiled=True)
        key_count = kv_piece.shape[0]
        kv_piece = kv_piece.reshape(key_count, 2, kv_local, head_width)
        key_slots = jnp.arange(key_count, dtype=jnp.int32)
        allowed = (segments[:, None] == seg_piece[None, :]) & (segments[:, None] >= 0) & (
            key_slots[None, :] <= slot_index[:, None]
        ) | (key_slots[None, :] == slot_index[:, None])
        scores = (
            jnp.einsum(
                "tagd,nad->tagn", queries, kv_piece[:, 0], preferred_element_type=jnp.float32
            )
            * scale
        )
        weights_full = jnp.where(allowed[:, None, None, :], jnp.exp(scores), 0.0)
        numerator = jnp.einsum(
            "tagn,nad->tagd",
            weights_full.astype(jnp.bfloat16),
            kv_piece[:, 1],
            preferred_element_type=jnp.float32,
        )
        numerator, denominator = (numerator, jnp.sum(weights_full, axis=-1))
        attended = (numerator / denominator[..., None]).astype(jnp.bfloat16).reshape(tokens_dev, -1)
        attn_terms = lax.dot_general(
            attended, out_full, (((1,), (1,)), ((), ())), preferred_element_type=jnp.float32
        )
        attn_sum = lax.psum_scatter(
            attn_terms.astype(jnp.bfloat16), "tensor", scatter_dimension=1, tiled=True
        ).astype(jnp.float32)
        after_attn = (incoming.astype(jnp.float32) + attn_sum).astype(jnp.bfloat16)
        moe_in = norm_rows(after_attn, ffn_gain[0], model_width)
        moe_rows = lax.all_gather(moe_in, "tensor", axis=1, tiled=True)
        shared_hidden = jnp.dot(
            moe_rows,
            shared_in_full.reshape(model_width, 2 * shared_local),
            preferred_element_type=jnp.float32,
        )
        shared_act = (
            jax.nn.silu(shared_hidden[:, :shared_local]) * shared_hidden[:, shared_local:]
        ).astype(jnp.bfloat16)
        shared_terms = lax.dot_general(
            shared_act,
            shared_down_full,
            (((1,), (1,)), ((), ())),
            preferred_element_type=jnp.float32,
        )
        shared_sum = lax.psum_scatter(
            shared_terms.astype(jnp.bfloat16), "tensor", scatter_dimension=1, tiled=True
        )
        shared_out = lax.optimization_barrier(shared_sum).astype(jnp.float32)
        logits = lax.psum(
            jnp.dot(moe_in.astype(jnp.float32), router_weight[0], precision=lax.Precision.HIGHEST),
            "tensor",
        )
        expert_ids = jnp.arange(logits.shape[1], dtype=jnp.int32)
        picked = jnp.sum(
            jnp.where(choices[:, :, None] == expert_ids[None, None, :], logits[:, None, :], 0.0),
            axis=2,
        )
        raised = jnp.exp(picked)
        gate_weights = raised / jnp.sum(raised, axis=1, keepdims=True)
        flat_choice = choices.reshape(-1)
        onehot = (flat_choice[:, None] == expert_ids[None, :]).astype(jnp.int32)
        slot_rank = jnp.sum(onehot * (jnp.cumsum(onehot, axis=0) - onehot), axis=1)
        slot_ids = flat_choice * capacity + slot_rank
        row_source = jnp.arange(tokens_dev * top_count, dtype=jnp.int32) // top_count
        table = jnp.zeros((experts_count * capacity,), jnp.int32).at[slot_ids].set(row_source)
        filled = jnp.zeros((experts_count * capacity,), jnp.bool_).at[slot_ids].set(True)
        outgoing = jnp.where(filled[:, None], moe_rows[table], jnp.zeros((), jnp.bfloat16))
        outgoing = outgoing.reshape(experts_count, capacity, model_width)
        returned = expert_path(
            lax.all_to_all(outgoing, "expert", split_axis=0, concat_axis=0, tiled=True),
            w_in_local,
            w_down_local,
        )
        combined = returned.reshape(experts_count * capacity, columns)[slot_ids].astype(jnp.float32)
        combined = combined * gate_weights.reshape(-1)[:, None]
        moe_out = jnp.sum(combined.reshape(tokens_dev, top_count, columns), axis=1)
        output = (after_attn.astype(jnp.float32) + shared_out + moe_out).astype(jnp.bfloat16)
        output, cache = (output, cache)
        states = jnp.where(active, states.at[micro_index].set(output), states)
        caches = jnp.where(active, caches.at[micro_index].set(cache), caches)
        if tick_index + 1 < ticks:
            carried_rows = passed_along(output, "section", 1)
    return (states[None], caches[None])


def solution(mesh):
    placed = (
        P(None, "expert", "tensor"),
        P(None, "expert"),
        P(),
        P("section", None, "expert", None),
        P("section", "tensor"),
        P("section", "tensor"),
        P("section", "expert", "tensor", None),
        P("section", "expert", "tensor"),
        P("section", "expert", None, "tensor"),
        P("section", "expert", "tensor"),
        P("section", "tensor", None),
        P("section", "expert", None, None, "tensor"),
        P("section", "expert", "tensor", None),
    )
    return jax.shard_map(
        local,
        mesh=mesh,
        in_specs=placed,
        out_specs=(
            P("section", None, "expert", "tensor"),
            P("section", None, "expert", None, "tensor"),
        ),
        check_vma=False,
    )
```

profile of v0, /device:TPU:0, one launch (start us, length us, event | category | flops | bytes accessed | tf_op | source)
XLA Modules:
  0.0 1194.6 jit_solution(9513238022251728753)
XLA Ops:
  10.7 5.8 psum.42
  19.0 9.3 all_gather.34
  29.2 118.6 %all-gather.16.cloned.1.call-done = bf16[1,2560,2,896]{3,2,0,1:T(2,128)(2,1)} async-done(((bf16[1,320,2,896]{3,2,0,1:T(2,128)(2,1)}), bf16[1,2560,2,896]{3,2,0,1:T(2,128)(2,1)}) %all-gather.16.cloned.1.call-update) | async-done | bytes 9175056 | tf_op jit(solution)/shard_map/all_gather | solution.py:83
  147.8 23.0 %copy.97 = bf16[1,2560,2,896]{1,3,2,0:T(8,128)(2,1)} copy(bf16[1,2560,2,896]{3,2,0,1:T(2,128)(2,1)} %all-gather.16.cloned.1.call-done) | data formatting | bytes 18350080 | tf_op jit(solution)/shard_map/reshape | solution.py:118
  170.8 6.2 fusion.78
  179.0 17.5 %all-gather.1 = s32[1,1024]{1,0:T(1,128)S(1)} all-gather(s32[1,128]{1,0:T(1,128)S(1)} %copy-done.12), channel_id=3, replica_groups=mesh['section'=2,'expert'=8,'tensor'=2] {'expert'}, dimensions={1}, use_global_device_ids=true | all-gather | bytes 4608 | tf_op jit(solution)/shard_map/all_gather | solution.py:128
  196.8 18.9 %all-gather.12.cloned.1.call-done = bf16[1024,512]{0,1:T(8,128)(2,1)} async-done(((bf16[128,512]{0,1:T(8,128)(2,1)}), bf16[1024,512]{0,1:T(8,128)(2,1)}) %all-gather.12.cloned.1.call-update) | async-done | bytes 1048592 | tf_op jit(solution)/shard_map/all_gather | solution.py:127
  215.7 2.4 fusion.8
  219.2 99.9 %all-gather.18.cloned.1.call-done = bf16[1,2560,1280]{2,1,0:T(8,128)(2,1)} async-done(((bf16[1,320,1280]{2,1,0:T(8,128)(2,1)}), bf16[1,2560,1280]{2,1,0:T(8,128)(2,1)}) %all-gather.18.cloned.1.call-update) | async-done | bytes 6553616 | tf_op jit(solution)/shard_map/all_gather | solution.py:84
  319.1 6.1 fusion.20
  326.9 2.4 scatter_custom_fusion
  329.5 2.4 scatter_custom_fusion.1
  331.9 7.6 reduce-scatter.7.cloned.1.call-done
  340.7 4.9 psum.43
  345.8 9.2 all_gather.39
  355.0 4.3 gather_fusion
  359.3 4.0 broadcast_select_fusion.1
  363.3 5.5 all-to-all-start
  368.9 7.7 copy.102
  376.5 63.8 %all-to-all-done = bf16[8,80,2560]{2,1,0:T(8,128)(2,1)} async-done(((bf16[8,80,2560]{2,1,0:T(8,128)(2,1)}), bf16[8,80,2560]{2,1,0:T(8,128)(2,1)}, u32[]{:S(2)}, u32[]{:S(2)}) %all-to-all-start) | async-done | bytes 3276832 | tf_op jit(solution)/shard_map/all_to_all | solution.py:198
  440.4 8.6 fusion.119
  449.5 1.5 copy-done.13
  451.0 4.1 convolution_convert_fusion.1
  456.5 41.8 %reduce-scatter.11.cloned.1.call-done = bf16[8,80,1280]{2,1,0:T(8,128)(2,1)} async-done(((bf16[8,80,2560]{2,1,0:T(8,128)(2,1)}), bf16[8,80,1280]{2,1,0:T(8,128)(2,1)}) %reduce-scatter.11.cloned.1.call-update) | async-done | bytes 1638416 | tf_op jit(solution)/shard_map/reduce_scatter | solution.py:56
  498.3 5.5 all-to-all-start.1
  503.9 238.1 %all-gather.20.cloned.1.call-done = bf16[1,2560,2,1536]{3,2,0,1:T(2,128)(2,1)} async-done(((bf16[1,320,2,1536]{3,2,0,1:T(2,128)(2,1)}), bf16[1,2560,2,1536]{3,2,0,1:T(2,128)(2,1)}) %all-gather.20.cloned.1.call-update) | async-done | bytes 15728656 | tf_op jit(solution)/shard_map/all_gather | solution.py:85
  742.0 10.2 copy.101
  752.2 5.5 copy-done.1
  757.7 3.4 fusion.118
  761.1 99.6 %all-gather.22.cloned.1.call-done = bf16[1,2560,1536]{2,1,0:T(8,128)(2,1)} async-done(((bf16[1,320,1536]{2,1,0:T(8,128)(2,1)}), bf16[1,2560,1536]{2,1,0:T(8,128)(2,1)}) %all-gather.22.cloned.1.call-update) | async-done | bytes 7864336 | tf_op jit(solution)/shard_map/all_gather | solution.py:86
  860.8 7.2 fusion.14
  868.4 5.2 psum.44
  874.4 8.0 reduce-scatter.9.cloned.1.call-done
  882.4 2.9 gather_fusion.1
  885.2 2.6 reshape.731
  887.9 2.5 multiply_reduce_fusion.1
  890.5 1.8 collective-permute-start
  893.7 5.0 psum.45
  898.8 9.5 all_gather.42
  908.3 6.2 fusion.76
  915.4 39.5 %all-gather.14.cloned.1.call-done = bf16[1024,512]{0,1:T(8,128)(2,1)} async-done(((bf16[128,512]{0,1:T(8,128)(2,1)}), bf16[1024,512]{0,1:T(8,128)(2,1)}) %all-gather.14.cloned.1.call-update) | async-done | bytes 1048592 | tf_op jit(solution)/shard_map/all_gather | solution.py:127
  955.0 2.5 fusion.10
  959.2 3.1 fusion.23
  962.4 15.0 %reduce-scatter.13.cloned.1.call-done = bf16[128,1280]{1,0:T(8,128)(2,1)} async-done(((bf16[128,2560]{1,0:T(8,128)(2,1)}), bf16[128,1280]{1,0:T(8,128)(2,1)}) %reduce-scatter.13.cloned.1.call-update) | async-done | bytes 327696 | tf_op jit(solution)/shard_map/reduce_scatter | solution.py:153
  978.5 4.9 psum.46
  984.6 9.0 all_gather.44
  993.6 4.3 gather_fusion.2
  997.9 2.2 broadcast_select_fusion
  1000.1 77.4 %all_to_all.20 = bf16[8,80,2560]{2,1,0:T(8,128)(2,1)S(1)} all-to-all(bf16[8,80,2560]{2,1,0:T(8,128)(2,1)S(1)} %broadcast_select_fusion), channel_id=1, replica_groups=mesh['section'=2,'expert'=8,'tensor'=2] {'expert'}, dimensions={0} | all-to-all | bytes 6553600 | tf_op jit(solution)/shard_map/all_to_all | solution.py:198
  1077.5 7.5 fusion.121
  1085.6 1.5 copy-done.14
  1087.1 4.1 convolution_convert_fusion
  1091.3 42.7 %reduce-scatter.17.cloned.1.call-done = bf16[8,80,1280]{2,1,0:T(8,128)(2,1)} async-done(((bf16[8,80,2560]{2,1,0:T(8,128)(2,1)}), bf16[8,80,1280]{2,1,0:T(8,128)(2,1)}) %reduce-scatter.17.cloned.1.call-update) | async-done | bytes 1638416 | tf_op jit(solution)/shard_map/reduce_scatter | solution.py:56
  1134.0 5.5 all-to-all-start.3
  1139.5 7.7 fusion.120
  1147.2 6.7 fusion.17
  1156.1 2.5 broadcast_select_fusion.5
  1158.9 5.3 psum.47
  1164.3 6.3 reduce-scatter.15.cloned.1.call-done
  1170.6 7.2 all-to-all-done.3
  1177.9 2.9 gather_fusion.3
  1180.8 2.7 reshape.732
  1183.4 1.6 multiply_reduce_fusion
  1185.1 2.2 fusion.88
  (137 shorter events, 26.3 us)
Async XLA Ops:
  7.2 860.9 %copy-start = (f32[1,1280,8]{1,2,0:T(8,128)S(1)}, f32[1,1280,8]{1,2,0:T(8,128)}, u32[]{:S(2)}) copy-start(f32[1,1280,8]{1,2,0:T(8,128)} %param.31) | copy-start | bytes 122884
  7.2 140.6 %all-gather.16.cloned.1.call-start = ((), (), s32[]{:S(2)}) async-start(), calls=%async_computation.18 | async-start | bytes 10321920 | tf_op jit(solution)/shard_map/all_gather | solution.py:83
  7.9 207.8 %all-gather.12.cloned.1.call-start = ((), (), s32[]{:S(2)}) async-start(), calls=%async_computation.10 | async-start | bytes 1179648 | tf_op jit(solution)/shard_map/all_gather | solution.py:127
  170.8 7.8 copy-start.10
  170.8 8.1 copy-start.11
  170.8 8.1 copy-start.12
  177.8 141.2 %all-gather.18.cloned.1.call-start = ((), (), s32[]{:S(2)}) async-start(), calls=%async_computation.19 | async-start | bytes 7372800 | tf_op jit(solution)/shard_map/all_gather | solution.py:84
  178.6 161.0 %reduce-scatter.7.cloned.1.call-start = ((), (), s32[]{:S(2)}) async-start(), calls=%async_computation.11 | async-start | bytes 983040 | tf_op jit(solution)/shard_map/reduce_scatter | solution.py:153
  196.7 21.4 %copy-start.8 = (pred[128,1024]{0,1:T(8,128)(4,1)}, pred[128,1024]{0,1:T(8,128)(4,1)S(1)}, u32[]{:S(2)}) copy-start(pred[128,1024]{0,1:T(8,128)(4,1)S(1)} %fusion.83) | copy-start | bytes 393220
  215.7 2.5 copy-start.15
  319.1 20.5 %copy-start.2 = (bf16[1,128,1280]{2,1,0:T(8,128)(2,1)S(1)}, bf16[1,128,1280]{2,1,0:T(8,128)(2,1)}, u32[]{:S(2)}) copy-start(bf16[1,128,1280]{2,1,0:T(8,128)(2,1)} %param.21) | copy-start | bytes 983044
  363.3 77.0 %all-to-all-start = ((bf16[8,80,2560]{2,1,0:T(8,128)(2,1)}), bf16[8,80,2560]{2,1,0:T(8,128)(2,1)}, u32[]{:S(2)}, u32[]{:S(2)}) async-start(bf16[8,80,2560]{2,1,0:T(8,128)(2,1)} %broadcast_select_fusion.1), calls=%async_computation.2 | async-start | bytes 6553600 | tf_op jit(solution)/shard_map/all_to_all | solution.py:198
  368.8 129.5 %reduce-scatter.11.cloned.1.call-start = ((), (), s32[]{:S(2)}) async-start(), calls=%async_computation.13 | async-start | bytes 4915200 | tf_op jit(solution)/shard_map/reduce_scatter | solution.py:56
  448.9 2.1 copy-start.13
  455.2 286.7 %all-gather.20.cloned.1.call-start = ((), (), s32[]{:S(2)}) async-start(), calls=%async_computation.20 | async-start | bytes 17694720 | tf_op jit(solution)/shard_map/all_gather | solution.py:85
  455.8 405.0 %all-gather.22.cloned.1.call-start = ((), (), s32[]{:S(2)}) async-start(), calls=%async_computation.21 | async-start | bytes 8847360 | tf_op jit(solution)/shard_map/all_gather | solution.py:86
  498.3 384.1 %all-to-all-start.1 = ((bf16[8,80,1280]{2,1,0:T(8,128)(2,1)}), bf16[8,80,1280]{2,1,0:T(8,128)(2,1)S(1)}, u32[]{:S(2)}, u32[]{:S(2)}) async-start(bf16[8,80,1280]{2,1,0:T(8,128)(2,1)} %reduce-scatter.11.cloned.1.call-done), calls=%async_computation.4 | async-start | bytes 3276800 | tf_op jit(solution)/shard_map/all_to_all | solution.py:59
  503.8 378.6 %reduce-scatter.9.cloned.1.call-start = ((), (), s32[]{:S(2)}) async-start(), calls=%async_computation.12 | async-start | bytes 983040 | tf_op jit(solution)/shard_map/reduce_scatter | solution.py:173
  752.2 5.5 copy-start.1
  868.0 86.9 %all-gather.14.cloned.1.call-start = ((), (), s32[]{:S(2)}) async-start(), calls=%async_computation.14 | async-start | bytes 1179648 | tf_op jit(solution)/shard_map/all_gather | solution.py:127
  887.9 2.5 copy-start.6
  890.5 3.2 copy-start.4
  890.5 3.0 collective-permute-start
  908.3 46.6 %copy-start.9 = (pred[128,1024]{0,1:T(8,128)(4,1)S(1)}, pred[128,1024]{0,1:T(8,128)(4,1)}, u32[]{:S(2)}) copy-start(pred[128,1024]{0,1:T(8,128)(4,1)} %copy-done.8) | copy-start | bytes 393220
  915.3 62.1 %reduce-scatter.13.cloned.1.call-start = ((), (), s32[]{:S(2)}) async-start(), calls=%async_computation.15 | async-start | bytes 983040 | tf_op jit(solution)/shard_map/reduce_scatter | solution.py:153
  955.0 2.5 copy-start.16
  955.0 3.6 slice-start
  957.5 1.7 slice-start.1
  962.3 171.7 %reduce-scatter.17.cloned.1.call-start = ((), (), s32[]{:S(2)}) async-start(), calls=%async_computation.17 | async-start | bytes 4915200 | tf_op jit(solution)/shard_map/reduce_scatter | solution.py:56
  1085.0 2.1 copy-start.14
  1134.0 43.9 %all-to-all-start.3 = ((bf16[8,80,1280]{2,1,0:T(8,128)(2,1)}), bf16[8,80,1280]{2,1,0:T(8,128)(2,1)S(1)}, u32[]{:S(2)}, u32[]{:S(2)}) async-start(bf16[8,80,1280]{2,1,0:T(8,128)(2,1)} %reduce-scatter.17.cloned.1.call-done), calls=%async_computation.9 | async-start | bytes 3276800 | tf_op jit(solution)/shard_map/all_to_all | solution.py:59
  1139.5 31.2 %reduce-scatter.15.cloned.1.call-start = ((), (), s32[]{:S(2)}) async-start(), calls=%async_computation.16 | async-start | bytes 983040 | tf_op jit(solution)/shard_map/reduce_scatter | solution.py:173
  1180.8 4.3 copy-start.3
  1183.4 1.6 copy-start.5
  1183.4 1.6 copy-start.7
Sparse Core Ops, SparseCore 0:
  10.2 137.5 all-gather.15
  177.9 37.7 all-gather.11
  217.9 101.1 all-gather.17
  325.3 14.2 reduce-scatter.6
  455.3 42.9 reduce-scatter.10
  500.3 241.5 all-gather.19
  744.1 116.5 all-gather.21
  868.1 14.1 reduce-scatter.8
  915.4 39.5 all-gather.13
  962.4 14.8 reduce-scatter.12
  1091.4 42.5 reduce-scatter.16
  1154.1 16.5 reduce-scatter.14
where the time goes:
time: 1200 us; the launch traced here: 1190 us
  waiting for transfers between devices  811 us (68%)
  blocking collectives  163 us (14%)
  matrix products  78.6 us (7%)
  local copies, waits for them, and re-layouts  77.1 us (6%)
  other arithmetic  31.2 us (3%)
  starting transfers between devices  18.7 us (2%)
  between operations  15.3 us (1%)
    all_gather x1, waiting for transfers between devices, local(): lax.all_gather(w_shared_in[0], 'expert', axis=0, tiled=True)  238 us
    all_gather x1, waiting for transfers between devices, local(): lax.all_gather(w_qkv[0], 'expert', axis=0, tiled=True)  119 us
    all_gather x1, waiting for transfers between devices, local(): lax.all_gather(w_out[0], 'expert', axis=0, tiled=True)  99.9 us
    all_gather x1, waiting for transfers between devices, local(): lax.all_gather(w_shared_down[0], 'expert', axis=0, tiled=True)  99.6 us
    reduce_scatter x2, waiting for transfers between devices, expert_path(): lax.psum_scatter(partial_value.astype(jnp.bfloat16), 'tensor', scatter_di...  84.5 us
    all_to_all x1, blocking collectives, local(): lax.all_to_all(outgoing, 'expert', split_axis=0, concat_axis=0, tiled=True)  77.4 us
    all_to_all x1, waiting for transfers between devices, local(): lax.all_to_all(outgoing, 'expert', split_axis=0, concat_axis=0, tiled=True)  63.8 us
    all_gather x2, waiting for transfers between devices, local(): lax.all_gather(cache.reshape(tokens_dev, -1), 'expert', axis=0, tiled=True)  58.4 us
  transfers between devices with their start and end apart: 16, of which 15 were waited for; matrix products, arithmetic and copies ran while one was open for 6% of the time, Pallas kernels for 0%

commit v1 on v0

--- a/solution.py
+++ b/solution.py
@@ -38,6 +38,11 @@
     return (widened * lax.rsqrt(squares / model_width + NORM_EPS)[:, None] * gain_row).astype(
         jnp.bfloat16
     )
+
+
+def terms_to_slots(terms):
+    by_slot = lax.all_to_all(terms, "expert", split_axis=0, concat_axis=1, tiled=True)
+    return lax.psum_scatter(by_slot, "tensor", scatter_dimension=1, tiled=True)
 
 
 def expert_path(full_rows, w_in_local, w_down_local):
@@ -79,14 +84,12 @@
     experts_count = lax.axis_size("expert")
     expert_id = lax.axis_index("expert")
     micro_count, tokens_dev, columns = hidden_in.shape
-    qkv_full, out_full, shared_in_full, shared_down_full = (
-        lax.all_gather(w_qkv[0], "expert", axis=0, tiled=True),
-        lax.all_gather(w_out[0], "expert", axis=0, tiled=True),
-        lax.all_gather(w_shared_in[0], "expert", axis=0, tiled=True),
-        lax.all_gather(w_shared_down[0], "expert", axis=0, tiled=True),
-    )
+    qkv_full = lax.all_gather(w_qkv[0], "expert", axis=0, tiled=True)
+    out_local = w_out[0]
+    shared_down_local = w_shared_down[0]
+    shared_in_cols = lax.all_to_all(w_shared_in[0], "expert", split_axis=2, concat_axis=0, tiled=True)
     model_width, kv_local, group_cols = qkv_full.shape
-    shared_local = shared_down_full.shape[1]
+    shared_cols = shared_in_cols.shape[2]
     head_width = HD
     group = group_cols // head_width - 2
     scale = head_width ** (-0.5)
@@ -147,32 +150,31 @@
         )
         numerator, denominator = (numerator, jnp.sum(weights_full, axis=-1))
         attended = (numerator / denominator[..., None]).astype(jnp.bfloat16).reshape(tokens_dev, -1)
+        attended_all = lax.all_gather(attended, "expert", axis=0, tiled=True)
         attn_terms = lax.dot_general(
-            attended, out_full, (((1,), (1,)), ((), ())), preferred_element_type=jnp.float32
-        )
-        attn_sum = lax.psum_scatter(
-            attn_terms.astype(jnp.bfloat16), "tensor", scatter_dimension=1, tiled=True
-        ).astype(jnp.float32)
+            attended_all, out_local, (((1,), (1,)), ((), ())), preferred_element_type=jnp.float32
+        )
+        attn_sum = terms_to_slots(attn_terms.astype(jnp.bfloat16)).astype(jnp.float32)
         after_attn = (incoming.astype(jnp.float32) + attn_sum).astype(jnp.bfloat16)
         moe_in = norm_rows(after_attn, ffn_gain[0], model_width)
         moe_rows = lax.all_gather(moe_in, "tensor", axis=1, tiled=True)
+        moe_all = lax.all_gather(moe_rows, "expert", axis=0, tiled=True)
         shared_hidden = jnp.dot(
-            moe_rows,
-            shared_in_full.reshape(model_width, 2 * shared_local),
+            moe_all,
+            shared_in_cols.reshape(model_width, 2 * shared_cols),
             preferred_element_type=jnp.float32,
         )
         shared_act = (
-            jax.nn.silu(shared_hidden[:, :shared_local]) * shared_hidden[:, shared_local:]
+            jax.nn.silu(shared_hidden[:, :shared_cols]) * shared_hidden[:, shared_cols:]
         ).astype(jnp.bfloat16)
+        shared_act = lax.all_gather(shared_act, "expert", axis=1, tiled=True)
         shared_terms = lax.dot_general(
             shared_act,
-            shared_down_full,
+            shared_down_local,
             (((1,), (1,)), ((), ())),
             preferred_element_type=jnp.float32,
         )
-        shared_sum = lax.psum_scatter(
-            shared_terms.astype(jnp.bfloat16), "tensor", scatter_dimension=1, tiled=True
-        )
+        shared_sum = terms_to_slots(shared_terms.astype(jnp.bfloat16))
         shared_out = lax.optimization_barrier(shared_sum).astype(jnp.float32)
         logits = lax.psum(
             jnp.dot(moe_in.astype(jnp.float32), router_weight[0], precision=lax.Precision.HIGHEST),

time: 1200 us -> 1180 us (0.983)
  blocking collectives: 163 us -> 126 us
  waiting for transfers between devices: 811 us -> 790 us
  starting transfers between devices: 18.7 us -> 36.4 us
  local copies, waits for them, and re-layouts: 77.1 us -> 91.4 us
    all_gather x4 -> x7, waiting for transfers between devices: 556 us -> 416 us  [the longest x2 141 us: local(): moe_all = lax.all_gather(moe_rows, 'expert', axis=0, tiled=True)]
    all_to_all x0 -> x3, waiting for transfers between devices: none -> 86.5 us  [the longest x1 86.4 us: local(): lax.all_to_all(w_shared_in[0], 'expert', split_axis=2, concat_axis=0, til...]
    all_to_all x2, waiting for transfers between devices: 7.25 us -> 52.6 us  [expert_path(): lax.all_to_all(summed, 'expert', split_axis=0, concat_axis=0, tiled=True)]
    all_to_all x1 -> x2, blocking collectives: 77.4 us -> 40.8 us  [terms_to_slots(): lax.all_to_all(terms, 'expert', split_axis=0, concat_axis=1, tiled=True)]
    all_to_all x0 -> x3, starting transfers between devices: none -> 13.1 us  [the longest x2 7.42 us: terms_to_slots(): lax.all_to_all(terms, 'expert', split_axis=0, concat_axis=1, tiled=True)]
    all_to_all x0 -> x10, local copies, waits for them, and re-layouts: none -> 12.1 us  [the longest x8 8.71 us: terms_to_slots(): lax.all_to_all(terms, 'expert', split_axis=0, concat_axis=1, tiled=True)]
    all_to_all x1 -> x2, waiting for transfers between devices: 63.8 us -> 69.7 us  [local(): lax.all_to_all(outgoing, 'expert', split_axis=0, concat_axis=0, tiled=True)]
    unnamed x41 -> x79, local copies, waits for them, and re-layouts: 27.3 us -> 23 us
  transfers between devices with their start and end apart: 16 -> 23, of which waited for: 15 -> 18; matrix products, arithmetic and copies ran while one was open for 6% -> 11% of each run, Pallas kernels for 0% -> 0%
where the time goes in v1:
time: 1180 us; the launch traced here: 1170 us
  waiting for transfers between devices  790 us (67%)
  blocking collectives  126 us (11%)
  local copies, waits for them, and re-layouts  91.4 us (8%)
  matrix products  70 us (6%)
  other arithmetic  40.5 us (3%)
  starting transfers between devices  36.4 us (3%)
  between operations  15.2 us (1%)
    all_gather x2, waiting for transfers between devices, local(): moe_all = lax.all_gather(moe_rows, 'expert', axis=0, tiled=True)  141 us
    all_gather x1, waiting for transfers between devices, local(): qkv_full = lax.all_gather(w_qkv[0], 'expert', axis=0, tiled=True)  119 us
    all_gather x2, waiting for transfers between devices, local(): attended_all = lax.all_gather(attended, 'expert', axis=0, tiled=True)  112 us
    all_to_all x1, waiting for transfers between devices, local(): lax.all_to_all(w_shared_in[0], 'expert', split_axis=2, concat_axis=0, til...  86.4 us
    reduce_scatter x2, waiting for transfers between devices, expert_path(): lax.psum_scatter(partial_value.astype(jnp.bfloat16), 'tensor', scatter_di...  75.7 us
    all_to_all x2, waiting for transfers between devices, local(): lax.all_to_all(outgoing, 'expert', split_axis=0, concat_axis=0, tiled=True)  69.7 us
    all_gather x2, waiting for transfers between devices, local(): lax.all_gather(cache.reshape(tokens_dev, -1), 'expert', axis=0, tiled=True)  58.4 us
    all_to_all x2, waiting for transfers between devices, expert_path(): lax.all_to_all(summed, 'expert', split_axis=0, concat_axis=0, tiled=True)  52.6 us
  transfers between devices with their start and end apart: 23, of which 18 were waited for; matrix products, arithmetic and copies ran while one was open for 11% of the time, Pallas kernels for 0%

profile of v1, /device:TPU:0, one launch (start us, length us, event | category | flops | bytes accessed | tf_op | source)
XLA Modules:
  0.0 1169.6 jit_solution(11774944104342150253)
XLA Ops:
  10.7 5.8 psum.42
  19.0 9.3 all_gather.43
  29.2 118.6 %all-gather.28.cloned.1.call-done = bf16[1,2560,2,896]{3,2,0,1:T(2,128)(2,1)} async-done(((bf16[1,320,2,896]{3,2,0,1:T(2,128)(2,1)}), bf16[1,2560,2,896]{3,2,0,1:T(2,128)(2,1)}) %all-gather.28.cloned.1.call-update) | async-done | bytes 9175056 | tf_op jit(solution)/shard_map/all_gather | solution.py:87
  147.8 23.0 %copy.131 = bf16[1,2560,2,896]{1,3,2,0:T(8,128)(2,1)} copy(bf16[1,2560,2,896]{3,2,0,1:T(2,128)(2,1)} %all-gather.28.cloned.1.call-done) | data formatting | bytes 18350080 | tf_op jit(solution)/shard_map/reshape | solution.py:121
  170.8 6.2 fusion.66
  177.8 17.5 %all-gather.1 = s32[1,1024]{1,0:T(1,128)S(1)} all-gather(s32[1,128]{1,0:T(1,128)S(1)} %copy-done.31), channel_id=3, replica_groups=mesh['section'=2,'expert'=8,'tensor'=2] {'expert'}, dimensions={1}, use_global_device_ids=true | all-gather | bytes 4608 | tf_op jit(solution)/shard_map/all_gather | solution.py:131
  195.6 20.1 %all-gather.12.cloned.1.call-done = bf16[1024,512]{0,1:T(8,128)(2,1)} async-done(((bf16[128,512]{0,1:T(8,128)(2,1)}), bf16[1024,512]{0,1:T(8,128)(2,1)}) %all-gather.12.cloned.1.call-update) | async-done | bytes 1048592 | tf_op jit(solution)/shard_map/all_gather | solution.py:130
  220.1 55.9 %all-gather.14.cloned.1.call-done = bf16[1024,1280]{0,1:T(8,128)(2,1)} async-done(((bf16[128,1280]{0,1:T(8,128)(2,1)}), bf16[1024,1280]{0,1:T(8,128)(2,1)}) %all-gather.14.cloned.1.call-update) | async-done | bytes 2621456 | tf_op jit(solution)/shard_map/all_gather | solution.py:153
  276.0 2.8 fusion.26
  278.9 20.4 %all_to_all.111 = bf16[8,128,320]{1,2,0:T(8,128)(2,1)S(1)} all-to-all(bf16[8,128,320]{1,2,0:T(8,128)(2,1)S(1)} %bitcast.249), channel_id=1, replica_groups=mesh['section'=2,'expert'=8,'tensor'=2] {'expert'}, dimensions={0} | all-to-all | bytes 1310720 | tf_op jit(solution)/shard_map/all_to_all | solution.py:44
  300.5 14.7 %reduce-scatter.7.cloned.1.call-done = bf16[128,1280]{1,0:T(8,128)(2,1)} async-done(((bf16[128,2560]{1,0:T(8,128)(2,1)}), bf16[128,1280]{1,0:T(8,128)(2,1)}) %reduce-scatter.7.cloned.1.call-update) | async-done | bytes 327696 | tf_op jit(solution)/shard_map/reduce_scatter | solution.py:45
  316.4 4.9 psum.43
  322.3 9.1 all_gather.48
  331.4 8.6 copy.99
  339.9 5.7 all-to-all-start.1
  352.9 4.4 gather_fusion
  357.3 3.9 broadcast_select_fusion.1
  361.2 86.4 %all-to-all-done.1 = bf16[320,2,1536]{0,1,2:T(2,128)(2,1)} async-done(((bf16[320,2,1536]{0,1,2:T(2,128)(2,1)}), bf16[320,2,1536]{0,1,2:T(2,128)(2,1)}, u32[]{:S(2)}, u32[]{:S(2)}) %all-to-all-start.1) | async-done | bytes 1966112 | tf_op jit(solution)/shard_map/all_to_all | solution.py:90
  447.6 4.5 all-to-all-start.3
  455.5 2.7 reshape.735
  458.2 9.5 all-gather.16.cloned.1.call-done
  467.8 5.3 fusion.100
  474.2 7.7 copy.139
  481.9 69.7 %all-to-all-done.3 = bf16[8,80,2560]{2,1,0:T(8,128)(2,1)} async-done(((bf16[8,80,2560]{2,1,0:T(8,128)(2,1)}), bf16[8,80,2560]{2,1,0:T(8,128)(2,1)}, u32[]{:S(2)}, u32[]{:S(2)}) %all-to-all-start.3) | async-done | bytes 3276832 | tf_op jit(solution)/shard_map/all_to_all | solution.py:200
  551.6 8.6 fusion.101
  562.3 4.1 convolution_convert_fusion.1
  566.6 3.1 fusion.18
  570.7 3.7 all-to-all-start.2
  574.4 37.9 %reduce-scatter.11.cloned.1.call-done = bf16[8,80,1280]{2,1,0:T(8,128)(2,1)} async-done(((bf16[8,80,2560]{2,1,0:T(8,128)(2,1)}), bf16[8,80,1280]{2,1,0:T(8,128)(2,1)}) %reduce-scatter.11.cloned.1.call-update) | async-done | bytes 1638416 | tf_op jit(solution)/shard_map/reduce_scatter | solution.py:61
  613.2 5.5 all-to-all-start.4
  621.6 5.0 psum.44
  626.8 30.4 %all-to-all-done.4 = bf16[8,80,1280]{2,1,0:T(8,128)(2,1)S(1)} async-done(((bf16[8,80,1280]{2,1,0:T(8,128)(2,1)}), bf16[8,80,1280]{2,1,0:T(8,128)(2,1)S(1)}, u32[]{:S(2)}, u32[]{:S(2)}) %all-to-all-start.4) | async-done | bytes 1638432 | tf_op jit(solution)/shard_map/all_to_all | solution.py:64
  657.1 2.9 gather_fusion.1
  660.0 3.7 reshape.744
  663.7 3.4 multiply_reduce_fusion.1
  671.0 5.0 psum.45
  676.1 9.5 all_gather.51
  685.6 6.1 fusion.64
  692.7 38.3 %all-gather.20.cloned.1.call-done = bf16[1024,512]{0,1:T(8,128)(2,1)} async-done(((bf16[128,512]{0,1:T(8,128)(2,1)}), bf16[1024,512]{0,1:T(8,128)(2,1)}) %all-gather.20.cloned.1.call-update) | async-done | bytes 1048592 | tf_op jit(solution)/shard_map/all_gather | solution.py:130
  735.5 55.9 %all-gather.22.cloned.1.call-done = bf16[1024,1280]{0,1:T(8,128)(2,1)} async-done(((bf16[128,1280]{0,1:T(8,128)(2,1)}), bf16[1024,1280]{0,1:T(8,128)(2,1)}) %all-gather.22.cloned.1.call-update) | async-done | bytes 2621456 | tf_op jit(solution)/shard_map/all_gather | solution.py:153
  791.3 2.8 fusion.27
  794.2 20.4 %all_to_all.112 = bf16[8,128,320]{1,2,0:T(8,128)(2,1)S(1)} all-to-all(bf16[8,128,320]{1,2,0:T(8,128)(2,1)S(1)} %bitcast.251), channel_id=1, replica_groups=mesh['section'=2,'expert'=8,'tensor'=2] {'expert'}, dimensions={0} | all-to-all | bytes 1310720 | tf_op jit(solution)/shard_map/all_to_all | solution.py:44
  815.8 14.7 %reduce-scatter.13.cloned.1.call-done = bf16[128,1280]{1,0:T(8,128)(2,1)} async-done(((bf16[128,2560]{1,0:T(8,128)(2,1)}), bf16[128,1280]{1,0:T(8,128)(2,1)}) %reduce-scatter.13.cloned.1.call-update) | async-done | bytes 327696 | tf_op jit(solution)/shard_map/reduce_scatter | solution.py:45
  831.7 4.9 psum.46
  837.8 9.1 all_gather.54
  847.9 4.4 gather_fusion.2
  852.3 4.0 broadcast_select_fusion
  856.3 5.4 all-to-all-start.7
  862.0 131.4 %all-gather.24.cloned.1.call-done = bf16[1024,2560]{1,0:T(8,128)(2,1)} async-done(((bf16[128,2560]{1,0:T(8,128)(2,1)}), bf16[1024,2560]{1,0:T(8,128)(2,1)}) %all-gather.24.cloned.1.call-update) | async-done | bytes 5242896 | tf_op jit(solution)/shard_map/all_gather | solution.py:161
  993.4 5.3 fusion.102
  999.9 8.6 fusion.103
  1010.6 4.1 convolution_convert_fusion
  1014.7 44.4 %all-gather.26.cloned.1.call-done = bf16[1024,1536]{0,1:T(8,128)(2,1)} async-done(((bf16[1024,192]{0,1:T(8,128)(2,1)}), bf16[1024,1536]{0,1:T(8,128)(2,1)}) %all-gather.26.cloned.1.call-update) | async-done | bytes 3145744 | tf_op jit(solution)/shard_map/all_gather | solution.py:170
  1059.1 3.1 fusion.19
  1063.1 3.7 all-to-all-start.6
  1066.8 37.8 %reduce-scatter.17.cloned.1.call-done = bf16[8,80,1280]{2,1,0:T(8,128)(2,1)} async-done(((bf16[8,80,2560]{2,1,0:T(8,128)(2,1)}), bf16[8,80,1280]{2,1,0:T(8,128)(2,1)}) %reduce-scatter.17.cloned.1.call-update) | async-done | bytes 1638416 | tf_op jit(solution)/shard_map/reduce_scatter | solution.py:61
  1105.4 5.5 all-to-all-start.8
  1117.3 3.6 broadcast_select_fusion.5
  1121.9 5.0 psum.47
  1127.2 22.2 %all-to-all-done.8 = bf16[8,80,1280]{2,1,0:T(8,128)(2,1)S(1)} async-done(((bf16[8,80,1280]{2,1,0:T(8,128)(2,1)}), bf16[8,80,1280]{2,1,0:T(8,128)(2,1)S(1)}, u32[]{:S(2)}, u32[]{:S(2)}) %all-to-all-start.8) | async-done | bytes 1638432 | tf_op jit(solution)/shard_map/all_to_all | solution.py:64
  1149.4 2.9 gather_fusion.3
  1152.2 3.7 reshape.745
  1156.0 3.4 multiply_reduce_fusion
  1159.4 3.2 fusion.72
  (205 shorter events, 61.2 us)
Async XLA Ops:
  7.2 559.5 %copy-start = (bf16[1,320,1536]{2,1,0:T(8,128)(2,1)S(1)}, bf16[1,320,1536]{2,1,0:T(8,128)(2,1)}, u32[]{:S(2)}) copy-start(bf16[1,320,1536]{2,1,0:T(8,128)(2,1)} %param.30) | copy-start | bytes 2949124
  7.2 140.6 %all-gather.28.cloned.1.call-start = ((), (), s32[]{:S(2)}) async-start(), calls=%async_computation.29 | async-start | bytes 10321920 | tf_op jit(solution)/shard_map/all_gather | solution.py:87
  7.9 207.8 %all-gather.12.cloned.1.call-start = ((), (), s32[]{:S(2)}) async-start(), calls=%async_computation.15 | async-start | bytes 1179648 | tf_op jit(solution)/shard_map/all_gather | solution.py:130
  170.8 7.0 copy-start.31
  177.7 98.2 %all-gather.14.cloned.1.call-start = ((), (), s32[]{:S(2)}) async-start(), calls=%async_computation.16 | async-start | bytes 2949120 | tf_op jit(solution)/shard_map/all_gather | solution.py:153
  195.5 22.7 %copy-start.17 = (pred[128,1024]{0,1:T(8,128)(4,1)}, pred[128,1024]{0,1:T(8,128)(4,1)S(1)}, u32[]{:S(2)}) copy-start(pred[128,1024]{0,1:T(8,128)(4,1)S(1)} %fusion.71) | copy-start | bytes 393220
  215.7 2.5 copy-start.34
  218.2 57.7 %copy-start.36 = (bf16[1,320,1280]{2,1,0:T(8,128)(2,1)S(1)}, bf16[1,320,1280]{2,1,0:T(8,128)(2,1)}, u32[]{:S(2)}) copy-start(bf16[1,320,1280]{2,1,0:T(8,128)(2,1)} %param.28) | copy-start | bytes 2457604
  220.1 95.2 %reduce-scatter.7.cloned.1.call-start = ((), (), s32[]{:S(2)}) async-start(), calls=%async_computation.17 | async-start | bytes 983040 | tf_op jit(solution)/shard_map/reduce_scatter | solution.py:45
  278.7 21.7 %copy-start.30 = (f32[1,1280]{1,0:T(1,128)S(1)}, f32[1,1280]{1,0:T(1,128)}, u32[]{:S(2)}) copy-start(f32[1,1280]{1,0:T(1,128)} %param.26) | copy-start | bytes 15364
  278.7 36.5 %copy-start.3 = (bf16[1,128,1280]{2,1,0:T(8,128)(2,1)S(1)}, bf16[1,128,1280]{2,1,0:T(8,128)(2,1)}, u32[]{:S(2)}) copy-start(bf16[1,128,1280]{2,1,0:T(8,128)(2,1)} %param.21) | copy-start | bytes 983044
  300.4 167.4 %all-gather.16.cloned.1.call-start = ((), (), s32[]{:S(2)}) async-start(), calls=%async_computation.18 | async-start | bytes 5898240 | tf_op jit(solution)/shard_map/all_gather | solution.py:161
  316.4 14.9 %copy-start.5 = (bf16[128,1280]{1,0:T(8,128)(2,1)}, bf16[128,1280]{1,0:T(8,128)(2,1)S(1)}, u32[]{:S(2)}) copy-start(bf16[128,1280]{1,0:T(8,128)(2,1)S(1)} %get-tuple-element.53) | copy-start | bytes 983044
  321.5 0.7 copy-start.7
  339.9 5.7 copy-start.21
  339.9 13.0 %copy-start.1 = (bf16[128,2560]{1,0:T(8,128)(2,1)S(1)}, bf16[128,2560]{1,0:T(8,128)(2,1)}, u32[]{:S(2)}) copy-start(bf16[128,2560]{1,0:T(8,128)(2,1)} %all_gather.48) | copy-start | bytes 1966084
  339.9 107.7 %all-to-all-start.1 = ((bf16[320,2,1536]{0,1,2:T(2,128)(2,1)}), bf16[320,2,1536]{0,1,2:T(2,128)(2,1)}, u32[]{:S(2)}, u32[]{:S(2)}) async-start(bf16[320,2,1536]{0,1,2:T(2,128)(2,1)} %bitcast.242), calls=%async_computation.2 | async-start | bytes 4718592 | tf_op jit(solution)/shard_map/all_to_all | solution.py:90
  347.7 2.6 copy-start.28
  350.2 7.1 copy-start.26
  352.9 4.4 copy-start.19
  447.6 104.0 %all-to-all-start.3 = ((bf16[8,80,2560]{2,1,0:T(8,128)(2,1)}), bf16[8,80,2560]{2,1,0:T(8,128)(2,1)}, u32[]{:S(2)}, u32[]{:S(2)}) async-start(bf16[8,80,2560]{2,1,0:T(8,128)(2,1)} %broadcast_select_fusion.1), calls=%async_computation.5 | async-start | bytes 6553600 | tf_op jit(solution)/shard_map/all_to_all | solution.py:200
  452.1 114.5 %all-gather.18.cloned.1.call-start = ((), (), s32[]{:S(2)}) async-start(), calls=%async_computation.19 | async-start | bytes 3538944 | tf_op jit(solution)/shard_map/all_gather | solution.py:170
  474.1 138.2 %reduce-scatter.11.cloned.1.call-start = ((), (), s32[]{:S(2)}) async-start(), calls=%async_computation.21 | async-start | bytes 4915200 | tf_op jit(solution)/shard_map/reduce_scatter | solution.py:61
  560.2 2.1 copy-start.32
  570.7 50.5 %copy-start.29 = (s32[512,1]{0,1:T(1,128)S(1)}, s32[512,1]{0,1:T(1,128)}, u32[]{:S(2)}) copy-start(s32[512,1]{0,1:T(1,128)} %copy-done.28) | copy-start | bytes 6148
  570.7 50.6 %copy-start.8 = (bf16[128,1280]{1,0:T(8,128)(2,1)S(1)}, bf16[128,1280]{1,0:T(8,128)(2,1)}, u32[]{:S(2)}) copy-start(bf16[128,1280]{1,0:T(8,128)(2,1)} %copy-done.7) | copy-start | bytes 983044
  570.7 50.6 %copy-start.16 = (f32[1,1280,8]{1,2,0:T(8,128)S(1)}, f32[1,1280,8]{1,2,0:T(8,128)}, u32[]{:S(2)}) copy-start(f32[1,1280,8]{1,2,0:T(8,128)} %param.31) | copy-start | bytes 122884
  570.7 55.9 %copy-start.22 = (s32[1,1,128,4]{2,3,1,0:T(4,128)S(1)}, s32[1,1,128,4]{2,3,1,0:T(4,128)}, u32[]{:S(2)}) copy-start(s32[1,1,128,4]{2,3,1,0:T(4,128)} %param.24) | copy-start | bytes 6148
  570.7 41.6 %all-to-all-start.2 = ((bf16[8,128,320]{1,2,0:T(8,128)(2,1)}), bf16[8,128,320]{1,2,0:T(8,128)(2,1)S(1)}, u32[]{:S(2)}, u32[]{:S(2)}) async-start(bf16[8,128,320]{1,2,0:T(8,128)(2,1)} %bitcast.232), calls=%async_computation.3 | async-start | bytes 1310720 | tf_op jit(solution)/shard_map/all_to_all | solution.py:44
  612.3 0.8 copy-start.10
  613.2 43.9 %all-to-all-start.4 = ((bf16[8,80,1280]{2,1,0:T(8,128)(2,1)}), bf16[8,80,1280]{2,1,0:T(8,128)(2,1)S(1)}, u32[]{:S(2)}, u32[]{:S(2)}) async-start(bf16[8,80,1280]{2,1,0:T(8,128)(2,1)} %reduce-scatter.11.cloned.1.call-done), calls=%async_computation.7 | async-start | bytes 3276800 | tf_op jit(solution)/shard_map/all_to_all | solution.py:64
  618.7 48.5 %reduce-scatter.9.cloned.1.call-start = ((), (), s32[]{:S(2)}) async-start(), calls=%async_computation.20 | async-start | bytes 983040 | tf_op jit(solution)/shard_map/reduce_scatter | solution.py:45
  621.0 110.1 %all-gather.20.cloned.1.call-start = ((), (), s32[]{:S(2)}) async-start(), calls=%async_computation.22 | async-start | bytes 1179648 | tf_op jit(solution)/shard_map/all_gather | solution.py:130
  621.3 38.7 %copy-start.24 = (s32[1024]{0:T(1024)}, s32[1024]{0:T(1024)S(1)}, u32[]{:S(2)}) copy-start(s32[1024]{0:T(1024)S(1)} %pad_clamp_fusion) | copy-start | bytes 12292
  660.0 7.2 copy-start.6
  663.7 7.1 copy-start.4
  668.3 2.8 copy-start.12
  668.3 2.5 collective-permute-start
  691.9 41.7 %copy-start.14 = (bf16[128,2,128]{0,2,1:T(8,128)(2,1)}, bf16[128,2,128]{0,2,1:T(8,128)(2,1)S(1)}, u32[]{:S(2)}) copy-start(bf16[128,2,128]{0,2,1:T(8,128)(2,1)S(1)} %pad_maximum_fusion.3) | copy-start | bytes 196612
  692.6 98.8 %all-gather.22.cloned.1.call-start = ((), (), s32[]{:S(2)}) async-start(), calls=%async_computation.23 | async-start | bytes 2949120 | tf_op jit(solution)/shard_map/all_gather | solution.py:153
  731.0 2.5 copy-start.18
  731.0 2.5 copy-start.35
  733.6 57.7 %copy-start.37 = (bf16[1,320,1280]{2,1,0:T(8,128)(2,1)S(1)}, bf16[1,320,1280]{2,1,0:T(8,128)(2,1)}, u32[]{:S(2)}) copy-start(bf16[1,320,1280]{2,1,0:T(8,128)(2,1)} %param.28) | copy-start | bytes 2457604
  735.4 95.1 %reduce-scatter.13.cloned.1.call-start = ((), (), s32[]{:S(2)}) async-start(), calls=%async_computation.24 | async-start | bytes 983040 | tf_op jit(solution)/shard_map/reduce_scatter | solution.py:45
  794.2 52.7 %copy-start.20 = (s32[1024]{0:T(1024)S(1)}, s32[1024]{0:T(1024)}, u32[]{:S(2)}) copy-start(s32[1024]{0:T(1024)} %copy-done.19) | copy-start | bytes 12292
  815.8 177.7 %all-gather.24.cloned.1.call-start = ((), (), s32[]{:S(2)}) async-start(), calls=%async_computation.25 | async-start | bytes 5898240 | tf_op jit(solution)/shard_map/all_gather | solution.py:161
  846.9 1.1 copy-start.2
  847.9 4.4 copy-start.27
  856.3 143.5 %all-to-all-start.7 = ((bf16[8,80,2560]{2,1,0:T(8,128)(2,1)}), bf16[8,80,2560]{2,1,0:T(8,128)(2,1)}, u32[]{:S(2)}, u32[]{:S(2)}) async-start(bf16[8,80,2560]{2,1,0:T(8,128)(2,1)} %broadcast_select_fusion), calls=%async_computation.12 | async-start | bytes 6553600 | tf_op jit(solution)/shard_map/all_to_all | solution.py:200
  861.8 197.3 %all-gather.26.cloned.1.call-start = ((), (), s32[]{:S(2)}) async-start(), calls=%async_computation.26 | async-start | bytes 3538944 | tf_op jit(solution)/shard_map/all_gather | solution.py:170
  999.8 104.8 %reduce-scatter.17.cloned.1.call-start = ((), (), s32[]{:S(2)}) async-start(), calls=%async_computation.28 | async-start | bytes 4915200 | tf_op jit(solution)/shard_map/reduce_scatter | solution.py:61
  1008.4 2.1 copy-start.33
  1063.1 53.3 %copy-start.15 = (bf16[128,2,128]{0,2,1:T(8,128)(2,1)S(1)}, bf16[128,2,128]{0,2,1:T(8,128)(2,1)}, u32[]{:S(2)}) copy-start(bf16[128,2,128]{0,2,1:T(8,128)(2,1)} %copy-done.14) | copy-start | bytes 196612
  1063.1 41.5 %all-to-all-start.6 = ((bf16[8,128,320]{1,2,0:T(8,128)(2,1)}), bf16[8,128,320]{1,2,0:T(8,128)(2,1)S(1)}, u32[]{:S(2)}, u32[]{:S(2)}) async-start(bf16[8,128,320]{1,2,0:T(8,128)(2,1)} %bitcast.230), calls=%async_computation.10 | async-start | bytes 1310720 | tf_op jit(solution)/shard_map/all_to_all | solution.py:44
  1066.8 60.2 %copy-start.23 = (s32[1,1,128,4]{2,3,1,0:T(4,128)S(1)}, s32[1,1,128,4]{2,3,1,0:T(4,128)}, u32[]{:S(2)}) copy-start(s32[1,1,128,4]{2,3,1,0:T(4,128)} %param.24) | copy-start | bytes 6148
  1066.8 82.5 %copy-start.25 = (s32[1024]{0:T(1024)S(1)}, s32[1024]{0:T(1024)}, u32[]{:S(2)}) copy-start(s32[1024]{0:T(1024)} %copy-done.24) | copy-start | bytes 12292
  1104.6 0.8 copy-start.11
  1105.4 43.9 %all-to-all-start.8 = ((bf16[8,80,1280]{2,1,0:T(8,128)(2,1)}), bf16[8,80,1280]{2,1,0:T(8,128)(2,1)S(1)}, u32[]{:S(2)}, u32[]{:S(2)}) async-start(bf16[8,80,1280]{2,1,0:T(8,128)(2,1)} %reduce-scatter.17.cloned.1.call-done), calls=%async_computation.14 | async-start | bytes 3276800 | tf_op jit(solution)/shard_map/all_to_all | solution.py:64
  1111.0 48.4 %reduce-scatter.15.cloned.1.call-start = ((), (), s32[]{:S(2)}) async-start(), calls=%async_computation.27 | async-start | bytes 983040 | tf_op jit(solution)/shard_map/reduce_scatter | solution.py:45
  1152.2 7.2 copy-start.9
  1152.2 7.2 copy-start.13
Sparse Core Ops, SparseCore 0:
  10.2 137.5 all-gather.27
  177.9 37.8 all-gather.11
  220.2 55.7 all-gather.13
  300.5 14.6 reduce-scatter.6
  331.5 136.2 all-gather.15
  474.3 92.3 all-gather.17
  569.0 43.3 reduce-scatter.10
  621.8 16.4 reduce-scatter.8
  692.7 38.2 all-gather.19
  735.5 55.7 all-gather.21
  815.9 14.6 reduce-scatter.12
  847.0 146.3 all-gather.23
  999.9 59.0 all-gather.25
  1061.2 43.3 reduce-scatter.16
  1113.8 16.5 reduce-scatter.14

commit v2 on v1

--- a/solution.py
+++ b/solution.py
@@ -88,6 +88,7 @@
     out_local = w_out[0]
     shared_down_local = w_shared_down[0]
     shared_in_cols = lax.all_to_all(w_shared_in[0], "expert", split_axis=2, concat_axis=0, tiled=True)
+    qkv_full, shared_in_cols = lax.optimization_barrier((qkv_full, shared_in_cols))
     model_width, kv_local, group_cols = qkv_full.shape
     shared_cols = shared_in_cols.shape[2]
     head_width = HD
@@ -191,16 +192,26 @@
         onehot = (flat_choice[:, None] == expert_ids[None, :]).astype(jnp.int32)
         slot_rank = jnp.sum(onehot * (jnp.cumsum(onehot, axis=0) - onehot), axis=1)
         slot_ids = flat_choice * capacity + slot_rank
-        row_source = jnp.arange(tokens_dev * top_count, dtype=jnp.int32) // top_count
-        table = jnp.zeros((experts_count * capacity,), jnp.int32).at[slot_ids].set(row_source)
-        filled = jnp.zeros((experts_count * capacity,), jnp.bool_).at[slot_ids].set(True)
-        outgoing = jnp.where(filled[:, None], moe_rows[table], jnp.zeros((), jnp.bfloat16))
-        outgoing = outgoing.reshape(experts_count, capacity, model_width)
-        returned = expert_path(
-            lax.all_to_all(outgoing, "expert", split_axis=0, concat_axis=0, tiled=True),
-            w_in_local,
-            w_down_local,
-        )
+        choices_all = lax.all_gather(choices, "expert", axis=0, tiled=False)
+        mine = jnp.any(choices_all == expert_id, axis=2)
+        mine_rank = jnp.cumsum(mine.astype(jnp.int32), axis=1) - 1
+        source_ids = jnp.broadcast_to(
+            jnp.arange(experts_count, dtype=jnp.int32)[:, None], mine.shape
+        )
+        token_ids = jnp.broadcast_to(jnp.arange(tokens_dev, dtype=jnp.int32)[None, :], mine.shape)
+        rank_at = jnp.where(mine, mine_rank, capacity)
+        table = (
+            jnp.zeros((experts_count, capacity), jnp.int32)
+            .at[source_ids, rank_at]
+            .set(source_ids * tokens_dev + token_ids, mode="drop")
+        )
+        filled = (
+            jnp.zeros((experts_count, capacity), jnp.bool_)
+            .at[source_ids, rank_at]
+            .set(True, mode="drop")
+        )
+        incoming_rows = jnp.where(filled[..., None], moe_all[table], jnp.zeros((), jnp.bfloat16))
+        returned = expert_path(incoming_rows, w_in_local, w_down_local)
         combined = returned.reshape(experts_count * capacity, columns)[slot_ids].astype(jnp.float32)
         combined = combined * gate_weights.reshape(-1)[:, None]
         moe_out = jnp.sum(combined.reshape(tokens_dev, top_count, columns), axis=1)

time: 1180 us -> 1110 us (0.941)
  waiting for transfers between devices: 790 us -> 662 us
  blocking collectives: 126 us -> 152 us
  other arithmetic: 40.5 us -> 62.4 us
  local copies, waits for them, and re-layouts: 91.4 us -> 110 us
    all_to_all x2 -> x0, waiting for transfers between devices: 69.7 us -> none  [local(): lax.all_to_all(outgoing, 'expert', split_axis=0, concat_axis=0, tiled=True)]
    all_gather x1, waiting for transfers between devices: 119 us -> 72.8 us  [local(): qkv_full = lax.all_gather(w_qkv[0], 'expert', axis=0, tiled=True)]
    all_gather x2, waiting for transfers between devices: 141 us -> 173 us  [local(): moe_all = lax.all_gather(moe_rows, 'expert', axis=0, tiled=True)]
    all_gather x0 -> x1, blocking collectives: none -> 26.2 us  [local(): choices_all = lax.all_gather(choices, 'expert', axis=0, tiled=False)]
    reshape x2 -> x0, local copies, waits for them, and re-layouts: 25.7 us -> none  [the longest x1 23 us: local(): qkv_full.reshape(model_width, -1)]
    another operation x9 -> x10, other arithmetic: 3.8 us -> 27.8 us  [the longest x1 23.6 us: local(): mine_rank = jnp.cumsum(mine.astype(jnp.int32), axis=1) - 1]
    unnamed x79 -> x78, local copies, waits for them, and re-layouts: 23 us -> 40.8 us
    all_to_all x2, waiting for transfers between devices: 52.6 us -> 35.7 us  [expert_path(): lax.all_to_all(summed, 'expert', split_axis=0, concat_axis=0, tiled=True)]
  transfers between devices with their start and end apart: 23 -> 21, of which waited for: 18 -> 18; matrix products, arithmetic and copies ran while one was open for 11% -> 13% of each run, Pallas kernels for 0% -> 0%
where the time goes in v2:
time: 1110 us; the launch traced here: 1100 us
  waiting for transfers between devices  662 us (60%)
  blocking collectives  152 us (14%)
  local copies, waits for them, and re-layouts  110 us (10%)
  matrix products  68.9 us (6%)
  other arithmetic  62.4 us (6%)
  starting transfers between devices  28 us (3%)
  between operations  15.1 us (1%)
    all_gather x2, waiting for transfers between devices, local(): moe_all = lax.all_gather(moe_rows, 'expert', axis=0, tiled=True)  173 us
    all_gather x2, waiting for transfers between devices, local(): attended_all = lax.all_gather(attended, 'expert', axis=0, tiled=True)  112 us
    all_gather x1, waiting for transfers between devices, local(): qkv_full = lax.all_gather(w_qkv[0], 'expert', axis=0, tiled=True)  72.8 us
    all_to_all x1, waiting for transfers between devices, local(): lax.all_to_all(w_shared_in[0], 'expert', split_axis=2, concat_axis=0, til...  72.6 us
    reduce_scatter x2, waiting for transfers between devices, expert_path(): lax.psum_scatter(partial_value.astype(jnp.bfloat16), 'tensor', scatter_di...  72.3 us
    all_gather x2, waiting for transfers between devices, local(): lax.all_gather(cache.reshape(tokens_dev, -1), 'expert', axis=0, tiled=True)  58.4 us
    all_to_all x2, blocking collectives, terms_to_slots(): lax.all_to_all(terms, 'expert', split_axis=0, concat_axis=1, tiled=True)  40.8 us
    unnamed x78, local copies, waits for them, and re-layouts  40.8 us
  transfers between devices with their start and end apart: 21, of which 18 were waited for; matrix products, arithmetic and copies ran while one was open for 13% of the time, Pallas kernels for 0%

profile of v2, /device:TPU:0, one launch (start us, length us, event | category | flops | bytes accessed | tf_op | source)
XLA Modules:
  0.0 1098.1 jit_solution(8027213520705379425)
XLA Ops:
  7.9 8.5 copy.136
  16.4 7.4 all-to-all-start
  25.3 4.9 psum.42
  31.4 9.2 all_gather.47
  40.9 72.6 %all-to-all-done = bf16[320,2,1536]{0,1,2:T(2,128)(2,1)S(1)} async-done(((bf16[320,2,1536]{0,1,2:T(2,128)(2,1)}), bf16[320,2,1536]{0,1,2:T(2,128)(2,1)S(1)}, u32[]{:S(2)}, u32[]{:S(2)}) %all-to-all-start) | async-done | bytes 1966112 | tf_op jit(solution)/shard_map/all_to_all | solution.py:90
  115.1 2.7 all_to_all.78
  117.8 72.8 %all-gather.29.cloned.1.call-done = bf16[1,2560,2,896]{3,2,0,1:T(2,128)(2,1)} async-done(((bf16[1,320,2,896]{3,2,0,1:T(2,128)(2,1)}), bf16[1,2560,2,896]{3,2,0,1:T(2,128)(2,1)}) %all-gather.29.cloned.1.call-update) | async-done | bytes 9175056 | tf_op jit(solution)/shard_map/all_gather | solution.py:87
  190.6 8.7 copy.189
  199.3 12.9 %copy.139 = bf16[1792,2560]{1,0:T(8,128)(2,1)} copy(bf16[1792,2560]{0,1:T(8,128)(2,1)} %bitcast.248) | data formatting | bytes 18350080 | tf_op jit(solution)/shard_map/dot_general | solution.py:121
  212.2 6.1 fusion.66
  219.2 17.5 %all-gather.1 = s32[1,1024]{1,0:T(1,128)S(1)} all-gather(s32[1,128]{1,0:T(1,128)S(1)} %copy-done.24), channel_id=3, replica_groups=mesh['section'=2,'expert'=8,'tensor'=2] {'expert'}, dimensions={1}, use_global_device_ids=true | all-gather | bytes 4608 | tf_op jit(solution)/shard_map/all_gather | solution.py:132
  237.0 20.1 %all-gather.13.cloned.1.call-done = bf16[1024,512]{0,1:T(8,128)(2,1)} async-done(((bf16[128,512]{0,1:T(8,128)(2,1)}), bf16[1024,512]{0,1:T(8,128)(2,1)}) %all-gather.13.cloned.1.call-update) | async-done | bytes 1048592 | tf_op jit(solution)/shard_map/all_gather | solution.py:131
  261.5 55.9 %all-gather.15.cloned.1.call-done = bf16[1024,1280]{0,1:T(8,128)(2,1)} async-done(((bf16[128,1280]{0,1:T(8,128)(2,1)}), bf16[1024,1280]{0,1:T(8,128)(2,1)}) %all-gather.15.cloned.1.call-update) | async-done | bytes 2621456 | tf_op jit(solution)/shard_map/all_gather | solution.py:154
  317.3 2.8 fusion.26
  320.3 20.4 %all_to_all.104 = bf16[8,128,320]{1,2,0:T(8,128)(2,1)S(1)} all-to-all(bf16[8,128,320]{1,2,0:T(8,128)(2,1)S(1)} %bitcast.261), channel_id=1, replica_groups=mesh['section'=2,'expert'=8,'tensor'=2] {'expert'}, dimensions={0} | all-to-all | bytes 1310720 | tf_op jit(solution)/shard_map/all_to_all | solution.py:44
  341.9 14.7 %reduce-scatter.7.cloned.1.call-done = bf16[128,1280]{1,0:T(8,128)(2,1)} async-done(((bf16[128,2560]{1,0:T(8,128)(2,1)}), bf16[128,1280]{1,0:T(8,128)(2,1)}) %reduce-scatter.7.cloned.1.call-update) | async-done | bytes 327696 | tf_op jit(solution)/shard_map/reduce_scatter | solution.py:45
  357.8 4.9 psum.43
  363.6 9.1 all_gather.52
  373.0 86.2 %all-gather.17.cloned.1.call-done = bf16[1024,2560]{1,0:T(8,128)(2,1)} async-done(((bf16[128,2560]{1,0:T(8,128)(2,1)}), bf16[1024,2560]{1,0:T(8,128)(2,1)}) %all-gather.17.cloned.1.call-update) | async-done | bytes 5242896 | tf_op jit(solution)/shard_map/all_gather | solution.py:162
  459.1 5.3 fusion.97
  465.6 26.2 %all-gather.2 = s32[8,1,128,4]{2,3,1,0:T(4,128)S(1)} all-gather(s32[1,1,128,4]{2,3,1,0:T(4,128)S(1)} %copy-done.15), channel_id=4, replica_groups=mesh['section'=2,'expert'=8,'tensor'=2] {'expert'}, dimensions={0}, use_global_device_ids=true | all-gather | bytes 18432 | tf_op jit(solution)/shard_map/all_gather | solution.py:195
  492.3 23.6 %compare_select_fusion = s32[8,128,1]{2,0,1:T(8,128)S(1)} fusion(pred[8,128,1]{2,0,1:T(8,128)(4,1)S(1)} %copy.148, s32[8,128,1]{2,0,1:T(8,128)S(1)} %copy.147), kind=kOutput, calls=%fused_computation.32 | output fusion | flops 135168 | bytes 9216 | tf_op jit(solution)/shard_map/jit(cumsum)/reduce_window_sum | solution.py:197
  516.8 4.3 scatter_custom_fusion.1
  521.1 4.7 scatter_custom_fusion
  526.1 7.7 copy.190
  533.8 11.3 %gather_fusion = bf16[640,2560]{1,0:T(8,128)(2,1)} fusion(bf16[1024,2560]{1,0:T(8,128)(2,1)} %all-gather.17.cloned.1.call-done, s32[1024]{0:T(1024)S(1)} %pad_clamp_fusion.1), kind=kCustom, calls=%fused_computation | custom fusion | bytes 6556160 | tf_op jit(solution)/shard_map/gather | solution.py:213
  547.4 7.6 fusion.98
  557.0 4.1 convolution_convert_fusion.1
  561.3 3.1 fusion.18
  565.3 3.5 all-to-all-start.2
  568.9 34.5 %reduce-scatter.11.cloned.1.call-done = bf16[8,80,1280]{2,1,0:T(8,128)(2,1)} async-done(((bf16[8,80,2560]{2,1,0:T(8,128)(2,1)}), bf16[8,80,1280]{2,1,0:T(8,128)(2,1)}) %reduce-scatter.11.cloned.1.call-update) | async-done | bytes 1638416 | tf_op jit(solution)/shard_map/reduce_scatter | solution.py:61
  604.3 5.5 all-to-all-start.3
  624.0 5.2 psum.44
  631.5 16.7 %all-to-all-done.3 = bf16[8,80,1280]{2,1,0:T(8,128)(2,1)S(1)} async-done(((bf16[8,80,1280]{2,1,0:T(8,128)(2,1)}), bf16[8,80,1280]{2,1,0:T(8,128)(2,1)S(1)}, u32[]{:S(2)}, u32[]{:S(2)}) %all-to-all-start.3) | async-done | bytes 1638432 | tf_op jit(solution)/shard_map/all_to_all | solution.py:64
  648.2 3.0 gather_fusion.1
  651.2 3.7 reshape.841
  654.9 3.4 multiply_reduce_fusion.1
  661.2 5.0 psum.45
  666.3 9.5 all_gather.56
  675.8 6.1 fusion.64
  682.9 38.3 %all-gather.21.cloned.1.call-done = bf16[1024,512]{0,1:T(8,128)(2,1)} async-done(((bf16[128,512]{0,1:T(8,128)(2,1)}), bf16[1024,512]{0,1:T(8,128)(2,1)}) %all-gather.21.cloned.1.call-update) | async-done | bytes 1048592 | tf_op jit(solution)/shard_map/all_gather | solution.py:131
  725.6 55.9 %all-gather.23.cloned.1.call-done = bf16[1024,1280]{0,1:T(8,128)(2,1)} async-done(((bf16[128,1280]{0,1:T(8,128)(2,1)}), bf16[1024,1280]{0,1:T(8,128)(2,1)}) %all-gather.23.cloned.1.call-update) | async-done | bytes 2621456 | tf_op jit(solution)/shard_map/all_gather | solution.py:154
  781.5 2.8 fusion.27
  784.4 20.4 %all_to_all.105 = bf16[8,128,320]{1,2,0:T(8,128)(2,1)S(1)} all-to-all(bf16[8,128,320]{1,2,0:T(8,128)(2,1)S(1)} %bitcast.263), channel_id=1, replica_groups=mesh['section'=2,'expert'=8,'tensor'=2] {'expert'}, dimensions={0} | all-to-all | bytes 1310720 | tf_op jit(solution)/shard_map/all_to_all | solution.py:44
  805.9 14.7 %reduce-scatter.13.cloned.1.call-done = bf16[128,1280]{1,0:T(8,128)(2,1)} async-done(((bf16[128,2560]{1,0:T(8,128)(2,1)}), bf16[128,1280]{1,0:T(8,128)(2,1)}) %reduce-scatter.13.cloned.1.call-update) | async-done | bytes 327696 | tf_op jit(solution)/shard_map/reduce_scatter | solution.py:45
  821.9 4.9 psum.46
  827.9 9.1 all_gather.59
  837.1 86.4 %all-gather.25.cloned.1.call-done = bf16[1024,2560]{1,0:T(8,128)(2,1)} async-done(((bf16[128,2560]{1,0:T(8,128)(2,1)}), bf16[1024,2560]{1,0:T(8,128)(2,1)}) %all-gather.25.cloned.1.call-update) | async-done | bytes 5242896 | tf_op jit(solution)/shard_map/all_gather | solution.py:162
  923.4 5.3 fusion.99
  930.1 11.3 %gather_fusion.2 = bf16[640,2560]{1,0:T(8,128)(2,1)} fusion(bf16[1024,2560]{1,0:T(8,128)(2,1)} %all-gather.25.cloned.1.call-done, s32[1024]{0:T(1024)S(1)} %copy-done.18), kind=kCustom, calls=%fused_computation.2 | custom fusion | bytes 6556160 | tf_op jit(solution)/shard_map/gather | solution.py:213
  943.7 7.6 fusion.100
  953.4 4.1 convolution_convert_fusion
  957.5 31.1 %all-gather.27.cloned.1.call-done = bf16[1024,1536]{0,1:T(8,128)(2,1)} async-done(((bf16[1024,192]{0,1:T(8,128)(2,1)}), bf16[1024,1536]{0,1:T(8,128)(2,1)}) %all-gather.27.cloned.1.call-update) | async-done | bytes 3145744 | tf_op jit(solution)/shard_map/all_gather | solution.py:171
  988.6 3.1 fusion.19
  992.7 3.7 all-to-all-start.5
  996.4 37.8 %reduce-scatter.17.cloned.1.call-done = bf16[8,80,1280]{2,1,0:T(8,128)(2,1)} async-done(((bf16[8,80,2560]{2,1,0:T(8,128)(2,1)}), bf16[8,80,1280]{2,1,0:T(8,128)(2,1)}) %reduce-scatter.17.cloned.1.call-update) | async-done | bytes 1638416 | tf_op jit(solution)/shard_map/reduce_scatter | solution.py:61
  1035.0 5.5 all-to-all-start.6
  1046.8 3.6 broadcast_select_fusion.5
  1051.5 5.3 psum.47
  1056.9 3.0 reduce-scatter.15.cloned.1.call-done
  1060.0 19.0 %all-to-all-done.6 = bf16[8,80,1280]{2,1,0:T(8,128)(2,1)S(1)} async-done(((bf16[8,80,1280]{2,1,0:T(8,128)(2,1)}), bf16[8,80,1280]{2,1,0:T(8,128)(2,1)S(1)}, u32[]{:S(2)}, u32[]{:S(2)}) %all-to-all-start.6) | async-done | bytes 1638432 | tf_op jit(solution)/shard_map/all_to_all | solution.py:64
  1078.9 2.9 gather_fusion.3
  1081.8 3.8 reshape.842
  1085.6 3.4 multiply_reduce_fusion
  (211 shorter events, 68.7 us)
Async XLA Ops:
  7.2 554.1 %copy-start = (bf16[1,320,1536]{2,1,0:T(8,128)(2,1)S(1)}, bf16[1,320,1536]{2,1,0:T(8,128)(2,1)}, u32[]{:S(2)}) copy-start(bf16[1,320,1536]{2,1,0:T(8,128)(2,1)} %param.30) | copy-start | bytes 2949124
  7.2 183.4 %all-gather.29.cloned.1.call-start = ((), (), s32[]{:S(2)}) async-start(), calls=%async_computation.27 | async-start | bytes 10321920 | tf_op jit(solution)/shard_map/all_gather | solution.py:87
  16.4 7.5 copy-start.33
  16.4 7.7 copy-start.22
  16.4 13.8 %copy-start.24 = (s32[1,128]{1,0:T(1,128)S(1)}, s32[1,128]{1,0:T(1,128)}, u32[]{:S(2)}) copy-start(s32[1,128]{1,0:T(1,128)} %param.22) | copy-start | bytes 1540
  16.4 97.0 %all-to-all-start = ((bf16[320,2,1536]{0,1,2:T(2,128)(2,1)}), bf16[320,2,1536]{0,1,2:T(2,128)(2,1)S(1)}, u32[]{:S(2)}, u32[]{:S(2)}) async-start(bf16[320,2,1536]{0,1,2:T(2,128)(2,1)} %bitcast.251), calls=%async_computation | async-start | bytes 4718592 | tf_op jit(solution)/shard_map/all_to_all | solution.py:90
  23.9 233.2 %all-gather.13.cloned.1.call-start = ((), (), s32[]{:S(2)}) async-start(), calls=%async_computation.13 | async-start | bytes 1179648 | tf_op jit(solution)/shard_map/all_gather | solution.py:131
  199.3 12.9 %copy-start.4 = (bf16[128,2560]{1,0:T(8,128)(2,1)S(1)}, bf16[128,2560]{1,0:T(8,128)(2,1)}, u32[]{:S(2)}) copy-start(bf16[128,2560]{1,0:T(8,128)(2,1)} %all_gather.47) | copy-start | bytes 1966084
  219.1 98.2 %all-gather.15.cloned.1.call-start = ((), (), s32[]{:S(2)}) async-start(), calls=%async_computation.14 | async-start | bytes 2949120 | tf_op jit(solution)/shard_map/all_gather | solution.py:154
  236.9 22.7 %copy-start.13 = (pred[128,1024]{0,1:T(8,128)(4,1)}, pred[128,1024]{0,1:T(8,128)(4,1)S(1)}, u32[]{:S(2)}) copy-start(pred[128,1024]{0,1:T(8,128)(4,1)S(1)} %fusion.71) | copy-start | bytes 393220
  257.1 2.5 copy-start.29
  259.6 57.7 %copy-start.31 = (bf16[1,320,1280]{2,1,0:T(8,128)(2,1)S(1)}, bf16[1,320,1280]{2,1,0:T(8,128)(2,1)}, u32[]{:S(2)}) copy-start(bf16[1,320,1280]{2,1,0:T(8,128)(2,1)} %param.28) | copy-start | bytes 2457604
  261.4 95.2 %reduce-scatter.7.cloned.1.call-start = ((), (), s32[]{:S(2)}) async-start(), calls=%async_computation.15 | async-start | bytes 983040 | tf_op jit(solution)/shard_map/reduce_scatter | solution.py:45
  320.1 21.7 %copy-start.23 = (f32[1,1280]{1,0:T(1,128)S(1)}, f32[1,1280]{1,0:T(1,128)}, u32[]{:S(2)}) copy-start(f32[1,1280]{1,0:T(1,128)} %param.26) | copy-start | bytes 15364
  320.1 36.5 %copy-start.1 = (bf16[1,128,1280]{2,1,0:T(8,128)(2,1)S(1)}, bf16[1,128,1280]{2,1,0:T(8,128)(2,1)}, u32[]{:S(2)}) copy-start(bf16[1,128,1280]{2,1,0:T(8,128)(2,1)} %param.21) | copy-start | bytes 983044
  341.8 117.4 %all-gather.17.cloned.1.call-start = ((), (), s32[]{:S(2)}) async-start(), calls=%async_computation.16 | async-start | bytes 5898240 | tf_op jit(solution)/shard_map/all_gather | solution.py:162
  362.9 0.7 copy-start.2
  372.7 188.5 %all-gather.19.cloned.1.call-start = ((), (), s32[]{:S(2)}) async-start(), calls=%async_computation.17 | async-start | bytes 3538944 | tf_op jit(solution)/shard_map/all_gather | solution.py:171
  459.1 6.4 copy-start.15
  464.5 51.7 %copy-start.26 = (s32[2]{0:T(128)S(1)}, s32[2]{0:T(128)}, u32[]{:S(2)}) copy-start(s32[2]{0:T(128)} %constant.173) | copy-start | bytes 28
  464.5 51.9 %copy-start.25 = (s32[2]{0:T(128)S(1)}, s32[2]{0:T(128)}, u32[]{:S(2)}) copy-start(s32[2]{0:T(128)} %constant.170) | copy-start | bytes 28
  465.5 137.9 %reduce-scatter.11.cloned.1.call-start = ((), (), s32[]{:S(2)}) async-start(), calls=%async_computation.19 | async-start | bytes 4915200 | tf_op jit(solution)/shard_map/reduce_scatter | solution.py:61
  525.9 19.2 %copy-start.20 = (pred[8,80]{1,0:T(8,128)(4,1)}, pred[8,80]{1,0:T(8,128)(4,1)S(1)}, u32[]{:S(2)}) copy-start(pred[8,80]{1,0:T(8,128)(4,1)S(1)} %reshape.836) | copy-start | bytes 1924
  533.8 11.4 %copy-start.17 = (s32[1024]{0:T(1024)}, s32[1024]{0:T(1024)S(1)}, u32[]{:S(2)}) copy-start(s32[1024]{0:T(1024)S(1)} %pad_clamp_fusion.1) | copy-start | bytes 12292
  554.9 2.1 copy-start.27
  565.3 38.1 %all-to-all-start.2 = ((bf16[8,128,320]{1,2,0:T(8,128)(2,1)}), bf16[8,128,320]{1,2,0:T(8,128)(2,1)S(1)}, u32[]{:S(2)}, u32[]{:S(2)}) async-start(bf16[8,128,320]{1,2,0:T(8,128)(2,1)} %bitcast.240), calls=%async_computation.3 | async-start | bytes 1310720 | tf_op jit(solution)/shard_map/all_to_all | solution.py:44
  603.4 0.9 copy-start.5
  604.3 43.9 %all-to-all-start.3 = ((bf16[8,80,1280]{2,1,0:T(8,128)(2,1)}), bf16[8,80,1280]{2,1,0:T(8,128)(2,1)S(1)}, u32[]{:S(2)}, u32[]{:S(2)}) async-start(bf16[8,80,1280]{2,1,0:T(8,128)(2,1)} %reduce-scatter.11.cloned.1.call-done), calls=%async_computation.6 | async-start | bytes 3276800 | tf_op jit(solution)/shard_map/all_to_all | solution.py:64
  609.8 21.7 %reduce-scatter.9.cloned.1.call-start = ((), (), s32[]{:S(2)}) async-start(), calls=%async_computation.18 | async-start | bytes 983040 | tf_op jit(solution)/shard_map/reduce_scatter | solution.py:45
  614.8 106.4 %all-gather.21.cloned.1.call-start = ((), (), s32[]{:S(2)}) async-start(), calls=%async_computation.20 | async-start | bytes 1179648 | tf_op jit(solution)/shard_map/all_gather | solution.py:131
  651.2 7.1 copy-start.11
  658.4 2.8 copy-start.7
  658.4 2.5 collective-permute-start
  682.0 41.7 %copy-start.9 = (bf16[128,2,128]{0,2,1:T(8,128)(2,1)}, bf16[128,2,128]{0,2,1:T(8,128)(2,1)S(1)}, u32[]{:S(2)}) copy-start(bf16[128,2,128]{0,2,1:T(8,128)(2,1)S(1)} %pad_maximum_fusion.3) | copy-start | bytes 196612
  682.7 98.7 %all-gather.23.cloned.1.call-start = ((), (), s32[]{:S(2)}) async-start(), calls=%async_computation.21 | async-start | bytes 2949120 | tf_op jit(solution)/shard_map/all_gather | solution.py:154
  721.2 2.5 copy-start.14
  721.2 2.5 copy-start.30
  723.7 57.7 %copy-start.32 = (bf16[1,320,1280]{2,1,0:T(8,128)(2,1)S(1)}, bf16[1,320,1280]{2,1,0:T(8,128)(2,1)}, u32[]{:S(2)}) copy-start(bf16[1,320,1280]{2,1,0:T(8,128)(2,1)} %param.28) | copy-start | bytes 2457604
  725.6 95.1 %reduce-scatter.13.cloned.1.call-start = ((), (), s32[]{:S(2)}) async-start(), calls=%async_computation.22 | async-start | bytes 983040 | tf_op jit(solution)/shard_map/reduce_scatter | solution.py:45
  805.9 117.5 %all-gather.25.cloned.1.call-start = ((), (), s32[]{:S(2)}) async-start(), calls=%async_computation.23 | async-start | bytes 5898240 | tf_op jit(solution)/shard_map/all_gather | solution.py:162
  837.0 93.1 %copy-start.18 = (s32[1024]{0:T(1024)S(1)}, s32[1024]{0:T(1024)}, u32[]{:S(2)}) copy-start(s32[1024]{0:T(1024)} %copy-done.17) | copy-start | bytes 12292
  837.0 151.6 %all-gather.27.cloned.1.call-start = ((), (), s32[]{:S(2)}) async-start(), calls=%async_computation.24 | async-start | bytes 3538944 | tf_op jit(solution)/shard_map/all_gather | solution.py:171
  929.8 11.6 %copy-start.21 = (pred[8,80]{1,0:T(8,128)(4,1)S(1)}, pred[8,80]{1,0:T(8,128)(4,1)}, u32[]{:S(2)}) copy-start(pred[8,80]{1,0:T(8,128)(4,1)} %copy-done.20) | copy-start | bytes 1924
  929.8 104.3 %reduce-scatter.17.cloned.1.call-start = ((), (), s32[]{:S(2)}) async-start(), calls=%async_computation.26 | async-start | bytes 4915200 | tf_op jit(solution)/shard_map/reduce_scatter | solution.py:61
  951.2 2.1 copy-start.28
  992.7 54.0 %copy-start.10 = (bf16[128,2,128]{0,2,1:T(8,128)(2,1)S(1)}, bf16[128,2,128]{0,2,1:T(8,128)(2,1)}, u32[]{:S(2)}) copy-start(bf16[128,2,128]{0,2,1:T(8,128)(2,1)} %copy-done.9) | copy-start | bytes 196612
  992.7 41.5 %all-to-all-start.5 = ((bf16[8,128,320]{1,2,0:T(8,128)(2,1)}), bf16[8,128,320]{1,2,0:T(8,128)(2,1)S(1)}, u32[]{:S(2)}, u32[]{:S(2)}) async-start(bf16[8,128,320]{1,2,0:T(8,128)(2,1)} %bitcast.238), calls=%async_computation.9 | async-start | bytes 1310720 | tf_op jit(solution)/shard_map/all_to_all | solution.py:44
  996.4 60.4 %copy-start.16 = (s32[1,1,128,4]{2,3,1,0:T(4,128)S(1)}, s32[1,1,128,4]{2,3,1,0:T(4,128)}, u32[]{:S(2)}) copy-start(s32[1,1,128,4]{2,3,1,0:T(4,128)} %param.24) | copy-start | bytes 6148
  996.4 82.5 %copy-start.19 = (s32[1024]{0:T(1024)S(1)}, s32[1024]{0:T(1024)}, u32[]{:S(2)}) copy-start(s32[1024]{0:T(1024)} %pad_clamp_fusion) | copy-start | bytes 12292
  1034.2 0.9 copy-start.6
  1035.0 43.9 %all-to-all-start.6 = ((bf16[8,80,1280]{2,1,0:T(8,128)(2,1)}), bf16[8,80,1280]{2,1,0:T(8,128)(2,1)S(1)}, u32[]{:S(2)}, u32[]{:S(2)}) async-start(bf16[8,80,1280]{2,1,0:T(8,128)(2,1)} %reduce-scatter.17.cloned.1.call-done), calls=%async_computation.12 | async-start | bytes 3276800 | tf_op jit(solution)/shard_map/all_to_all | solution.py:64
  1040.5 19.4 %reduce-scatter.15.cloned.1.call-start = ((), (), s32[]{:S(2)}) async-start(), calls=%async_computation.25 | async-start | bytes 983040 | tf_op jit(solution)/shard_map/reduce_scatter | solution.py:45
  1081.8 7.1 copy-start.3
  1081.8 7.2 copy-start.8
  1081.8 7.2 copy-start.12
Sparse Core Ops, SparseCore 0:
  10.2 180.3 all-gather.28
  219.2 37.8 all-gather.12
  261.6 55.7 all-gather.14
  341.9 14.6 reduce-scatter.6
  372.8 86.2 all-gather.16
  465.6 58.8 all-gather.18
  561.3 42.0 reduce-scatter.10
  614.9 16.5 reduce-scatter.8
  682.9 38.2 all-gather.20
  725.7 55.7 all-gather.22
  806.0 14.6 reduce-scatter.12
  837.1 86.2 all-gather.24
  929.9 58.6 all-gather.26
  990.7 43.3 reduce-scatter.16
  1043.4 16.5 reduce-scatter.14

commit v3 on v2

--- a/solution.py
+++ b/solution.py
@@ -88,7 +88,10 @@
     out_local = w_out[0]
     shared_down_local = w_shared_down[0]
     shared_in_cols = lax.all_to_all(w_shared_in[0], "expert", split_axis=2, concat_axis=0, tiled=True)
-    qkv_full, shared_in_cols = lax.optimization_barrier((qkv_full, shared_in_cols))
+    choices_every = lax.all_gather(expert_choice[0], "expert", axis=0, tiled=False)
+    qkv_full, shared_in_cols, choices_every = lax.optimization_barrier(
+        (qkv_full, shared_in_cols, choices_every)
+    )
     model_width, kv_local, group_cols = qkv_full.shape
     shared_cols = shared_in_cols.shape[2]
     head_width = HD
@@ -129,10 +132,12 @@
             [key_rows.reshape(tokens_dev, -1), value_rows.reshape(tokens_dev, -1)], axis=1
         )
         kv_piece = lax.all_gather(cache.reshape(tokens_dev, -1), "expert", axis=0, tiled=True)
-        seg_piece = lax.all_gather(segments, "expert", axis=0, tiled=True)
         key_count = kv_piece.shape[0]
         kv_piece = kv_piece.reshape(key_count, 2, kv_local, head_width)
         key_slots = jnp.arange(key_count, dtype=jnp.int32)
+        ends = jnp.cumsum(lengths)
+        seg_piece = jnp.sum((key_slots[:, None] >= ends[None, :]).astype(jnp.int32), axis=1)
+        seg_piece = jnp.where(key_slots < ends[-1], seg_piece, -1)
         allowed = (segments[:, None] == seg_piece[None, :]) & (segments[:, None] >= 0) & (
             key_slots[None, :] <= slot_index[:, None]
         ) | (key_slots[None, :] == slot_index[:, None])
@@ -192,7 +197,7 @@
         onehot = (flat_choice[:, None] == expert_ids[None, :]).astype(jnp.int32)
         slot_rank = jnp.sum(onehot * (jnp.cumsum(onehot, axis=0) - onehot), axis=1)
         slot_ids = flat_choice * capacity + slot_rank
-        choices_all = lax.all_gather(choices, "expert", axis=0, tiled=False)
+        choices_all = choices_every[:, micro_index]
         mine = jnp.any(choices_all == expert_id, axis=2)
         mine_rank = jnp.cumsum(mine.astype(jnp.int32), axis=1) - 1
         source_ids = jnp.broadcast_to(

time: 1110 us -> 1080 us (0.973)
  waiting for transfers between devices: 662 us -> 576 us
  blocking collectives: 152 us -> 211 us
    all_to_all x1, waiting for transfers between devices: 72.6 us -> 0.01 us  [local(): lax.all_to_all(w_shared_in[0], 'expert', split_axis=2, concat_axis=0, til...]
    all_gather x2 -> x1, blocking collectives: 43.6 us -> 103 us  [local(): lax.all_gather(expert_choice[0], 'expert', axis=0, tiled=False)]
    all_gather x1, waiting for transfers between devices: 72.8 us -> 42.8 us  [local(): qkv_full = lax.all_gather(w_qkv[0], 'expert', axis=0, tiled=True)]
    all_gather x2, waiting for transfers between devices: 58.4 us -> 74.4 us  [local(): lax.all_gather(cache.reshape(tokens_dev, -1), 'expert', axis=0, tiled=True)]
  transfers between devices with their start and end apart: 21 -> 21, of which waited for: 18 -> 17; matrix products, arithmetic and copies ran while one was open for 13% -> 13% of each run, Pallas kernels for 0% -> 0%
where the time goes in v3:
time: 1080 us; the launch traced here: 1070 us
  waiting for transfers between devices  576 us (53%)
  blocking collectives  211 us (20%)
  local copies, waits for them, and re-layouts  111 us (10%)
  matrix products  68.9 us (6%)
  other arithmetic  63.1 us (6%)
  starting transfers between devices  27.8 us (3%)
  between operations  15.2 us (1%)
    all_gather x2, waiting for transfers between devices, local(): moe_all = lax.all_gather(moe_rows, 'expert', axis=0, tiled=True)  173 us
    all_gather x2, waiting for transfers between devices, local(): attended_all = lax.all_gather(attended, 'expert', axis=0, tiled=True)  112 us
    all_gather x1, blocking collectives, local(): lax.all_gather(expert_choice[0], 'expert', axis=0, tiled=False)  103 us
    all_gather x2, waiting for transfers between devices, local(): lax.all_gather(cache.reshape(tokens_dev, -1), 'expert', axis=0, tiled=True)  74.4 us
    reduce_scatter x2, waiting for transfers between devices, expert_path(): lax.psum_scatter(partial_value.astype(jnp.bfloat16), 'tensor', scatter_di...  73.2 us
    all_gather x1, waiting for transfers between devices, local(): qkv_full = lax.all_gather(w_qkv[0], 'expert', axis=0, tiled=True)  42.8 us
    all_to_all x2, blocking collectives, terms_to_slots(): lax.all_to_all(terms, 'expert', split_axis=0, concat_axis=1, tiled=True)  40.8 us
    unnamed x78, local copies, waits for them, and re-layouts  40.8 us
  transfers between devices with their start and end apart: 21, of which 17 were waited for; matrix products, arithmetic and copies ran while one was open for 13% of the time, Pallas kernels for 0%

profile of v3, /device:TPU:0, one launch (start us, length us, event | category | flops | bytes accessed | tf_op | source)
XLA Modules:
  0.0 1073.2 jit_solution(2205056200885225519)
XLA Ops:
  7.9 8.5 copy.136
  16.5 7.4 all-to-all-start
  25.3 4.9 psum.42
  30.2 102.9 %all_gather.44 = s32[8,1,128,4]{2,3,1,0:T(4,128)S(1)} all-gather(s32[1,1,128,4]{2,3,1,0:T(4,128)S(1)} %copy-done.15), channel_id=1, replica_groups=mesh['section'=2,'expert'=8,'tensor'=2] {'expert'}, dimensions={0}, use_global_device_ids=true | all-gather | bytes 18432 | tf_op jit(solution)/shard_map/all_gather | solution.py:91
  134.3 9.1 all_gather.42
  145.4 2.7 all_to_all.78
  148.1 42.8 %all-gather.27.cloned.1.call-done = bf16[1,2560,2,896]{3,2,0,1:T(2,128)(2,1)} async-done(((bf16[1,320,2,896]{3,2,0,1:T(2,128)(2,1)}), bf16[1,2560,2,896]{3,2,0,1:T(2,128)(2,1)}) %all-gather.27.cloned.1.call-update) | async-done | bytes 9175056 | tf_op jit(solution)/shard_map/all_gather | solution.py:87
  190.9 8.7 copy.189
  199.6 12.9 %copy.139 = bf16[1792,2560]{1,0:T(8,128)(2,1)} copy(bf16[1792,2560]{0,1:T(8,128)(2,1)} %bitcast.254) | data formatting | bytes 18350080 | tf_op jit(solution)/shard_map/dot_general | solution.py:124
  212.4 6.1 fusion.66
  221.1 36.1 %all-gather.11.cloned.1.call-done = bf16[1024,512]{0,1:T(8,128)(2,1)} async-done(((bf16[128,512]{0,1:T(8,128)(2,1)}), bf16[1024,512]{0,1:T(8,128)(2,1)}) %all-gather.11.cloned.1.call-update) | async-done | bytes 1048592 | tf_op jit(solution)/shard_map/all_gather | solution.py:134
  257.2 2.5 fusion
  261.6 55.9 %all-gather.13.cloned.1.call-done = bf16[1024,1280]{0,1:T(8,128)(2,1)} async-done(((bf16[128,1280]{0,1:T(8,128)(2,1)}), bf16[1024,1280]{0,1:T(8,128)(2,1)}) %all-gather.13.cloned.1.call-update) | async-done | bytes 2621456 | tf_op jit(solution)/shard_map/all_gather | solution.py:159
  317.4 2.8 fusion.26
  320.3 20.4 %all_to_all.104 = bf16[8,128,320]{1,2,0:T(8,128)(2,1)S(1)} all-to-all(bf16[8,128,320]{1,2,0:T(8,128)(2,1)S(1)} %bitcast.267), channel_id=1, replica_groups=mesh['section'=2,'expert'=8,'tensor'=2] {'expert'}, dimensions={0} | all-to-all | bytes 1310720 | tf_op jit(solution)/shard_map/all_to_all | solution.py:44
  342.0 14.7 %reduce-scatter.7.cloned.1.call-done = bf16[128,1280]{1,0:T(8,128)(2,1)} async-done(((bf16[128,2560]{1,0:T(8,128)(2,1)}), bf16[128,1280]{1,0:T(8,128)(2,1)}) %reduce-scatter.7.cloned.1.call-update) | async-done | bytes 327696 | tf_op jit(solution)/shard_map/reduce_scatter | solution.py:45
  357.9 4.9 psum.43
  363.7 9.3 all_gather.47
  373.1 86.4 %all-gather.15.cloned.1.call-done = bf16[1024,2560]{1,0:T(8,128)(2,1)} async-done(((bf16[128,2560]{1,0:T(8,128)(2,1)}), bf16[1024,2560]{1,0:T(8,128)(2,1)}) %all-gather.15.cloned.1.call-update) | async-done | bytes 5242896 | tf_op jit(solution)/shard_map/all_gather | solution.py:167
  459.5 5.3 fusion.99
  465.9 7.7 copy.190
  474.2 23.6 %compare_select_fusion = s32[8,128,1]{2,0,1:T(8,128)S(1)} fusion(pred[8,128,1]{2,0,1:T(8,128)(4,1)S(1)} %copy.148, s32[8,128,1]{2,0,1:T(8,128)S(1)} %copy.147), kind=kOutput, calls=%fused_computation.32 | output fusion | flops 135168 | bytes 9216 | tf_op jit(solution)/shard_map/jit(cumsum)/reduce_window_sum | solution.py:202
  498.6 4.3 scatter_custom_fusion.1
  502.9 4.7 scatter_custom_fusion
  507.9 11.4 %gather_fusion = bf16[640,2560]{1,0:T(8,128)(2,1)} fusion(bf16[1024,2560]{1,0:T(8,128)(2,1)} %all-gather.15.cloned.1.call-done, s32[1024]{0:T(1024)S(1)} %pad_clamp_fusion.1), kind=kCustom, calls=%fused_computation | custom fusion | bytes 6556160 | tf_op jit(solution)/shard_map/gather | solution.py:218
  521.5 7.6 fusion.100
  531.2 4.1 convolution_convert_fusion.1
  535.4 3.1 fusion.18
  539.5 3.5 all-to-all-start.2
  543.0 35.4 %reduce-scatter.11.cloned.1.call-done = bf16[8,80,1280]{2,1,0:T(8,128)(2,1)} async-done(((bf16[8,80,2560]{2,1,0:T(8,128)(2,1)}), bf16[8,80,1280]{2,1,0:T(8,128)(2,1)}) %reduce-scatter.11.cloned.1.call-update) | async-done | bytes 1638416 | tf_op jit(solution)/shard_map/reduce_scatter | solution.py:61
  579.3 5.5 all-to-all-start.3
  599.0 5.2 psum.44
  606.5 16.7 %all-to-all-done.3 = bf16[8,80,1280]{2,1,0:T(8,128)(2,1)S(1)} async-done(((bf16[8,80,1280]{2,1,0:T(8,128)(2,1)}), bf16[8,80,1280]{2,1,0:T(8,128)(2,1)S(1)}, u32[]{:S(2)}, u32[]{:S(2)}) %all-to-all-start.3) | async-done | bytes 1638432 | tf_op jit(solution)/shard_map/all_to_all | solution.py:64
  623.3 3.0 gather_fusion.1
  626.3 3.7 reshape.862
  630.0 3.4 multiply_reduce_fusion.1
  636.3 5.0 psum.45
  641.4 9.5 all_gather.50
  650.9 6.1 fusion.64
  658.0 38.3 %all-gather.19.cloned.1.call-done = bf16[1024,512]{0,1:T(8,128)(2,1)} async-done(((bf16[128,512]{0,1:T(8,128)(2,1)}), bf16[1024,512]{0,1:T(8,128)(2,1)}) %all-gather.19.cloned.1.call-update) | async-done | bytes 1048592 | tf_op jit(solution)/shard_map/all_gather | solution.py:134
  696.3 2.5 fusion.2
  700.7 55.9 %all-gather.21.cloned.1.call-done = bf16[1024,1280]{0,1:T(8,128)(2,1)} async-done(((bf16[128,1280]{0,1:T(8,128)(2,1)}), bf16[1024,1280]{0,1:T(8,128)(2,1)}) %all-gather.21.cloned.1.call-update) | async-done | bytes 2621456 | tf_op jit(solution)/shard_map/all_gather | solution.py:159
  756.6 2.8 fusion.27
  759.5 20.4 %all_to_all.105 = bf16[8,128,320]{1,2,0:T(8,128)(2,1)S(1)} all-to-all(bf16[8,128,320]{1,2,0:T(8,128)(2,1)S(1)} %bitcast.269), channel_id=1, replica_groups=mesh['section'=2,'expert'=8,'tensor'=2] {'expert'}, dimensions={0} | all-to-all | bytes 1310720 | tf_op jit(solution)/shard_map/all_to_all | solution.py:44
  781.0 14.7 %reduce-scatter.13.cloned.1.call-done = bf16[128,1280]{1,0:T(8,128)(2,1)} async-done(((bf16[128,2560]{1,0:T(8,128)(2,1)}), bf16[128,1280]{1,0:T(8,128)(2,1)}) %reduce-scatter.13.cloned.1.call-update) | async-done | bytes 327696 | tf_op jit(solution)/shard_map/reduce_scatter | solution.py:45
  796.9 4.9 psum.46
  803.0 9.1 all_gather.53
  812.2 86.4 %all-gather.23.cloned.1.call-done = bf16[1024,2560]{1,0:T(8,128)(2,1)} async-done(((bf16[128,2560]{1,0:T(8,128)(2,1)}), bf16[1024,2560]{1,0:T(8,128)(2,1)}) %all-gather.23.cloned.1.call-update) | async-done | bytes 5242896 | tf_op jit(solution)/shard_map/all_gather | solution.py:167
  898.5 5.3 fusion.101
  905.2 11.3 %gather_fusion.2 = bf16[640,2560]{1,0:T(8,128)(2,1)} fusion(bf16[1024,2560]{1,0:T(8,128)(2,1)} %all-gather.23.cloned.1.call-done, s32[1024]{0:T(1024)S(1)} %copy-done.18), kind=kCustom, calls=%fused_computation.2 | custom fusion | bytes 6556160 | tf_op jit(solution)/shard_map/gather | solution.py:218
  918.8 7.6 fusion.102
  928.5 4.1 convolution_convert_fusion
  932.6 31.1 %all-gather.25.cloned.1.call-done = bf16[1024,1536]{0,1:T(8,128)(2,1)} async-done(((bf16[1024,192]{0,1:T(8,128)(2,1)}), bf16[1024,1536]{0,1:T(8,128)(2,1)}) %all-gather.25.cloned.1.call-update) | async-done | bytes 3145744 | tf_op jit(solution)/shard_map/all_gather | solution.py:176
  963.7 3.1 fusion.19
  967.7 3.7 all-to-all-start.5
  971.5 37.8 %reduce-scatter.17.cloned.1.call-done = bf16[8,80,1280]{2,1,0:T(8,128)(2,1)} async-done(((bf16[8,80,2560]{2,1,0:T(8,128)(2,1)}), bf16[8,80,1280]{2,1,0:T(8,128)(2,1)}) %reduce-scatter.17.cloned.1.call-update) | async-done | bytes 1638416 | tf_op jit(solution)/shard_map/reduce_scatter | solution.py:61
  1010.1 5.5 all-to-all-start.6
  1021.9 3.6 broadcast_select_fusion.5
  1026.5 5.3 psum.47
  1032.0 3.0 reduce-scatter.15.cloned.1.call-done
  1035.0 19.0 %all-to-all-done.6 = bf16[8,80,1280]{2,1,0:T(8,128)(2,1)S(1)} async-done(((bf16[8,80,1280]{2,1,0:T(8,128)(2,1)}), bf16[8,80,1280]{2,1,0:T(8,128)(2,1)S(1)}, u32[]{:S(2)}, u32[]{:S(2)}) %all-to-all-start.6) | async-done | bytes 1638432 | tf_op jit(solution)/shard_map/all_to_all | solution.py:64
  1054.0 2.9 gather_fusion.3
  1056.9 3.8 reshape.863
  1060.6 3.4 multiply_reduce_fusion
  (213 shorter events, 64.8 us)
Async XLA Ops:
  7.2 528.3 %copy-start = (bf16[1,320,1536]{2,1,0:T(8,128)(2,1)S(1)}, bf16[1,320,1536]{2,1,0:T(8,128)(2,1)}, u32[]{:S(2)}) copy-start(bf16[1,320,1536]{2,1,0:T(8,128)(2,1)} %param.30) | copy-start | bytes 2949124
  7.2 183.7 %all-gather.27.cloned.1.call-start = ((), (), s32[]{:S(2)}) async-start(), calls=%async_computation.27 | async-start | bytes 10321920 | tf_op jit(solution)/shard_map/all_gather | solution.py:87
  16.4 7.5 copy-start.33
  16.4 7.7 copy-start.22
  16.4 13.8 %copy-start.15 = (s32[1,1,128,4]{2,3,1,0:T(4,128)S(1)}, s32[1,1,128,4]{2,3,1,0:T(4,128)}, u32[]{:S(2)}) copy-start(s32[1,1,128,4]{2,3,1,0:T(4,128)} %param.24) | copy-start | bytes 6148
  16.4 116.7 %copy-start.24 = (s32[1,128]{1,0:T(1,128)S(1)}, s32[1,128]{1,0:T(1,128)}, u32[]{:S(2)}) copy-start(s32[1,128]{1,0:T(1,128)} %param.22) | copy-start | bytes 1540
  16.5 127.2 %all-to-all-start = ((bf16[320,2,1536]{0,1,2:T(2,128)(2,1)}), bf16[320,2,1536]{0,1,2:T(2,128)(2,1)S(1)}, u32[]{:S(2)}, u32[]{:S(2)}) async-start(bf16[320,2,1536]{0,1,2:T(2,128)(2,1)} %bitcast.257), calls=%async_computation | async-start | bytes 4718592 | tf_op jit(solution)/shard_map/all_to_all | solution.py:90
  23.9 233.3 %all-gather.11.cloned.1.call-start = ((), (), s32[]{:S(2)}) async-start(), calls=%async_computation.13 | async-start | bytes 1179648 | tf_op jit(solution)/shard_map/all_gather | solution.py:134
  199.6 12.9 %copy-start.4 = (bf16[128,2560]{1,0:T(8,128)(2,1)S(1)}, bf16[128,2560]{1,0:T(8,128)(2,1)}, u32[]{:S(2)}) copy-start(bf16[128,2560]{1,0:T(8,128)(2,1)} %all_gather.42) | copy-start | bytes 1966084
  219.4 98.1 %all-gather.13.cloned.1.call-start = ((), (), s32[]{:S(2)}) async-start(), calls=%async_computation.14 | async-start | bytes 2949120 | tf_op jit(solution)/shard_map/all_gather | solution.py:159
  221.0 38.7 %copy-start.13 = (pred[128,1024]{0,1:T(8,128)(4,1)}, pred[128,1024]{0,1:T(8,128)(4,1)S(1)}, u32[]{:S(2)}) copy-start(pred[128,1024]{0,1:T(8,128)(4,1)S(1)} %fusion.71) | copy-start | bytes 393220
  257.2 2.5 copy-start.29
  259.7 57.7 %copy-start.31 = (bf16[1,320,1280]{2,1,0:T(8,128)(2,1)S(1)}, bf16[1,320,1280]{2,1,0:T(8,128)(2,1)}, u32[]{:S(2)}) copy-start(bf16[1,320,1280]{2,1,0:T(8,128)(2,1)} %param.28) | copy-start | bytes 2457604
  261.5 95.2 %reduce-scatter.7.cloned.1.call-start = ((), (), s32[]{:S(2)}) async-start(), calls=%async_computation.15 | async-start | bytes 983040 | tf_op jit(solution)/shard_map/reduce_scatter | solution.py:45
  320.2 21.7 %copy-start.23 = (f32[1,1280]{1,0:T(1,128)S(1)}, f32[1,1280]{1,0:T(1,128)}, u32[]{:S(2)}) copy-start(f32[1,1280]{1,0:T(1,128)} %param.26) | copy-start | bytes 15364
  320.2 36.5 %copy-start.1 = (bf16[1,128,1280]{2,1,0:T(8,128)(2,1)S(1)}, bf16[1,128,1280]{2,1,0:T(8,128)(2,1)}, u32[]{:S(2)}) copy-start(bf16[1,128,1280]{2,1,0:T(8,128)(2,1)} %param.21) | copy-start | bytes 983044
  341.9 117.6 %all-gather.15.cloned.1.call-start = ((), (), s32[]{:S(2)}) async-start(), calls=%async_computation.16 | async-start | bytes 5898240 | tf_op jit(solution)/shard_map/all_gather | solution.py:167
  363.0 0.7 copy-start.2
  373.0 162.4 %all-gather.17.cloned.1.call-start = ((), (), s32[]{:S(2)}) async-start(), calls=%async_computation.17 | async-start | bytes 3538944 | tf_op jit(solution)/shard_map/all_gather | solution.py:176
  465.8 112.7 %reduce-scatter.11.cloned.1.call-start = ((), (), s32[]{:S(2)}) async-start(), calls=%async_computation.19 | async-start | bytes 4915200 | tf_op jit(solution)/shard_map/reduce_scatter | solution.py:61
  465.9 32.2 %copy-start.26 = (s32[2]{0:T(128)S(1)}, s32[2]{0:T(128)}, u32[]{:S(2)}) copy-start(s32[2]{0:T(128)} %constant.176) | copy-start | bytes 28
  465.9 32.5 %copy-start.25 = (s32[2]{0:T(128)S(1)}, s32[2]{0:T(128)}, u32[]{:S(2)}) copy-start(s32[2]{0:T(128)} %constant.173) | copy-start | bytes 28
  507.8 11.6 %copy-start.20 = (pred[8,80]{1,0:T(8,128)(4,1)}, pred[8,80]{1,0:T(8,128)(4,1)S(1)}, u32[]{:S(2)}) copy-start(pred[8,80]{1,0:T(8,128)(4,1)S(1)} %reshape.857) | copy-start | bytes 1924
  507.9 11.4 %copy-start.17 = (s32[1024]{0:T(1024)}, s32[1024]{0:T(1024)S(1)}, u32[]{:S(2)}) copy-start(s32[1024]{0:T(1024)S(1)} %pad_clamp_fusion.1) | copy-start | bytes 12292
  529.1 2.1 copy-start.27
  539.5 39.0 %all-to-all-start.2 = ((bf16[8,128,320]{1,2,0:T(8,128)(2,1)}), bf16[8,128,320]{1,2,0:T(8,128)(2,1)S(1)}, u32[]{:S(2)}, u32[]{:S(2)}) async-start(bf16[8,128,320]{1,2,0:T(8,128)(2,1)} %bitcast.246), calls=%async_computation.3 | async-start | bytes 1310720 | tf_op jit(solution)/shard_map/all_to_all | solution.py:44
  578.5 0.9 copy-start.5
  579.3 43.9 %all-to-all-start.3 = ((bf16[8,80,1280]{2,1,0:T(8,128)(2,1)}), bf16[8,80,1280]{2,1,0:T(8,128)(2,1)S(1)}, u32[]{:S(2)}, u32[]{:S(2)}) async-start(bf16[8,80,1280]{2,1,0:T(8,128)(2,1)} %reduce-scatter.11.cloned.1.call-done), calls=%async_computation.6 | async-start | bytes 3276800 | tf_op jit(solution)/shard_map/all_to_all | solution.py:64
  584.9 21.7 %reduce-scatter.9.cloned.1.call-start = ((), (), s32[]{:S(2)}) async-start(), calls=%async_computation.18 | async-start | bytes 983040 | tf_op jit(solution)/shard_map/reduce_scatter | solution.py:45
  589.9 106.4 %all-gather.19.cloned.1.call-start = ((), (), s32[]{:S(2)}) async-start(), calls=%async_computation.20 | async-start | bytes 1179648 | tf_op jit(solution)/shard_map/all_gather | solution.py:134
  626.3 7.1 copy-start.11
  633.5 2.8 copy-start.7
  633.5 2.5 collective-permute-start
  657.1 41.7 %copy-start.9 = (bf16[128,2,128]{0,2,1:T(8,128)(2,1)}, bf16[128,2,128]{0,2,1:T(8,128)(2,1)S(1)}, u32[]{:S(2)}) copy-start(bf16[128,2,128]{0,2,1:T(8,128)(2,1)S(1)} %pad_maximum_fusion.3) | copy-start | bytes 196612
  657.8 98.7 %all-gather.21.cloned.1.call-start = ((), (), s32[]{:S(2)}) async-start(), calls=%async_computation.21 | async-start | bytes 2949120 | tf_op jit(solution)/shard_map/all_gather | solution.py:159
  696.3 2.5 copy-start.14
  696.3 2.5 copy-start.30
  698.8 57.7 %copy-start.32 = (bf16[1,320,1280]{2,1,0:T(8,128)(2,1)S(1)}, bf16[1,320,1280]{2,1,0:T(8,128)(2,1)}, u32[]{:S(2)}) copy-start(bf16[1,320,1280]{2,1,0:T(8,128)(2,1)} %param.28) | copy-start | bytes 2457604
  700.7 95.1 %reduce-scatter.13.cloned.1.call-start = ((), (), s32[]{:S(2)}) async-start(), calls=%async_computation.22 | async-start | bytes 983040 | tf_op jit(solution)/shard_map/reduce_scatter | solution.py:45
  781.0 117.5 %all-gather.23.cloned.1.call-start = ((), (), s32[]{:S(2)}) async-start(), calls=%async_computation.23 | async-start | bytes 5898240 | tf_op jit(solution)/shard_map/all_gather | solution.py:167
  812.1 93.1 %copy-start.18 = (s32[1024]{0:T(1024)S(1)}, s32[1024]{0:T(1024)}, u32[]{:S(2)}) copy-start(s32[1024]{0:T(1024)} %copy-done.17) | copy-start | bytes 12292
  812.1 151.6 %all-gather.25.cloned.1.call-start = ((), (), s32[]{:S(2)}) async-start(), calls=%async_computation.24 | async-start | bytes 3538944 | tf_op jit(solution)/shard_map/all_gather | solution.py:176
  904.9 11.6 %copy-start.21 = (pred[8,80]{1,0:T(8,128)(4,1)S(1)}, pred[8,80]{1,0:T(8,128)(4,1)}, u32[]{:S(2)}) copy-start(pred[8,80]{1,0:T(8,128)(4,1)} %copy-done.20) | copy-start | bytes 1924
  904.9 104.3 %reduce-scatter.17.cloned.1.call-start = ((), (), s32[]{:S(2)}) async-start(), calls=%async_computation.26 | async-start | bytes 4915200 | tf_op jit(solution)/shard_map/reduce_scatter | solution.py:61
  926.3 2.1 copy-start.28
  967.7 54.0 %copy-start.10 = (bf16[128,2,128]{0,2,1:T(8,128)(2,1)S(1)}, bf16[128,2,128]{0,2,1:T(8,128)(2,1)}, u32[]{:S(2)}) copy-start(bf16[128,2,128]{0,2,1:T(8,128)(2,1)} %copy-done.9) | copy-start | bytes 196612
  967.7 41.5 %all-to-all-start.5 = ((bf16[8,128,320]{1,2,0:T(8,128)(2,1)}), bf16[8,128,320]{1,2,0:T(8,128)(2,1)S(1)}, u32[]{:S(2)}, u32[]{:S(2)}) async-start(bf16[8,128,320]{1,2,0:T(8,128)(2,1)} %bitcast.244), calls=%async_computation.9 | async-start | bytes 1310720 | tf_op jit(solution)/shard_map/all_to_all | solution.py:44
  971.5 60.4 %copy-start.16 = (s32[1,1,128,4]{2,3,1,0:T(4,128)S(1)}, s32[1,1,128,4]{2,3,1,0:T(4,128)}, u32[]{:S(2)}) copy-start(s32[1,1,128,4]{2,3,1,0:T(4,128)} %param.24) | copy-start | bytes 6148
  971.5 82.5 %copy-start.19 = (s32[1024]{0:T(1024)S(1)}, s32[1024]{0:T(1024)}, u32[]{:S(2)}) copy-start(s32[1024]{0:T(1024)} %pad_clamp_fusion) | copy-start | bytes 12292
  1009.2 0.9 copy-start.6
  1010.1 43.9 %all-to-all-start.6 = ((bf16[8,80,1280]{2,1,0:T(8,128)(2,1)}), bf16[8,80,1280]{2,1,0:T(8,128)(2,1)S(1)}, u32[]{:S(2)}, u32[]{:S(2)}) async-start(bf16[8,80,1280]{2,1,0:T(8,128)(2,1)} %reduce-scatter.17.cloned.1.call-done), calls=%async_computation.12 | async-start | bytes 3276800 | tf_op jit(solution)/shard_map/all_to_all | solution.py:64
  1015.6 19.4 %reduce-scatter.15.cloned.1.call-start = ((), (), s32[]{:S(2)}) async-start(), calls=%async_computation.25 | async-start | bytes 983040 | tf_op jit(solution)/shard_map/reduce_scatter | solution.py:45
  1056.9 7.1 copy-start.3
  1056.9 7.2 copy-start.8
  1056.9 7.2 copy-start.12
Sparse Core Ops, SparseCore 0:
  10.2 180.6 all-gather.26
  219.5 37.6 all-gather.10
  261.7 55.7 all-gather.12
  342.0 14.6 reduce-scatter.6
  373.1 86.2 all-gather.14
  465.9 58.6 all-gather.16
  535.5 42.9 reduce-scatter.10
  590.0 16.5 reduce-scatter.8
  658.0 38.2 all-gather.18
  700.8 55.7 all-gather.20
  781.1 14.6 reduce-scatter.12
  812.2 86.2 all-gather.22
  905.0 58.6 all-gather.24
  965.8 43.3 reduce-scatter.16
  1018.5 16.5 reduce-scatter.14

commit v4 on v3

--- a/solution.py
+++ b/solution.py
@@ -38,6 +38,15 @@
     return (widened * lax.rsqrt(squares / model_width + NORM_EPS)[:, None] * gain_row).astype(
         jnp.bfloat16
     )
+
+
+def gather_slots(rows):
+    count = lax.axis_size("expert")
+    half = rows.shape[1] // 2
+    first = lax.all_gather(rows[:, :half], "expert", axis=0, tiled=True)
+    copies = jnp.broadcast_to(rows[None, :, half:], (count,) + rows[:, half:].shape)
+    second = lax.all_to_all(copies, "expert", split_axis=0, concat_axis=0, tiled=True)
+    return jnp.concatenate([first, second.reshape(first.shape[0], -1)], axis=1)
 
 
 def terms_to_slots(terms):
@@ -156,7 +165,7 @@
         )
         numerator, denominator = (numerator, jnp.sum(weights_full, axis=-1))
         attended = (numerator / denominator[..., None]).astype(jnp.bfloat16).reshape(tokens_dev, -1)
-        attended_all = lax.all_gather(attended, "expert", axis=0, tiled=True)
+        attended_all = gather_slots(attended)
         attn_terms = lax.dot_general(
             attended_all, out_local, (((1,), (1,)), ((), ())), preferred_element_type=jnp.float32
         )
@@ -164,7 +173,7 @@
         after_attn = (incoming.astype(jnp.float32) + attn_sum).astype(jnp.bfloat16)
         moe_in = norm_rows(after_attn, ffn_gain[0], model_width)
         moe_rows = lax.all_gather(moe_in, "tensor", axis=1, tiled=True)
-        moe_all = lax.all_gather(moe_rows, "expert", axis=0, tiled=True)
+        moe_all = gather_slots(moe_rows)
         shared_hidden = jnp.dot(
             moe_all,
             shared_in_cols.reshape(model_width, 2 * shared_cols),

time: 1080 us -> 1110 us (1.028)
  starting transfers between devices: 27.8 us -> 46.4 us
    all_gather x4, waiting for transfers between devices: 284 us -> 38.2 us  [gather_slots(): first = lax.all_gather(rows[:, :half], 'expert', axis=0, tiled=True)]
    all_to_all x0 -> x4, waiting for transfers between devices: none -> 240 us  [gather_slots(): lax.all_to_all(copies, 'expert', split_axis=0, concat_axis=0, tiled=True)]
    all_to_all x0 -> x4, starting transfers between devices: none -> 18.3 us  [gather_slots(): lax.all_to_all(copies, 'expert', split_axis=0, concat_axis=0, tiled=True)]
    unnamed x78 -> x84, local copies, waits for them, and re-layouts: 40.8 us -> 42 us
  transfers between devices with their start and end apart: 21 -> 25, of which waited for: 17 -> 21; matrix products, arithmetic and copies ran while one was open for 13% -> 14% of each run, Pallas kernels for 0% -> 0%
where the time goes in v4:
time: 1110 us; the launch traced here: 1100 us
  waiting for transfers between devices  571 us (51%)
  blocking collectives  210 us (19%)
  local copies, waits for them, and re-layouts  122 us (11%)
  other arithmetic  70.1 us (6%)
  matrix products  67.7 us (6%)
  starting transfers between devices  46.4 us (4%)
  between operations  15.2 us (1%)
    all_to_all x4, waiting for transfers between devices, gather_slots(): lax.all_to_all(copies, 'expert', split_axis=0, concat_axis=0, tiled=True)  240 us
    all_gather x1, blocking collectives, local(): lax.all_gather(expert_choice[0], 'expert', axis=0, tiled=False)  103 us
    all_gather x2, waiting for transfers between devices, local(): lax.all_gather(cache.reshape(tokens_dev, -1), 'expert', axis=0, tiled=True)  74.5 us
    reduce_scatter x2, waiting for transfers between devices, expert_path(): lax.psum_scatter(partial_value.astype(jnp.bfloat16), 'tensor', scatter_di...  73.3 us
    all_gather x1, waiting for transfers between devices, local(): qkv_full = lax.all_gather(w_qkv[0], 'expert', axis=0, tiled=True)  42.7 us
    unnamed x84, local copies, waits for them, and re-layouts  42 us
    all_to_all x2, blocking collectives, terms_to_slots(): lax.all_to_all(terms, 'expert', split_axis=0, concat_axis=1, tiled=True)  40.2 us
    all_gather x4, waiting for transfers between devices, gather_slots(): first = lax.all_gather(rows[:, :half], 'expert', axis=0, tiled=True)  38.2 us
  transfers between devices with their start and end apart: 25, of which 21 were waited for; matrix products, arithmetic and copies ran while one was open for 14% of the time, Pallas kernels for 0%

profile of v4, /device:TPU:0, one launch (start us, length us, event | category | flops | bytes accessed | tf_op | source)
XLA Modules:
  0.0 1101.8 jit_solution(7312611991677646142)
XLA Ops:
  7.9 8.5 copy.140
  16.5 7.4 all-to-all-start
  25.3 4.9 psum.42
  30.2 102.9 %all_gather.44 = s32[8,1,128,4]{2,3,1,0:T(4,128)S(1)} all-gather(s32[1,1,128,4]{2,3,1,0:T(4,128)S(1)} %copy-done.19), channel_id=1, replica_groups=mesh['section'=2,'expert'=8,'tensor'=2] {'expert'}, dimensions={0}, use_global_device_ids=true | all-gather | bytes 18432 | tf_op jit(solution)/shard_map/all_gather | solution.py:100
  134.3 9.1 all_gather.42
  148.1 42.7 %all-gather.27.cloned.1.call-done = bf16[1,2560,2,896]{3,2,0,1:T(2,128)(2,1)} async-done(((bf16[1,320,2,896]{3,2,0,1:T(2,128)(2,1)}), bf16[1,2560,2,896]{3,2,0,1:T(2,128)(2,1)}) %all-gather.27.cloned.1.call-update) | async-done | bytes 9175056 | tf_op jit(solution)/shard_map/all_gather | solution.py:96
  190.9 8.7 copy.199
  199.6 12.9 %copy.143 = bf16[1792,2560]{1,0:T(8,128)(2,1)} copy(bf16[1792,2560]{0,1:T(8,128)(2,1)} %bitcast.252) | data formatting | bytes 18350080 | tf_op jit(solution)/shard_map/dot_general | solution.py:133
  212.4 6.1 fusion.84
  221.1 36.1 %all-gather.11.cloned.1.call-done = bf16[1024,512]{0,1:T(8,128)(2,1)} async-done(((bf16[128,512]{0,1:T(8,128)(2,1)}), bf16[1024,512]{0,1:T(8,128)(2,1)}) %all-gather.11.cloned.1.call-update) | async-done | bytes 1048592 | tf_op jit(solution)/shard_map/all_gather | solution.py:143
  262.1 3.7 all-to-all-start.1
  266.7 35.3 %all-to-all-done.1 = bf16[8,128,640]{1,2,0:T(8,128)(2,1)S(1)} async-done(((bf16[8,128,640]{1,2,0:T(8,128)(2,1)}), bf16[8,128,640]{1,2,0:T(8,128)(2,1)S(1)}, u32[]{:S(2)}, u32[]{:S(2)}) %all-to-all-start.1) | async-done | bytes 1310752 | tf_op jit(solution)/shard_map/all_to_all | solution.py:48
  303.4 19.0 %all-gather.13.cloned.1.call-done = bf16[1024,640]{1,0:T(8,128)(2,1)} async-done(((bf16[128,640]{1,0:T(8,128)(2,1)}), bf16[1024,640]{1,0:T(8,128)(2,1)}) %all-gather.13.cloned.1.call-update) | async-done | bytes 1310736 | tf_op jit(solution)/shard_map/all_gather | solution.py:46
  325.3 20.2 %all_to_all.124 = bf16[8,128,320]{1,2,0:T(8,128)(2,1)S(1)} all-to-all(bf16[8,128,320]{1,2,0:T(8,128)(2,1)S(1)} %bitcast.265), channel_id=1, replica_groups=mesh['section'=2,'expert'=8,'tensor'=2] {'expert'}, dimensions={0} | all-to-all | bytes 1310720 | tf_op jit(solution)/shard_map/all_to_all | solution.py:53
  346.7 14.7 %reduce-scatter.7.cloned.1.call-done = bf16[128,1280]{1,0:T(8,128)(2,1)} async-done(((bf16[128,2560]{1,0:T(8,128)(2,1)}), bf16[128,1280]{1,0:T(8,128)(2,1)}) %reduce-scatter.7.cloned.1.call-update) | async-done | bytes 327696 | tf_op jit(solution)/shard_map/reduce_scatter | solution.py:54
  362.6 4.9 psum.43
  368.4 9.0 all_gather.47
  379.9 5.5 all-to-all-start.3
  386.0 7.7 copy.200
  393.8 80.8 %all-to-all-done.3 = bf16[8,128,1280]{2,1,0:T(8,128)(2,1)} async-done(((bf16[8,128,1280]{2,1,0:T(8,128)(2,1)}), bf16[8,128,1280]{2,1,0:T(8,128)(2,1)}, u32[]{:S(2)}, u32[]{:S(2)}) %all-to-all-start.3) | async-done | bytes 2621472 | tf_op jit(solution)/shard_map/all_to_all | solution.py:48
  474.8 5.3 fusion.119
  481.8 23.6 %compare_select_fusion = s32[8,128,1]{2,0,1:T(8,128)S(1)} fusion(pred[8,128,1]{2,0,1:T(8,128)(4,1)S(1)} %copy.154, s32[8,128,1]{2,0,1:T(8,128)S(1)} %copy.153), kind=kOutput, calls=%fused_computation.42 | output fusion | flops 135168 | bytes 9216 | tf_op jit(solution)/shard_map/jit(cumsum)/reduce_window_sum | solution.py:211
  506.1 4.3 scatter_custom_fusion.1
  510.6 4.7 scatter_custom_fusion
  515.5 5.2 pad_maximum_fusion
  520.7 11.4 %gather_fusion = bf16[640,2560]{1,0:T(8,128)(2,1)} fusion(bf16[1024,2560]{1,0:T(8,128)(2,1)} %pad_maximum_fusion, s32[1024]{0:T(1024)S(1)} %pad_clamp_fusion.1), kind=kCustom, calls=%fused_computation | custom fusion | bytes 6556160 | tf_op jit(solution)/shard_map/gather | solution.py:227
  534.3 7.6 fusion.125
  544.0 4.1 convolution_convert_fusion.1
  548.2 3.1 fusion.32
  552.2 4.0 all-to-all-start.4
  556.2 35.4 %reduce-scatter.11.cloned.1.call-done = bf16[8,80,1280]{2,1,0:T(8,128)(2,1)} async-done(((bf16[8,80,2560]{2,1,0:T(8,128)(2,1)}), bf16[8,80,1280]{2,1,0:T(8,128)(2,1)}) %reduce-scatter.11.cloned.1.call-update) | async-done | bytes 1638416 | tf_op jit(solution)/shard_map/reduce_scatter | solution.py:70
  592.4 5.5 all-to-all-start.5
  608.5 5.1 psum.44
  614.5 5.2 reduce-scatter.9.cloned.1.call-done
  619.7 16.7 %all-to-all-done.5 = bf16[8,80,1280]{2,1,0:T(8,128)(2,1)S(1)} async-done(((bf16[8,80,1280]{2,1,0:T(8,128)(2,1)}), bf16[8,80,1280]{2,1,0:T(8,128)(2,1)S(1)}, u32[]{:S(2)}, u32[]{:S(2)}) %all-to-all-start.5) | async-done | bytes 1638432 | tf_op jit(solution)/shard_map/all_to_all | solution.py:73
  639.2 3.7 reshape.882
  643.0 3.4 multiply_reduce_fusion.1
  649.2 5.0 psum.45
  654.3 9.5 all_gather.50
  663.8 6.1 fusion.82
  670.9 38.4 %all-gather.19.cloned.1.call-done = bf16[1024,512]{0,1:T(8,128)(2,1)} async-done(((bf16[128,512]{0,1:T(8,128)(2,1)}), bf16[1024,512]{0,1:T(8,128)(2,1)}) %all-gather.19.cloned.1.call-update) | async-done | bytes 1048592 | tf_op jit(solution)/shard_map/all_gather | solution.py:143
  714.1 3.6 all-to-all-start.6
  718.7 35.3 %all-to-all-done.6 = bf16[8,128,640]{1,2,0:T(8,128)(2,1)S(1)} async-done(((bf16[8,128,640]{1,2,0:T(8,128)(2,1)}), bf16[8,128,640]{1,2,0:T(8,128)(2,1)S(1)}, u32[]{:S(2)}, u32[]{:S(2)}) %all-to-all-start.6) | async-done | bytes 1310752 | tf_op jit(solution)/shard_map/all_to_all | solution.py:48
  755.4 19.0 %all-gather.21.cloned.1.call-done = bf16[1024,640]{1,0:T(8,128)(2,1)} async-done(((bf16[128,640]{1,0:T(8,128)(2,1)}), bf16[1024,640]{1,0:T(8,128)(2,1)}) %all-gather.21.cloned.1.call-update) | async-done | bytes 1310736 | tf_op jit(solution)/shard_map/all_gather | solution.py:46
  777.5 20.0 %all_to_all.125 = bf16[8,128,320]{1,2,0:T(8,128)(2,1)S(1)} all-to-all(bf16[8,128,320]{1,2,0:T(8,128)(2,1)S(1)} %bitcast.267), channel_id=1, replica_groups=mesh['section'=2,'expert'=8,'tensor'=2] {'expert'}, dimensions={0} | all-to-all | bytes 1310720 | tf_op jit(solution)/shard_map/all_to_all | solution.py:53
  798.6 14.8 %reduce-scatter.13.cloned.1.call-done = bf16[128,1280]{1,0:T(8,128)(2,1)} async-done(((bf16[128,2560]{1,0:T(8,128)(2,1)}), bf16[128,1280]{1,0:T(8,128)(2,1)}) %reduce-scatter.13.cloned.1.call-update) | async-done | bytes 327696 | tf_op jit(solution)/shard_map/reduce_scatter | solution.py:54
  814.5 4.9 psum.46
  820.5 9.0 all_gather.53
  831.9 5.5 all-to-all-start.8
  838.3 88.3 %all-to-all-done.8 = bf16[8,128,1280]{2,1,0:T(8,128)(2,1)} async-done(((bf16[8,128,1280]{2,1,0:T(8,128)(2,1)}), bf16[8,128,1280]{2,1,0:T(8,128)(2,1)}, u32[]{:S(2)}, u32[]{:S(2)}) %all-to-all-start.8) | async-done | bytes 2621472 | tf_op jit(solution)/shard_map/all_to_all | solution.py:48
  926.7 5.3 fusion.118
  933.2 5.2 pad_maximum_fusion.1
  938.4 11.6 %gather_fusion.2 = bf16[640,2560]{1,0:T(8,128)(2,1)} fusion(bf16[1024,2560]{1,0:T(8,128)(2,1)} %pad_maximum_fusion.1, s32[1024]{0:T(1024)S(1)} %copy-done.22), kind=kCustom, calls=%fused_computation.2 | custom fusion | bytes 6556160 | tf_op jit(solution)/shard_map/gather | solution.py:227
  952.2 7.6 fusion.126
  962.2 4.1 convolution_convert_fusion
  966.4 25.9 %all-gather.25.cloned.1.call-done = bf16[1024,1536]{0,1:T(8,128)(2,1)} async-done(((bf16[1024,192]{0,1:T(8,128)(2,1)}), bf16[1024,1536]{0,1:T(8,128)(2,1)}) %all-gather.25.cloned.1.call-update) | async-done | bytes 3145744 | tf_op jit(solution)/shard_map/all_gather | solution.py:185
  996.3 3.6 all-to-all-start.9
  999.9 37.9 %reduce-scatter.17.cloned.1.call-done = bf16[8,80,1280]{2,1,0:T(8,128)(2,1)} async-done(((bf16[8,80,2560]{2,1,0:T(8,128)(2,1)}), bf16[8,80,1280]{2,1,0:T(8,128)(2,1)}) %reduce-scatter.17.cloned.1.call-update) | async-done | bytes 1638416 | tf_op jit(solution)/shard_map/reduce_scatter | solution.py:70
  1038.6 5.5 all-to-all-start.10
  1050.4 3.6 broadcast_select_fusion.5
  1055.1 5.3 psum.47
  1063.6 19.0 %all-to-all-done.10 = bf16[8,80,1280]{2,1,0:T(8,128)(2,1)S(1)} async-done(((bf16[8,80,1280]{2,1,0:T(8,128)(2,1)}), bf16[8,80,1280]{2,1,0:T(8,128)(2,1)S(1)}, u32[]{:S(2)}, u32[]{:S(2)}) %all-to-all-start.10) | async-done | bytes 1638432 | tf_op jit(solution)/shard_map/all_to_all | solution.py:73
  1085.4 3.8 reshape.883
  1089.2 3.4 multiply_reduce_fusion
  (239 shorter events, 97.1 us)
Async XLA Ops:
  7.2 541.0 %copy-start = (bf16[1,320,1536]{2,1,0:T(8,128)(2,1)S(1)}, bf16[1,320,1536]{2,1,0:T(8,128)(2,1)}, u32[]{:S(2)}) copy-start(bf16[1,320,1536]{2,1,0:T(8,128)(2,1)} %param.30) | copy-start | bytes 2949124
  7.2 183.7 %all-gather.27.cloned.1.call-start = ((), (), s32[]{:S(2)}) async-start(), calls=%async_computation.31 | async-start | bytes 10321920 | tf_op jit(solution)/shard_map/all_gather | solution.py:96
  16.4 7.5 copy-start.35
  16.4 7.7 copy-start.25
  16.4 13.8 %copy-start.19 = (s32[1,1,128,4]{2,3,1,0:T(4,128)S(1)}, s32[1,1,128,4]{2,3,1,0:T(4,128)}, u32[]{:S(2)}) copy-start(s32[1,1,128,4]{2,3,1,0:T(4,128)} %param.24) | copy-start | bytes 6148
  16.4 116.7 %copy-start.27 = (s32[1,128]{1,0:T(1,128)S(1)}, s32[1,128]{1,0:T(1,128)}, u32[]{:S(2)}) copy-start(s32[1,128]{1,0:T(1,128)} %param.22) | copy-start | bytes 1540
  16.5 127.2 %all-to-all-start = ((bf16[320,2,1536]{0,1,2:T(2,128)(2,1)}), bf16[320,2,1536]{0,1,2:T(2,128)(2,1)S(1)}, u32[]{:S(2)}, u32[]{:S(2)}) async-start(bf16[320,2,1536]{0,1,2:T(2,128)(2,1)} %bitcast.255), calls=%async_computation | async-start | bytes 4718592 | tf_op jit(solution)/shard_map/all_to_all | solution.py:99
  23.9 233.3 %all-gather.11.cloned.1.call-start = ((), (), s32[]{:S(2)}) async-start(), calls=%async_computation.17 | async-start | bytes 1179648 | tf_op jit(solution)/shard_map/all_gather | solution.py:143
  24.2 119.3 %copy-start.17 = (f32[1280]{0:T(1024)}, f32[1280]{0:T(1024)S(1)}, u32[]{:S(2)}) copy-start(f32[1280]{0:T(1024)S(1)} %reduce.33) | copy-start | bytes 15364
  199.6 12.9 %copy-start.4 = (bf16[128,2560]{1,0:T(8,128)(2,1)S(1)}, bf16[128,2560]{1,0:T(8,128)(2,1)}, u32[]{:S(2)}) copy-start(bf16[128,2560]{1,0:T(8,128)(2,1)} %all_gather.42) | copy-start | bytes 1966084
  220.9 38.7 %copy-start.13 = (pred[128,1024]{0,1:T(8,128)(4,1)}, pred[128,1024]{0,1:T(8,128)(4,1)S(1)}, u32[]{:S(2)}) copy-start(pred[128,1024]{0,1:T(8,128)(4,1)S(1)} %fusion.89) | copy-start | bytes 393220
  257.2 2.5 copy-start.32
  262.1 60.3 %copy-start.34 = (bf16[1,320,1280]{2,1,0:T(8,128)(2,1)S(1)}, bf16[1,320,1280]{2,1,0:T(8,128)(2,1)}, u32[]{:S(2)}) copy-start(bf16[1,320,1280]{2,1,0:T(8,128)(2,1)} %param.28) | copy-start | bytes 2457604
  262.1 39.9 %all-to-all-start.1 = ((bf16[8,128,640]{1,2,0:T(8,128)(2,1)}), bf16[8,128,640]{1,2,0:T(8,128)(2,1)S(1)}, u32[]{:S(2)}, u32[]{:S(2)}) async-start(bf16[8,128,640]{1,2,0:T(8,128)(2,1)} %broadcast_in_dim.108), calls=%async_computation.1 | async-start | bytes 2621440 | tf_op jit(solution)/shard_map/all_to_all | solution.py:48
  265.8 56.6 %all-gather.13.cloned.1.call-start = ((), (), s32[]{:S(2)}) async-start(), calls=%async_computation.18 | async-start | bytes 1474560 | tf_op jit(solution)/shard_map/all_gather | solution.py:46
  266.7 94.7 %reduce-scatter.7.cloned.1.call-start = ((), (), s32[]{:S(2)}) async-start(), calls=%async_computation.19 | async-start | bytes 983040 | tf_op jit(solution)/shard_map/reduce_scatter | solution.py:54
  325.2 21.5 %copy-start.26 = (f32[1,1280]{1,0:T(1,128)S(1)}, f32[1,1280]{1,0:T(1,128)}, u32[]{:S(2)}) copy-start(f32[1,1280]{1,0:T(1,128)} %param.26) | copy-start | bytes 15364
  325.2 36.2 %copy-start.1 = (bf16[1,128,1280]{2,1,0:T(8,128)(2,1)S(1)}, bf16[1,128,1280]{2,1,0:T(8,128)(2,1)}, u32[]{:S(2)}) copy-start(bf16[1,128,1280]{2,1,0:T(8,128)(2,1)} %param.21) | copy-start | bytes 983044
  346.7 33.2 %copy-start.15 = (f32[1280]{0:T(1024)}, f32[1280]{0:T(1024)S(1)}, u32[]{:S(2)}) copy-start(f32[1280]{0:T(1024)S(1)} %reduce.34) | copy-start | bytes 15364
  367.7 0.7 copy-start.2
  379.9 94.7 %all-to-all-start.3 = ((bf16[8,128,1280]{2,1,0:T(8,128)(2,1)}), bf16[8,128,1280]{2,1,0:T(8,128)(2,1)}, u32[]{:S(2)}, u32[]{:S(2)}) async-start(bf16[8,128,1280]{2,1,0:T(8,128)(2,1)} %broadcast_in_dim.109), calls=%async_computation.4 | async-start | bytes 5242880 | tf_op jit(solution)/shard_map/all_to_all | solution.py:48
  385.4 89.4 %all-gather.15.cloned.1.call-start = ((), (), s32[]{:S(2)}) async-start(), calls=%async_computation.20 | async-start | bytes 2949120 | tf_op jit(solution)/shard_map/all_gather | solution.py:46
  386.0 162.2 %all-gather.17.cloned.1.call-start = ((), (), s32[]{:S(2)}) async-start(), calls=%async_computation.21 | async-start | bytes 3538944 | tf_op jit(solution)/shard_map/all_gather | solution.py:185
  480.1 25.5 %copy-start.29 = (s32[2]{0:T(128)S(1)}, s32[2]{0:T(128)}, u32[]{:S(2)}) copy-start(s32[2]{0:T(128)} %constant.173) | copy-start | bytes 28
  480.1 25.7 %copy-start.28 = (s32[2]{0:T(128)S(1)}, s32[2]{0:T(128)}, u32[]{:S(2)}) copy-start(s32[2]{0:T(128)} %constant.176) | copy-start | bytes 28
  481.1 110.4 %reduce-scatter.11.cloned.1.call-start = ((), (), s32[]{:S(2)}) async-start(), calls=%async_computation.23 | async-start | bytes 4915200 | tf_op jit(solution)/shard_map/reduce_scatter | solution.py:70
  515.5 16.6 %copy-start.23 = (pred[8,80]{1,0:T(8,128)(4,1)}, pred[8,80]{1,0:T(8,128)(4,1)S(1)}, u32[]{:S(2)}) copy-start(pred[8,80]{1,0:T(8,128)(4,1)S(1)} %reshape.877) | copy-start | bytes 1924
  515.5 5.2 copy-start.21
  541.9 2.1 copy-start.30
  552.2 39.4 %all-to-all-start.4 = ((bf16[8,128,320]{1,2,0:T(8,128)(2,1)}), bf16[8,128,320]{1,2,0:T(8,128)(2,1)S(1)}, u32[]{:S(2)}, u32[]{:S(2)}) async-start(bf16[8,128,320]{1,2,0:T(8,128)(2,1)} %bitcast.246), calls=%async_computation.5 | async-start | bytes 1310720 | tf_op jit(solution)/shard_map/all_to_all | solution.py:53
  591.6 0.8 copy-start.5
  592.4 43.9 %all-to-all-start.5 = ((bf16[8,80,1280]{2,1,0:T(8,128)(2,1)}), bf16[8,80,1280]{2,1,0:T(8,128)(2,1)S(1)}, u32[]{:S(2)}, u32[]{:S(2)}) async-start(bf16[8,80,1280]{2,1,0:T(8,128)(2,1)} %reduce-scatter.11.cloned.1.call-done), calls=%async_computation.8 | async-start | bytes 3276800 | tf_op jit(solution)/shard_map/all_to_all | solution.py:73
  597.9 21.7 %reduce-scatter.9.cloned.1.call-start = ((), (), s32[]{:S(2)}) async-start(), calls=%async_computation.22 | async-start | bytes 983040 | tf_op jit(solution)/shard_map/reduce_scatter | solution.py:54
  603.0 106.3 %all-gather.19.cloned.1.call-start = ((), (), s32[]{:S(2)}) async-start(), calls=%async_computation.24 | async-start | bytes 1179648 | tf_op jit(solution)/shard_map/all_gather | solution.py:143
  639.2 7.1 copy-start.11
  643.0 11.2 %copy-start.18 = (f32[1280]{0:T(1024)S(1)}, f32[1280]{0:T(1024)}, u32[]{:S(2)}) copy-start(f32[1280]{0:T(1024)} %copy-done.17) | copy-start | bytes 15364
  646.5 2.8 copy-start.7
  646.5 2.5 collective-permute-start
  670.1 41.7 %copy-start.9 = (bf16[128,2,128]{0,2,1:T(8,128)(2,1)}, bf16[128,2,128]{0,2,1:T(8,128)(2,1)S(1)}, u32[]{:S(2)}) copy-start(bf16[128,2,128]{0,2,1:T(8,128)(2,1)S(1)} %pad_maximum_fusion.5) | copy-start | bytes 196612
  709.2 2.5 copy-start.14
  709.2 2.5 copy-start.33
  714.1 39.8 %all-to-all-start.6 = ((bf16[8,128,640]{1,2,0:T(8,128)(2,1)}), bf16[8,128,640]{1,2,0:T(8,128)(2,1)S(1)}, u32[]{:S(2)}, u32[]{:S(2)}) async-start(bf16[8,128,640]{1,2,0:T(8,128)(2,1)} %broadcast_in_dim.119), calls=%async_computation.9 | async-start | bytes 2621440 | tf_op jit(solution)/shard_map/all_to_all | solution.py:48
  717.7 56.6 %all-gather.21.cloned.1.call-start = ((), (), s32[]{:S(2)}) async-start(), calls=%async_computation.25 | async-start | bytes 1474560 | tf_op jit(solution)/shard_map/all_gather | solution.py:46
  718.6 94.7 %reduce-scatter.13.cloned.1.call-start = ((), (), s32[]{:S(2)}) async-start(), calls=%async_computation.26 | async-start | bytes 983040 | tf_op jit(solution)/shard_map/reduce_scatter | solution.py:54
  777.3 42.1 %copy-start.16 = (f32[1280]{0:T(1024)S(1)}, f32[1280]{0:T(1024)}, u32[]{:S(2)}) copy-start(f32[1280]{0:T(1024)} %copy-done.15) | copy-start | bytes 15364
  831.9 94.7 %all-to-all-start.8 = ((bf16[8,128,1280]{2,1,0:T(8,128)(2,1)}), bf16[8,128,1280]{2,1,0:T(8,128)(2,1)}, u32[]{:S(2)}, u32[]{:S(2)}) async-start(bf16[8,128,1280]{2,1,0:T(8,128)(2,1)} %broadcast_in_dim.120), calls=%async_computation.12 | async-start | bytes 5242880 | tf_op jit(solution)/shard_map/all_to_all | solution.py:48
  837.4 89.3 %all-gather.23.cloned.1.call-start = ((), (), s32[]{:S(2)}) async-start(), calls=%async_computation.27 | async-start | bytes 2949120 | tf_op jit(solution)/shard_map/all_gather | solution.py:46
  838.0 154.2 %all-gather.25.cloned.1.call-start = ((), (), s32[]{:S(2)}) async-start(), calls=%async_computation.28 | async-start | bytes 3538944 | tf_op jit(solution)/shard_map/all_gather | solution.py:185
  933.1 5.3 copy-start.22
  933.1 104.6 %reduce-scatter.17.cloned.1.call-start = ((), (), s32[]{:S(2)}) async-start(), calls=%async_computation.30 | async-start | bytes 4915200 | tf_op jit(solution)/shard_map/reduce_scatter | solution.py:70
  938.4 11.6 %copy-start.24 = (pred[8,80]{1,0:T(8,128)(4,1)S(1)}, pred[8,80]{1,0:T(8,128)(4,1)}, u32[]{:S(2)}) copy-start(pred[8,80]{1,0:T(8,128)(4,1)} %copy-done.23) | copy-start | bytes 1924
  959.8 2.4 copy-start.31
  996.3 41.5 %all-to-all-start.9 = ((bf16[8,128,320]{1,2,0:T(8,128)(2,1)}), bf16[8,128,320]{1,2,0:T(8,128)(2,1)S(1)}, u32[]{:S(2)}, u32[]{:S(2)}) async-start(bf16[8,128,320]{1,2,0:T(8,128)(2,1)} %bitcast.244), calls=%async_computation.13 | async-start | bytes 1310720 | tf_op jit(solution)/shard_map/all_to_all | solution.py:53
  999.9 49.6 %copy-start.10 = (bf16[128,2,128]{0,2,1:T(8,128)(2,1)S(1)}, bf16[128,2,128]{0,2,1:T(8,128)(2,1)}, u32[]{:S(2)}) copy-start(bf16[128,2,128]{0,2,1:T(8,128)(2,1)} %copy-done.9) | copy-start | bytes 196612
  999.9 60.5 %copy-start.20 = (s32[1,1,128,4]{2,3,1,0:T(4,128)S(1)}, s32[1,1,128,4]{2,3,1,0:T(4,128)}, u32[]{:S(2)}) copy-start(s32[1,1,128,4]{2,3,1,0:T(4,128)} %param.24) | copy-start | bytes 6148
  1037.8 0.9 copy-start.6
  1038.6 43.9 %all-to-all-start.10 = ((bf16[8,80,1280]{2,1,0:T(8,128)(2,1)}), bf16[8,80,1280]{2,1,0:T(8,128)(2,1)S(1)}, u32[]{:S(2)}, u32[]{:S(2)}) async-start(bf16[8,80,1280]{2,1,0:T(8,128)(2,1)} %reduce-scatter.17.cloned.1.call-done), calls=%async_computation.16 | async-start | bytes 3276800 | tf_op jit(solution)/shard_map/all_to_all | solution.py:73
  1044.1 19.4 %reduce-scatter.15.cloned.1.call-start = ((), (), s32[]{:S(2)}) async-start(), calls=%async_computation.29 | async-start | bytes 983040 | tf_op jit(solution)/shard_map/reduce_scatter | solution.py:54
  1085.4 7.1 copy-start.3
  1085.4 7.2 copy-start.8
  1085.4 7.2 copy-start.12
Sparse Core Ops, SparseCore 0:
  10.2 180.6 all-gather.26
  219.5 37.6 all-gather.10
  269.4 52.9 all-gather.12
  346.8 14.5 reduce-scatter.6
  388.9 85.8 all-gather.14
  481.3 58.9 all-gather.16
  548.3 43.2 reduce-scatter.10
  603.1 16.5 reduce-scatter.8
  670.9 38.2 all-gather.18
  721.2 53.0 all-gather.20
  798.7 14.6 reduce-scatter.12
  840.7 85.9 all-gather.22
  933.2 58.9 all-gather.24
  994.3 43.3 reduce-scatter.16
  1047.0 16.5 reduce-scatter.14

commit v5 on v3

--- a/solution.py
+++ b/solution.py
@@ -1,3 +1,5 @@
+import functools
+
 import jax
 import jax.numpy as jnp
 from jax import lax
@@ -38,6 +40,21 @@
     return (widened * lax.rsqrt(squares / model_width + NORM_EPS)[:, None] * gain_row).astype(
         jnp.bfloat16
     )
+
+
+def swap_cores(value):
+    count = lax.axis_size("section")
+    return lax.ppermute(value, "section", [(source, (source + 1) % count) for source in range(count)])
+
+
+def paired_gather(value, axis, split_axis, active):
+    value = jnp.where(active, value, swap_cores(value))
+    first, second = jnp.split(value, 2, axis=split_axis)
+    gathered = lax.all_gather(jnp.where(active, first, second), "expert", axis=axis, tiled=True)
+    theirs = swap_cores(gathered)
+    lead = jnp.where(active, gathered, theirs)
+    trail = jnp.where(active, theirs, gathered)
+    return jnp.concatenate([lead, trail], axis=split_axis)
 
 
 def terms_to_slots(terms):
@@ -112,6 +129,11 @@
             section_id == 0, hidden_in[min(tick_index, micro_count - 1)], carried_rows
         )
         active = (tick_index - section_id >= 0) & (tick_index - section_id < micro_count)
+        if micro_count == 1 and sections == 2:
+            expert_gather = functools.partial(paired_gather, active=active)
+        else:
+            def expert_gather(value, axis, split_axis):
+                return lax.all_gather(value, "expert", axis=axis, tiled=True)
         segments = segment_ids[micro_index]
         lengths = prompt_lengths[micro_index]
         choices = expert_choice[0, micro_index]
@@ -131,7 +153,7 @@
         cache = jnp.stack(
             [key_rows.reshape(tokens_dev, -1), value_rows.reshape(tokens_dev, -1)], axis=1
         )
-        kv_piece = lax.all_gather(cache.reshape(tokens_dev, -1), "expert", axis=0, tiled=True)
+        kv_piece = expert_gather(cache.reshape(tokens_dev, -1), 0, 1)
         key_count = kv_piece.shape[0]
         kv_piece = kv_piece.reshape(key_count, 2, kv_local, head_width)
         key_slots = jnp.arange(key_count, dtype=jnp.int32)
@@ -156,7 +178,7 @@
         )
         numerator, denominator = (numerator, jnp.sum(weights_full, axis=-1))
         attended = (numerator / denominator[..., None]).astype(jnp.bfloat16).reshape(tokens_dev, -1)
-        attended_all = lax.all_gather(attended, "expert", axis=0, tiled=True)
+        attended_all = expert_gather(attended, 0, 1)
         attn_terms = lax.dot_general(
             attended_all, out_local, (((1,), (1,)), ((), ())), preferred_element_type=jnp.float32
         )
@@ -164,7 +186,7 @@
         after_attn = (incoming.astype(jnp.float32) + attn_sum).astype(jnp.bfloat16)
         moe_in = norm_rows(after_attn, ffn_gain[0], model_width)
         moe_rows = lax.all_gather(moe_in, "tensor", axis=1, tiled=True)
-        moe_all = lax.all_gather(moe_rows, "expert", axis=0, tiled=True)
+        moe_all = expert_gather(moe_rows, 0, 1)
         shared_hidden = jnp.dot(
             moe_all,
             shared_in_cols.reshape(model_width, 2 * shared_cols),
@@ -173,7 +195,7 @@
         shared_act = (
             jax.nn.silu(shared_hidden[:, :shared_cols]) * shared_hidden[:, shared_cols:]
         ).astype(jnp.bfloat16)
-        shared_act = lax.all_gather(shared_act, "expert", axis=1, tiled=True)
+        shared_act = expert_gather(shared_act, 1, 0)
         shared_terms = lax.dot_general(
             shared_act,
             shared_down_local,

time: 1080 us -> 1030 us (0.954)
  waiting for transfers between devices: 576 us -> 429 us
  blocking collectives: 211 us -> 308 us
  other arithmetic: 63.1 us -> 85.7 us
  matrix products: 68.9 us -> 53.9 us
    all_gather x8 -> x6, waiting for transfers between devices: 390 us -> 244 us  [paired_gather(): lax.all_gather(jnp.where(active, first, second), 'expert', axis=axis, til...]
    all_gather x0 -> x2, blocking collectives: none -> 55 us  [paired_gather(): lax.all_gather(jnp.where(active, first, second), 'expert', axis=axis, til...]
    all_to_all x2 -> x4, blocking collectives: 40.8 us -> 84.7 us  [terms_to_slots(): lax.all_to_all(terms, 'expert', split_axis=0, concat_axis=1, tiled=True)]
    reduce_scatter x2, waiting for transfers between devices: 73.2 us -> 35.4 us  [expert_path(): lax.psum_scatter(partial_value.astype(jnp.bfloat16), 'tensor', scatter_di...]
    ppermute x0 -> x16, waiting for transfers between devices: none -> 31.4 us  [swap_cores(): lax.ppermute(value, 'section', [(source, (source + 1) % count) for source...]
    select_n x0 -> x24, other arithmetic: none -> 18.3 us  [the longest x8 12.2 us: paired_gather(): lead = jnp.where(active, gathered, theirs)]
    unnamed x78 -> x80, local copies, waits for them, and re-layouts: 40.8 us -> 38.4 us
  transfers between devices with their start and end apart: 21 -> 33, of which waited for: 17 -> 29; matrix products, arithmetic and copies ran while one was open for 13% -> 14% of each run, Pallas kernels for 0% -> 0%
where the time goes in v5:
time: 1030 us; the launch traced here: 1020 us
  waiting for transfers between devices  429 us (42%)
  blocking collectives  308 us (30%)
  local copies, waits for them, and re-layouts  106 us (10%)
  other arithmetic  85.7 us (8%)
  matrix products  53.9 us (5%)
  starting transfers between devices  22.3 us (2%)
  between operations  15.3 us (1%)
    all_gather x6, waiting for transfers between devices, paired_gather(): lax.all_gather(jnp.where(active, first, second), 'expert', axis=axis, til...  244 us
    all_gather x1, blocking collectives, local(): lax.all_gather(expert_choice[0], 'expert', axis=0, tiled=False)  102 us
    all_to_all x4, blocking collectives, terms_to_slots(): lax.all_to_all(terms, 'expert', split_axis=0, concat_axis=1, tiled=True)  84.7 us
    all_gather x2, blocking collectives, paired_gather(): lax.all_gather(jnp.where(active, first, second), 'expert', axis=axis, til...  55 us
    all_gather x1, waiting for transfers between devices, local(): qkv_full = lax.all_gather(w_qkv[0], 'expert', axis=0, tiled=True)  42.6 us
    unnamed x80, local copies, waits for them, and re-layouts  38.4 us
    reduce_scatter x4, waiting for transfers between devices, terms_to_slots(): return lax.psum_scatter(by_slot, 'tensor', scatter_dimension=1, tiled=True)  37.9 us
    reduce_scatter x2, waiting for transfers between devices, expert_path(): lax.psum_scatter(partial_value.astype(jnp.bfloat16), 'tensor', scatter_di...  35.4 us
  transfers between devices with their start and end apart: 33, of which 29 were waited for; matrix products, arithmetic and copies ran while one was open for 14% of the time, Pallas kernels for 0%

profile of v5, /device:TPU:0, one launch (start us, length us, event | category | flops | bytes accessed | tf_op | source)
XLA Modules:
  0.0 1020.3 jit_solution(13464938864178165217)
XLA Ops:
  7.9 8.5 copy.150
  16.5 7.4 all-to-all-start
  25.9 4.9 psum.42
  30.8 102.3 %all_gather.44 = s32[8,1,128,4]{2,3,1,0:T(4,128)S(1)} all-gather(s32[1,1,128,4]{2,3,1,0:T(4,128)S(1)} %copy-done.19), channel_id=1, replica_groups=mesh['section'=2,'expert'=8,'tensor'=2] {'expert'}, dimensions={0}, use_global_device_ids=true | all-gather | bytes 18432 | tf_op jit(solution)/shard_map/all_gather | solution.py:108
  134.4 9.1 all_gather.42
  148.2 42.6 %all-gather.21.cloned.1.call-done = bf16[1,2560,2,896]{3,2,0,1:T(2,128)(2,1)} async-done(((bf16[1,320,2,896]{3,2,0,1:T(2,128)(2,1)}), bf16[1,2560,2,896]{3,2,0,1:T(2,128)(2,1)}) %all-gather.21.cloned.1.call-update) | async-done | bytes 9175056 | tf_op jit(solution)/shard_map/all_gather | solution.py:104
  190.9 8.7 copy.207
  199.6 12.9 %copy.153 = bf16[1792,2560]{1,0:T(8,128)(2,1)} copy(bf16[1792,2560]{0,1:T(8,128)(2,1)} %bitcast.248) | data formatting | bytes 18350080 | tf_op jit(solution)/shard_map/dot_general | solution.py:146
  212.4 6.2 fusion.102
  220.2 27.5 %all_gather.45 = bf16[1024,256]{0,1:T(8,128)(2,1)S(1)} all-gather(bf16[128,256]{0,1:T(8,128)(2,1)S(1)} %slice_select_fusion.7), channel_id=1, replica_groups=mesh['section'=2,'expert'=8,'tensor'=2] {'expert'}, dimensions={0}, use_global_device_ids=true | all-gather | bytes 589824 | tf_op jit(solution)/shard_map/all_gather | solution.py:53
  255.1 38.9 %all-gather.9.cloned.1.call-done = bf16[1024,640]{1,0:T(8,128)(2,1)} async-done(((bf16[128,640]{1,0:T(8,128)(2,1)}), bf16[1024,640]{1,0:T(8,128)(2,1)}) %all-gather.9.cloned.1.call-update) | async-done | bytes 1310736 | tf_op jit(solution)/shard_map/all_gather | solution.py:53
  294.0 3.2 collective-permute-done.3
  300.1 21.0 %all_to_all.104 = bf16[8,128,320]{1,2,0:T(8,128)(2,1)S(1)} all-to-all(bf16[8,128,320]{1,2,0:T(8,128)(2,1)S(1)} %bitcast.261), channel_id=1, replica_groups=mesh['section'=2,'expert'=8,'tensor'=2] {'expert'}, dimensions={0} | all-to-all | bytes 1310720 | tf_op jit(solution)/shard_map/all_to_all | solution.py:61
  322.3 14.7 %reduce-scatter.7.cloned.1.call-done = bf16[128,1280]{1,0:T(8,128)(2,1)} async-done(((bf16[128,2560]{1,0:T(8,128)(2,1)}), bf16[128,1280]{1,0:T(8,128)(2,1)}) %reduce-scatter.7.cloned.1.call-update) | async-done | bytes 327696 | tf_op jit(solution)/shard_map/reduce_scatter | solution.py:62
  338.2 4.9 psum.43
  344.0 9.0 all_gather.47
  356.0 54.8 %all-gather.11.cloned.1.call-done = bf16[1024,1280]{1,0:T(8,128)(2,1)} async-done(((bf16[128,1280]{1,0:T(8,128)(2,1)}), bf16[1024,1280]{1,0:T(8,128)(2,1)}) %all-gather.11.cloned.1.call-update) | async-done | bytes 2621456 | tf_op jit(solution)/shard_map/all_gather | solution.py:53
  410.8 7.7 copy.208
  419.2 23.6 %compare_select_fusion = s32[8,128,1]{2,0,1:T(8,128)S(1)} fusion(pred[8,128,1]{2,0,1:T(8,128)(4,1)S(1)} %copy.164, s32[8,128,1]{2,0,1:T(8,128)S(1)} %copy.163), kind=kOutput, calls=%fused_computation.58 | output fusion | flops 135168 | bytes 9216 | tf_op jit(solution)/shard_map/jit(cumsum)/reduce_window_sum | solution.py:224
  443.5 4.3 scatter_custom_fusion.1
  448.0 4.7 scatter_custom_fusion
  452.9 2.9 broadcast_select_fusion.5
  462.2 11.3 %gather_fusion = bf16[640,2560]{1,0:T(8,128)(2,1)} fusion(bf16[1024,2560]{1,0:T(8,128)(2,1)} %pad_maximum_fusion, s32[1024]{0:T(1024)S(1)} %pad_clamp_fusion.1), kind=kCustom, calls=%fused_computation | custom fusion | bytes 6556160 | tf_op jit(solution)/shard_map/gather | solution.py:240
  473.6 3.9 broadcast_select_fusion.1
  478.5 8.6 fusion.141
  489.2 4.1 convolution_convert_fusion.1
  493.4 28.6 %all-gather.13.cloned.1.call-done = bf16[512,1536]{0,1:T(8,128)(2,1)} async-done(((bf16[512,192]{0,1:T(8,128)(2,1)}), bf16[512,1536]{0,1:T(8,128)(2,1)}) %all-gather.13.cloned.1.call-update) | async-done | bytes 1572880 | tf_op jit(solution)/shard_map/all_gather | solution.py:53
  522.0 3.6 collective-permute-done.7
  528.8 21.3 %all_to_all.105 = bf16[8,128,320]{1,2,0:T(8,128)(2,1)} all-to-all(bf16[8,128,320]{1,2,0:T(8,128)(2,1)S(1)} %bitcast.263), channel_id=1, replica_groups=mesh['section'=2,'expert'=8,'tensor'=2] {'expert'}, dimensions={0} | all-to-all | bytes 1310720 | tf_op jit(solution)/shard_map/all_to_all | solution.py:61
  550.1 17.7 %reduce-scatter.11.cloned.1.call-done = bf16[8,80,1280]{2,1,0:T(8,128)(2,1)} async-done(((bf16[8,80,2560]{2,1,0:T(8,128)(2,1)}), bf16[8,80,1280]{2,1,0:T(8,128)(2,1)}) %reduce-scatter.11.cloned.1.call-update) | async-done | bytes 1638416 | tf_op jit(solution)/shard_map/reduce_scatter | solution.py:78
  567.9 5.5 all-to-all-start.3
  584.0 5.0 psum.44
  589.9 5.2 reduce-scatter.9.cloned.1.call-done
  595.1 16.7 %all-to-all-done.3 = bf16[8,80,1280]{2,1,0:T(8,128)(2,1)S(1)} async-done(((bf16[8,80,1280]{2,1,0:T(8,128)(2,1)}), bf16[8,80,1280]{2,1,0:T(8,128)(2,1)S(1)}, u32[]{:S(2)}, u32[]{:S(2)}) %all-to-all-start.3) | async-done | bytes 1638432 | tf_op jit(solution)/shard_map/all_to_all | solution.py:81
  611.7 2.9 gather_fusion.1
  614.6 3.7 reshape.862
  618.3 3.4 multiply_reduce_fusion.1
  624.6 5.0 psum.45
  629.7 9.5 all_gather.50
  639.2 6.1 fusion.100
  646.9 27.5 %all_gather.51 = bf16[1024,256]{0,1:T(8,128)(2,1)S(1)} all-gather(bf16[128,256]{0,1:T(8,128)(2,1)S(1)} %slice_select_fusion.6), channel_id=1, replica_groups=mesh['section'=2,'expert'=8,'tensor'=2] {'expert'}, dimensions={0}, use_global_device_ids=true | all-gather | bytes 589824 | tf_op jit(solution)/shard_map/all_gather | solution.py:53
  681.7 39.0 %all-gather.15.cloned.1.call-done = bf16[1024,640]{1,0:T(8,128)(2,1)} async-done(((bf16[128,640]{1,0:T(8,128)(2,1)}), bf16[1024,640]{1,0:T(8,128)(2,1)}) %all-gather.15.cloned.1.call-update) | async-done | bytes 1310736 | tf_op jit(solution)/shard_map/all_gather | solution.py:53
  720.7 3.2 collective-permute-done.12
  726.7 21.0 %all_to_all.106 = bf16[8,128,320]{1,2,0:T(8,128)(2,1)S(1)} all-to-all(bf16[8,128,320]{1,2,0:T(8,128)(2,1)S(1)} %bitcast.264), channel_id=1, replica_groups=mesh['section'=2,'expert'=8,'tensor'=2] {'expert'}, dimensions={0} | all-to-all | bytes 1310720 | tf_op jit(solution)/shard_map/all_to_all | solution.py:61
  748.9 14.7 %reduce-scatter.13.cloned.1.call-done = bf16[128,1280]{1,0:T(8,128)(2,1)} async-done(((bf16[128,2560]{1,0:T(8,128)(2,1)}), bf16[128,1280]{1,0:T(8,128)(2,1)}) %reduce-scatter.13.cloned.1.call-update) | async-done | bytes 327696 | tf_op jit(solution)/shard_map/reduce_scatter | solution.py:62
  764.8 4.9 psum.46
  770.9 9.0 all_gather.53
  783.1 54.6 %all-gather.17.cloned.1.call-done = bf16[1024,1280]{1,0:T(8,128)(2,1)} async-done(((bf16[128,1280]{1,0:T(8,128)(2,1)}), bf16[1024,1280]{1,0:T(8,128)(2,1)}) %all-gather.17.cloned.1.call-update) | async-done | bytes 2621456 | tf_op jit(solution)/shard_map/all_gather | solution.py:53
  837.7 5.1 collective-permute-done.14
  851.3 11.3 %gather_fusion.2 = bf16[640,2560]{1,0:T(8,128)(2,1)} fusion(bf16[1024,2560]{1,0:T(8,128)(2,1)} %pad_maximum_fusion.1, s32[1024]{0:T(1024)S(1)} %copy-done.22), kind=kCustom, calls=%fused_computation.2 | custom fusion | bytes 6556160 | tf_op jit(solution)/shard_map/gather | solution.py:240
  862.6 3.9 broadcast_select_fusion
  868.6 8.6 fusion.142
  879.3 4.1 convolution_convert_fusion
  883.4 28.0 %all-gather.19.cloned.1.call-done = bf16[512,1536]{0,1:T(8,128)(2,1)} async-done(((bf16[512,192]{0,1:T(8,128)(2,1)}), bf16[512,1536]{0,1:T(8,128)(2,1)}) %all-gather.19.cloned.1.call-update) | async-done | bytes 1572880 | tf_op jit(solution)/shard_map/all_gather | solution.py:53
  911.4 3.6 collective-permute-done.16
  918.2 21.3 %all_to_all.107 = bf16[8,128,320]{1,2,0:T(8,128)(2,1)} all-to-all(bf16[8,128,320]{1,2,0:T(8,128)(2,1)S(1)} %bitcast.266), channel_id=1, replica_groups=mesh['section'=2,'expert'=8,'tensor'=2] {'expert'}, dimensions={0} | all-to-all | bytes 1310720 | tf_op jit(solution)/shard_map/all_to_all | solution.py:61
  939.5 17.6 %reduce-scatter.17.cloned.1.call-done = bf16[8,80,1280]{2,1,0:T(8,128)(2,1)} async-done(((bf16[8,80,2560]{2,1,0:T(8,128)(2,1)}), bf16[8,80,1280]{2,1,0:T(8,128)(2,1)}) %reduce-scatter.17.cloned.1.call-update) | async-done | bytes 1638416 | tf_op jit(solution)/shard_map/reduce_scatter | solution.py:78
  957.2 5.5 all-to-all-start.6
  969.2 3.6 broadcast_select_fusion.27
  973.9 5.0 psum.47
  979.1 3.3 reduce-scatter.15.cloned.1.call-done
  982.4 18.7 %all-to-all-done.6 = bf16[8,80,1280]{2,1,0:T(8,128)(2,1)S(1)} async-done(((bf16[8,80,1280]{2,1,0:T(8,128)(2,1)}), bf16[8,80,1280]{2,1,0:T(8,128)(2,1)S(1)}, u32[]{:S(2)}, u32[]{:S(2)}) %all-to-all-start.6) | async-done | bytes 1638432 | tf_op jit(solution)/shard_map/all_to_all | solution.py:81
  1004.0 3.7 reshape.863
  1007.6 3.4 multiply_reduce_fusion
  (270 shorter events, 101.9 us)
Async XLA Ops:
  7.2 520.3 %copy-start = (bf16[1,320,1536]{2,1,0:T(8,128)(2,1)S(1)}, bf16[1,320,1536]{2,1,0:T(8,128)(2,1)}, u32[]{:S(2)}) copy-start(bf16[1,320,1536]{2,1,0:T(8,128)(2,1)} %param.30) | copy-start | bytes 2949124
  7.2 183.7 %all-gather.21.cloned.1.call-start = ((), (), s32[]{:S(2)}) async-start(), calls=%async_computation.25 | async-start | bytes 10321920 | tf_op jit(solution)/shard_map/all_gather | solution.py:104
  16.4 7.5 copy-start.34
  16.4 8.3 copy-start.25
  16.4 14.4 %copy-start.19 = (s32[1,1,128,4]{2,3,1,0:T(4,128)S(1)}, s32[1,1,128,4]{2,3,1,0:T(4,128)}, u32[]{:S(2)}) copy-start(s32[1,1,128,4]{2,3,1,0:T(4,128)} %param.24) | copy-start | bytes 6148
  16.4 116.8 %copy-start.27 = (s32[1,128]{1,0:T(1,128)S(1)}, s32[1,128]{1,0:T(1,128)}, u32[]{:S(2)}) copy-start(s32[1,128]{1,0:T(1,128)} %param.22) | copy-start | bytes 1540
  16.5 127.3 %all-to-all-start = ((bf16[320,2,1536]{0,1,2:T(2,128)(2,1)}), bf16[320,2,1536]{0,1,2:T(2,128)(2,1)S(1)}, u32[]{:S(2)}, u32[]{:S(2)}) async-start(bf16[320,2,1536]{0,1,2:T(2,128)(2,1)} %bitcast.251), calls=%async_computation | async-start | bytes 4718592 | tf_op jit(solution)/shard_map/all_to_all | solution.py:107
  23.9 270.2 %all-gather.9.cloned.1.call-start = ((), (), s32[]{:S(2)}) async-start(), calls=%async_computation.13 | async-start | bytes 1474560 | tf_op jit(solution)/shard_map/all_gather | solution.py:53
  24.7 118.8 %copy-start.17 = (f32[1280]{0:T(1024)}, f32[1280]{0:T(1024)S(1)}, u32[]{:S(2)}) copy-start(f32[1280]{0:T(1024)S(1)} %reduce.33) | copy-start | bytes 15364
  199.6 12.9 %copy-start.4 = (bf16[128,2560]{1,0:T(8,128)(2,1)S(1)}, bf16[128,2560]{1,0:T(8,128)(2,1)}, u32[]{:S(2)}) copy-start(bf16[128,2560]{1,0:T(8,128)(2,1)} %all_gather.42) | copy-start | bytes 1966084
  218.7 1.4 collective-permute-start
  247.7 1.9 collective-permute-start.1
  247.9 3.2 copy-start.13
  252.4 1.7 collective-permute-start.2
  254.9 44.0 %copy-start.32 = (bf16[1,320,1280]{2,1,0:T(8,128)(2,1)S(1)}, bf16[1,320,1280]{2,1,0:T(8,128)(2,1)}, u32[]{:S(2)}) copy-start(bf16[1,320,1280]{2,1,0:T(8,128)(2,1)} %param.28) | copy-start | bytes 2457604
  254.9 82.1 %reduce-scatter.7.cloned.1.call-start = ((), (), s32[]{:S(2)}) async-start(), calls=%async_computation.14 | async-start | bytes 983040 | tf_op jit(solution)/shard_map/reduce_scatter | solution.py:62
  294.0 3.2 collective-permute-start.3
  299.9 22.4 %copy-start.26 = (f32[1,1280]{1,0:T(1,128)S(1)}, f32[1,1280]{1,0:T(1,128)}, u32[]{:S(2)}) copy-start(f32[1,1280]{1,0:T(1,128)} %param.26) | copy-start | bytes 15364
  299.9 37.1 %copy-start.1 = (bf16[1,128,1280]{2,1,0:T(8,128)(2,1)S(1)}, bf16[1,128,1280]{2,1,0:T(8,128)(2,1)}, u32[]{:S(2)}) copy-start(bf16[1,128,1280]{2,1,0:T(8,128)(2,1)} %param.21) | copy-start | bytes 983044
  322.2 88.6 %all-gather.11.cloned.1.call-start = ((), (), s32[]{:S(2)}) async-start(), calls=%async_computation.15 | async-start | bytes 2949120 | tf_op jit(solution)/shard_map/all_gather | solution.py:53
  322.3 33.6 %copy-start.15 = (f32[1280]{0:T(1024)}, f32[1280]{0:T(1024)S(1)}, u32[]{:S(2)}) copy-start(f32[1280]{0:T(1024)S(1)} %reduce.34) | copy-start | bytes 15364
  353.0 2.1 collective-permute-start.4
  356.0 166.0 %all-gather.13.cloned.1.call-start = ((), (), s32[]{:S(2)}) async-start(), calls=%async_computation.16 | async-start | bytes 1769472 | tf_op jit(solution)/shard_map/all_gather | solution.py:53
  410.8 42.1 %collective-permute-start.5 = (bf16[1024,1280]{1,0:T(8,128)(2,1)}, bf16[1024,1280]{1,0:T(8,128)(2,1)}, u32[]{:S(2)}, u32[]{:S(2)}) collective-permute-start(bf16[1024,1280]{1,0:T(8,128)(2,1)} %all-gather.11.cloned.1.call-done), channel_id=1, source_target_pairs={{0,16},{16,0},{1,17},{17,1},{2,18},{18,2},{3,19},{19,3},{4,20},{20... | collective-permute-start | bytes 7864328 | tf_op jit(solution)/shard_map/ppermute | solution.py:47
  410.8 32.2 %copy-start.29 = (s32[2]{0:T(128)S(1)}, s32[2]{0:T(128)}, u32[]{:S(2)}) copy-start(s32[2]{0:T(128)} %constant.173) | copy-start | bytes 28
  410.8 32.4 %copy-start.28 = (s32[2]{0:T(128)S(1)}, s32[2]{0:T(128)}, u32[]{:S(2)}) copy-start(s32[2]{0:T(128)} %constant.176) | copy-start | bytes 28
  452.8 20.7 %copy-start.23 = (pred[8,80]{1,0:T(8,128)(4,1)}, pred[8,80]{1,0:T(8,128)(4,1)S(1)}, u32[]{:S(2)}) copy-start(pred[8,80]{1,0:T(8,128)(4,1)S(1)} %reshape.857) | copy-start | bytes 1924
  452.9 9.4 copy-start.21
  455.8 2.7 copy-start.5
  461.7 15.8 %collective-permute-start.6 = (bf16[1024,192]{0,1:T(8,128)(2,1)}, bf16[1024,192]{0,1:T(8,128)(2,1)}, u32[]{:S(2)}, u32[]{:S(2)}) collective-permute-start(bf16[1024,192]{0,1:T(8,128)(2,1)} %fusion.81), channel_id=1, source_target_pairs={{0,16},{16,0},{1,17},{17,1},{2,18},{18,2},{3,19},{19,3},{4,20},{20... | collective-permute-start | bytes 1179656 | tf_op jit(solution)/shard_map/ppermute | solution.py:47
  478.4 89.4 %reduce-scatter.11.cloned.1.call-start = ((), (), s32[]{:S(2)}) async-start(), calls=%async_computation.18 | async-start | bytes 4915200 | tf_op jit(solution)/shard_map/reduce_scatter | solution.py:78
  522.0 3.6 collective-permute-start.7
  567.9 43.9 %all-to-all-start.3 = ((bf16[8,80,1280]{2,1,0:T(8,128)(2,1)}), bf16[8,80,1280]{2,1,0:T(8,128)(2,1)S(1)}, u32[]{:S(2)}, u32[]{:S(2)}) async-start(bf16[8,80,1280]{2,1,0:T(8,128)(2,1)} %reduce-scatter.11.cloned.1.call-done), calls=%async_computation.6 | async-start | bytes 3276800 | tf_op jit(solution)/shard_map/all_to_all | solution.py:81
  573.3 21.7 %reduce-scatter.9.cloned.1.call-start = ((), (), s32[]{:S(2)}) async-start(), calls=%async_computation.17 | async-start | bytes 983040 | tf_op jit(solution)/shard_map/reduce_scatter | solution.py:62
  578.4 142.4 %all-gather.15.cloned.1.call-start = ((), (), s32[]{:S(2)}) async-start(), calls=%async_computation.19 | async-start | bytes 1474560 | tf_op jit(solution)/shard_map/all_gather | solution.py:53
  618.3 3.4 copy-start.11
  618.3 11.3 %copy-start.18 = (f32[1280]{0:T(1024)S(1)}, f32[1280]{0:T(1024)}, u32[]{:S(2)}) copy-start(f32[1280]{0:T(1024)} %copy-done.17) | copy-start | bytes 15364
  621.8 2.8 copy-start.7
  621.8 2.5 collective-permute-start.8
  645.5 31.1 %copy-start.9 = (bf16[128,2,128]{0,2,1:T(8,128)(2,1)}, bf16[128,2,128]{0,2,1:T(8,128)(2,1)S(1)}, u32[]{:S(2)}) copy-start(bf16[128,2,128]{0,2,1:T(8,128)(2,1)S(1)} %pad_maximum_fusion.7) | copy-start | bytes 196612
  645.5 1.4 collective-permute-start.9
  674.4 1.9 collective-permute-start.10
  679.2 1.7 collective-permute-start.11
  681.6 43.9 %copy-start.33 = (bf16[1,320,1280]{2,1,0:T(8,128)(2,1)S(1)}, bf16[1,320,1280]{2,1,0:T(8,128)(2,1)}, u32[]{:S(2)}) copy-start(bf16[1,320,1280]{2,1,0:T(8,128)(2,1)} %param.28) | copy-start | bytes 2457604
  681.6 82.1 %reduce-scatter.13.cloned.1.call-start = ((), (), s32[]{:S(2)}) async-start(), calls=%async_computation.20 | async-start | bytes 983040 | tf_op jit(solution)/shard_map/reduce_scatter | solution.py:62
  720.7 3.2 collective-permute-start.12
  726.6 43.2 %copy-start.16 = (f32[1280]{0:T(1024)S(1)}, f32[1280]{0:T(1024)}, u32[]{:S(2)}) copy-start(f32[1280]{0:T(1024)} %copy-done.15) | copy-start | bytes 15364
  748.9 88.8 %all-gather.17.cloned.1.call-start = ((), (), s32[]{:S(2)}) async-start(), calls=%async_computation.21 | async-start | bytes 2949120 | tf_op jit(solution)/shard_map/all_gather | solution.py:53
  779.9 2.1 collective-permute-start.13
  782.8 128.6 %all-gather.19.cloned.1.call-start = ((), (), s32[]{:S(2)}) async-start(), calls=%async_computation.22 | async-start | bytes 1769472 | tf_op jit(solution)/shard_map/all_gather | solution.py:53
  837.7 7.5 copy-start.6
  837.7 5.1 collective-permute-start.14
  847.4 3.9 copy-start.22
  851.2 11.5 %copy-start.24 = (pred[8,80]{1,0:T(8,128)(4,1)S(1)}, pred[8,80]{1,0:T(8,128)(4,1)}, u32[]{:S(2)}) copy-start(pred[8,80]{1,0:T(8,128)(4,1)} %copy-done.23) | copy-start | bytes 1924
  851.2 15.4 %collective-permute-start.15 = (bf16[1024,192]{0,1:T(8,128)(2,1)}, bf16[1024,192]{0,1:T(8,128)(2,1)}, u32[]{:S(2)}, u32[]{:S(2)}) collective-permute-start(bf16[1024,192]{0,1:T(8,128)(2,1)} %fusion.80), channel_id=1, source_target_pairs={{0,16},{16,0},{1,17},{17,1},{2,18},{18,2},{3,19},{19,3},{4,20},{20... | collective-permute-start | bytes 1179656 | tf_op jit(solution)/shard_map/ppermute | solution.py:47
  868.5 88.7 %reduce-scatter.17.cloned.1.call-start = ((), (), s32[]{:S(2)}) async-start(), calls=%async_computation.24 | async-start | bytes 4915200 | tf_op jit(solution)/shard_map/reduce_scatter | solution.py:78
  911.4 3.6 collective-permute-start.16
  939.5 28.8 %copy-start.10 = (bf16[128,2,128]{0,2,1:T(8,128)(2,1)S(1)}, bf16[128,2,128]{0,2,1:T(8,128)(2,1)}, u32[]{:S(2)}) copy-start(bf16[128,2,128]{0,2,1:T(8,128)(2,1)} %copy-done.9) | copy-start | bytes 196612
  957.2 43.9 %all-to-all-start.6 = ((bf16[8,80,1280]{2,1,0:T(8,128)(2,1)}), bf16[8,80,1280]{2,1,0:T(8,128)(2,1)S(1)}, u32[]{:S(2)}, u32[]{:S(2)}) async-start(bf16[8,80,1280]{2,1,0:T(8,128)(2,1)} %reduce-scatter.17.cloned.1.call-done), calls=%async_computation.12 | async-start | bytes 3276800 | tf_op jit(solution)/shard_map/all_to_all | solution.py:81
  962.7 16.3 %copy-start.20 = (s32[1,1,128,4]{2,3,1,0:T(4,128)S(1)}, s32[1,1,128,4]{2,3,1,0:T(4,128)}, u32[]{:S(2)}) copy-start(s32[1,1,128,4]{2,3,1,0:T(4,128)} %param.24) | copy-start | bytes 6148
  962.7 19.8 %reduce-scatter.15.cloned.1.call-start = ((), (), s32[]{:S(2)}) async-start(), calls=%async_computation.23 | async-start | bytes 983040 | tf_op jit(solution)/shard_map/reduce_scatter | solution.py:62
  1007.6 3.5 copy-start.3
  1007.6 3.5 copy-start.8
  1007.6 3.5 copy-start.12
  (4 other events, 7.0 us)
Sparse Core Ops, SparseCore 0:
  10.2 180.6 all-gather.20
  255.0 39.0 all-gather.8
  322.3 14.6 reduce-scatter.6
  356.1 54.6 all-gather.10
  478.6 43.3 all-gather.12
  524.2 43.6 reduce-scatter.10
  578.5 16.5 reduce-scatter.8
  681.7 38.9 all-gather.14
  749.0 14.6 reduce-scatter.12
  782.9 54.6 all-gather.16
  868.6 42.7 all-gather.18
  913.5 43.5 reduce-scatter.16
  965.9 16.5 reduce-scatter.14

commit v6 on v5

--- a/solution.py
+++ b/solution.py
@@ -34,12 +34,10 @@
     )
 
 
-def norm_rows(values_in, gain_row, model_width):
-    widened = values_in.astype(jnp.float32)
-    squares = lax.psum(jnp.sum(widened * widened, axis=-1), "tensor")
-    return (widened * lax.rsqrt(squares / model_width + NORM_EPS)[:, None] * gain_row).astype(
-        jnp.bfloat16
-    )
+def norm_full_rows(values_in, gain_full):
+    widened = lax.all_gather(values_in, "tensor", axis=1, tiled=True).astype(jnp.float32)
+    squares = jnp.mean(widened * widened, axis=-1)
+    return (widened * lax.rsqrt(squares + NORM_EPS)[:, None] * gain_full).astype(jnp.bfloat16)
 
 
 def swap_cores(value):
@@ -106,8 +104,13 @@
     shared_down_local = w_shared_down[0]
     shared_in_cols = lax.all_to_all(w_shared_in[0], "expert", split_axis=2, concat_axis=0, tiled=True)
     choices_every = lax.all_gather(expert_choice[0], "expert", axis=0, tiled=False)
-    qkv_full, shared_in_cols, choices_every = lax.optimization_barrier(
-        (qkv_full, shared_in_cols, choices_every)
+    router_full = lax.all_gather(router_weight[0], "tensor", axis=0, tiled=True)
+    attn_gain_full = lax.all_gather(attn_gain[0], "tensor", axis=0, tiled=True)
+    ffn_gain_full = lax.all_gather(ffn_gain[0], "tensor", axis=0, tiled=True)
+    qkv_full, shared_in_cols, choices_every, router_full, attn_gain_full, ffn_gain_full = (
+        lax.optimization_barrier(
+            (qkv_full, shared_in_cols, choices_every, router_full, attn_gain_full, ffn_gain_full)
+        )
     )
     model_width, kv_local, group_cols = qkv_full.shape
     shared_cols = shared_in_cols.shape[2]
@@ -141,8 +144,7 @@
         member = segments[:, None] == jnp.arange(lengths.shape[0], dtype=jnp.int32)[None, :]
         first_slot = jnp.sum(jnp.where(member, starts[None, :], 0), axis=1)
         positions = jnp.where(segments >= 0, slot_index - first_slot, 0).astype(jnp.float32)
-        normed = norm_rows(incoming, attn_gain[0], model_width)
-        normed_full = lax.all_gather(normed, "tensor", axis=1, tiled=True)
+        normed_full = norm_full_rows(incoming, attn_gain_full)
         projected = jnp.dot(
             normed_full, qkv_full.reshape(model_width, -1), preferred_element_type=jnp.float32
         )
@@ -184,8 +186,7 @@
         )
         attn_sum = terms_to_slots(attn_terms.astype(jnp.bfloat16)).astype(jnp.float32)
         after_attn = (incoming.astype(jnp.float32) + attn_sum).astype(jnp.bfloat16)
-        moe_in = norm_rows(after_attn, ffn_gain[0], model_width)
-        moe_rows = lax.all_gather(moe_in, "tensor", axis=1, tiled=True)
+        moe_rows = norm_full_rows(after_attn, ffn_gain_full)
         moe_all = expert_gather(moe_rows, 0, 1)
         shared_hidden = jnp.dot(
             moe_all,
@@ -204,9 +205,8 @@
         )
         shared_sum = terms_to_slots(shared_terms.astype(jnp.bfloat16))
         shared_out = lax.optimization_barrier(shared_sum).astype(jnp.float32)
-        logits = lax.psum(
-            jnp.dot(moe_in.astype(jnp.float32), router_weight[0], precision=lax.Precision.HIGHEST),
-            "tensor",
+        logits = jnp.dot(
+            moe_rows.astype(jnp.float32), router_full, precision=lax.Precision.HIGHEST
         )
         expert_ids = jnp.arange(logits.shape[1], dtype=jnp.int32)
         picked = jnp.sum(

time: 1030 us -> 1020 us (level)
  blocking collectives: 308 us -> 292 us
  waiting for transfers between devices: 429 us -> 418 us
    psum x6 -> x0, blocking collectives: 29.8 us -> none  [the longest x4 19.8 us: norm_rows(): squares = lax.psum(jnp.sum(widened * widened, axis=-1), 'tensor')]
    all_gather x4 -> x7, blocking collectives: 36.6 us -> 52.1 us  [the longest x4 38.8 us: norm_full_rows(): lax.all_gather(values_in, 'tensor', axis=1, tiled=True).astype(jnp.float32)]
    unnamed x80 -> x90, local copies, waits for them, and re-layouts: 38.4 us -> 40.7 us
  transfers between devices with their start and end apart: 33 -> 33, of which waited for: 29 -> 29; matrix products, arithmetic and copies ran while one was open for 14% -> 16% of each run, Pallas kernels for 0% -> 0%
where the time goes in v6:
time: 1020 us; the launch traced here: 1010 us
  waiting for transfers between devices  418 us (41%)
  blocking collectives  292 us (29%)
  local copies, waits for them, and re-layouts  115 us (11%)
  other arithmetic  91.5 us (9%)
  matrix products  56.5 us (6%)
  starting transfers between devices  22.5 us (2%)
  between operations  15.3 us (2%)
    all_gather x6, waiting for transfers between devices, paired_gather(): lax.all_gather(jnp.where(active, first, second), 'expert', axis=axis, til...  244 us
    all_gather x1, blocking collectives, local(): lax.all_gather(expert_choice[0], 'expert', axis=0, tiled=False)  99.9 us
    all_to_all x4, blocking collectives, terms_to_slots(): lax.all_to_all(terms, 'expert', split_axis=0, concat_axis=1, tiled=True)  84.7 us
    all_gather x2, blocking collectives, paired_gather(): lax.all_gather(jnp.where(active, first, second), 'expert', axis=axis, til...  55 us
    reduce_scatter x4, waiting for transfers between devices, terms_to_slots(): return lax.psum_scatter(by_slot, 'tensor', scatter_dimension=1, tiled=True)  43.8 us
    unnamed x90, local copies, waits for them, and re-layouts  40.7 us
    all_gather x4, blocking collectives, norm_full_rows(): lax.all_gather(values_in, 'tensor', axis=1, tiled=True).astype(jnp.float32)  38.8 us
    all_gather x1, waiting for transfers between devices, local(): qkv_full = lax.all_gather(w_qkv[0], 'expert', axis=0, tiled=True)  37 us
  transfers between devices with their start and end apart: 33, of which 29 were waited for; matrix products, arithmetic and copies ran while one was open for 16% of the time, Pallas kernels for 0%

profile of v6, /device:TPU:0, one launch (start us, length us, event | category | flops | bytes accessed | tf_op | source)
XLA Modules:
  0.0 1009.9 jit_solution(7740539105196891757)
XLA Ops:
  7.9 8.5 copy.152
  16.5 7.4 all-to-all-start
  24.0 4.4 all-gather.2
  28.4 4.4 all-gather.3
  34.1 99.9 %all_gather.53 = s32[8,1,128,4]{2,3,1,0:T(4,128)} all-gather(s32[1,1,128,4]{2,3,1,0:T(4,128)S(1)} %copy-done.19), channel_id=1, replica_groups=mesh['section'=2,'expert'=8,'tensor'=2] {'expert'}, dimensions={0}, use_global_device_ids=true | all-gather | bytes 18432 | tf_op jit(solution)/shard_map/all_gather | solution.py:106
  134.0 4.7 all-gather.1
  140.5 7.8 all_gather.51
  153.9 37.0 %all-gather.24.cloned.1.call-done = bf16[1,2560,2,896]{3,2,0,1:T(2,128)(2,1)} async-done(((bf16[1,320,2,896]{3,2,0,1:T(2,128)(2,1)}), bf16[1,2560,2,896]{3,2,0,1:T(2,128)(2,1)}) %all-gather.24.cloned.1.call-update) | async-done | bytes 9175056 | tf_op jit(solution)/shard_map/all_gather | solution.py:102
  190.8 8.7 copy.209
  199.6 12.9 %copy.155 = bf16[1792,2560]{1,0:T(8,128)(2,1)} copy(bf16[1792,2560]{0,1:T(8,128)(2,1)} %bitcast.240) | data formatting | bytes 18350080 | tf_op jit(solution)/shard_map/dot_general | solution.py:148
  212.5 6.2 fusion.98
  220.3 27.5 %all_gather.57 = bf16[1024,256]{0,1:T(8,128)(2,1)S(1)} all-gather(bf16[128,256]{0,1:T(8,128)(2,1)S(1)} %slice_select_fusion.7), channel_id=1, replica_groups=mesh['section'=2,'expert'=8,'tensor'=2] {'expert'}, dimensions={0}, use_global_device_ids=true | all-gather | bytes 589824 | tf_op jit(solution)/shard_map/all_gather | solution.py:51
  255.3 38.9 %all-gather.12.cloned.1.call-done = bf16[1024,640]{1,0:T(8,128)(2,1)} async-done(((bf16[128,640]{1,0:T(8,128)(2,1)}), bf16[1024,640]{1,0:T(8,128)(2,1)}) %all-gather.12.cloned.1.call-update) | async-done | bytes 1310736 | tf_op jit(solution)/shard_map/all_gather | solution.py:51
  294.2 3.2 collective-permute-done.3
  300.2 21.0 %all_to_all.104 = bf16[8,128,320]{1,2,0:T(8,128)(2,1)S(1)} all-to-all(bf16[8,128,320]{1,2,0:T(8,128)(2,1)S(1)} %bitcast.253), channel_id=1, replica_groups=mesh['section'=2,'expert'=8,'tensor'=2] {'expert'}, dimensions={0} | all-to-all | bytes 1310720 | tf_op jit(solution)/shard_map/all_to_all | solution.py:59
  322.4 14.8 %reduce-scatter.7.cloned.1.call-done = bf16[128,1280]{1,0:T(8,128)(2,1)} async-done(((bf16[128,2560]{1,0:T(8,128)(2,1)}), bf16[128,1280]{1,0:T(8,128)(2,1)}) %reduce-scatter.7.cloned.1.call-update) | async-done | bytes 327696 | tf_op jit(solution)/shard_map/reduce_scatter | solution.py:60
  338.2 10.1 %all_gather.59 = bf16[128,2560]{1,0:T(8,128)(2,1)S(1)} all-gather(bf16[128,1280]{1,0:T(8,128)(2,1)S(1)} %add_convert_fusion.3), channel_id=1, replica_groups=mesh['section'=2,'expert'=8,'tensor'=2] {'tensor'}, dimensions={1}, use_global_device_ids=true | all-gather | bytes 983040 | tf_op jit(solution)/shard_map/all_gather | solution.py:38
  352.1 54.8 %all-gather.14.cloned.1.call-done = bf16[1024,1280]{1,0:T(8,128)(2,1)} async-done(((bf16[128,1280]{1,0:T(8,128)(2,1)}), bf16[1024,1280]{1,0:T(8,128)(2,1)}) %all-gather.14.cloned.1.call-update) | async-done | bytes 2621456 | tf_op jit(solution)/shard_map/all_gather | solution.py:51
  406.9 7.7 copy.210
  415.3 23.6 %compare_select_fusion = s32[8,128,1]{2,0,1:T(8,128)S(1)} fusion(pred[8,128,1]{2,0,1:T(8,128)(4,1)S(1)} %copy.166, s32[8,128,1]{2,0,1:T(8,128)S(1)} %copy.165), kind=kOutput, calls=%fused_computation.66 | output fusion | flops 135168 | bytes 9216 | tf_op jit(solution)/shard_map/jit(cumsum)/reduce_window_sum | solution.py:224
  439.6 4.3 scatter_custom_fusion.1
  444.1 4.7 scatter_custom_fusion
  449.0 2.9 broadcast_select_fusion.5
  458.3 11.3 %gather_fusion = bf16[640,2560]{1,0:T(8,128)(2,1)} fusion(bf16[1024,2560]{1,0:T(8,128)(2,1)} %pad_maximum_fusion, s32[1024]{0:T(1024)S(1)} %pad_clamp_fusion.1), kind=kCustom, calls=%fused_computation | custom fusion | bytes 6556160 | tf_op jit(solution)/shard_map/gather | solution.py:240
  469.7 3.9 broadcast_select_fusion.1
  474.6 8.6 fusion.136
  485.3 4.1 convolution_convert_fusion.1
  489.4 28.7 %all-gather.16.cloned.1.call-done = bf16[512,1536]{0,1:T(8,128)(2,1)} async-done(((bf16[512,192]{0,1:T(8,128)(2,1)}), bf16[512,1536]{0,1:T(8,128)(2,1)}) %all-gather.16.cloned.1.call-update) | async-done | bytes 1572880 | tf_op jit(solution)/shard_map/all_gather | solution.py:51
  518.1 3.6 collective-permute-done.7
  524.9 21.3 %all_to_all.105 = bf16[8,128,320]{1,2,0:T(8,128)(2,1)} all-to-all(bf16[8,128,320]{1,2,0:T(8,128)(2,1)S(1)} %bitcast.255), channel_id=1, replica_groups=mesh['section'=2,'expert'=8,'tensor'=2] {'expert'}, dimensions={0} | all-to-all | bytes 1310720 | tf_op jit(solution)/shard_map/all_to_all | solution.py:59
  546.2 17.7 %reduce-scatter.11.cloned.1.call-done = bf16[8,80,1280]{2,1,0:T(8,128)(2,1)} async-done(((bf16[8,80,2560]{2,1,0:T(8,128)(2,1)}), bf16[8,80,1280]{2,1,0:T(8,128)(2,1)}) %reduce-scatter.11.cloned.1.call-update) | async-done | bytes 1638416 | tf_op jit(solution)/shard_map/reduce_scatter | solution.py:76
  563.9 5.5 all-to-all-start.3
  575.1 3.1 reduce-window.19
  595.2 5.9 reduce-scatter.9.cloned.1.call-done
  601.1 6.8 all-to-all-done.3
  607.9 3.0 gather_fusion.1
  610.9 3.7 reshape.880
  614.6 3.4 multiply_reduce_fusion.1
  620.7 10.7 %all_gather.62 = bf16[128,2560]{1,0:T(8,128)(2,1)S(1)} all-gather(bf16[128,1280]{1,0:T(8,128)(2,1)S(1)} %bitcast_select_fusion.2), channel_id=1, replica_groups=mesh['section'=2,'expert'=8,'tensor'=2] {'tensor'}, dimensions={1}, use_global_device_ids=true | all-gather | bytes 983040 | tf_op jit(solution)/shard_map/all_gather | solution.py:38
  631.6 6.2 fusion.95
  639.4 27.5 %all_gather.63 = bf16[1024,256]{0,1:T(8,128)(2,1)S(1)} all-gather(bf16[128,256]{0,1:T(8,128)(2,1)S(1)} %slice_select_fusion.6), channel_id=1, replica_groups=mesh['section'=2,'expert'=8,'tensor'=2] {'expert'}, dimensions={0}, use_global_device_ids=true | all-gather | bytes 589824 | tf_op jit(solution)/shard_map/all_gather | solution.py:51
  674.1 39.1 %all-gather.18.cloned.1.call-done = bf16[1024,640]{1,0:T(8,128)(2,1)} async-done(((bf16[128,640]{1,0:T(8,128)(2,1)}), bf16[1024,640]{1,0:T(8,128)(2,1)}) %all-gather.18.cloned.1.call-update) | async-done | bytes 1310736 | tf_op jit(solution)/shard_map/all_gather | solution.py:51
  713.2 3.2 collective-permute-done.12
  719.2 21.0 %all_to_all.106 = bf16[8,128,320]{1,2,0:T(8,128)(2,1)S(1)} all-to-all(bf16[8,128,320]{1,2,0:T(8,128)(2,1)S(1)} %bitcast.256), channel_id=1, replica_groups=mesh['section'=2,'expert'=8,'tensor'=2] {'expert'}, dimensions={0} | all-to-all | bytes 1310720 | tf_op jit(solution)/shard_map/all_to_all | solution.py:59
  741.4 14.7 %reduce-scatter.13.cloned.1.call-done = bf16[128,1280]{1,0:T(8,128)(2,1)} async-done(((bf16[128,2560]{1,0:T(8,128)(2,1)}), bf16[128,1280]{1,0:T(8,128)(2,1)}) %reduce-scatter.13.cloned.1.call-update) | async-done | bytes 327696 | tf_op jit(solution)/shard_map/reduce_scatter | solution.py:60
  757.2 10.1 %all_gather.65 = bf16[128,2560]{1,0:T(8,128)(2,1)S(1)} all-gather(bf16[128,1280]{1,0:T(8,128)(2,1)S(1)} %add_convert_fusion.1), channel_id=1, replica_groups=mesh['section'=2,'expert'=8,'tensor'=2] {'tensor'}, dimensions={1}, use_global_device_ids=true | all-gather | bytes 983040 | tf_op jit(solution)/shard_map/all_gather | solution.py:38
  771.3 54.6 %all-gather.20.cloned.1.call-done = bf16[1024,1280]{1,0:T(8,128)(2,1)} async-done(((bf16[128,1280]{1,0:T(8,128)(2,1)}), bf16[1024,1280]{1,0:T(8,128)(2,1)}) %all-gather.20.cloned.1.call-update) | async-done | bytes 2621456 | tf_op jit(solution)/shard_map/all_gather | solution.py:51
  825.9 5.1 collective-permute-done.14
  833.4 3.8 fusion.134
  841.0 11.4 %gather_fusion.2 = bf16[640,2560]{1,0:T(8,128)(2,1)} fusion(bf16[1024,2560]{1,0:T(8,128)(2,1)} %pad_maximum_fusion.1, s32[1024]{0:T(1024)S(1)} %copy-done.23), kind=kCustom, calls=%fused_computation.2 | custom fusion | bytes 6556160 | tf_op jit(solution)/shard_map/gather | solution.py:240
  852.3 3.9 broadcast_select_fusion
  858.3 8.6 fusion.138
  869.0 4.1 convolution_convert_fusion
  873.1 28.0 %all-gather.22.cloned.1.call-done = bf16[512,1536]{0,1:T(8,128)(2,1)} async-done(((bf16[512,192]{0,1:T(8,128)(2,1)}), bf16[512,1536]{0,1:T(8,128)(2,1)}) %all-gather.22.cloned.1.call-update) | async-done | bytes 1572880 | tf_op jit(solution)/shard_map/all_gather | solution.py:51
  901.1 3.6 collective-permute-done.16
  907.9 21.3 %all_to_all.107 = bf16[8,128,320]{1,2,0:T(8,128)(2,1)} all-to-all(bf16[8,128,320]{1,2,0:T(8,128)(2,1)S(1)} %bitcast.258), channel_id=1, replica_groups=mesh['section'=2,'expert'=8,'tensor'=2] {'expert'}, dimensions={0} | all-to-all | bytes 1310720 | tf_op jit(solution)/shard_map/all_to_all | solution.py:59
  929.2 17.6 %reduce-scatter.17.cloned.1.call-done = bf16[8,80,1280]{2,1,0:T(8,128)(2,1)} async-done(((bf16[8,80,2560]{2,1,0:T(8,128)(2,1)}), bf16[8,80,1280]{2,1,0:T(8,128)(2,1)}) %reduce-scatter.17.cloned.1.call-update) | async-done | bytes 1638416 | tf_op jit(solution)/shard_map/reduce_scatter | solution.py:76
  946.9 5.5 all-to-all-start.6
  958.3 3.5 broadcast_select_fusion.27
  963.7 8.4 reduce-scatter.15.cloned.1.call-done
  972.0 18.7 %all-to-all-done.6 = bf16[8,80,1280]{2,1,0:T(8,128)(2,1)S(1)} async-done(((bf16[8,80,1280]{2,1,0:T(8,128)(2,1)}), bf16[8,80,1280]{2,1,0:T(8,128)(2,1)S(1)}, u32[]{:S(2)}, u32[]{:S(2)}) %all-to-all-start.6) | async-done | bytes 1638432 | tf_op jit(solution)/shard_map/all_to_all | solution.py:79
  990.8 2.9 gather_fusion.3
  993.7 3.7 reshape.881
  997.3 3.4 multiply_reduce_fusion
  (279 shorter events, 107.8 us)
Async XLA Ops:
  7.2 516.4 %copy-start = (bf16[1,320,1536]{2,1,0:T(8,128)(2,1)S(1)}, bf16[1,320,1536]{2,1,0:T(8,128)(2,1)}, u32[]{:S(2)}) copy-start(bf16[1,320,1536]{2,1,0:T(8,128)(2,1)} %param.30) | copy-start | bytes 2949124
  7.2 183.7 %all-gather.24.cloned.1.call-start = ((), (), s32[]{:S(2)}) async-start(), calls=%async_computation.25 | async-start | bytes 10321920 | tf_op jit(solution)/shard_map/all_gather | solution.py:102
  16.4 7.5 copy-start.28
  16.4 11.9 %copy-start.29 = (f32[1,1280]{1,0:T(1,128)S(1)}, f32[1,1280]{1,0:T(1,128)}, u32[]{:S(2)}) copy-start(f32[1,1280]{1,0:T(1,128)} %param.26) | copy-start | bytes 15364
  16.4 16.9 %copy-start.39 = (s32[1,8]{1,0:T(1,128)S(1)}, s32[1,8]{1,0:T(1,128)}, u32[]{:S(2)}) copy-start(s32[1,8]{1,0:T(1,128)} %param.23) | copy-start | bytes 100
  16.4 17.7 %copy-start.19 = (s32[1,1,128,4]{2,3,1,0:T(4,128)S(1)}, s32[1,1,128,4]{2,3,1,0:T(4,128)}, u32[]{:S(2)}) copy-start(s32[1,1,128,4]{2,3,1,0:T(4,128)} %param.24) | copy-start | bytes 6148
  16.4 117.6 %copy-start.21 = (f32[1,1280,8]{1,2,0:T(8,128)S(1)}, f32[1,1280,8]{1,2,0:T(8,128)}, u32[]{:S(2)}) copy-start(f32[1,1280,8]{1,2,0:T(8,128)} %param.31) | copy-start | bytes 122884
  16.5 122.9 %copy-start.30 = (s32[1,128]{1,0:T(1,128)S(1)}, s32[1,128]{1,0:T(1,128)}, u32[]{:S(2)}) copy-start(s32[1,128]{1,0:T(1,128)} %param.22) | copy-start | bytes 1540
  16.5 132.9 %all-to-all-start = ((bf16[320,2,1536]{0,1,2:T(2,128)(2,1)}), bf16[320,2,1536]{0,1,2:T(2,128)(2,1)S(1)}, u32[]{:S(2)}, u32[]{:S(2)}) async-start(bf16[320,2,1536]{0,1,2:T(2,128)(2,1)} %bitcast.243), calls=%async_computation | async-start | bytes 4718592 | tf_op jit(solution)/shard_map/all_to_all | solution.py:105
  23.9 270.3 %all-gather.12.cloned.1.call-start = ((), (), s32[]{:S(2)}) async-start(), calls=%async_computation.13 | async-start | bytes 1474560 | tf_op jit(solution)/shard_map/all_gather | solution.py:51
  28.4 184.1 %copy-start.16 = (f32[2560]{0:T(1024)}, f32[2560]{0:T(1024)S(1)}, u32[]{:S(2)}) copy-start(f32[2560]{0:T(1024)S(1)} %reduce.33) | copy-start | bytes 30724
  199.6 12.9 %copy-start.2 = (bf16[128,2560]{1,0:T(8,128)(2,1)S(1)}, bf16[128,2560]{1,0:T(8,128)(2,1)}, u32[]{:S(2)}) copy-start(bf16[128,2560]{1,0:T(8,128)(2,1)} %copy-done.1) | copy-start | bytes 1966084
  212.5 6.5 copy-start.25
  212.5 35.3 %copy-start.31 = (s32[1,128]{1,0:T(1,128)S(1)}, s32[1,128]{1,0:T(1,128)}, u32[]{:S(2)}) copy-start(s32[1,128]{1,0:T(1,128)} %param.22) | copy-start | bytes 1540
  212.5 35.3 %copy-start.32 = (s32[128]{0:T(128)S(1)}, s32[128]{0:T(128)}, u32[]{:S(2)}) copy-start(s32[128]{0:T(128)} %get-tuple-element.93) | copy-start | bytes 1540
  218.9 1.4 collective-permute-start
  247.8 1.9 collective-permute-start.1
  252.5 1.7 collective-permute-start.2
  255.0 44.0 %copy-start.37 = (bf16[1,320,1280]{2,1,0:T(8,128)(2,1)S(1)}, bf16[1,320,1280]{2,1,0:T(8,128)(2,1)}, u32[]{:S(2)}) copy-start(bf16[1,320,1280]{2,1,0:T(8,128)(2,1)} %param.28) | copy-start | bytes 2457604
  255.0 82.1 %reduce-scatter.7.cloned.1.call-start = ((), (), s32[]{:S(2)}) async-start(), calls=%async_computation.14 | async-start | bytes 983040 | tf_op jit(solution)/shard_map/reduce_scatter | solution.py:60
  294.2 3.2 collective-permute-start.3
  300.0 37.1 %copy-start.3 = (bf16[1,128,1280]{2,1,0:T(8,128)(2,1)S(1)}, bf16[1,128,1280]{2,1,0:T(8,128)(2,1)}, u32[]{:S(2)}) copy-start(bf16[1,128,1280]{2,1,0:T(8,128)(2,1)} %param.21) | copy-start | bytes 983044
  321.2 27.3 %copy-start.11 = (f32[2560]{0:T(1024)S(1)}, f32[2560]{0:T(1024)}, u32[]{:S(2)}) copy-start(f32[2560]{0:T(1024)} %reduce.34) | copy-start | bytes 30724
  322.3 84.6 %all-gather.14.cloned.1.call-start = ((), (), s32[]{:S(2)}) async-start(), calls=%async_computation.15 | async-start | bytes 2949120 | tf_op jit(solution)/shard_map/all_gather | solution.py:51
  348.8 2.2 collective-permute-start.4
  352.1 166.1 %all-gather.16.cloned.1.call-start = ((), (), s32[]{:S(2)}) async-start(), calls=%async_computation.16 | async-start | bytes 1769472 | tf_op jit(solution)/shard_map/all_gather | solution.py:51
  406.9 42.1 %collective-permute-start.5 = (bf16[1024,1280]{1,0:T(8,128)(2,1)}, bf16[1024,1280]{1,0:T(8,128)(2,1)}, u32[]{:S(2)}, u32[]{:S(2)}) collective-permute-start(bf16[1024,1280]{1,0:T(8,128)(2,1)} %all-gather.14.cloned.1.call-done), channel_id=1, source_target_pairs={{0,16},{16,0},{1,17},{17,1},{2,18},{18,2},{3,19},{19,3},{4,20},{20... | collective-permute-start | bytes 7864328 | tf_op jit(solution)/shard_map/ppermute | solution.py:45
  406.9 7.8 copy-start.18
  406.9 32.2 %copy-start.34 = (s32[2]{0:T(128)S(1)}, s32[2]{0:T(128)}, u32[]{:S(2)}) copy-start(s32[2]{0:T(128)} %constant.173) | copy-start | bytes 28
  406.9 32.4 %copy-start.33 = (s32[2]{0:T(128)S(1)}, s32[2]{0:T(128)}, u32[]{:S(2)}) copy-start(s32[2]{0:T(128)} %constant.176) | copy-start | bytes 28
  448.9 20.7 %copy-start.26 = (pred[8,80]{1,0:T(8,128)(4,1)}, pred[8,80]{1,0:T(8,128)(4,1)S(1)}, u32[]{:S(2)}) copy-start(pred[8,80]{1,0:T(8,128)(4,1)S(1)} %reshape.875) | copy-start | bytes 1924
  449.0 9.4 copy-start.22
  457.8 15.7 %collective-permute-start.6 = (bf16[1024,192]{0,1:T(8,128)(2,1)}, bf16[1024,192]{0,1:T(8,128)(2,1)}, u32[]{:S(2)}, u32[]{:S(2)}) collective-permute-start(bf16[1024,192]{0,1:T(8,128)(2,1)} %fusion.93), channel_id=1, source_target_pairs={{0,16},{16,0},{1,17},{17,1},{2,18},{18,2},{3,19},{19,3},{4,20},{20... | collective-permute-start | bytes 1179656 | tf_op jit(solution)/shard_map/ppermute | solution.py:45
  474.6 89.4 %reduce-scatter.11.cloned.1.call-start = ((), (), s32[]{:S(2)}) async-start(), calls=%async_computation.18 | async-start | bytes 4915200 | tf_op jit(solution)/shard_map/reduce_scatter | solution.py:76
  518.1 3.6 collective-permute-start.7
  563.9 43.9 %all-to-all-start.3 = ((bf16[8,80,1280]{2,1,0:T(8,128)(2,1)}), bf16[8,80,1280]{2,1,0:T(8,128)(2,1)S(1)}, u32[]{:S(2)}, u32[]{:S(2)}) async-start(bf16[8,80,1280]{2,1,0:T(8,128)(2,1)} %reduce-scatter.11.cloned.1.call-done), calls=%async_computation.6 | async-start | bytes 3276800 | tf_op jit(solution)/shard_map/all_to_all | solution.py:79
  569.4 31.6 %reduce-scatter.9.cloned.1.call-start = ((), (), s32[]{:S(2)}) async-start(), calls=%async_computation.17 | async-start | bytes 983040 | tf_op jit(solution)/shard_map/reduce_scatter | solution.py:60
  584.5 128.7 %all-gather.18.cloned.1.call-start = ((), (), s32[]{:S(2)}) async-start(), calls=%async_computation.19 | async-start | bytes 1474560 | tf_op jit(solution)/shard_map/all_gather | solution.py:51
  610.9 3.7 copy-start.13
  618.0 13.6 %copy-start.17 = (f32[2560]{0:T(1024)S(1)}, f32[2560]{0:T(1024)}, u32[]{:S(2)}) copy-start(f32[2560]{0:T(1024)} %copy-done.16) | copy-start | bytes 30724
  618.1 13.5 %copy-start.7 = (bf16[128,1280]{1,0:T(8,128)(2,1)}, bf16[128,1280]{1,0:T(8,128)(2,1)S(1)}, u32[]{:S(2)}) copy-start(bf16[128,1280]{1,0:T(8,128)(2,1)S(1)} %add_convert_fusion.2) | copy-start | bytes 983044
  618.1 2.5 collective-permute-start.8
  637.9 1.4 collective-permute-start.9
  666.9 1.9 collective-permute-start.10
  671.6 1.7 collective-permute-start.11
  674.0 43.9 %copy-start.38 = (bf16[1,320,1280]{2,1,0:T(8,128)(2,1)S(1)}, bf16[1,320,1280]{2,1,0:T(8,128)(2,1)}, u32[]{:S(2)}) copy-start(bf16[1,320,1280]{2,1,0:T(8,128)(2,1)} %param.28) | copy-start | bytes 2457604
  674.1 82.1 %reduce-scatter.13.cloned.1.call-start = ((), (), s32[]{:S(2)}) async-start(), calls=%async_computation.20 | async-start | bytes 983040 | tf_op jit(solution)/shard_map/reduce_scatter | solution.py:60
  713.2 3.2 collective-permute-start.12
  740.2 27.3 %copy-start.12 = (f32[2560]{0:T(1024)S(1)}, f32[2560]{0:T(1024)}, u32[]{:S(2)}) copy-start(f32[2560]{0:T(1024)} %reduce.34) | copy-start | bytes 30724
  741.3 84.5 %all-gather.20.cloned.1.call-start = ((), (), s32[]{:S(2)}) async-start(), calls=%async_computation.21 | async-start | bytes 2949120 | tf_op jit(solution)/shard_map/all_gather | solution.py:51
  767.8 2.2 collective-permute-start.13
  771.0 130.1 %all-gather.22.cloned.1.call-start = ((), (), s32[]{:S(2)}) async-start(), calls=%async_computation.22 | async-start | bytes 1769472 | tf_op jit(solution)/shard_map/all_gather | solution.py:51
  825.9 5.1 collective-permute-start.14
  837.2 3.8 copy-start.23
  840.8 11.5 %copy-start.27 = (pred[8,80]{1,0:T(8,128)(4,1)S(1)}, pred[8,80]{1,0:T(8,128)(4,1)}, u32[]{:S(2)}) copy-start(pred[8,80]{1,0:T(8,128)(4,1)} %copy-done.26) | copy-start | bytes 1924
  840.8 15.4 %collective-permute-start.15 = (bf16[1024,192]{0,1:T(8,128)(2,1)}, bf16[1024,192]{0,1:T(8,128)(2,1)}, u32[]{:S(2)}, u32[]{:S(2)}) collective-permute-start(bf16[1024,192]{0,1:T(8,128)(2,1)} %fusion.92), channel_id=1, source_target_pairs={{0,16},{16,0},{1,17},{17,1},{2,18},{18,2},{3,19},{19,3},{4,20},{20... | collective-permute-start | bytes 1179656 | tf_op jit(solution)/shard_map/ppermute | solution.py:45
  858.2 88.7 %reduce-scatter.17.cloned.1.call-start = ((), (), s32[]{:S(2)}) async-start(), calls=%async_computation.24 | async-start | bytes 4915200 | tf_op jit(solution)/shard_map/reduce_scatter | solution.py:76
  901.1 3.6 collective-permute-start.16
  946.9 43.9 %all-to-all-start.6 = ((bf16[8,80,1280]{2,1,0:T(8,128)(2,1)}), bf16[8,80,1280]{2,1,0:T(8,128)(2,1)S(1)}, u32[]{:S(2)}, u32[]{:S(2)}) async-start(bf16[8,80,1280]{2,1,0:T(8,128)(2,1)} %reduce-scatter.17.cloned.1.call-done), calls=%async_computation.12 | async-start | bytes 3276800 | tf_op jit(solution)/shard_map/all_to_all | solution.py:79
  952.4 11.1 %copy-start.20 = (s32[1,1,128,4]{2,3,1,0:T(4,128)S(1)}, s32[1,1,128,4]{2,3,1,0:T(4,128)}, u32[]{:S(2)}) copy-start(s32[1,1,128,4]{2,3,1,0:T(4,128)} %param.24) | copy-start | bytes 6148
  952.4 38.4 %copy-start.24 = (s32[1024]{0:T(1024)S(1)}, s32[1024]{0:T(1024)}, u32[]{:S(2)}) copy-start(s32[1024]{0:T(1024)} %pad_clamp_fusion) | copy-start | bytes 12292
  952.4 19.7 %reduce-scatter.15.cloned.1.call-start = ((), (), s32[]{:S(2)}) async-start(), calls=%async_computation.23 | async-start | bytes 983040 | tf_op jit(solution)/shard_map/reduce_scatter | solution.py:60
  997.3 3.4 copy-start.8
  997.3 3.4 copy-start.9
  (9 other events, 18.3 us)
Sparse Core Ops, SparseCore 0:
  10.2 180.6 all-gather.23
  255.1 39.0 all-gather.11
  322.4 14.6 reduce-scatter.6
  352.2 54.6 all-gather.13
  474.7 43.4 all-gather.15
  520.3 43.5 reduce-scatter.10
  584.6 16.4 reduce-scatter.8
  674.2 38.9 all-gather.17
  741.4 14.6 reduce-scatter.12
  771.1 54.6 all-gather.19
  858.3 42.7 all-gather.21
  903.2 43.5 reduce-scatter.16
  955.6 16.4 reduce-scatter.14

commit v7 on v6

--- a/solution.py
+++ b/solution.py
@@ -35,7 +35,7 @@
 
 
 def norm_full_rows(values_in, gain_full):
-    widened = lax.all_gather(values_in, "tensor", axis=1, tiled=True).astype(jnp.float32)
+    widened = tensor_gather(values_in, 1).astype(jnp.float32)
     squares = jnp.mean(widened * widened, axis=-1)
     return (widened * lax.rsqrt(squares + NORM_EPS)[:, None] * gain_full).astype(jnp.bfloat16)
 
@@ -55,9 +55,34 @@
     return jnp.concatenate([lead, trail], axis=split_axis)
 
 
+def swap_tensor(value):
+    count = lax.axis_size("tensor")
+    return lax.ppermute(value, "tensor", [(source, (source + 1) % count) for source in range(count)])
+
+
+def tensor_sum_scatter(value, axis):
+    if lax.axis_size("tensor") != 2:
+        return lax.psum_scatter(value, "tensor", scatter_dimension=axis, tiled=True)
+    first, second = jnp.split(value, 2, axis=axis)
+    lower = lax.axis_index("tensor") == 0
+    kept = jnp.where(lower, first, second)
+    sent = jnp.where(lower, second, first)
+    return (kept.astype(jnp.float32) + swap_tensor(sent).astype(jnp.float32)).astype(value.dtype)
+
+
+def tensor_gather(value, axis):
+    if lax.axis_size("tensor") != 2:
+        return lax.all_gather(value, "tensor", axis=axis, tiled=True)
+    other = swap_tensor(value)
+    lower = lax.axis_index("tensor") == 0
+    return jnp.concatenate(
+        [jnp.where(lower, value, other), jnp.where(lower, other, value)], axis=axis
+    )
+
+
 def terms_to_slots(terms):
     by_slot = lax.all_to_all(terms, "expert", split_axis=0, concat_axis=1, tiled=True)
-    return lax.psum_scatter(by_slot, "tensor", scatter_dimension=1, tiled=True)
+    return tensor_sum_scatter(by_slot, 1)
 
 
 def expert_path(full_rows, w_in_local, w_down_local):
@@ -73,9 +98,7 @@
     )
     partial_value = jnp.dot(activated, w_down_local, preferred_element_type=jnp.float32)
     partial_value = partial_value.reshape(sources, slot_count, model_width)
-    summed = lax.psum_scatter(
-        partial_value.astype(jnp.bfloat16), "tensor", scatter_dimension=2, tiled=True
-    )
+    summed = tensor_sum_scatter(partial_value.astype(jnp.bfloat16), 2)
     return lax.all_to_all(summed, "expert", split_axis=0, concat_axis=0, tiled=True)
 
 

time: 1020 us -> 975 us (0.956)
  blocking collectives: 292 us -> 207 us
  other arithmetic: 91.5 us -> 111 us
  starting transfers between devices: 22.5 us -> 40.8 us
    ppermute x0 -> x10, waiting for transfers between devices: none -> 93.9 us  [swap_tensor(): lax.ppermute(value, 'tensor', [(source, (source + 1) % count) for source...]
    reduce_scatter x6 -> x0, waiting for transfers between devices: 79.1 us -> none  [the longest x4 43.8 us: terms_to_slots(): return lax.psum_scatter(by_slot, 'tensor', scatter_dimension=1, tiled=True)]
    all_to_all x4 -> x2, blocking collectives: 84.7 us -> 42.2 us  [terms_to_slots(): lax.all_to_all(terms, 'expert', split_axis=0, concat_axis=1, tiled=True)]
    all_gather x4 -> x0, blocking collectives: 38.8 us -> none  [norm_full_rows(): lax.all_gather(values_in, 'tensor', axis=1, tiled=True).astype(jnp.float32)]
    all_gather x6, waiting for transfers between devices: 244 us -> 221 us  [paired_gather(): lax.all_gather(jnp.where(active, first, second), 'expert', axis=axis, til...]
    ppermute x0 -> x10, starting transfers between devices: none -> 14.9 us  [swap_tensor(): lax.ppermute(value, 'tensor', [(source, (source + 1) % count) for source...]
    convert_element_type x0 -> x4, other arithmetic: none -> 10.6 us  [tensor_sum_scatter(): (kept.astype(jnp.float32) + swap_tensor(sent).astype(jnp.float32)).astype...]
    unnamed x90 -> x134, local copies, waits for them, and re-layouts: 40.7 us -> 44.4 us
  transfers between devices with their start and end apart: 33 -> 39, of which waited for: 29 -> 29; matrix products, arithmetic and copies ran while one was open for 16% -> 21% of each run, Pallas kernels for 0% -> 0%
where the time goes in v7:
time: 975 us; the launch traced here: 964 us
  waiting for transfers between devices  419 us (43%)
  blocking collectives  207 us (21%)
  local copies, waits for them, and re-layouts  120 us (12%)
  other arithmetic  111 us (11%)
  matrix products  51 us (5%)
  starting transfers between devices  40.8 us (4%)
  between operations  15.8 us (2%)
    all_gather x6, waiting for transfers between devices, paired_gather(): lax.all_gather(jnp.where(active, first, second), 'expert', axis=axis, til...  221 us
    ppermute x10, waiting for transfers between devices, swap_tensor(): lax.ppermute(value, 'tensor', [(source, (source + 1) % count) for source...  93.9 us
    all_gather x1, blocking collectives, local(): lax.all_gather(expert_choice[0], 'expert', axis=0, tiled=False)  92.6 us
    all_gather x2, blocking collectives, paired_gather(): lax.all_gather(jnp.where(active, first, second), 'expert', axis=axis, til...  54.9 us
    all_gather x1, waiting for transfers between devices, local(): qkv_full = lax.all_gather(w_qkv[0], 'expert', axis=0, tiled=True)  44.6 us
    unnamed x134, local copies, waits for them, and re-layouts  44.4 us
    all_to_all x2, blocking collectives, terms_to_slots(): lax.all_to_all(terms, 'expert', split_axis=0, concat_axis=1, tiled=True)  42.2 us
    all_to_all x2, waiting for transfers between devices, expert_path(): lax.all_to_all(summed, 'expert', split_axis=0, concat_axis=0, tiled=True)  30.9 us
  transfers between devices with their start and end apart: 39, of which 29 were waited for; matrix products, arithmetic and copies ran while one was open for 21% of the time, Pallas kernels for 0%

profile of v7, /device:TPU:0, one launch (start us, length us, event | category | flops | bytes accessed | tf_op | source)
XLA Modules:
  0.0 963.8 jit_solution(15131519908834474498)
XLA Ops:
  7.9 8.5 copy.164
  16.5 7.4 all-to-all-start
  27.2 8.1 all-gather.2
  35.3 4.4 all-gather.3
  41.0 92.6 %all_gather.40 = s32[8,1,128,4]{2,3,1,0:T(4,128)} all-gather(s32[1,1,128,4]{2,3,1,0:T(4,128)S(1)} %copy-done.37), channel_id=1, replica_groups=mesh['section'=2,'expert'=8,'tensor'=2] {'expert'}, dimensions={0}, use_global_device_ids=true | all-gather | bytes 18432 | tf_op jit(solution)/shard_map/all_gather | solution.py:129
  133.7 4.7 all-gather.1
  143.5 2.8 all_to_all.78
  146.3 44.6 %all-gather.24.cloned.1.call-done = bf16[1,2560,2,896]{3,2,0,1:T(2,128)(2,1)} async-done(((bf16[1,320,2,896]{3,2,0,1:T(2,128)(2,1)}), bf16[1,2560,2,896]{3,2,0,1:T(2,128)(2,1)}) %all-gather.24.cloned.1.call-update) | async-done | bytes 9175056 | tf_op jit(solution)/shard_map/all_gather | solution.py:125
  190.8 8.8 copy.233
  199.6 12.8 %copy.167 = bf16[1792,2560]{1,0:T(8,128)(2,1)} copy(bf16[1792,2560]{0,1:T(8,128)(2,1)} %bitcast.242) | data formatting | bytes 18350080 | tf_op jit(solution)/shard_map/dot_general | solution.py:171
  212.4 6.2 fusion.98
  220.2 27.5 %all_gather.44 = bf16[1024,256]{0,1:T(8,128)(2,1)S(1)} all-gather(bf16[128,256]{0,1:T(8,128)(2,1)S(1)} %slice_select_fusion.7), channel_id=1, replica_groups=mesh['section'=2,'expert'=8,'tensor'=2] {'expert'}, dimensions={0}, use_global_device_ids=true | all-gather | bytes 589824 | tf_op jit(solution)/shard_map/all_gather | solution.py:51
  255.1 38.9 %all-gather.12.cloned.1.call-done = bf16[1024,640]{1,0:T(8,128)(2,1)} async-done(((bf16[128,640]{1,0:T(8,128)(2,1)}), bf16[1024,640]{1,0:T(8,128)(2,1)}) %all-gather.12.cloned.1.call-update) | async-done | bytes 1310736 | tf_op jit(solution)/shard_map/all_gather | solution.py:51
  294.1 3.2 collective-permute-done.4
  300.1 21.2 %all_to_all.104 = bf16[8,128,320]{1,2,0:T(8,128)(2,1)S(1)} all-to-all(bf16[8,128,320]{1,2,0:T(8,128)(2,1)S(1)} %bitcast.257), channel_id=1, replica_groups=mesh['section'=2,'expert'=8,'tensor'=2] {'expert'}, dimensions={0} | all-to-all | bytes 1310720 | tf_op jit(solution)/shard_map/all_to_all | solution.py:84
  323.2 6.5 collective-permute-done.5
  331.4 5.6 collective-permute-done.6
  340.6 56.1 %all-gather.14.cloned.1.call-done = bf16[1024,1280]{1,0:T(8,128)(2,1)} async-done(((bf16[128,1280]{1,0:T(8,128)(2,1)}), bf16[1024,1280]{1,0:T(8,128)(2,1)}) %all-gather.14.cloned.1.call-update) | async-done | bytes 2621456 | tf_op jit(solution)/shard_map/all_gather | solution.py:51
  396.7 7.8 copy.234
  405.7 23.6 %compare_select_fusion = s32[8,128,1]{2,0,1:T(8,128)S(1)} fusion(pred[8,128,1]{2,0,1:T(8,128)(4,1)S(1)} %copy.180, s32[8,128,1]{2,0,1:T(8,128)S(1)} %copy.179), kind=kOutput, calls=%fused_computation.70 | output fusion | flops 135168 | bytes 9216 | tf_op jit(solution)/shard_map/jit(cumsum)/reduce_window_sum | solution.py:247
  430.6 3.0 broadcast_select_fusion.5
  439.0 4.5 scatter_custom_fusion.1
  443.7 4.7 scatter_custom_fusion
  449.6 5.2 pad_maximum_fusion
  454.8 11.5 %gather_fusion = bf16[640,2560]{1,0:T(8,128)(2,1)} fusion(bf16[1024,2560]{1,0:T(8,128)(2,1)} %pad_maximum_fusion, s32[1024]{0:T(1024)S(1)} %pad_clamp_fusion.1), kind=kCustom, calls=%fused_computation | custom fusion | bytes 6556160 | tf_op jit(solution)/shard_map/gather | solution.py:263
  468.5 8.9 fusion.142
  477.4 15.7 %all-gather.16.cloned.1.call-done = bf16[512,1536]{0,1:T(8,128)(2,1)} async-done(((bf16[512,192]{0,1:T(8,128)(2,1)}), bf16[512,1536]{0,1:T(8,128)(2,1)}) %all-gather.16.cloned.1.call-update) | async-done | bytes 1572880 | tf_op jit(solution)/shard_map/all_gather | solution.py:51
  493.1 2.8 fusion.33
  496.4 2.9 convolution_convert_fusion.1
  504.6 3.5 all-to-all-start.2
  508.1 30.6 %collective-permute-done.12 = bf16[8,80,1280]{2,1,0:T(8,128)(2,1)} collective-permute-done((bf16[8,80,1280]{2,1,0:T(8,128)(2,1)}, bf16[8,80,1280]{2,1,0:T(8,128)(2,1)}, u32[]{:S(2)}, u32[]{:S(2)}) %collective-permute-start.12) | collective-permute-done | bytes 1638432 | tf_op jit(solution)/shard_map/ppermute | solution.py:60
  538.7 4.2 add_convert_fusion.1
  543.8 3.7 all-to-all-start.3
  553.5 3.1 reduce-window.19
  576.7 8.9 all-to-all-done.3
  585.6 3.0 gather_fusion.1
  588.6 3.7 reshape.880
  592.3 3.4 multiply_reduce_fusion.1
  601.0 8.6 collective-permute-done.14
  609.9 6.2 fusion.95
  617.7 27.4 %all_gather.48 = bf16[1024,256]{0,1:T(8,128)(2,1)S(1)} all-gather(bf16[128,256]{0,1:T(8,128)(2,1)S(1)} %slice_select_fusion.6), channel_id=1, replica_groups=mesh['section'=2,'expert'=8,'tensor'=2] {'expert'}, dimensions={0}, use_global_device_ids=true | all-gather | bytes 589824 | tf_op jit(solution)/shard_map/all_gather | solution.py:51
  652.4 40.0 %all-gather.18.cloned.1.call-done = bf16[1024,640]{1,0:T(8,128)(2,1)} async-done(((bf16[128,640]{1,0:T(8,128)(2,1)}), bf16[1024,640]{1,0:T(8,128)(2,1)}) %all-gather.18.cloned.1.call-update) | async-done | bytes 1310736 | tf_op jit(solution)/shard_map/all_gather | solution.py:51
  692.3 3.2 collective-permute-done.18
  698.3 21.0 %all_to_all.105 = bf16[8,128,320]{1,2,0:T(8,128)(2,1)S(1)} all-to-all(bf16[8,128,320]{1,2,0:T(8,128)(2,1)S(1)} %bitcast.258), channel_id=1, replica_groups=mesh['section'=2,'expert'=8,'tensor'=2] {'expert'}, dimensions={0} | all-to-all | bytes 1310720 | tf_op jit(solution)/shard_map/all_to_all | solution.py:84
  721.3 6.5 collective-permute-done.19
  729.5 5.6 collective-permute-done.20
  738.9 55.8 %all-gather.20.cloned.1.call-done = bf16[1024,1280]{1,0:T(8,128)(2,1)} async-done(((bf16[128,1280]{1,0:T(8,128)(2,1)}), bf16[1024,1280]{1,0:T(8,128)(2,1)}) %all-gather.20.cloned.1.call-update) | async-done | bytes 2621456 | tf_op jit(solution)/shard_map/all_gather | solution.py:51
  794.8 5.1 collective-permute-done.22
  799.9 2.4 broadcast_select_fusion.3
  807.6 5.3 pad_maximum_fusion.1
  812.9 11.5 %gather_fusion.2 = bf16[640,2560]{1,0:T(8,128)(2,1)} fusion(bf16[1024,2560]{1,0:T(8,128)(2,1)} %pad_maximum_fusion.1, s32[1024]{0:T(1024)S(1)} %copy-done.40), kind=kCustom, calls=%fused_computation.2 | custom fusion | bytes 6556160 | tf_op jit(solution)/shard_map/gather | solution.py:263
  826.6 8.9 fusion.144
  835.5 15.0 %all-gather.22.cloned.1.call-done = bf16[512,1536]{0,1:T(8,128)(2,1)} async-done(((bf16[512,192]{0,1:T(8,128)(2,1)}), bf16[512,1536]{0,1:T(8,128)(2,1)}) %all-gather.22.cloned.1.call-update) | async-done | bytes 1572880 | tf_op jit(solution)/shard_map/all_gather | solution.py:51
  850.5 2.8 fusion.32
  853.8 2.9 convolution_convert_fusion
  862.0 3.5 all-to-all-start.5
  865.5 30.6 %collective-permute-done.26 = bf16[8,80,1280]{2,1,0:T(8,128)(2,1)} collective-permute-done((bf16[8,80,1280]{2,1,0:T(8,128)(2,1)}, bf16[8,80,1280]{2,1,0:T(8,128)(2,1)}, u32[]{:S(2)}, u32[]{:S(2)}) %collective-permute-start.26) | collective-permute-done | bytes 1638432 | tf_op jit(solution)/shard_map/ppermute | solution.py:60
  896.1 4.2 add_convert_fusion
  901.1 4.0 all-to-all-start.6
  910.7 3.6 broadcast_select_fusion.41
  921.2 22.0 %all-to-all-done.6 = bf16[8,80,1280]{2,1,0:T(8,128)(2,1)S(1)} async-done(((bf16[8,80,1280]{2,1,0:T(8,128)(2,1)}), bf16[8,80,1280]{2,1,0:T(8,128)(2,1)S(1)}, u32[]{:S(2)}, u32[]{:S(2)}) %all-to-all-start.6) | async-done | bytes 1638432 | tf_op jit(solution)/shard_map/all_to_all | solution.py:102
  943.2 2.9 gather_fusion.3
  946.1 3.7 reshape.881
  949.7 3.4 multiply_reduce_fusion
  (337 shorter events, 127.1 us)
Async XLA Ops:
  7.2 495.2 %copy-start = (bf16[1,320,1536]{2,1,0:T(8,128)(2,1)S(1)}, bf16[1,320,1536]{2,1,0:T(8,128)(2,1)}, u32[]{:S(2)}) copy-start(bf16[1,320,1536]{2,1,0:T(8,128)(2,1)} %param.30) | copy-start | bytes 2949124
  7.2 183.7 %all-gather.24.cloned.1.call-start = ((), (), s32[]{:S(2)}) async-start(), calls=%async_computation.13 | async-start | bytes 10321920 | tf_op jit(solution)/shard_map/all_gather | solution.py:125
  16.4 18.8 %copy-start.47 = (f32[1,1280]{1,0:T(1,128)S(1)}, f32[1,1280]{1,0:T(1,128)}, u32[]{:S(2)}) copy-start(f32[1,1280]{1,0:T(1,128)} %param.26) | copy-start | bytes 15364
  16.5 23.8 %copy-start.57 = (s32[1,8]{1,0:T(1,128)S(1)}, s32[1,8]{1,0:T(1,128)}, u32[]{:S(2)}) copy-start(s32[1,8]{1,0:T(1,128)} %param.23) | copy-start | bytes 100
  16.5 24.6 %copy-start.37 = (s32[1,1,128,4]{2,3,1,0:T(4,128)S(1)}, s32[1,1,128,4]{2,3,1,0:T(4,128)}, u32[]{:S(2)}) copy-start(s32[1,1,128,4]{2,3,1,0:T(4,128)} %param.24) | copy-start | bytes 6148
  16.5 117.2 %copy-start.38 = (f32[1,1280,8]{1,2,0:T(8,128)S(1)}, f32[1,1280,8]{1,2,0:T(8,128)}, u32[]{:S(2)}) copy-start(f32[1,1280,8]{1,2,0:T(8,128)} %param.31) | copy-start | bytes 122884
  16.5 122.6 %copy-start.48 = (s32[1,128]{1,0:T(1,128)S(1)}, s32[1,128]{1,0:T(1,128)}, u32[]{:S(2)}) copy-start(s32[1,128]{1,0:T(1,128)} %param.22) | copy-start | bytes 1540
  16.5 125.3 %all-to-all-start = ((bf16[320,2,1536]{0,1,2:T(2,128)(2,1)}), bf16[320,2,1536]{0,1,2:T(2,128)(2,1)S(1)}, u32[]{:S(2)}, u32[]{:S(2)}) async-start(bf16[320,2,1536]{0,1,2:T(2,128)(2,1)} %bitcast.245), calls=%async_computation | async-start | bytes 4718592 | tf_op jit(solution)/shard_map/all_to_all | solution.py:128
  23.9 270.1 %all-gather.12.cloned.1.call-start = ((), (), s32[]{:S(2)}) async-start(), calls=%async_computation.7 | async-start | bytes 1474560 | tf_op jit(solution)/shard_map/all_gather | solution.py:51
  25.7 114.1 %collective-permute-start = (bf16[128,1280]{1,0:T(8,128)(2,1)}, bf16[128,1280]{1,0:T(8,128)(2,1)}, u32[]{:S(2)}, u32[]{:S(2)}) collective-permute-start(bf16[128,1280]{1,0:T(8,128)(2,1)} %bitcast_select_fusion.3), channel_id=1, source_target_pairs={{0,1},{1,0},{2,3},{3,2},{4,5},{5,4},{6,7},{7,6},{8,9},{9,8},{10,11... | collective-permute-start | bytes 983048 | tf_op jit(solution)/shard_map/ppermute | solution.py:60
  35.3 177.1 %copy-start.33 = (f32[2560]{0:T(1024)}, f32[2560]{0:T(1024)S(1)}, u32[]{:S(2)}) copy-start(f32[2560]{0:T(1024)S(1)} %reduce.33) | copy-start | bytes 30724
  199.6 12.8 %copy-start.14 = (bf16[128,1280]{1,0:T(8,128)(2,1)S(1)}, bf16[128,1280]{1,0:T(8,128)(2,1)}, u32[]{:S(2)}) copy-start(bf16[128,1280]{1,0:T(8,128)(2,1)} %copy-done.13) | copy-start | bytes 983044
  199.6 12.8 %copy-start.16 = (bf16[128,1280]{1,0:T(8,128)(2,1)S(1)}, bf16[128,1280]{1,0:T(8,128)(2,1)}, u32[]{:S(2)}) copy-start(bf16[128,1280]{1,0:T(8,128)(2,1)} %copy-done.15) | copy-start | bytes 983044
  212.4 35.3 %copy-start.49 = (s32[1,128]{1,0:T(1,128)S(1)}, s32[1,128]{1,0:T(1,128)}, u32[]{:S(2)}) copy-start(s32[1,128]{1,0:T(1,128)} %param.22) | copy-start | bytes 1540
  212.4 35.3 %copy-start.50 = (s32[128]{0:T(128)S(1)}, s32[128]{0:T(128)}, u32[]{:S(2)}) copy-start(s32[128]{0:T(128)} %get-tuple-element.109) | copy-start | bytes 1540
  218.7 1.4 collective-permute-start.1
  247.7 1.9 collective-permute-start.2
  252.4 1.7 collective-permute-start.3
  254.9 44.0 %copy-start.55 = (bf16[1,320,1280]{2,1,0:T(8,128)(2,1)S(1)}, bf16[1,320,1280]{2,1,0:T(8,128)(2,1)}, u32[]{:S(2)}) copy-start(bf16[1,320,1280]{2,1,0:T(8,128)(2,1)} %param.28) | copy-start | bytes 2457604
  254.9 141.8 %all-gather.14.cloned.1.call-start = ((), (), s32[]{:S(2)}) async-start(), calls=%async_computation.8 | async-start | bytes 2949120 | tf_op jit(solution)/shard_map/all_gather | solution.py:51
  294.1 3.2 collective-permute-start.4
  300.1 29.7 %copy-start.7 = (bf16[1,128,1280]{2,1,0:T(8,128)(2,1)S(1)}, bf16[1,128,1280]{2,1,0:T(8,128)(2,1)}, u32[]{:S(2)}) copy-start(bf16[1,128,1280]{2,1,0:T(8,128)(2,1)} %param.21) | copy-start | bytes 983044
  321.6 15.7 %copy-start.31 = (f32[2560]{0:T(1024)S(1)}, f32[2560]{0:T(1024)}, u32[]{:S(2)}) copy-start(f32[2560]{0:T(1024)} %reduce.34) | copy-start | bytes 30724
  321.7 8.0 collective-permute-start.5
  329.9 7.1 collective-permute-start.6
  337.6 2.2 collective-permute-start.7
  340.6 152.5 %all-gather.16.cloned.1.call-start = ((), (), s32[]{:S(2)}) async-start(), calls=%async_computation.9 | async-start | bytes 1769472 | tf_op jit(solution)/shard_map/all_gather | solution.py:51
  396.7 33.9 %collective-permute-start.8 = (bf16[1024,1280]{1,0:T(8,128)(2,1)}, bf16[1024,1280]{1,0:T(8,128)(2,1)}, u32[]{:S(2)}, u32[]{:S(2)}) collective-permute-start(bf16[1024,1280]{1,0:T(8,128)(2,1)} %all-gather.14.cloned.1.call-done), channel_id=1, source_target_pairs={{0,16},{16,0},{1,17},{17,1},{2,18},{18,2},{3,19},{19,3},{4,20},{20... | collective-permute-start | bytes 7864328 | tf_op jit(solution)/shard_map/ppermute | solution.py:45
  396.7 32.9 %copy-start.52 = (s32[2]{0:T(128)S(1)}, s32[2]{0:T(128)}, u32[]{:S(2)}) copy-start(s32[2]{0:T(128)} %constant.175) | copy-start | bytes 28
  396.7 33.1 %copy-start.51 = (s32[2]{0:T(128)S(1)}, s32[2]{0:T(128)}, u32[]{:S(2)}) copy-start(s32[2]{0:T(128)} %constant.178) | copy-start | bytes 28
  437.0 11.6 %collective-permute-start.9 = (bf16[1024,192]{0,1:T(8,128)(2,1)}, bf16[1024,192]{0,1:T(8,128)(2,1)}, u32[]{:S(2)}, u32[]{:S(2)}) collective-permute-start(bf16[1024,192]{0,1:T(8,128)(2,1)} %fusion.93), channel_id=1, source_target_pairs={{0,16},{16,0},{1,17},{17,1},{2,18},{18,2},{3,19},{19,3},{4,20},{20... | collective-permute-start | bytes 1179656 | tf_op jit(solution)/shard_map/ppermute | solution.py:45
  448.5 17.8 %copy-start.44 = (pred[8,80]{1,0:T(8,128)(4,1)}, pred[8,80]{1,0:T(8,128)(4,1)S(1)}, u32[]{:S(2)}) copy-start(pred[8,80]{1,0:T(8,128)(4,1)S(1)} %reshape.875) | copy-start | bytes 1924
  493.1 9.1 collective-permute-start.10
  500.7 38.0 %collective-permute-start.12 = (bf16[8,80,1280]{2,1,0:T(8,128)(2,1)}, bf16[8,80,1280]{2,1,0:T(8,128)(2,1)}, u32[]{:S(2)}, u32[]{:S(2)}) collective-permute-start(bf16[8,80,1280]{2,1,0:T(8,128)(2,1)} %broadcast_select_fusion.7), channel_id=1, source_target_pairs={{0,1},{1,0},{2,3},{3,2},{4,5},{5,4},{6,7},{7,6},{8,9},{9,8},{10,11... | collective-permute-start | bytes 4915208 | tf_op jit(solution)/shard_map/ppermute | solution.py:60
  504.6 38.3 %all-to-all-start.2 = ((bf16[8,128,320]{1,2,0:T(8,128)(2,1)}), bf16[8,128,320]{1,2,0:T(8,128)(2,1)S(1)}, u32[]{:S(2)}, u32[]{:S(2)}) async-start(bf16[8,128,320]{1,2,0:T(8,128)(2,1)} %bitcast.236), calls=%async_computation.2 | async-start | bytes 1310720 | tf_op jit(solution)/shard_map/all_to_all | solution.py:84
  543.8 41.8 %all-to-all-start.3 = ((bf16[8,80,1280]{2,1,0:T(8,128)(2,1)}), bf16[8,80,1280]{2,1,0:T(8,128)(2,1)S(1)}, u32[]{:S(2)}, u32[]{:S(2)}) async-start(bf16[8,80,1280]{2,1,0:T(8,128)(2,1)} %add_convert_fusion.1), calls=%async_computation.3 | async-start | bytes 3276800 | tf_op jit(solution)/shard_map/all_to_all | solution.py:102
  547.5 144.8 %all-gather.18.cloned.1.call-start = ((), (), s32[]{:S(2)}) async-start(), calls=%async_computation.10 | async-start | bytes 1474560 | tf_op jit(solution)/shard_map/all_gather | solution.py:51
  572.6 23.1 %collective-permute-start.11 = (bf16[128,1280]{1,0:T(8,128)(2,1)}, bf16[128,1280]{1,0:T(8,128)(2,1)}, u32[]{:S(2)}, u32[]{:S(2)}) collective-permute-start(bf16[128,1280]{1,0:T(8,128)(2,1)} %broadcast_select_fusion.31), channel_id=1, source_target_pairs={{0,1},{1,0},{2,3},{3,2},{4,5},{5,4},{6,7},{7,6},{8,9},{9,8},{10,11... | collective-permute-start | bytes 983048 | tf_op jit(solution)/shard_map/ppermute | solution.py:60
  596.8 13.0 %copy-start.34 = (f32[2560]{0:T(1024)S(1)}, f32[2560]{0:T(1024)}, u32[]{:S(2)}) copy-start(f32[2560]{0:T(1024)} %copy-done.33) | copy-start | bytes 30724
  596.9 12.9 %copy-start.23 = (bf16[128,1280]{1,0:T(8,128)(2,1)}, bf16[128,1280]{1,0:T(8,128)(2,1)S(1)}, u32[]{:S(2)}) copy-start(bf16[128,1280]{1,0:T(8,128)(2,1)S(1)} %add_convert_fusion.6) | copy-start | bytes 983044
  596.9 2.5 collective-permute-start.13
  599.5 10.1 %collective-permute-start.14 = (bf16[128,1280]{1,0:T(8,128)(2,1)S(1)}, bf16[128,1280]{1,0:T(8,128)(2,1)S(1)}, u32[]{:S(2)}, u32[]{:S(2)}) collective-permute-start(bf16[128,1280]{1,0:T(8,128)(2,1)S(1)} %bitcast_select_fusion.2), channel_id=1, source_target_pairs={{0,1},{1,0},{2,3},{3,2},{4,5},{5,4},{6,7},{7,6},{8,9},{9,8},{10,11... | collective-permute-start | bytes 983048 | tf_op jit(solution)/shard_map/ppermute | solution.py:60
  616.1 31.0 %copy-start.25 = (bf16[128,2,1,128]{0,3,2,1:T(8,128)(2,1)}, bf16[128,2,1,128]{0,3,2,1:T(8,128)(2,1)S(1)}, u32[]{:S(2)}) copy-start(bf16[128,2,1,128]{0,3,2,1:T(8,128)(2,1)S(1)} %slice.285) | copy-start | bytes 196612
  616.2 31.0 %copy-start.27 = (bf16[128,2,128]{0,2,1:T(8,128)(2,1)}, bf16[128,2,128]{0,2,1:T(8,128)(2,1)S(1)}, u32[]{:S(2)}) copy-start(bf16[128,2,128]{0,2,1:T(8,128)(2,1)S(1)} %pad_maximum_fusion.13) | copy-start | bytes 196612
  616.2 1.4 collective-permute-start.15
  645.1 1.9 collective-permute-start.16
  649.8 1.7 collective-permute-start.17
  652.3 44.8 %copy-start.56 = (bf16[1,320,1280]{2,1,0:T(8,128)(2,1)S(1)}, bf16[1,320,1280]{2,1,0:T(8,128)(2,1)}, u32[]{:S(2)}) copy-start(bf16[1,320,1280]{2,1,0:T(8,128)(2,1)} %param.28) | copy-start | bytes 2457604
  652.3 142.5 %all-gather.20.cloned.1.call-start = ((), (), s32[]{:S(2)}) async-start(), calls=%async_computation.11 | async-start | bytes 2949120 | tf_op jit(solution)/shard_map/all_gather | solution.py:51
  692.3 3.2 collective-permute-start.18
  719.6 15.8 %copy-start.32 = (f32[2560]{0:T(1024)S(1)}, f32[2560]{0:T(1024)}, u32[]{:S(2)}) copy-start(f32[2560]{0:T(1024)} %reduce.34) | copy-start | bytes 30724
  719.8 8.0 collective-permute-start.19
  728.0 7.1 collective-permute-start.20
  735.7 2.2 collective-permute-start.21
  738.7 111.9 %all-gather.22.cloned.1.call-start = ((), (), s32[]{:S(2)}) async-start(), calls=%async_computation.12 | async-start | bytes 1769472 | tf_op jit(solution)/shard_map/all_gather | solution.py:51
  794.8 5.1 collective-permute-start.22
  804.9 1.8 collective-permute-start.23
  812.9 11.5 %copy-start.45 = (pred[8,80]{1,0:T(8,128)(4,1)S(1)}, pred[8,80]{1,0:T(8,128)(4,1)}, u32[]{:S(2)}) copy-start(pred[8,80]{1,0:T(8,128)(4,1)} %copy-done.44) | copy-start | bytes 1924
  850.5 9.1 collective-permute-start.24
  858.1 38.0 %collective-permute-start.26 = (bf16[8,80,1280]{2,1,0:T(8,128)(2,1)}, bf16[8,80,1280]{2,1,0:T(8,128)(2,1)}, u32[]{:S(2)}, u32[]{:S(2)}) collective-permute-start(bf16[8,80,1280]{2,1,0:T(8,128)(2,1)} %broadcast_select_fusion.6), channel_id=1, source_target_pairs={{0,1},{1,0},{2,3},{3,2},{4,5},{5,4},{6,7},{7,6},{8,9},{9,8},{10,11... | collective-permute-start | bytes 4915208 | tf_op jit(solution)/shard_map/ppermute | solution.py:60
  862.0 38.3 %all-to-all-start.5 = ((bf16[8,128,320]{1,2,0:T(8,128)(2,1)}), bf16[8,128,320]{1,2,0:T(8,128)(2,1)S(1)}, u32[]{:S(2)}, u32[]{:S(2)}) async-start(bf16[8,128,320]{1,2,0:T(8,128)(2,1)} %bitcast.234), calls=%async_computation.5 | async-start | bytes 1310720 | tf_op jit(solution)/shard_map/all_to_all | solution.py:84
  901.1 42.1 %all-to-all-start.6 = ((bf16[8,80,1280]{2,1,0:T(8,128)(2,1)}), bf16[8,80,1280]{2,1,0:T(8,128)(2,1)S(1)}, u32[]{:S(2)}, u32[]{:S(2)}) async-start(bf16[8,80,1280]{2,1,0:T(8,128)(2,1)} %add_convert_fusion), calls=%async_computation.6 | async-start | bytes 3276800 | tf_op jit(solution)/shard_map/all_to_all | solution.py:102
  909.9 33.3 %copy-start.42 = (s32[1024]{0:T(1024)S(1)}, s32[1024]{0:T(1024)}, u32[]{:S(2)}) copy-start(s32[1024]{0:T(1024)} %pad_clamp_fusion) | copy-start | bytes 12292
  919.6 33.6 %collective-permute-start.25 = (bf16[128,1280]{1,0:T(8,128)(2,1)}, bf16[128,1280]{1,0:T(8,128)(2,1)}, u32[]{:S(2)}, u32[]{:S(2)}) collective-permute-start(bf16[128,1280]{1,0:T(8,128)(2,1)} %broadcast_select_fusion.25), channel_id=1, source_target_pairs={{0,1},{1,0},{2,3},{3,2},{4,5},{5,4},{6,7},{7,6},{8,9},{9,8},{10,11... | collective-permute-start | bytes 983048 | tf_op jit(solution)/shard_map/ppermute | solution.py:60
  (33 other events, 139.2 us)
Sparse Core Ops, SparseCore 0:
  10.2 180.5 all-gather.23
  255.0 39.0 all-gather.11
  340.7 55.9 all-gather.13
  449.7 43.3 all-gather.15
  652.4 39.8 all-gather.17
  738.8 55.9 all-gather.19
  807.7 42.7 all-gather.21

commit v8 on v7

--- a/solution.py
+++ b/solution.py
@@ -53,6 +53,15 @@
     lead = jnp.where(active, gathered, theirs)
     trail = jnp.where(active, theirs, gathered)
     return jnp.concatenate([lead, trail], axis=split_axis)
+
+
+def running_count(flags, axis):
+    size = flags.shape[axis]
+    steps = jnp.arange(size, dtype=jnp.int32)
+    lower = (steps[:, None] >= steps[None, :]).astype(jnp.bfloat16)
+    counted = jnp.tensordot(lower, flags.astype(jnp.bfloat16), axes=((1,), (axis,)),
+                            preferred_element_type=jnp.float32)
+    return jnp.moveaxis(counted, 0, axis).astype(jnp.int32)
 
 
 def swap_tensor(value):
@@ -240,11 +249,11 @@
         gate_weights = raised / jnp.sum(raised, axis=1, keepdims=True)
         flat_choice = choices.reshape(-1)
         onehot = (flat_choice[:, None] == expert_ids[None, :]).astype(jnp.int32)
-        slot_rank = jnp.sum(onehot * (jnp.cumsum(onehot, axis=0) - onehot), axis=1)
+        slot_rank = jnp.sum(onehot * (running_count(onehot, 0) - onehot), axis=1)
         slot_ids = flat_choice * capacity + slot_rank
         choices_all = choices_every[:, micro_index]
         mine = jnp.any(choices_all == expert_id, axis=2)
-        mine_rank = jnp.cumsum(mine.astype(jnp.int32), axis=1) - 1
+        mine_rank = running_count(mine, 1) - 1
         source_ids = jnp.broadcast_to(
             jnp.arange(experts_count, dtype=jnp.int32)[:, None], mine.shape
         )

time: 975 us -> 946 us (0.970)
  other arithmetic: 111 us -> 76.9 us
    another operation x10 -> x7, other arithmetic: 30 us -> 1.92 us  [the longest x1 23.6 us: local(): mine_rank = jnp.cumsum(mine.astype(jnp.int32), axis=1) - 1]
    all_to_all x2, waiting for transfers between devices: 30.9 us -> 40.7 us  [expert_path(): lax.all_to_all(summed, 'expert', split_axis=0, concat_axis=0, tiled=True)]
    unnamed x134 -> x131, local copies, waits for them, and re-layouts: 44.4 us -> 44.1 us
  transfers between devices with their start and end apart: 39 -> 39, of which waited for: 29 -> 29; matrix products, arithmetic and copies ran while one was open for 21% -> 18% of each run, Pallas kernels for 0% -> 0%
where the time goes in v8:
time: 946 us; the launch traced here: 935 us
  waiting for transfers between devices  428 us (45%)
  blocking collectives  207 us (22%)
  local copies, waits for them, and re-layouts  115 us (12%)
  other arithmetic  76.9 us (8%)
  matrix products  52.1 us (6%)
  starting transfers between devices  40.8 us (4%)
  between operations  15.8 us (2%)
    all_gather x6, waiting for transfers between devices, paired_gather(): lax.all_gather(jnp.where(active, first, second), 'expert', axis=axis, til...  222 us
    ppermute x10, waiting for transfers between devices, swap_tensor(): lax.ppermute(value, 'tensor', [(source, (source + 1) % count) for source...  93.8 us
    all_gather x1, blocking collectives, local(): lax.all_gather(expert_choice[0], 'expert', axis=0, tiled=False)  92.5 us
    all_gather x2, blocking collectives, paired_gather(): lax.all_gather(jnp.where(active, first, second), 'expert', axis=axis, til...  54.9 us
    all_gather x1, waiting for transfers between devices, local(): qkv_full = lax.all_gather(w_qkv[0], 'expert', axis=0, tiled=True)  44.7 us
    unnamed x131, local copies, waits for them, and re-layouts  44.1 us
    all_to_all x2, blocking collectives, terms_to_slots(): lax.all_to_all(terms, 'expert', split_axis=0, concat_axis=1, tiled=True)  42.2 us
    all_to_all x2, waiting for transfers between devices, expert_path(): lax.all_to_all(summed, 'expert', split_axis=0, concat_axis=0, tiled=True)  40.7 us
  transfers between devices with their start and end apart: 39, of which 29 were waited for; matrix products, arithmetic and copies ran while one was open for 18% of the time, Pallas kernels for 0%

profile of v8, /device:TPU:0, one launch (start us, length us, event | category | flops | bytes accessed | tf_op | source)
XLA Modules:
  0.0 935.5 jit_solution(11389894729743060194)
XLA Ops:
  7.9 8.5 copy.111
  16.5 7.4 all-to-all-start
  27.2 8.1 all-gather.2
  35.3 4.4 all-gather.3
  41.1 92.5 %all_gather.40 = s32[8,1,128,4]{2,3,1,0:T(4,128)} all-gather(s32[1,1,128,4]{2,3,1,0:T(4,128)S(1)} %copy-done.37), channel_id=1, replica_groups=mesh['section'=2,'expert'=8,'tensor'=2] {'expert'}, dimensions={0}, use_global_device_ids=true | all-gather | bytes 18432 | tf_op jit(solution)/shard_map/all_gather | solution.py:138
  133.5 4.7 all-gather.1
  143.5 2.7 all_to_all.78
  146.2 44.7 %all-gather.24.cloned.1.call-done = bf16[1,2560,2,896]{3,2,0,1:T(2,128)(2,1)} async-done(((bf16[1,320,2,896]{3,2,0,1:T(2,128)(2,1)}), bf16[1,2560,2,896]{3,2,0,1:T(2,128)(2,1)}) %all-gather.24.cloned.1.call-update) | async-done | bytes 9175056 | tf_op jit(solution)/shard_map/all_gather | solution.py:134
  190.8 8.7 copy.171
  199.6 12.8 %copy.114 = bf16[1792,2560]{1,0:T(8,128)(2,1)} copy(bf16[1792,2560]{0,1:T(8,128)(2,1)} %bitcast.233) | data formatting | bytes 18350080 | tf_op jit(solution)/shard_map/dot_general | solution.py:180
  212.4 6.2 fusion.103
  220.2 27.5 %all_gather.44 = bf16[1024,256]{0,1:T(8,128)(2,1)S(1)} all-gather(bf16[128,256]{0,1:T(8,128)(2,1)S(1)} %slice_select_fusion.7), channel_id=1, replica_groups=mesh['section'=2,'expert'=8,'tensor'=2] {'expert'}, dimensions={0}, use_global_device_ids=true | all-gather | bytes 589824 | tf_op jit(solution)/shard_map/all_gather | solution.py:51
  255.1 38.9 %all-gather.12.cloned.1.call-done = bf16[1024,640]{1,0:T(8,128)(2,1)} async-done(((bf16[128,640]{1,0:T(8,128)(2,1)}), bf16[1024,640]{1,0:T(8,128)(2,1)}) %all-gather.12.cloned.1.call-update) | async-done | bytes 1310736 | tf_op jit(solution)/shard_map/all_gather | solution.py:51
  294.1 3.2 collective-permute-done.4
  300.1 21.2 %all_to_all.104 = bf16[8,128,320]{1,2,0:T(8,128)(2,1)S(1)} all-to-all(bf16[8,128,320]{1,2,0:T(8,128)(2,1)S(1)} %bitcast.248), channel_id=1, replica_groups=mesh['section'=2,'expert'=8,'tensor'=2] {'expert'}, dimensions={0} | all-to-all | bytes 1310720 | tf_op jit(solution)/shard_map/all_to_all | solution.py:93
  323.2 6.5 collective-permute-done.5
  331.4 5.6 collective-permute-done.6
  340.6 56.1 %all-gather.14.cloned.1.call-done = bf16[1024,1280]{1,0:T(8,128)(2,1)} async-done(((bf16[128,1280]{1,0:T(8,128)(2,1)}), bf16[1024,1280]{1,0:T(8,128)(2,1)}) %all-gather.14.cloned.1.call-update) | async-done | bytes 2621456 | tf_op jit(solution)/shard_map/all_gather | solution.py:51
  396.7 7.9 copy.172
  407.0 2.2 fusion.141
  410.8 4.3 scatter_custom_fusion.1
  415.3 4.7 scatter_custom_fusion
  421.2 5.3 pad_maximum_fusion
  426.5 11.4 %gather_fusion = bf16[640,2560]{1,0:T(8,128)(2,1)} fusion(bf16[1024,2560]{1,0:T(8,128)(2,1)} %pad_maximum_fusion, s32[1024]{0:T(1024)S(1)} %pad_clamp_fusion.1), kind=kCustom, calls=%fused_computation | custom fusion | bytes 6556160 | tf_op jit(solution)/shard_map/gather | solution.py:272
  437.9 2.2 broadcast_select_fusion.1
  440.1 8.8 fusion.146
  449.0 15.8 %all-gather.16.cloned.1.call-done = bf16[512,1536]{0,1:T(8,128)(2,1)} async-done(((bf16[512,192]{0,1:T(8,128)(2,1)}), bf16[512,1536]{0,1:T(8,128)(2,1)}) %all-gather.16.cloned.1.call-update) | async-done | bytes 1572880 | tf_op jit(solution)/shard_map/all_gather | solution.py:51
  464.8 2.8 fusion.33
  468.1 2.9 convolution_convert_fusion.1
  476.3 3.5 all-to-all-start.2
  479.8 30.5 %collective-permute-done.12 = bf16[8,80,1280]{2,1,0:T(8,128)(2,1)} collective-permute-done((bf16[8,80,1280]{2,1,0:T(8,128)(2,1)}, bf16[8,80,1280]{2,1,0:T(8,128)(2,1)}, u32[]{:S(2)}, u32[]{:S(2)}) %collective-permute-start.12) | collective-permute-done | bytes 1638432 | tf_op jit(solution)/shard_map/ppermute | solution.py:69
  510.3 4.2 add_convert_fusion.1
  515.4 3.8 all-to-all-start.3
  538.6 18.6 %all-to-all-done.3 = bf16[8,80,1280]{2,1,0:T(8,128)(2,1)S(1)} async-done(((bf16[8,80,1280]{2,1,0:T(8,128)(2,1)}), bf16[8,80,1280]{2,1,0:T(8,128)(2,1)S(1)}, u32[]{:S(2)}, u32[]{:S(2)}) %all-to-all-start.3) | async-done | bytes 1638432 | tf_op jit(solution)/shard_map/all_to_all | solution.py:111
  557.2 3.0 gather_fusion.1
  560.2 3.7 reshape.818
  563.9 3.4 multiply_reduce_fusion.1
  572.7 8.6 collective-permute-done.14
  581.5 6.2 fusion.100
  589.4 27.4 %all_gather.48 = bf16[1024,256]{0,1:T(8,128)(2,1)S(1)} all-gather(bf16[128,256]{0,1:T(8,128)(2,1)S(1)} %slice_select_fusion.6), channel_id=1, replica_groups=mesh['section'=2,'expert'=8,'tensor'=2] {'expert'}, dimensions={0}, use_global_device_ids=true | all-gather | bytes 589824 | tf_op jit(solution)/shard_map/all_gather | solution.py:51
  624.0 40.0 %all-gather.18.cloned.1.call-done = bf16[1024,640]{1,0:T(8,128)(2,1)} async-done(((bf16[128,640]{1,0:T(8,128)(2,1)}), bf16[1024,640]{1,0:T(8,128)(2,1)}) %all-gather.18.cloned.1.call-update) | async-done | bytes 1310736 | tf_op jit(solution)/shard_map/all_gather | solution.py:51
  664.0 3.2 collective-permute-done.18
  670.0 21.0 %all_to_all.105 = bf16[8,128,320]{1,2,0:T(8,128)(2,1)S(1)} all-to-all(bf16[8,128,320]{1,2,0:T(8,128)(2,1)S(1)} %bitcast.249), channel_id=1, replica_groups=mesh['section'=2,'expert'=8,'tensor'=2] {'expert'}, dimensions={0} | all-to-all | bytes 1310720 | tf_op jit(solution)/shard_map/all_to_all | solution.py:93
  693.0 6.5 collective-permute-done.19
  701.2 5.6 collective-permute-done.20
  710.6 55.8 %all-gather.20.cloned.1.call-done = bf16[1024,1280]{1,0:T(8,128)(2,1)} async-done(((bf16[128,1280]{1,0:T(8,128)(2,1)}), bf16[1024,1280]{1,0:T(8,128)(2,1)}) %all-gather.20.cloned.1.call-update) | async-done | bytes 2621456 | tf_op jit(solution)/shard_map/all_gather | solution.py:51
  766.5 5.1 collective-permute-done.22
  771.6 2.4 broadcast_select_fusion.3
  774.0 2.2 fusion.140
  779.3 5.2 pad_maximum_fusion.1
  784.6 11.5 %gather_fusion.2 = bf16[640,2560]{1,0:T(8,128)(2,1)} fusion(bf16[1024,2560]{1,0:T(8,128)(2,1)} %pad_maximum_fusion.1, s32[1024]{0:T(1024)S(1)} %copy-done.40), kind=kCustom, calls=%fused_computation.2 | custom fusion | bytes 6556160 | tf_op jit(solution)/shard_map/gather | solution.py:272
  798.3 8.9 fusion.148
  807.3 15.0 %all-gather.22.cloned.1.call-done = bf16[512,1536]{0,1:T(8,128)(2,1)} async-done(((bf16[512,192]{0,1:T(8,128)(2,1)}), bf16[512,1536]{0,1:T(8,128)(2,1)}) %all-gather.22.cloned.1.call-update) | async-done | bytes 1572880 | tf_op jit(solution)/shard_map/all_gather | solution.py:51
  822.2 2.8 fusion.32
  825.5 2.9 convolution_convert_fusion
  833.7 3.5 all-to-all-start.5
  837.2 30.6 %collective-permute-done.26 = bf16[8,80,1280]{2,1,0:T(8,128)(2,1)} collective-permute-done((bf16[8,80,1280]{2,1,0:T(8,128)(2,1)}, bf16[8,80,1280]{2,1,0:T(8,128)(2,1)}, u32[]{:S(2)}, u32[]{:S(2)}) %collective-permute-start.26) | collective-permute-done | bytes 1638432 | tf_op jit(solution)/shard_map/ppermute | solution.py:69
  867.8 4.2 add_convert_fusion
  872.8 4.0 all-to-all-start.6
  882.4 3.6 broadcast_select_fusion.41
  892.8 22.1 %all-to-all-done.6 = bf16[8,80,1280]{2,1,0:T(8,128)(2,1)S(1)} async-done(((bf16[8,80,1280]{2,1,0:T(8,128)(2,1)}), bf16[8,80,1280]{2,1,0:T(8,128)(2,1)S(1)}, u32[]{:S(2)}, u32[]{:S(2)}) %all-to-all-start.6) | async-done | bytes 1638432 | tf_op jit(solution)/shard_map/all_to_all | solution.py:111
  914.9 2.9 gather_fusion.3
  917.8 3.7 reshape.819
  921.4 3.4 multiply_reduce_fusion
  (323 shorter events, 112.4 us)
Async XLA Ops:
  7.2 466.9 %copy-start = (bf16[1,320,1536]{2,1,0:T(8,128)(2,1)S(1)}, bf16[1,320,1536]{2,1,0:T(8,128)(2,1)}, u32[]{:S(2)}) copy-start(bf16[1,320,1536]{2,1,0:T(8,128)(2,1)} %param.30) | copy-start | bytes 2949124
  7.2 183.7 %all-gather.24.cloned.1.call-start = ((), (), s32[]{:S(2)}) async-start(), calls=%async_computation.13 | async-start | bytes 10321920 | tf_op jit(solution)/shard_map/all_gather | solution.py:134
  16.4 10.7 %copy-start.46 = (f32[1,1280]{1,0:T(1,128)S(1)}, f32[1,1280]{1,0:T(1,128)}, u32[]{:S(2)}) copy-start(f32[1,1280]{1,0:T(1,128)} %param.25) | copy-start | bytes 15364
  16.4 18.8 %copy-start.47 = (f32[1,1280]{1,0:T(1,128)S(1)}, f32[1,1280]{1,0:T(1,128)}, u32[]{:S(2)}) copy-start(f32[1,1280]{1,0:T(1,128)} %param.26) | copy-start | bytes 15364
  16.4 23.8 %copy-start.57 = (s32[1,8]{1,0:T(1,128)S(1)}, s32[1,8]{1,0:T(1,128)}, u32[]{:S(2)}) copy-start(s32[1,8]{1,0:T(1,128)} %param.23) | copy-start | bytes 100
  16.4 24.6 %copy-start.37 = (s32[1,1,128,4]{2,3,1,0:T(4,128)S(1)}, s32[1,1,128,4]{2,3,1,0:T(4,128)}, u32[]{:S(2)}) copy-start(s32[1,1,128,4]{2,3,1,0:T(4,128)} %param.24) | copy-start | bytes 6148
  16.5 117.1 %copy-start.38 = (f32[1,1280,8]{1,2,0:T(8,128)S(1)}, f32[1,1280,8]{1,2,0:T(8,128)}, u32[]{:S(2)}) copy-start(f32[1,1280,8]{1,2,0:T(8,128)} %param.31) | copy-start | bytes 122884
  16.5 122.4 %copy-start.48 = (s32[1,128]{1,0:T(1,128)S(1)}, s32[1,128]{1,0:T(1,128)}, u32[]{:S(2)}) copy-start(s32[1,128]{1,0:T(1,128)} %param.22) | copy-start | bytes 1540
  16.5 125.3 %all-to-all-start = ((bf16[320,2,1536]{0,1,2:T(2,128)(2,1)}), bf16[320,2,1536]{0,1,2:T(2,128)(2,1)S(1)}, u32[]{:S(2)}, u32[]{:S(2)}) async-start(bf16[320,2,1536]{0,1,2:T(2,128)(2,1)} %bitcast.236), calls=%async_computation | async-start | bytes 4718592 | tf_op jit(solution)/shard_map/all_to_all | solution.py:137
  23.9 270.2 %all-gather.12.cloned.1.call-start = ((), (), s32[]{:S(2)}) async-start(), calls=%async_computation.7 | async-start | bytes 1474560 | tf_op jit(solution)/shard_map/all_gather | solution.py:51
  25.7 114.1 %collective-permute-start = (bf16[128,1280]{1,0:T(8,128)(2,1)}, bf16[128,1280]{1,0:T(8,128)(2,1)}, u32[]{:S(2)}, u32[]{:S(2)}) collective-permute-start(bf16[128,1280]{1,0:T(8,128)(2,1)} %bitcast_select_fusion.3), channel_id=1, source_target_pairs={{0,1},{1,0},{2,3},{3,2},{4,5},{5,4},{6,7},{7,6},{8,9},{9,8},{10,11... | collective-permute-start | bytes 983048 | tf_op jit(solution)/shard_map/ppermute | solution.py:69
  35.3 177.1 %copy-start.34 = (f32[2560]{0:T(1024)}, f32[2560]{0:T(1024)S(1)}, u32[]{:S(2)}) copy-start(f32[2560]{0:T(1024)S(1)} %reduce.33) | copy-start | bytes 30724
  199.6 12.8 %copy-start.14 = (bf16[128,1280]{1,0:T(8,128)(2,1)S(1)}, bf16[128,1280]{1,0:T(8,128)(2,1)}, u32[]{:S(2)}) copy-start(bf16[128,1280]{1,0:T(8,128)(2,1)} %copy-done.13) | copy-start | bytes 983044
  199.6 12.8 %copy-start.16 = (bf16[128,1280]{1,0:T(8,128)(2,1)S(1)}, bf16[128,1280]{1,0:T(8,128)(2,1)}, u32[]{:S(2)}) copy-start(bf16[128,1280]{1,0:T(8,128)(2,1)} %copy-done.15) | copy-start | bytes 983044
  212.4 35.3 %copy-start.49 = (s32[1,128]{1,0:T(1,128)S(1)}, s32[1,128]{1,0:T(1,128)}, u32[]{:S(2)}) copy-start(s32[1,128]{1,0:T(1,128)} %param.22) | copy-start | bytes 1540
  212.4 35.3 %copy-start.50 = (s32[128]{0:T(128)S(1)}, s32[128]{0:T(128)}, u32[]{:S(2)}) copy-start(s32[128]{0:T(128)} %get-tuple-element.109) | copy-start | bytes 1540
  218.7 1.4 collective-permute-start.1
  247.7 1.9 collective-permute-start.2
  252.4 1.7 collective-permute-start.3
  254.9 44.0 %copy-start.55 = (bf16[1,320,1280]{2,1,0:T(8,128)(2,1)S(1)}, bf16[1,320,1280]{2,1,0:T(8,128)(2,1)}, u32[]{:S(2)}) copy-start(bf16[1,320,1280]{2,1,0:T(8,128)(2,1)} %param.28) | copy-start | bytes 2457604
  254.9 141.8 %all-gather.14.cloned.1.call-start = ((), (), s32[]{:S(2)}) async-start(), calls=%async_computation.8 | async-start | bytes 2949120 | tf_op jit(solution)/shard_map/all_gather | solution.py:51
  294.1 3.2 collective-permute-start.4
  300.1 29.7 %copy-start.7 = (bf16[1,128,1280]{2,1,0:T(8,128)(2,1)S(1)}, bf16[1,128,1280]{2,1,0:T(8,128)(2,1)}, u32[]{:S(2)}) copy-start(bf16[1,128,1280]{2,1,0:T(8,128)(2,1)} %param.21) | copy-start | bytes 983044
  321.6 15.7 %copy-start.32 = (f32[2560]{0:T(1024)S(1)}, f32[2560]{0:T(1024)}, u32[]{:S(2)}) copy-start(f32[2560]{0:T(1024)} %reduce.34) | copy-start | bytes 30724
  321.7 8.0 collective-permute-start.5
  329.9 7.1 collective-permute-start.6
  337.6 2.2 collective-permute-start.7
  340.6 124.2 %all-gather.16.cloned.1.call-start = ((), (), s32[]{:S(2)}) async-start(), calls=%async_computation.9 | async-start | bytes 1769472 | tf_op jit(solution)/shard_map/all_gather | solution.py:51
  396.7 8.3 collective-permute-start.8
  410.3 9.9 %collective-permute-start.9 = (bf16[1024,192]{0,1:T(8,128)(2,1)}, bf16[1024,192]{0,1:T(8,128)(2,1)}, u32[]{:S(2)}, u32[]{:S(2)}) collective-permute-start(bf16[1024,192]{0,1:T(8,128)(2,1)} %fusion.98), channel_id=1, source_target_pairs={{0,16},{16,0},{1,17},{17,1},{2,18},{18,2},{3,19},{19,3},{4,20},{20... | collective-permute-start | bytes 1179656 | tf_op jit(solution)/shard_map/ppermute | solution.py:45
  420.2 17.7 %copy-start.44 = (pred[8,80]{1,0:T(8,128)(4,1)}, pred[8,80]{1,0:T(8,128)(4,1)S(1)}, u32[]{:S(2)}) copy-start(pred[8,80]{1,0:T(8,128)(4,1)S(1)} %reshape.813) | copy-start | bytes 1924
  464.8 9.1 collective-permute-start.10
  472.4 38.0 %collective-permute-start.12 = (bf16[8,80,1280]{2,1,0:T(8,128)(2,1)}, bf16[8,80,1280]{2,1,0:T(8,128)(2,1)}, u32[]{:S(2)}, u32[]{:S(2)}) collective-permute-start(bf16[8,80,1280]{2,1,0:T(8,128)(2,1)} %broadcast_select_fusion.7), channel_id=1, source_target_pairs={{0,1},{1,0},{2,3},{3,2},{4,5},{5,4},{6,7},{7,6},{8,9},{9,8},{10,11... | collective-permute-start | bytes 4915208 | tf_op jit(solution)/shard_map/ppermute | solution.py:69
  476.3 38.3 %all-to-all-start.2 = ((bf16[8,128,320]{1,2,0:T(8,128)(2,1)}), bf16[8,128,320]{1,2,0:T(8,128)(2,1)S(1)}, u32[]{:S(2)}, u32[]{:S(2)}) async-start(bf16[8,128,320]{1,2,0:T(8,128)(2,1)} %bitcast.227), calls=%async_computation.2 | async-start | bytes 1310720 | tf_op jit(solution)/shard_map/all_to_all | solution.py:93
  515.4 41.8 %all-to-all-start.3 = ((bf16[8,80,1280]{2,1,0:T(8,128)(2,1)}), bf16[8,80,1280]{2,1,0:T(8,128)(2,1)S(1)}, u32[]{:S(2)}, u32[]{:S(2)}) async-start(bf16[8,80,1280]{2,1,0:T(8,128)(2,1)} %add_convert_fusion.1), calls=%async_computation.3 | async-start | bytes 3276800 | tf_op jit(solution)/shard_map/all_to_all | solution.py:111
  519.1 144.8 %all-gather.18.cloned.1.call-start = ((), (), s32[]{:S(2)}) async-start(), calls=%async_computation.10 | async-start | bytes 1474560 | tf_op jit(solution)/shard_map/all_gather | solution.py:51
  534.5 32.9 %collective-permute-start.11 = (bf16[128,1280]{1,0:T(8,128)(2,1)}, bf16[128,1280]{1,0:T(8,128)(2,1)}, u32[]{:S(2)}, u32[]{:S(2)}) collective-permute-start(bf16[128,1280]{1,0:T(8,128)(2,1)} %broadcast_select_fusion.31), channel_id=1, source_target_pairs={{0,1},{1,0},{2,3},{3,2},{4,5},{5,4},{6,7},{7,6},{8,9},{9,8},{10,11... | collective-permute-start | bytes 983048 | tf_op jit(solution)/shard_map/ppermute | solution.py:69
  568.5 13.0 %copy-start.35 = (f32[2560]{0:T(1024)S(1)}, f32[2560]{0:T(1024)}, u32[]{:S(2)}) copy-start(f32[2560]{0:T(1024)} %copy-done.34) | copy-start | bytes 30724
  568.6 12.9 %copy-start.24 = (bf16[128,1280]{1,0:T(8,128)(2,1)}, bf16[128,1280]{1,0:T(8,128)(2,1)S(1)}, u32[]{:S(2)}) copy-start(bf16[128,1280]{1,0:T(8,128)(2,1)S(1)} %add_convert_fusion.6) | copy-start | bytes 983044
  568.6 2.5 collective-permute-start.13
  571.2 10.1 %collective-permute-start.14 = (bf16[128,1280]{1,0:T(8,128)(2,1)S(1)}, bf16[128,1280]{1,0:T(8,128)(2,1)S(1)}, u32[]{:S(2)}, u32[]{:S(2)}) collective-permute-start(bf16[128,1280]{1,0:T(8,128)(2,1)S(1)} %bitcast_select_fusion.2), channel_id=1, source_target_pairs={{0,1},{1,0},{2,3},{3,2},{4,5},{5,4},{6,7},{7,6},{8,9},{9,8},{10,11... | collective-permute-start | bytes 983048 | tf_op jit(solution)/shard_map/ppermute | solution.py:69
  587.8 31.0 %copy-start.26 = (bf16[128,2,1,128]{0,3,2,1:T(8,128)(2,1)}, bf16[128,2,1,128]{0,3,2,1:T(8,128)(2,1)S(1)}, u32[]{:S(2)}) copy-start(bf16[128,2,1,128]{0,3,2,1:T(8,128)(2,1)S(1)} %slice.273) | copy-start | bytes 196612
  587.9 31.0 %copy-start.28 = (bf16[128,2,128]{0,2,1:T(8,128)(2,1)}, bf16[128,2,128]{0,2,1:T(8,128)(2,1)S(1)}, u32[]{:S(2)}) copy-start(bf16[128,2,128]{0,2,1:T(8,128)(2,1)S(1)} %pad_maximum_fusion.13) | copy-start | bytes 196612
  587.9 1.4 collective-permute-start.15
  616.8 1.9 collective-permute-start.16
  621.5 1.7 collective-permute-start.17
  624.0 44.8 %copy-start.56 = (bf16[1,320,1280]{2,1,0:T(8,128)(2,1)S(1)}, bf16[1,320,1280]{2,1,0:T(8,128)(2,1)}, u32[]{:S(2)}) copy-start(bf16[1,320,1280]{2,1,0:T(8,128)(2,1)} %param.28) | copy-start | bytes 2457604
  624.0 142.5 %all-gather.20.cloned.1.call-start = ((), (), s32[]{:S(2)}) async-start(), calls=%async_computation.11 | async-start | bytes 2949120 | tf_op jit(solution)/shard_map/all_gather | solution.py:51
  664.0 3.2 collective-permute-start.18
  691.2 15.8 %copy-start.33 = (f32[2560]{0:T(1024)S(1)}, f32[2560]{0:T(1024)}, u32[]{:S(2)}) copy-start(f32[2560]{0:T(1024)} %reduce.34) | copy-start | bytes 30724
  691.5 8.0 collective-permute-start.19
  699.7 7.1 collective-permute-start.20
  707.3 2.2 collective-permute-start.21
  710.3 111.9 %all-gather.22.cloned.1.call-start = ((), (), s32[]{:S(2)}) async-start(), calls=%async_computation.12 | async-start | bytes 1769472 | tf_op jit(solution)/shard_map/all_gather | solution.py:51
  766.5 5.1 collective-permute-start.22
  776.6 1.8 collective-permute-start.23
  784.6 11.5 %copy-start.45 = (pred[8,80]{1,0:T(8,128)(4,1)S(1)}, pred[8,80]{1,0:T(8,128)(4,1)}, u32[]{:S(2)}) copy-start(pred[8,80]{1,0:T(8,128)(4,1)} %copy-done.44) | copy-start | bytes 1924
  822.2 9.0 collective-permute-start.24
  829.8 38.0 %collective-permute-start.26 = (bf16[8,80,1280]{2,1,0:T(8,128)(2,1)}, bf16[8,80,1280]{2,1,0:T(8,128)(2,1)}, u32[]{:S(2)}, u32[]{:S(2)}) collective-permute-start(bf16[8,80,1280]{2,1,0:T(8,128)(2,1)} %broadcast_select_fusion.6), channel_id=1, source_target_pairs={{0,1},{1,0},{2,3},{3,2},{4,5},{5,4},{6,7},{7,6},{8,9},{9,8},{10,11... | collective-permute-start | bytes 4915208 | tf_op jit(solution)/shard_map/ppermute | solution.py:69
  833.7 38.3 %all-to-all-start.5 = ((bf16[8,128,320]{1,2,0:T(8,128)(2,1)}), bf16[8,128,320]{1,2,0:T(8,128)(2,1)S(1)}, u32[]{:S(2)}, u32[]{:S(2)}) async-start(bf16[8,128,320]{1,2,0:T(8,128)(2,1)} %bitcast.225), calls=%async_computation.5 | async-start | bytes 1310720 | tf_op jit(solution)/shard_map/all_to_all | solution.py:93
  872.0 9.6 %copy-start.27 = (bf16[128,2,1,128]{0,3,2,1:T(8,128)(2,1)S(1)}, bf16[128,2,1,128]{0,3,2,1:T(8,128)(2,1)}, u32[]{:S(2)}) copy-start(bf16[128,2,1,128]{0,3,2,1:T(8,128)(2,1)} %copy-done.26) | copy-start | bytes 196612
  872.8 42.0 %all-to-all-start.6 = ((bf16[8,80,1280]{2,1,0:T(8,128)(2,1)}), bf16[8,80,1280]{2,1,0:T(8,128)(2,1)S(1)}, u32[]{:S(2)}, u32[]{:S(2)}) async-start(bf16[8,80,1280]{2,1,0:T(8,128)(2,1)} %add_convert_fusion), calls=%async_computation.6 | async-start | bytes 3276800 | tf_op jit(solution)/shard_map/all_to_all | solution.py:111
  881.6 33.3 %copy-start.42 = (s32[1024]{0:T(1024)S(1)}, s32[1024]{0:T(1024)}, u32[]{:S(2)}) copy-start(s32[1024]{0:T(1024)} %pad_clamp_fusion) | copy-start | bytes 12292
  891.2 33.6 %collective-permute-start.25 = (bf16[128,1280]{1,0:T(8,128)(2,1)}, bf16[128,1280]{1,0:T(8,128)(2,1)}, u32[]{:S(2)}, u32[]{:S(2)}) collective-permute-start(bf16[128,1280]{1,0:T(8,128)(2,1)} %broadcast_select_fusion.25), channel_id=1, source_target_pairs={{0,1},{1,0},{2,3},{3,2},{4,5},{5,4},{6,7},{7,6},{8,9},{9,8},{10,11... | collective-permute-start | bytes 983048 | tf_op jit(solution)/shard_map/ppermute | solution.py:69
  (33 other events, 141.2 us)
Sparse Core Ops, SparseCore 0:
  10.2 180.5 all-gather.23
  255.0 39.0 all-gather.11
  340.7 55.9 all-gather.13
  421.3 43.4 all-gather.15
  624.1 39.8 all-gather.17
  710.5 55.9 all-gather.19
  779.4 42.7 all-gather.21

commit v9 on v8

--- a/solution.py
+++ b/solution.py
@@ -89,12 +89,32 @@
     )
 
 
-def terms_to_slots(terms):
-    by_slot = lax.all_to_all(terms, "expert", split_axis=0, concat_axis=1, tiled=True)
-    return tensor_sum_scatter(by_slot, 1)
-
-
-def expert_path(full_rows, w_in_local, w_down_local):
+def paired_apply(step, value, in_axis, out_axis, active):
+    if active is None:
+        return step(value)
+    value = jnp.where(active, value, swap_cores(value))
+    first, second = jnp.split(value, 2, axis=in_axis)
+    done = step(jnp.where(active, first, second))
+    theirs = swap_cores(done)
+    return jnp.concatenate(
+        [jnp.where(active, done, theirs), jnp.where(active, theirs, done)], axis=out_axis
+    )
+
+
+def terms_to_slots(terms, active):
+    count = lax.axis_size("expert")
+    blocks = terms.reshape(count, terms.shape[0] // count, terms.shape[1])
+
+    def step(part):
+        by_slot = lax.all_to_all(
+            part.reshape(-1, part.shape[2]), "expert", split_axis=0, concat_axis=1, tiled=True
+        )
+        return tensor_sum_scatter(by_slot, 1)
+
+    return paired_apply(step, blocks, 1, 0, active)
+
+
+def expert_path(full_rows, w_in_local, w_down_local, active):
     sources, slot_count, model_width = full_rows.shape
     local_width = w_down_local.shape[0]
     hidden = jnp.dot(
@@ -107,8 +127,12 @@
     )
     partial_value = jnp.dot(activated, w_down_local, preferred_element_type=jnp.float32)
     partial_value = partial_value.reshape(sources, slot_count, model_width)
-    summed = tensor_sum_scatter(partial_value.astype(jnp.bfloat16), 2)
-    return lax.all_to_all(summed, "expert", split_axis=0, concat_axis=0, tiled=True)
+
+    def step(part):
+        summed = tensor_sum_scatter(part, 2)
+        return lax.all_to_all(summed, "expert", split_axis=0, concat_axis=0, tiled=True)
+
+    return paired_apply(step, partial_value.astype(jnp.bfloat16), 1, 1, active)
 
 
 def local(
@@ -164,7 +188,8 @@
             section_id == 0, hidden_in[min(tick_index, micro_count - 1)], carried_rows
         )
         active = (tick_index - section_id >= 0) & (tick_index - section_id < micro_count)
-        if micro_count == 1 and sections == 2:
+        pair_active = active if micro_count == 1 and sections == 2 else None
+        if pair_active is not None:
             expert_gather = functools.partial(paired_gather, active=active)
         else:
             def expert_gather(value, axis, split_axis):
@@ -216,7 +241,7 @@
         attn_terms = lax.dot_general(
             attended_all, out_local, (((1,), (1,)), ((), ())), preferred_element_type=jnp.float32
         )
-        attn_sum = terms_to_slots(attn_terms.astype(jnp.bfloat16)).astype(jnp.float32)
+        attn_sum = terms_to_slots(attn_terms.astype(jnp.bfloat16), pair_active).astype(jnp.float32)
         after_attn = (incoming.astype(jnp.float32) + attn_sum).astype(jnp.bfloat16)
         moe_rows = norm_full_rows(after_attn, ffn_gain_full)
         moe_all = expert_gather(moe_rows, 0, 1)
@@ -235,7 +260,7 @@
             (((1,), (1,)), ((), ())),
             preferred_element_type=jnp.float32,
         )
-        shared_sum = terms_to_slots(shared_terms.astype(jnp.bfloat16))
+        shared_sum = terms_to_slots(shared_terms.astype(jnp.bfloat16), pair_active)
         shared_out = lax.optimization_barrier(shared_sum).astype(jnp.float32)
         logits = jnp.dot(
             moe_rows.astype(jnp.float32), router_full, precision=lax.Precision.HIGHEST
@@ -270,7 +295,7 @@
             .set(True, mode="drop")
         )
         incoming_rows = jnp.where(filled[..., None], moe_all[table], jnp.zeros((), jnp.bfloat16))
-        returned = expert_path(incoming_rows, w_in_local, w_down_local)
+        returned = expert_path(incoming_rows, w_in_local, w_down_local, pair_active)
         combined = returned.reshape(experts_count * capacity, columns)[slot_ids].astype(jnp.float32)
         combined = combined * gate_weights.reshape(-1)[:, None]
         moe_out = jnp.sum(combined.reshape(tokens_dev, top_count, columns), axis=1)

time: 946 us -> 929 us (0.982)
  waiting for transfers between devices: 428 us -> 441 us
  local copies, waits for them, and re-layouts: 115 us -> 104 us
  blocking collectives: 207 us -> 196 us
  other arithmetic: 76.9 us -> 66.1 us
    all_gather x6, waiting for transfers between devices: 222 us -> 273 us  [paired_gather(): lax.all_gather(jnp.where(active, first, second), 'expert', axis=axis, til...]
    ppermute x10, waiting for transfers between devices: 93.8 us -> 55.9 us  [swap_tensor(): lax.ppermute(value, 'tensor', [(source, (source + 1) % count) for source...]
    all_to_all x4, waiting for transfers between devices: 40.7 us -> 27.2 us  [the longest x2 27.2 us: step(): lax.all_to_all(summed, 'expert', split_axis=0, concat_axis=0, tiled=True)]
    all_to_all x2, blocking collectives: 42.2 us -> 31 us  [step(): lax.all_to_all(part.reshape(-1, part.shape[2]), 'expert', split_axis=0, c...]
    ppermute x16 -> x28, waiting for transfers between devices: 25.7 us -> 36.7 us  [swap_cores(): lax.ppermute(value, 'section', [(source, (source + 1) % count) for source...]
    select_n x0 -> x18, other arithmetic: none -> 10.7 us  [the longest x6 5.12 us: paired_apply(): value = jnp.where(active, value, swap_cores(value))]
    unnamed x131 -> x97, local copies, waits for them, and re-layouts: 44.1 us -> 37.8 us
  transfers between devices with their start and end apart: 39 -> 51, of which waited for: 29 -> 36; matrix products, arithmetic and copies ran while one was open for 18% -> 13% of each run, Pallas kernels for 0% -> 0%
where the time goes in v9:
time: 929 us; the launch traced here: 919 us
  waiting for transfers between devices  441 us (47%)
  blocking collectives  196 us (21%)
  local copies, waits for them, and re-layouts  104 us (11%)
  other arithmetic  66.1 us (7%)
  matrix products  51.2 us (6%)
  starting transfers between devices  45.3 us (5%)
  between operations  15.8 us (2%)
    all_gather x6, waiting for transfers between devices, paired_gather(): lax.all_gather(jnp.where(active, first, second), 'expert', axis=axis, til...  273 us
    all_gather x1, blocking collectives, local(): lax.all_gather(expert_choice[0], 'expert', axis=0, tiled=False)  92.6 us
    ppermute x10, waiting for transfers between devices, swap_tensor(): lax.ppermute(value, 'tensor', [(source, (source + 1) % count) for source...  55.9 us
    all_gather x2, blocking collectives, paired_gather(): lax.all_gather(jnp.where(active, first, second), 'expert', axis=axis, til...  55.2 us
    all_gather x1, waiting for transfers between devices, local(): qkv_full = lax.all_gather(w_qkv[0], 'expert', axis=0, tiled=True)  46.3 us
    unnamed x97, local copies, waits for them, and re-layouts  37.8 us
    ppermute x28, waiting for transfers between devices, swap_cores(): lax.ppermute(value, 'section', [(source, (source + 1) % count) for source...  36.7 us
    all_to_all x2, blocking collectives, step(): lax.all_to_all(part.reshape(-1, part.shape[2]), 'expert', split_axis=0, c...  31 us
  transfers between devices with their start and end apart: 51, of which 36 were waited for; matrix products, arithmetic and copies ran while one was open for 13% of the time, Pallas kernels for 0%

profile of v9, /device:TPU:0, one launch (start us, length us, event | category | flops | bytes accessed | tf_op | source)
XLA Modules:
  0.0 919.1 jit_solution(12755835047869128708)
XLA Ops:
  7.9 8.5 copy.144
  16.5 7.4 all-to-all-start
  27.2 8.1 all-gather.2
  35.3 4.4 all-gather.3
  40.5 92.6 %all_gather.40 = s32[8,1,128,4]{2,3,1,0:T(4,128)S(1)} all-gather(s32[1,1,128,4]{2,3,1,0:T(4,128)S(1)} %copy-done.26), channel_id=1, replica_groups=mesh['section'=2,'expert'=8,'tensor'=2] {'expert'}, dimensions={0}, use_global_device_ids=true | all-gather | bytes 18432 | tf_op jit(solution)/shard_map/all_gather | solution.py:162
  133.1 4.7 all-gather.1
  141.9 2.7 all_to_all.70
  144.6 46.3 %all-gather.24.cloned.1.call-done = bf16[1,2560,2,896]{3,2,0,1:T(2,128)(2,1)} async-done(((bf16[1,320,2,896]{3,2,0,1:T(2,128)(2,1)}), bf16[1,2560,2,896]{3,2,0,1:T(2,128)(2,1)}) %all-gather.24.cloned.1.call-update) | async-done | bytes 9175056 | tf_op jit(solution)/shard_map/all_gather | solution.py:158
  190.8 8.7 copy.200
  199.6 12.8 %copy.147 = bf16[1792,2560]{1,0:T(8,128)(2,1)} copy(bf16[1792,2560]{0,1:T(8,128)(2,1)} %bitcast.233) | data formatting | bytes 18350080 | tf_op jit(solution)/shard_map/dot_general | solution.py:205
  212.3 6.2 fusion.103
  220.2 27.5 %all_gather.44 = bf16[1024,256]{0,1:T(8,128)(2,1)S(1)} all-gather(bf16[128,256]{0,1:T(8,128)(2,1)S(1)} %slice_select_fusion.13), channel_id=1, replica_groups=mesh['section'=2,'expert'=8,'tensor'=2] {'expert'}, dimensions={0}, use_global_device_ids=true | all-gather | bytes 589824 | tf_op jit(solution)/shard_map/all_gather | solution.py:51
  255.1 39.0 %all-gather.12.cloned.1.call-done = bf16[1024,640]{1,0:T(8,128)(2,1)} async-done(((bf16[128,640]{1,0:T(8,128)(2,1)}), bf16[1024,640]{1,0:T(8,128)(2,1)}) %all-gather.12.cloned.1.call-update) | async-done | bytes 1310736 | tf_op jit(solution)/shard_map/all_gather | solution.py:51
  294.0 3.2 collective-permute-done.4
  302.9 15.4 %all_to_all.92 = bf16[8,64,320]{2,1,0:T(8,128)(2,1)S(1)} all-to-all(bf16[8,64,320]{2,1,0:T(8,128)(2,1)S(1)} %copy.155), channel_id=1, replica_groups=mesh['section'=2,'expert'=8,'tensor'=2] {'expert'}, dimensions={0} | all-to-all | bytes 655360 | tf_op jit(solution)/shard_map/all_to_all | solution.py:109
  320.4 3.9 collective-permute-done.6
  327.5 8.3 collective-permute-done.8
  339.3 53.9 %all-gather.14.cloned.1.call-done = bf16[1024,1280]{1,0:T(8,128)(2,1)} async-done(((bf16[128,1280]{1,0:T(8,128)(2,1)}), bf16[1024,1280]{1,0:T(8,128)(2,1)}) %all-gather.14.cloned.1.call-update) | async-done | bytes 2621456 | tf_op jit(solution)/shard_map/all_gather | solution.py:51
  393.2 7.7 copy.201
  401.4 4.3 scatter_custom_fusion.1
  405.9 4.3 scatter_custom_fusion
  410.4 2.9 broadcast_select_fusion.7
  413.2 2.8 pad_maximum_fusion
  416.0 2.2 fusion.141
  419.7 11.5 %gather_fusion = bf16[640,2560]{1,0:T(8,128)(2,1)} fusion(bf16[1024,2560]{1,0:T(8,128)(2,1)} %pad_maximum_fusion, s32[1024]{0:T(1024)S(1)} %pad_clamp_fusion.1), kind=kCustom, calls=%fused_computation | custom fusion | bytes 6556160 | tf_op jit(solution)/shard_map/gather | solution.py:297
  433.5 7.6 fusion.142
  443.1 4.1 convolution_convert_fusion.1
  448.3 44.1 %all-gather.16.cloned.1.call-done = bf16[512,1536]{0,1:T(8,128)(2,1)} async-done(((bf16[512,192]{0,1:T(8,128)(2,1)}), bf16[512,1536]{0,1:T(8,128)(2,1)}) %all-gather.16.cloned.1.call-update) | async-done | bytes 1572880 | tf_op jit(solution)/shard_map/all_gather | solution.py:51
  492.3 2.3 broadcast_select_fusion.3
  503.9 4.1 all-to-all-start.2
  508.0 11.6 %collective-permute-done.17 = bf16[8,40,1280]{2,1,0:T(8,128)(2,1)} collective-permute-done((bf16[8,40,1280]{2,1,0:T(8,128)(2,1)}, bf16[8,40,1280]{2,1,0:T(8,128)(2,1)}, u32[]{:S(2)}, u32[]{:S(2)}) %collective-permute-start.17) | collective-permute-done | bytes 819232 | tf_op jit(solution)/shard_map/ppermute | solution.py:69
  519.6 2.3 add_convert_fusion.1
  522.0 3.5 all-to-all-start.3
  530.1 16.0 %all-to-all-done.3 = bf16[8,40,1280]{2,1,0:T(8,128)(2,1)S(1)} async-done(((bf16[8,40,1280]{2,1,0:T(8,128)(2,1)}), bf16[8,40,1280]{2,1,0:T(8,128)(2,1)S(1)}, u32[]{:S(2)}, u32[]{:S(2)}) %all-to-all-start.3) | async-done | bytes 819232 | tf_op jit(solution)/shard_map/all_to_all | solution.py:133
  550.1 3.3 gather_fusion.1
  553.4 3.7 reshape.842
  557.1 3.4 multiply_reduce_fusion.1
  565.5 8.5 collective-permute-done.20
  574.3 6.2 fusion.100
  582.1 27.7 %all_gather.48 = bf16[1024,256]{0,1:T(8,128)(2,1)S(1)} all-gather(bf16[128,256]{0,1:T(8,128)(2,1)S(1)} %slice_select_fusion.12), channel_id=1, replica_groups=mesh['section'=2,'expert'=8,'tensor'=2] {'expert'}, dimensions={0}, use_global_device_ids=true | all-gather | bytes 589824 | tf_op jit(solution)/shard_map/all_gather | solution.py:51
  617.1 39.1 %all-gather.18.cloned.1.call-done = bf16[1024,640]{1,0:T(8,128)(2,1)} async-done(((bf16[128,640]{1,0:T(8,128)(2,1)}), bf16[1024,640]{1,0:T(8,128)(2,1)}) %all-gather.18.cloned.1.call-update) | async-done | bytes 1310736 | tf_op jit(solution)/shard_map/all_gather | solution.py:51
  656.2 3.2 collective-permute-done.24
  665.0 15.6 %all_to_all.93 = bf16[8,64,320]{2,1,0:T(8,128)(2,1)S(1)} all-to-all(bf16[8,64,320]{2,1,0:T(8,128)(2,1)S(1)} %copy.172), channel_id=1, replica_groups=mesh['section'=2,'expert'=8,'tensor'=2] {'expert'}, dimensions={0} | all-to-all | bytes 655360 | tf_op jit(solution)/shard_map/all_to_all | solution.py:109
  682.7 3.8 collective-permute-done.26
  689.7 8.3 collective-permute-done.28
  701.6 53.9 %all-gather.20.cloned.1.call-done = bf16[1024,1280]{1,0:T(8,128)(2,1)} async-done(((bf16[128,1280]{1,0:T(8,128)(2,1)}), bf16[1024,1280]{1,0:T(8,128)(2,1)}) %all-gather.20.cloned.1.call-update) | async-done | bytes 2621456 | tf_op jit(solution)/shard_map/all_gather | solution.py:51
  755.5 5.1 collective-permute-done.30
  760.6 2.4 broadcast_select_fusion.5
  763.0 2.2 fusion.140
  765.2 2.7 pad_maximum_fusion.1
  769.1 11.3 %gather_fusion.2 = bf16[640,2560]{1,0:T(8,128)(2,1)} fusion(bf16[1024,2560]{1,0:T(8,128)(2,1)} %pad_maximum_fusion.1, s32[1024]{0:T(1024)S(1)} %copy-done.30), kind=kCustom, calls=%fused_computation.2 | custom fusion | bytes 6556160 | tf_op jit(solution)/shard_map/gather | solution.py:297
  782.7 7.6 fusion.144
  792.4 4.1 convolution_convert_fusion
  798.8 42.9 %all-gather.22.cloned.1.call-done = bf16[512,1536]{0,1:T(8,128)(2,1)} async-done(((bf16[512,192]{0,1:T(8,128)(2,1)}), bf16[512,1536]{0,1:T(8,128)(2,1)}) %all-gather.22.cloned.1.call-update) | async-done | bytes 1572880 | tf_op jit(solution)/shard_map/all_gather | solution.py:51
  841.8 2.3 broadcast_select_fusion
  853.4 4.1 all-to-all-start.5
  857.5 11.5 %collective-permute-done.37 = bf16[8,40,1280]{2,1,0:T(8,128)(2,1)} collective-permute-done((bf16[8,40,1280]{2,1,0:T(8,128)(2,1)}, bf16[8,40,1280]{2,1,0:T(8,128)(2,1)}, u32[]{:S(2)}, u32[]{:S(2)}) %collective-permute-start.37) | collective-permute-done | bytes 819232 | tf_op jit(solution)/shard_map/ppermute | solution.py:69
  869.0 2.4 add_convert_fusion
  871.4 3.9 all-to-all-start.6
  878.2 2.5 broadcast_select_fusion.47
  884.5 11.3 %all-to-all-done.6 = bf16[8,40,1280]{2,1,0:T(8,128)(2,1)S(1)} async-done(((bf16[8,40,1280]{2,1,0:T(8,128)(2,1)}), bf16[8,40,1280]{2,1,0:T(8,128)(2,1)S(1)}, u32[]{:S(2)}, u32[]{:S(2)}) %all-to-all-start.6) | async-done | bytes 819232 | tf_op jit(solution)/shard_map/all_to_all | solution.py:133
  899.8 2.9 gather_fusion.3
  902.7 3.7 reshape.843
  906.3 3.4 multiply_reduce_fusion
  (345 shorter events, 115.4 us)
Async XLA Ops:
  7.2 489.1 %copy-start = (bf16[1,320,1536]{2,1,0:T(8,128)(2,1)S(1)}, bf16[1,320,1536]{2,1,0:T(8,128)(2,1)}, u32[]{:S(2)}) copy-start(bf16[1,320,1536]{2,1,0:T(8,128)(2,1)} %param.30) | copy-start | bytes 2949124
  7.2 183.7 %all-gather.24.cloned.1.call-start = ((), (), s32[]{:S(2)}) async-start(), calls=%async_computation.13 | async-start | bytes 10321920 | tf_op jit(solution)/shard_map/all_gather | solution.py:158
  16.4 23.2 %copy-start.44 = (s32[1,8]{1,0:T(1,128)S(1)}, s32[1,8]{1,0:T(1,128)}, u32[]{:S(2)}) copy-start(s32[1,8]{1,0:T(1,128)} %param.23) | copy-start | bytes 100
  16.5 24.0 %copy-start.26 = (s32[1,1,128,4]{2,3,1,0:T(4,128)S(1)}, s32[1,1,128,4]{2,3,1,0:T(4,128)}, u32[]{:S(2)}) copy-start(s32[1,1,128,4]{2,3,1,0:T(4,128)} %param.24) | copy-start | bytes 6148
  16.5 116.6 %copy-start.28 = (f32[1,1280,8]{1,2,0:T(8,128)S(1)}, f32[1,1280,8]{1,2,0:T(8,128)}, u32[]{:S(2)}) copy-start(f32[1,1280,8]{1,2,0:T(8,128)} %param.31) | copy-start | bytes 122884
  16.5 121.4 %copy-start.37 = (s32[1,128]{1,0:T(1,128)S(1)}, s32[1,128]{1,0:T(1,128)}, u32[]{:S(2)}) copy-start(s32[1,128]{1,0:T(1,128)} %param.22) | copy-start | bytes 1540
  16.5 123.7 %all-to-all-start = ((bf16[320,2,1536]{0,1,2:T(2,128)(2,1)}), bf16[320,2,1536]{0,1,2:T(2,128)(2,1)S(1)}, u32[]{:S(2)}, u32[]{:S(2)}) async-start(bf16[320,2,1536]{0,1,2:T(2,128)(2,1)} %bitcast.236), calls=%async_computation | async-start | bytes 4718592 | tf_op jit(solution)/shard_map/all_to_all | solution.py:161
  23.9 270.1 %all-gather.12.cloned.1.call-start = ((), (), s32[]{:S(2)}) async-start(), calls=%async_computation.7 | async-start | bytes 1474560 | tf_op jit(solution)/shard_map/all_gather | solution.py:51
  25.7 112.5 %collective-permute-start = (bf16[128,1280]{1,0:T(8,128)(2,1)}, bf16[128,1280]{1,0:T(8,128)(2,1)}, u32[]{:S(2)}, u32[]{:S(2)}) collective-permute-start(bf16[128,1280]{1,0:T(8,128)(2,1)} %bitcast_select_fusion.3), channel_id=1, source_target_pairs={{0,1},{1,0},{2,3},{3,2},{4,5},{5,4},{6,7},{7,6},{8,9},{9,8},{10,11... | collective-permute-start | bytes 983048 | tf_op jit(solution)/shard_map/ppermute | solution.py:69
  39.7 296.4 %copy-start.24 = (f32[2560]{0:T(1024)}, f32[2560]{0:T(1024)S(1)}, u32[]{:S(2)}) copy-start(f32[2560]{0:T(1024)S(1)} %reduce.34) | copy-start | bytes 30724
  218.6 29.0 %copy-start.19 = (bf16[128,2,128]{0,2,1:T(8,128)(2,1)}, bf16[128,2,128]{0,2,1:T(8,128)(2,1)S(1)}, u32[]{:S(2)}) copy-start(bf16[128,2,128]{0,2,1:T(8,128)(2,1)S(1)} %pad_maximum_fusion.16) | copy-start | bytes 196612
  218.7 1.4 collective-permute-start.1
  247.7 1.9 collective-permute-start.2
  252.4 1.7 collective-permute-start.3
  254.8 44.0 %copy-start.42 = (bf16[1,320,1280]{2,1,0:T(8,128)(2,1)S(1)}, bf16[1,320,1280]{2,1,0:T(8,128)(2,1)}, u32[]{:S(2)}) copy-start(bf16[1,320,1280]{2,1,0:T(8,128)(2,1)} %param.28) | copy-start | bytes 2457604
  254.8 138.4 %all-gather.14.cloned.1.call-start = ((), (), s32[]{:S(2)}) async-start(), calls=%async_computation.8 | async-start | bytes 2949120 | tf_op jit(solution)/shard_map/all_gather | solution.py:51
  294.0 3.2 collective-permute-start.4
  300.0 2.2 collective-permute-start.5
  302.6 23.2 %copy-start.1 = (bf16[1,128,1280]{2,1,0:T(8,128)(2,1)S(1)}, bf16[1,128,1280]{2,1,0:T(8,128)(2,1)}, u32[]{:S(2)}) copy-start(bf16[1,128,1280]{2,1,0:T(8,128)(2,1)} %param.21) | copy-start | bytes 983044
  318.9 5.4 collective-permute-start.6
  324.3 1.5 collective-permute-start.7
  325.9 9.8 %collective-permute-start.8 = (bf16[128,1280]{1,0:T(8,128)(2,1)S(1)}, bf16[128,1280]{1,0:T(8,128)(2,1)S(1)}, u32[]{:S(2)}, u32[]{:S(2)}) collective-permute-start(bf16[128,1280]{1,0:T(8,128)(2,1)S(1)} %add_convert_fusion.5), channel_id=1, source_target_pairs={{0,1},{1,0},{2,3},{3,2},{4,5},{5,4},{6,7},{7,6},{8,9},{9,8},{10,11... | collective-permute-start | bytes 983048 | tf_op jit(solution)/shard_map/ppermute | solution.py:69
  336.3 2.2 collective-permute-start.9
  339.3 153.0 %all-gather.16.cloned.1.call-start = ((), (), s32[]{:S(2)}) async-start(), calls=%async_computation.9 | async-start | bytes 1769472 | tf_op jit(solution)/shard_map/all_gather | solution.py:51
  393.2 17.1 %collective-permute-start.10 = (bf16[1024,1280]{1,0:T(8,128)(2,1)}, bf16[1024,1280]{1,0:T(8,128)(2,1)}, u32[]{:S(2)}, u32[]{:S(2)}) collective-permute-start(bf16[1024,1280]{1,0:T(8,128)(2,1)} %all-gather.14.cloned.1.call-done), channel_id=1, source_target_pairs={{0,16},{16,0},{1,17},{17,1},{2,18},{18,2},{3,19},{19,3},{4,20},{20... | collective-permute-start | bytes 7864328 | tf_op jit(solution)/shard_map/ppermute | solution.py:45
  410.3 20.9 %copy-start.33 = (pred[8,80]{1,0:T(8,128)(4,1)}, pred[8,80]{1,0:T(8,128)(4,1)S(1)}, u32[]{:S(2)}) copy-start(pred[8,80]{1,0:T(8,128)(4,1)S(1)} %reshape.837) | copy-start | bytes 1924
  419.2 28.1 %collective-permute-start.11 = (bf16[1024,192]{0,1:T(8,128)(2,1)}, bf16[1024,192]{0,1:T(8,128)(2,1)}, u32[]{:S(2)}, u32[]{:S(2)}) collective-permute-start(bf16[1024,192]{0,1:T(8,128)(2,1)} %fusion.98), channel_id=1, source_target_pairs={{0,16},{16,0},{1,17},{17,1},{2,18},{18,2},{3,19},{19,3},{4,20},{20... | collective-permute-start | bytes 1179656 | tf_op jit(solution)/shard_map/ppermute | solution.py:45
  447.3 45.1 %collective-permute-start.16 = (bf16[8,80,2560]{2,1,0:T(8,128)(2,1)}, bf16[8,80,2560]{2,1,0:T(8,128)(2,1)}, u32[]{:S(2)}, u32[]{:S(2)}) collective-permute-start(bf16[8,80,2560]{2,1,0:T(8,128)(2,1)} %convolution_convert_fusion.1), channel_id=1, source_target_pairs={{0,16},{16,0},{1,17},{17,1},{2,18},{18,2},{3,19},{19,3},{4,20},{20... | collective-permute-start | bytes 9830408 | tf_op jit(solution)/shard_map/ppermute | solution.py:45
  492.3 3.6 collective-permute-start.12
  497.6 3.0 collective-permute-start.13
  499.1 20.5 %collective-permute-start.17 = (bf16[8,40,1280]{2,1,0:T(8,128)(2,1)}, bf16[8,40,1280]{2,1,0:T(8,128)(2,1)}, u32[]{:S(2)}, u32[]{:S(2)}) collective-permute-start(bf16[8,40,1280]{2,1,0:T(8,128)(2,1)} %broadcast_select_fusion.19), channel_id=1, source_target_pairs={{0,1},{1,0},{2,3},{3,2},{4,5},{5,4},{6,7},{7,6},{8,9},{9,8},{10,11... | collective-permute-start | bytes 2457608 | tf_op jit(solution)/shard_map/ppermute | solution.py:69
  503.9 18.1 %all-to-all-start.2 = ((bf16[8,64,320]{2,1,0:T(8,128)(2,1)}), bf16[8,64,320]{2,1,0:T(8,128)(2,1)}, u32[]{:S(2)}, u32[]{:S(2)}) async-start(bf16[8,64,320]{2,1,0:T(8,128)(2,1)} %copy.159), calls=%async_computation.2 | async-start | bytes 786432 | tf_op jit(solution)/shard_map/all_to_all | solution.py:109
  522.0 24.1 %all-to-all-start.3 = ((bf16[8,40,1280]{2,1,0:T(8,128)(2,1)}), bf16[8,40,1280]{2,1,0:T(8,128)(2,1)S(1)}, u32[]{:S(2)}, u32[]{:S(2)}) async-start(bf16[8,40,1280]{2,1,0:T(8,128)(2,1)} %add_convert_fusion.1), calls=%async_computation.3 | async-start | bytes 1638400 | tf_op jit(solution)/shard_map/all_to_all | solution.py:133
  525.5 130.6 %all-gather.18.cloned.1.call-start = ((), (), s32[]{:S(2)}) async-start(), calls=%async_computation.10 | async-start | bytes 1474560 | tf_op jit(solution)/shard_map/all_gather | solution.py:51
  526.3 23.7 %copy-start.31 = (s32[1024]{0:T(1024)}, s32[1024]{0:T(1024)S(1)}, u32[]{:S(2)}) copy-start(s32[1024]{0:T(1024)S(1)} %pad_clamp_fusion) | copy-start | bytes 12292
  528.5 17.5 %collective-permute-start.14 = (bf16[64,1280]{1,0:T(8,128)(2,1)S(1)}, bf16[64,1280]{1,0:T(8,128)(2,1)S(1)}, u32[]{:S(2)}, u32[]{:S(2)}) collective-permute-start(bf16[64,1280]{1,0:T(8,128)(2,1)S(1)} %broadcast_select_fusion.54), channel_id=1, source_target_pairs={{0,1},{1,0},{2,3},{3,2},{4,5},{5,4},{6,7},{7,6},{8,9},{9,8},{10,11... | collective-permute-start | bytes 491528 | tf_op jit(solution)/shard_map/ppermute | solution.py:69
  546.0 2.6 collective-permute-start.18
  546.1 2.5 collective-permute-start.15
  560.6 3.3 collective-permute-start.19
  564.0 10.1 %collective-permute-start.20 = (bf16[128,1280]{1,0:T(8,128)(2,1)S(1)}, bf16[128,1280]{1,0:T(8,128)(2,1)S(1)}, u32[]{:S(2)}, u32[]{:S(2)}) collective-permute-start(bf16[128,1280]{1,0:T(8,128)(2,1)S(1)} %bitcast_select_fusion.2), channel_id=1, source_target_pairs={{0,1},{1,0},{2,3},{3,2},{4,5},{5,4},{6,7},{7,6},{8,9},{9,8},{10,11... | collective-permute-start | bytes 983048 | tf_op jit(solution)/shard_map/ppermute | solution.py:69
  580.6 31.3 %copy-start.21 = (bf16[128,2,128]{0,2,1:T(8,128)(2,1)}, bf16[128,2,128]{0,2,1:T(8,128)(2,1)S(1)}, u32[]{:S(2)}) copy-start(bf16[128,2,128]{0,2,1:T(8,128)(2,1)S(1)} %pad_maximum_fusion.17) | copy-start | bytes 196612
  580.6 1.4 collective-permute-start.21
  609.8 1.9 collective-permute-start.22
  614.5 1.7 collective-permute-start.23
  617.0 44.0 %copy-start.43 = (bf16[1,320,1280]{2,1,0:T(8,128)(2,1)S(1)}, bf16[1,320,1280]{2,1,0:T(8,128)(2,1)}, u32[]{:S(2)}) copy-start(bf16[1,320,1280]{2,1,0:T(8,128)(2,1)} %param.28) | copy-start | bytes 2457604
  617.0 138.5 %all-gather.20.cloned.1.call-start = ((), (), s32[]{:S(2)}) async-start(), calls=%async_computation.11 | async-start | bytes 2949120 | tf_op jit(solution)/shard_map/all_gather | solution.py:51
  656.2 3.2 collective-permute-start.24
  662.2 2.2 collective-permute-start.25
  681.2 5.4 collective-permute-start.26
  686.6 1.5 collective-permute-start.27
  688.2 9.8 %collective-permute-start.28 = (bf16[128,1280]{1,0:T(8,128)(2,1)S(1)}, bf16[128,1280]{1,0:T(8,128)(2,1)S(1)}, u32[]{:S(2)}, u32[]{:S(2)}) collective-permute-start(bf16[128,1280]{1,0:T(8,128)(2,1)S(1)} %add_convert_fusion.3), channel_id=1, source_target_pairs={{0,1},{1,0},{2,3},{3,2},{4,5},{5,4},{6,7},{7,6},{8,9},{9,8},{10,11... | collective-permute-start | bytes 983048 | tf_op jit(solution)/shard_map/ppermute | solution.py:69
  698.5 2.2 collective-permute-start.29
  701.6 140.2 %all-gather.22.cloned.1.call-start = ((), (), s32[]{:S(2)}) async-start(), calls=%async_computation.12 | async-start | bytes 1769472 | tf_op jit(solution)/shard_map/all_gather | solution.py:51
  755.5 5.1 collective-permute-start.30
  769.0 27.9 %collective-permute-start.31 = (bf16[1024,192]{0,1:T(8,128)(2,1)}, bf16[1024,192]{0,1:T(8,128)(2,1)}, u32[]{:S(2)}, u32[]{:S(2)}) collective-permute-start(bf16[1024,192]{0,1:T(8,128)(2,1)} %fusion.97), channel_id=1, source_target_pairs={{0,16},{16,0},{1,17},{17,1},{2,18},{18,2},{3,19},{19,3},{4,20},{20... | collective-permute-start | bytes 1179656 | tf_op jit(solution)/shard_map/ppermute | solution.py:45
  796.5 45.3 %collective-permute-start.36 = (bf16[8,80,2560]{2,1,0:T(8,128)(2,1)}, bf16[8,80,2560]{2,1,0:T(8,128)(2,1)}, u32[]{:S(2)}, u32[]{:S(2)}) collective-permute-start(bf16[8,80,2560]{2,1,0:T(8,128)(2,1)} %convolution_convert_fusion), channel_id=1, source_target_pairs={{0,16},{16,0},{1,17},{17,1},{2,18},{18,2},{3,19},{19,3},{4,20},{20... | collective-permute-start | bytes 9830408 | tf_op jit(solution)/shard_map/ppermute | solution.py:45
  841.7 3.6 collective-permute-start.32
  847.0 3.0 collective-permute-start.33
  848.5 20.5 %collective-permute-start.37 = (bf16[8,40,1280]{2,1,0:T(8,128)(2,1)}, bf16[8,40,1280]{2,1,0:T(8,128)(2,1)}, u32[]{:S(2)}, u32[]{:S(2)}) collective-permute-start(bf16[8,40,1280]{2,1,0:T(8,128)(2,1)} %broadcast_select_fusion.18), channel_id=1, source_target_pairs={{0,1},{1,0},{2,3},{3,2},{4,5},{5,4},{6,7},{7,6},{8,9},{9,8},{10,11... | collective-permute-start | bytes 2457608 | tf_op jit(solution)/shard_map/ppermute | solution.py:69
  853.4 18.0 %all-to-all-start.5 = ((bf16[8,64,320]{2,1,0:T(8,128)(2,1)}), bf16[8,64,320]{2,1,0:T(8,128)(2,1)}, u32[]{:S(2)}, u32[]{:S(2)}) async-start(bf16[8,64,320]{2,1,0:T(8,128)(2,1)} %copy.176), calls=%async_computation.5 | async-start | bytes 786432 | tf_op jit(solution)/shard_map/all_to_all | solution.py:109
  871.4 24.4 %all-to-all-start.6 = ((bf16[8,40,1280]{2,1,0:T(8,128)(2,1)}), bf16[8,40,1280]{2,1,0:T(8,128)(2,1)S(1)}, u32[]{:S(2)}, u32[]{:S(2)}) async-start(bf16[8,40,1280]{2,1,0:T(8,128)(2,1)} %add_convert_fusion), calls=%async_computation.6 | async-start | bytes 1638400 | tf_op jit(solution)/shard_map/all_to_all | solution.py:133
  882.9 12.9 %collective-permute-start.34 = (bf16[64,1280]{1,0:T(8,128)(2,1)S(1)}, bf16[64,1280]{1,0:T(8,128)(2,1)S(1)}, u32[]{:S(2)}, u32[]{:S(2)}) collective-permute-start(bf16[64,1280]{1,0:T(8,128)(2,1)S(1)} %broadcast_select_fusion.52), channel_id=1, source_target_pairs={{0,1},{1,0},{2,3},{3,2},{4,5},{5,4},{6,7},{7,6},{8,9},{9,8},{10,11... | collective-permute-start | bytes 491528 | tf_op jit(solution)/shard_map/ppermute | solution.py:69
  895.8 2.6 collective-permute-start.38
  895.9 2.5 collective-permute-start.35
  (32 other events, 243.5 us)
Sparse Core Ops, SparseCore 0:
  10.2 180.5 all-gather.23
  254.9 39.0 all-gather.11
  339.4 53.7 all-gather.13
  448.4 43.8 all-gather.15
  617.1 38.9 all-gather.17
  701.7 53.7 all-gather.19
  798.9 42.7 all-gather.21

commit v10 on v9

--- a/solution.py
+++ b/solution.py
@@ -163,9 +163,27 @@
     router_full = lax.all_gather(router_weight[0], "tensor", axis=0, tiled=True)
     attn_gain_full = lax.all_gather(attn_gain[0], "tensor", axis=0, tiled=True)
     ffn_gain_full = lax.all_gather(ffn_gain[0], "tensor", axis=0, tiled=True)
-    qkv_full, shared_in_cols, choices_every, router_full, attn_gain_full, ffn_gain_full = (
-        lax.optimization_barrier(
-            (qkv_full, shared_in_cols, choices_every, router_full, attn_gain_full, ffn_gain_full)
+    w_in_local = w_in[0, 0]
+    w_down_local = w_down[0, 0]
+    (
+        qkv_full,
+        shared_in_cols,
+        choices_every,
+        router_full,
+        attn_gain_full,
+        ffn_gain_full,
+        w_in_local,
+        w_down_local,
+    ) = lax.optimization_barrier(
+        (
+            qkv_full,
+            shared_in_cols,
+            choices_every,
+            router_full,
+            attn_gain_full,
+            ffn_gain_full,
+            w_in_local,
+            w_down_local,
         )
     )
     model_width, kv_local, group_cols = qkv_full.shape
@@ -176,8 +194,6 @@
     top_count = expert_choice.shape[-1]
     capacity = 5 * tokens_dev * top_count // (4 * experts_count)
     slot_index = expert_id * tokens_dev + jnp.arange(tokens_dev, dtype=jnp.int32)
-    w_in_local = w_in[0, 0]
-    w_down_local = w_down[0, 0]
     carried_rows = jnp.zeros((tokens_dev, columns), jnp.bfloat16)
     states = jnp.zeros((micro_count, tokens_dev, columns), jnp.bfloat16)
     caches = jnp.zeros((micro_count, tokens_dev, 2, kv_local * head_width), jnp.bfloat16)
@@ -253,11 +269,11 @@
         shared_act = (
             jax.nn.silu(shared_hidden[:, :shared_cols]) * shared_hidden[:, shared_cols:]
         ).astype(jnp.bfloat16)
-        shared_act = expert_gather(shared_act, 1, 0)
+        shared_act = expert_gather(shared_act.T, 0, 1)
         shared_terms = lax.dot_general(
             shared_act,
             shared_down_local,
-            (((1,), (1,)), ((), ())),
+            (((0,), (1,)), ((), ())),
             preferred_element_type=jnp.float32,
         )
         shared_sum = terms_to_slots(shared_terms.astype(jnp.bfloat16), pair_active)

time: 929 us -> 926 us (level)
    unnamed x97 -> x99, local copies, waits for them, and re-layouts: 37.8 us -> 34.8 us
where the time goes in v10:
time: 926 us; the launch traced here: 916 us
  waiting for transfers between devices  441 us (48%)
  blocking collectives  196 us (21%)
  local copies, waits for them, and re-layouts  101 us (11%)
  other arithmetic  64.5 us (7%)
  matrix products  52.7 us (6%)
  starting transfers between devices  45.3 us (5%)
  between operations  15.8 us (2%)
    all_gather x6, waiting for transfers between devices, paired_gather(): lax.all_gather(jnp.where(active, first, second), 'expert', axis=axis, til...  273 us
    all_gather x1, blocking collectives, local(): lax.all_gather(expert_choice[0], 'expert', axis=0, tiled=False)  92.6 us
    ppermute x10, waiting for transfers between devices, swap_tensor(): lax.ppermute(value, 'tensor', [(source, (source + 1) % count) for source...  55.9 us
    all_gather x2, blocking collectives, paired_gather(): lax.all_gather(jnp.where(active, first, second), 'expert', axis=axis, til...  55.2 us
    all_gather x1, waiting for transfers between devices, local(): qkv_full = lax.all_gather(w_qkv[0], 'expert', axis=0, tiled=True)  46.3 us
    ppermute x28, waiting for transfers between devices, swap_cores(): lax.ppermute(value, 'section', [(source, (source + 1) % count) for source...  36.7 us
    unnamed x99, local copies, waits for them, and re-layouts  34.8 us
    all_to_all x2, blocking collectives, step(): lax.all_to_all(part.reshape(-1, part.shape[2]), 'expert', split_axis=0, c...  31 us
  transfers between devices with their start and end apart: 51, of which 36 were waited for; matrix products, arithmetic and copies ran while one was open for 13% of the time, Pallas kernels for 0%

profile of v10, /device:TPU:0, one launch (start us, length us, event | category | flops | bytes accessed | tf_op | source)
XLA Modules:
  0.0 916.1 jit_solution(2371832351229270840)
XLA Ops:
  7.9 8.5 copy.144
  16.5 7.4 all-to-all-start
  27.2 8.1 all-gather.2
  35.3 4.4 all-gather.3
  40.5 92.6 %all_gather.40 = s32[8,1,128,4]{2,3,1,0:T(4,128)S(1)} all-gather(s32[1,1,128,4]{2,3,1,0:T(4,128)S(1)} %copy-done.27), channel_id=1, replica_groups=mesh['section'=2,'expert'=8,'tensor'=2] {'expert'}, dimensions={0}, use_global_device_ids=true | all-gather | bytes 18432 | tf_op jit(solution)/shard_map/all_gather | solution.py:162
  133.1 4.7 all-gather.1
  141.9 2.7 all_to_all.70
  144.6 46.3 %all-gather.24.cloned.1.call-done = bf16[1,2560,2,896]{3,2,0,1:T(2,128)(2,1)} async-done(((bf16[1,320,2,896]{3,2,0,1:T(2,128)(2,1)}), bf16[1,2560,2,896]{3,2,0,1:T(2,128)(2,1)}) %all-gather.24.cloned.1.call-update) | async-done | bytes 9175056 | tf_op jit(solution)/shard_map/all_gather | solution.py:158
  190.8 8.7 copy.200
  199.5 12.7 %copy.147 = bf16[1792,2560]{1,0:T(8,128)(2,1)} copy(bf16[1792,2560]{0,1:T(8,128)(2,1)} %bitcast.235) | data formatting | bytes 18350080 | tf_op jit(solution)/shard_map/dot_general | solution.py:221
  212.3 6.2 fusion.105
  220.1 27.5 %all_gather.44 = bf16[1024,256]{0,1:T(8,128)(2,1)S(1)} all-gather(bf16[128,256]{0,1:T(8,128)(2,1)S(1)} %slice_select_fusion.13), channel_id=1, replica_groups=mesh['section'=2,'expert'=8,'tensor'=2] {'expert'}, dimensions={0}, use_global_device_ids=true | all-gather | bytes 589824 | tf_op jit(solution)/shard_map/all_gather | solution.py:51
  255.0 39.0 %all-gather.12.cloned.1.call-done = bf16[1024,640]{1,0:T(8,128)(2,1)} async-done(((bf16[128,640]{1,0:T(8,128)(2,1)}), bf16[1024,640]{1,0:T(8,128)(2,1)}) %all-gather.12.cloned.1.call-update) | async-done | bytes 1310736 | tf_op jit(solution)/shard_map/all_gather | solution.py:51
  294.0 3.2 collective-permute-done.4
  302.9 15.4 %all_to_all.92 = bf16[8,64,320]{2,1,0:T(8,128)(2,1)S(1)} all-to-all(bf16[8,64,320]{2,1,0:T(8,128)(2,1)S(1)} %copy.155), channel_id=1, replica_groups=mesh['section'=2,'expert'=8,'tensor'=2] {'expert'}, dimensions={0} | all-to-all | bytes 655360 | tf_op jit(solution)/shard_map/all_to_all | solution.py:109
  320.3 3.8 collective-permute-done.6
  327.4 8.3 collective-permute-done.8
  339.3 53.9 %all-gather.14.cloned.1.call-done = bf16[1024,1280]{1,0:T(8,128)(2,1)} async-done(((bf16[128,1280]{1,0:T(8,128)(2,1)}), bf16[1024,1280]{1,0:T(8,128)(2,1)}) %all-gather.14.cloned.1.call-update) | async-done | bytes 2621456 | tf_op jit(solution)/shard_map/all_gather | solution.py:51
  393.6 4.3 scatter_custom_fusion.1
  398.1 4.3 scatter_custom_fusion
  402.6 7.9 copy.201
  410.5 2.4 broadcast_select_fusion.7
  412.9 2.7 pad_maximum_fusion
  419.3 11.5 %gather_fusion = bf16[640,2560]{1,0:T(8,128)(2,1)} fusion(bf16[1024,2560]{1,0:T(8,128)(2,1)} %pad_maximum_fusion, s32[1024]{0:T(1024)S(1)} %pad_clamp_fusion.1), kind=kCustom, calls=%fused_computation | custom fusion | bytes 6556160 | tf_op jit(solution)/shard_map/gather | solution.py:313
  433.1 7.7 fusion.148
  440.8 4.7 convolution_convert_fusion.1
  446.6 44.1 %all-gather.16.cloned.1.call-done = bf16[1536,512]{1,0:T(8,128)(2,1)} async-done(((bf16[192,512]{1,0:T(8,128)(2,1)}), bf16[1536,512]{1,0:T(8,128)(2,1)}) %all-gather.16.cloned.1.call-update) | async-done | bytes 1572880 | tf_op jit(solution)/shard_map/all_gather | solution.py:51
  490.6 2.3 broadcast_select_fusion.3
  502.2 4.1 all-to-all-start.2
  506.3 11.6 %collective-permute-done.17 = bf16[8,40,1280]{2,1,0:T(8,128)(2,1)} collective-permute-done((bf16[8,40,1280]{2,1,0:T(8,128)(2,1)}, bf16[8,40,1280]{2,1,0:T(8,128)(2,1)}, u32[]{:S(2)}, u32[]{:S(2)}) %collective-permute-start.17) | collective-permute-done | bytes 819232 | tf_op jit(solution)/shard_map/ppermute | solution.py:69
  517.9 2.3 add_convert_fusion.1
  520.2 3.5 all-to-all-start.3
  528.3 16.0 %all-to-all-done.3 = bf16[8,40,1280]{2,1,0:T(8,128)(2,1)S(1)} async-done(((bf16[8,40,1280]{2,1,0:T(8,128)(2,1)}), bf16[8,40,1280]{2,1,0:T(8,128)(2,1)S(1)}, u32[]{:S(2)}, u32[]{:S(2)}) %all-to-all-start.3) | async-done | bytes 819232 | tf_op jit(solution)/shard_map/all_to_all | solution.py:133
  548.3 3.4 gather_fusion.1
  551.7 3.7 reshape.847
  555.4 3.4 multiply_reduce_fusion.1
  563.8 8.5 collective-permute-done.20
  572.6 6.2 fusion.102
  580.4 27.7 %all_gather.48 = bf16[1024,256]{0,1:T(8,128)(2,1)S(1)} all-gather(bf16[128,256]{0,1:T(8,128)(2,1)S(1)} %slice_select_fusion.12), channel_id=1, replica_groups=mesh['section'=2,'expert'=8,'tensor'=2] {'expert'}, dimensions={0}, use_global_device_ids=true | all-gather | bytes 589824 | tf_op jit(solution)/shard_map/all_gather | solution.py:51
  615.3 39.1 %all-gather.18.cloned.1.call-done = bf16[1024,640]{1,0:T(8,128)(2,1)} async-done(((bf16[128,640]{1,0:T(8,128)(2,1)}), bf16[1024,640]{1,0:T(8,128)(2,1)}) %all-gather.18.cloned.1.call-update) | async-done | bytes 1310736 | tf_op jit(solution)/shard_map/all_gather | solution.py:51
  654.4 3.2 collective-permute-done.24
  663.3 15.6 %all_to_all.93 = bf16[8,64,320]{2,1,0:T(8,128)(2,1)S(1)} all-to-all(bf16[8,64,320]{2,1,0:T(8,128)(2,1)S(1)} %copy.172), channel_id=1, replica_groups=mesh['section'=2,'expert'=8,'tensor'=2] {'expert'}, dimensions={0} | all-to-all | bytes 655360 | tf_op jit(solution)/shard_map/all_to_all | solution.py:109
  681.0 3.9 collective-permute-done.26
  688.0 8.3 collective-permute-done.28
  699.9 53.9 %all-gather.20.cloned.1.call-done = bf16[1024,1280]{1,0:T(8,128)(2,1)} async-done(((bf16[128,1280]{1,0:T(8,128)(2,1)}), bf16[1024,1280]{1,0:T(8,128)(2,1)}) %all-gather.20.cloned.1.call-update) | async-done | bytes 2621456 | tf_op jit(solution)/shard_map/all_gather | solution.py:51
  753.8 5.1 collective-permute-done.30
  758.9 2.4 broadcast_select_fusion.5
  761.3 2.2 fusion.146
  763.5 2.7 pad_maximum_fusion.1
  767.4 11.3 %gather_fusion.2 = bf16[640,2560]{1,0:T(8,128)(2,1)} fusion(bf16[1024,2560]{1,0:T(8,128)(2,1)} %pad_maximum_fusion.1, s32[1024]{0:T(1024)S(1)} %copy-done.31), kind=kCustom, calls=%fused_computation.2 | custom fusion | bytes 6556160 | tf_op jit(solution)/shard_map/gather | solution.py:313
  781.0 7.7 fusion.150
  788.7 4.7 convolution_convert_fusion
  795.8 42.9 %all-gather.22.cloned.1.call-done = bf16[1536,512]{1,0:T(8,128)(2,1)} async-done(((bf16[192,512]{1,0:T(8,128)(2,1)}), bf16[1536,512]{1,0:T(8,128)(2,1)}) %all-gather.22.cloned.1.call-update) | async-done | bytes 1572880 | tf_op jit(solution)/shard_map/all_gather | solution.py:51
  838.7 2.3 broadcast_select_fusion
  850.3 4.1 all-to-all-start.5
  854.4 11.6 %collective-permute-done.37 = bf16[8,40,1280]{2,1,0:T(8,128)(2,1)} collective-permute-done((bf16[8,40,1280]{2,1,0:T(8,128)(2,1)}, bf16[8,40,1280]{2,1,0:T(8,128)(2,1)}, u32[]{:S(2)}, u32[]{:S(2)}) %collective-permute-start.37) | collective-permute-done | bytes 819232 | tf_op jit(solution)/shard_map/ppermute | solution.py:69
  866.0 2.4 add_convert_fusion
  868.3 3.9 all-to-all-start.6
  875.2 2.5 broadcast_select_fusion.47
  881.4 11.4 %all-to-all-done.6 = bf16[8,40,1280]{2,1,0:T(8,128)(2,1)S(1)} async-done(((bf16[8,40,1280]{2,1,0:T(8,128)(2,1)}), bf16[8,40,1280]{2,1,0:T(8,128)(2,1)S(1)}, u32[]{:S(2)}, u32[]{:S(2)}) %all-to-all-start.6) | async-done | bytes 819232 | tf_op jit(solution)/shard_map/all_to_all | solution.py:133
  896.8 2.9 gather_fusion.3
  899.7 3.7 reshape.848
  903.3 3.4 multiply_reduce_fusion
  906.8 2.2 fusion.117
  (345 shorter events, 111.2 us)
Async XLA Ops:
  7.2 487.4 %copy-start = (bf16[1,320,1536]{2,1,0:T(8,128)(2,1)S(1)}, bf16[1,320,1536]{2,1,0:T(8,128)(2,1)}, u32[]{:S(2)}) copy-start(bf16[1,320,1536]{2,1,0:T(8,128)(2,1)} %param.30) | copy-start | bytes 2949124
  7.2 183.7 %all-gather.24.cloned.1.call-start = ((), (), s32[]{:S(2)}) async-start(), calls=%async_computation.13 | async-start | bytes 10321920 | tf_op jit(solution)/shard_map/all_gather | solution.py:158
  16.5 24.0 %copy-start.27 = (s32[1,1,128,4]{2,3,1,0:T(4,128)S(1)}, s32[1,1,128,4]{2,3,1,0:T(4,128)}, u32[]{:S(2)}) copy-start(s32[1,1,128,4]{2,3,1,0:T(4,128)} %param.24) | copy-start | bytes 6148
  16.5 116.6 %copy-start.29 = (f32[1,1280,8]{1,2,0:T(8,128)S(1)}, f32[1,1280,8]{1,2,0:T(8,128)}, u32[]{:S(2)}) copy-start(f32[1,1280,8]{1,2,0:T(8,128)} %param.31) | copy-start | bytes 122884
  16.5 121.4 %copy-start.38 = (s32[1,128]{1,0:T(1,128)S(1)}, s32[1,128]{1,0:T(1,128)}, u32[]{:S(2)}) copy-start(s32[1,128]{1,0:T(1,128)} %param.22) | copy-start | bytes 1540
  16.5 123.7 %all-to-all-start = ((bf16[320,2,1536]{0,1,2:T(2,128)(2,1)}), bf16[320,2,1536]{0,1,2:T(2,128)(2,1)S(1)}, u32[]{:S(2)}, u32[]{:S(2)}) async-start(bf16[320,2,1536]{0,1,2:T(2,128)(2,1)} %bitcast.238), calls=%async_computation | async-start | bytes 4718592 | tf_op jit(solution)/shard_map/all_to_all | solution.py:161
  23.9 270.1 %all-gather.12.cloned.1.call-start = ((), (), s32[]{:S(2)}) async-start(), calls=%async_computation.7 | async-start | bytes 1474560 | tf_op jit(solution)/shard_map/all_gather | solution.py:51
  25.7 112.5 %collective-permute-start = (bf16[128,1280]{1,0:T(8,128)(2,1)}, bf16[128,1280]{1,0:T(8,128)(2,1)}, u32[]{:S(2)}, u32[]{:S(2)}) collective-permute-start(bf16[128,1280]{1,0:T(8,128)(2,1)} %bitcast_select_fusion.3), channel_id=1, source_target_pairs={{0,1},{1,0},{2,3},{3,2},{4,5},{5,4},{6,7},{7,6},{8,9},{9,8},{10,11... | collective-permute-start | bytes 983048 | tf_op jit(solution)/shard_map/ppermute | solution.py:69
  39.7 296.3 %copy-start.25 = (f32[2560]{0:T(1024)}, f32[2560]{0:T(1024)S(1)}, u32[]{:S(2)}) copy-start(f32[2560]{0:T(1024)S(1)} %reduce.34) | copy-start | bytes 30724
  218.6 29.0 %copy-start.20 = (bf16[128,2,128]{0,2,1:T(8,128)(2,1)}, bf16[128,2,128]{0,2,1:T(8,128)(2,1)S(1)}, u32[]{:S(2)}) copy-start(bf16[128,2,128]{0,2,1:T(8,128)(2,1)S(1)} %pad_maximum_fusion.16) | copy-start | bytes 196612
  218.6 1.4 collective-permute-start.1
  247.6 1.9 collective-permute-start.2
  252.3 1.7 collective-permute-start.3
  254.8 44.0 %copy-start.43 = (bf16[1,320,1280]{2,1,0:T(8,128)(2,1)S(1)}, bf16[1,320,1280]{2,1,0:T(8,128)(2,1)}, u32[]{:S(2)}) copy-start(bf16[1,320,1280]{2,1,0:T(8,128)(2,1)} %param.28) | copy-start | bytes 2457604
  254.8 138.4 %all-gather.14.cloned.1.call-start = ((), (), s32[]{:S(2)}) async-start(), calls=%async_computation.8 | async-start | bytes 2949120 | tf_op jit(solution)/shard_map/all_gather | solution.py:51
  294.0 3.2 collective-permute-start.4
  300.0 2.2 collective-permute-start.5
  318.8 5.4 collective-permute-start.6
  324.3 1.5 collective-permute-start.7
  325.9 9.8 %collective-permute-start.8 = (bf16[128,1280]{1,0:T(8,128)(2,1)S(1)}, bf16[128,1280]{1,0:T(8,128)(2,1)S(1)}, u32[]{:S(2)}, u32[]{:S(2)}) collective-permute-start(bf16[128,1280]{1,0:T(8,128)(2,1)S(1)} %add_convert_fusion.5), channel_id=1, source_target_pairs={{0,1},{1,0},{2,3},{3,2},{4,5},{5,4},{6,7},{7,6},{8,9},{9,8},{10,11... | collective-permute-start | bytes 983048 | tf_op jit(solution)/shard_map/ppermute | solution.py:69
  335.8 57.6 %copy-start.40 = (s32[2]{0:T(128)S(1)}, s32[2]{0:T(128)}, u32[]{:S(2)}) copy-start(s32[2]{0:T(128)} %constant.167) | copy-start | bytes 28
  335.8 57.7 %copy-start.39 = (s32[2]{0:T(128)S(1)}, s32[2]{0:T(128)}, u32[]{:S(2)}) copy-start(s32[2]{0:T(128)} %constant.170) | copy-start | bytes 28
  336.3 2.2 collective-permute-start.9
  339.3 151.3 %all-gather.16.cloned.1.call-start = ((), (), s32[]{:S(2)}) async-start(), calls=%async_computation.9 | async-start | bytes 1769472 | tf_op jit(solution)/shard_map/all_gather | solution.py:51
  393.2 17.2 %collective-permute-start.10 = (bf16[1024,1280]{1,0:T(8,128)(2,1)}, bf16[1024,1280]{1,0:T(8,128)(2,1)}, u32[]{:S(2)}, u32[]{:S(2)}) collective-permute-start(bf16[1024,1280]{1,0:T(8,128)(2,1)} %all-gather.14.cloned.1.call-done), channel_id=1, source_target_pairs={{0,16},{16,0},{1,17},{17,1},{2,18},{18,2},{3,19},{19,3},{4,20},{20... | collective-permute-start | bytes 7864328 | tf_op jit(solution)/shard_map/ppermute | solution.py:45
  402.5 28.3 %copy-start.34 = (pred[8,80]{1,0:T(8,128)(4,1)}, pred[8,80]{1,0:T(8,128)(4,1)S(1)}, u32[]{:S(2)}) copy-start(pred[8,80]{1,0:T(8,128)(4,1)S(1)} %reshape.842) | copy-start | bytes 1924
  418.8 26.7 %collective-permute-start.11 = (bf16[192,1024]{1,0:T(8,128)(2,1)}, bf16[192,1024]{1,0:T(8,128)(2,1)}, u32[]{:S(2)}, u32[]{:S(2)}) collective-permute-start(bf16[192,1024]{1,0:T(8,128)(2,1)} %fusion.115), channel_id=1, source_target_pairs={{0,16},{16,0},{1,17},{17,1},{2,18},{18,2},{3,19},{19,3},{4,20},{20... | collective-permute-start | bytes 1179656 | tf_op jit(solution)/shard_map/ppermute | solution.py:45
  445.6 45.1 %collective-permute-start.16 = (bf16[8,80,2560]{2,1,0:T(8,128)(2,1)}, bf16[8,80,2560]{2,1,0:T(8,128)(2,1)}, u32[]{:S(2)}, u32[]{:S(2)}) collective-permute-start(bf16[8,80,2560]{2,1,0:T(8,128)(2,1)} %bitcast.45), channel_id=1, source_target_pairs={{0,16},{16,0},{1,17},{17,1},{2,18},{18,2},{3,19},{19,3},{4,20},{20... | collective-permute-start | bytes 9830408 | tf_op jit(solution)/shard_map/ppermute | solution.py:45
  490.6 3.6 collective-permute-start.12
  495.8 3.0 collective-permute-start.13
  497.4 20.5 %collective-permute-start.17 = (bf16[8,40,1280]{2,1,0:T(8,128)(2,1)}, bf16[8,40,1280]{2,1,0:T(8,128)(2,1)}, u32[]{:S(2)}, u32[]{:S(2)}) collective-permute-start(bf16[8,40,1280]{2,1,0:T(8,128)(2,1)} %broadcast_select_fusion.19), channel_id=1, source_target_pairs={{0,1},{1,0},{2,3},{3,2},{4,5},{5,4},{6,7},{7,6},{8,9},{9,8},{10,11... | collective-permute-start | bytes 2457608 | tf_op jit(solution)/shard_map/ppermute | solution.py:69
  502.2 18.0 %all-to-all-start.2 = ((bf16[8,64,320]{2,1,0:T(8,128)(2,1)}), bf16[8,64,320]{2,1,0:T(8,128)(2,1)}, u32[]{:S(2)}, u32[]{:S(2)}) async-start(bf16[8,64,320]{2,1,0:T(8,128)(2,1)} %copy.159), calls=%async_computation.2 | async-start | bytes 786432 | tf_op jit(solution)/shard_map/all_to_all | solution.py:109
  520.2 24.1 %all-to-all-start.3 = ((bf16[8,40,1280]{2,1,0:T(8,128)(2,1)}), bf16[8,40,1280]{2,1,0:T(8,128)(2,1)S(1)}, u32[]{:S(2)}, u32[]{:S(2)}) async-start(bf16[8,40,1280]{2,1,0:T(8,128)(2,1)} %add_convert_fusion.1), calls=%async_computation.3 | async-start | bytes 1638400 | tf_op jit(solution)/shard_map/all_to_all | solution.py:133
  523.8 130.7 %all-gather.18.cloned.1.call-start = ((), (), s32[]{:S(2)}) async-start(), calls=%async_computation.10 | async-start | bytes 1474560 | tf_op jit(solution)/shard_map/all_gather | solution.py:51
  524.6 23.7 %copy-start.32 = (s32[1024]{0:T(1024)}, s32[1024]{0:T(1024)S(1)}, u32[]{:S(2)}) copy-start(s32[1024]{0:T(1024)S(1)} %pad_clamp_fusion) | copy-start | bytes 12292
  526.8 17.5 %collective-permute-start.14 = (bf16[64,1280]{1,0:T(8,128)(2,1)S(1)}, bf16[64,1280]{1,0:T(8,128)(2,1)S(1)}, u32[]{:S(2)}, u32[]{:S(2)}) collective-permute-start(bf16[64,1280]{1,0:T(8,128)(2,1)S(1)} %broadcast_select_fusion.54), channel_id=1, source_target_pairs={{0,1},{1,0},{2,3},{3,2},{4,5},{5,4},{6,7},{7,6},{8,9},{9,8},{10,11... | collective-permute-start | bytes 491528 | tf_op jit(solution)/shard_map/ppermute | solution.py:69
  544.3 2.6 collective-permute-start.18
  544.4 2.5 collective-permute-start.15
  558.9 3.3 collective-permute-start.19
  562.3 10.1 %collective-permute-start.20 = (bf16[128,1280]{1,0:T(8,128)(2,1)S(1)}, bf16[128,1280]{1,0:T(8,128)(2,1)S(1)}, u32[]{:S(2)}, u32[]{:S(2)}) collective-permute-start(bf16[128,1280]{1,0:T(8,128)(2,1)S(1)} %bitcast_select_fusion.2), channel_id=1, source_target_pairs={{0,1},{1,0},{2,3},{3,2},{4,5},{5,4},{6,7},{7,6},{8,9},{9,8},{10,11... | collective-permute-start | bytes 983048 | tf_op jit(solution)/shard_map/ppermute | solution.py:69
  578.9 31.3 %copy-start.22 = (bf16[128,2,128]{0,2,1:T(8,128)(2,1)}, bf16[128,2,128]{0,2,1:T(8,128)(2,1)S(1)}, u32[]{:S(2)}) copy-start(bf16[128,2,128]{0,2,1:T(8,128)(2,1)S(1)} %pad_maximum_fusion.17) | copy-start | bytes 196612
  578.9 1.4 collective-permute-start.21
  608.1 1.9 collective-permute-start.22
  612.8 1.7 collective-permute-start.23
  615.3 44.0 %copy-start.44 = (bf16[1,320,1280]{2,1,0:T(8,128)(2,1)S(1)}, bf16[1,320,1280]{2,1,0:T(8,128)(2,1)}, u32[]{:S(2)}) copy-start(bf16[1,320,1280]{2,1,0:T(8,128)(2,1)} %param.28) | copy-start | bytes 2457604
  615.3 138.5 %all-gather.20.cloned.1.call-start = ((), (), s32[]{:S(2)}) async-start(), calls=%async_computation.11 | async-start | bytes 2949120 | tf_op jit(solution)/shard_map/all_gather | solution.py:51
  654.4 3.2 collective-permute-start.24
  660.4 2.2 collective-permute-start.25
  679.4 5.4 collective-permute-start.26
  684.9 1.5 collective-permute-start.27
  686.5 9.8 %collective-permute-start.28 = (bf16[128,1280]{1,0:T(8,128)(2,1)S(1)}, bf16[128,1280]{1,0:T(8,128)(2,1)S(1)}, u32[]{:S(2)}, u32[]{:S(2)}) collective-permute-start(bf16[128,1280]{1,0:T(8,128)(2,1)S(1)} %add_convert_fusion.3), channel_id=1, source_target_pairs={{0,1},{1,0},{2,3},{3,2},{4,5},{5,4},{6,7},{7,6},{8,9},{9,8},{10,11... | collective-permute-start | bytes 983048 | tf_op jit(solution)/shard_map/ppermute | solution.py:69
  696.8 2.2 collective-permute-start.29
  699.8 138.8 %all-gather.22.cloned.1.call-start = ((), (), s32[]{:S(2)}) async-start(), calls=%async_computation.12 | async-start | bytes 1769472 | tf_op jit(solution)/shard_map/all_gather | solution.py:51
  753.8 5.1 collective-permute-start.30
  767.2 26.6 %collective-permute-start.31 = (bf16[192,1024]{1,0:T(8,128)(2,1)}, bf16[192,1024]{1,0:T(8,128)(2,1)}, u32[]{:S(2)}, u32[]{:S(2)}) collective-permute-start(bf16[192,1024]{1,0:T(8,128)(2,1)} %fusion.116), channel_id=1, source_target_pairs={{0,16},{16,0},{1,17},{17,1},{2,18},{18,2},{3,19},{19,3},{4,20},{20... | collective-permute-start | bytes 1179656 | tf_op jit(solution)/shard_map/ppermute | solution.py:45
  793.4 45.3 %collective-permute-start.36 = (bf16[8,80,2560]{2,1,0:T(8,128)(2,1)}, bf16[8,80,2560]{2,1,0:T(8,128)(2,1)}, u32[]{:S(2)}, u32[]{:S(2)}) collective-permute-start(bf16[8,80,2560]{2,1,0:T(8,128)(2,1)} %bitcast.71), channel_id=1, source_target_pairs={{0,16},{16,0},{1,17},{17,1},{2,18},{18,2},{3,19},{19,3},{4,20},{20... | collective-permute-start | bytes 9830408 | tf_op jit(solution)/shard_map/ppermute | solution.py:45
  838.7 3.6 collective-permute-start.32
  843.9 3.1 collective-permute-start.33
  845.5 20.5 %collective-permute-start.37 = (bf16[8,40,1280]{2,1,0:T(8,128)(2,1)}, bf16[8,40,1280]{2,1,0:T(8,128)(2,1)}, u32[]{:S(2)}, u32[]{:S(2)}) collective-permute-start(bf16[8,40,1280]{2,1,0:T(8,128)(2,1)} %broadcast_select_fusion.18), channel_id=1, source_target_pairs={{0,1},{1,0},{2,3},{3,2},{4,5},{5,4},{6,7},{7,6},{8,9},{9,8},{10,11... | collective-permute-start | bytes 2457608 | tf_op jit(solution)/shard_map/ppermute | solution.py:69
  850.3 18.1 %all-to-all-start.5 = ((bf16[8,64,320]{2,1,0:T(8,128)(2,1)}), bf16[8,64,320]{2,1,0:T(8,128)(2,1)}, u32[]{:S(2)}, u32[]{:S(2)}) async-start(bf16[8,64,320]{2,1,0:T(8,128)(2,1)} %copy.176), calls=%async_computation.5 | async-start | bytes 786432 | tf_op jit(solution)/shard_map/all_to_all | solution.py:109
  868.3 24.4 %all-to-all-start.6 = ((bf16[8,40,1280]{2,1,0:T(8,128)(2,1)}), bf16[8,40,1280]{2,1,0:T(8,128)(2,1)S(1)}, u32[]{:S(2)}, u32[]{:S(2)}) async-start(bf16[8,40,1280]{2,1,0:T(8,128)(2,1)} %add_convert_fusion), calls=%async_computation.6 | async-start | bytes 1638400 | tf_op jit(solution)/shard_map/all_to_all | solution.py:133
  879.8 12.9 %collective-permute-start.34 = (bf16[64,1280]{1,0:T(8,128)(2,1)S(1)}, bf16[64,1280]{1,0:T(8,128)(2,1)S(1)}, u32[]{:S(2)}, u32[]{:S(2)}) collective-permute-start(bf16[64,1280]{1,0:T(8,128)(2,1)S(1)} %broadcast_select_fusion.52), channel_id=1, source_target_pairs={{0,1},{1,0},{2,3},{3,2},{4,5},{5,4},{6,7},{7,6},{8,9},{9,8},{10,11... | collective-permute-start | bytes 491528 | tf_op jit(solution)/shard_map/ppermute | solution.py:69
  892.8 2.6 collective-permute-start.38
  892.8 2.5 collective-permute-start.35
  (33 other events, 292.5 us)
Sparse Core Ops, SparseCore 0:
  10.2 180.5 all-gather.23
  254.9 39.0 all-gather.11
  339.4 53.7 all-gather.13
  446.7 43.8 all-gather.15
  615.4 38.9 all-gather.17
  700.0 53.7 all-gather.19
  795.9 42.7 all-gather.21

commit v11 on v10

--- a/solution.py
+++ b/solution.py
@@ -99,6 +99,16 @@
     return jnp.concatenate(
         [jnp.where(active, done, theirs), jnp.where(active, theirs, done)], axis=out_axis
     )
+
+
+def layer_weights(shard, owner):
+    count = lax.axis_size("expert")
+
+    def step(part):
+        return lax.all_gather(part, "expert", axis=0, tiled=False)
+
+    stacked = paired_apply(step, shard, 0, 1, owner)
+    return stacked.reshape((count * shard.shape[0],) + shard.shape[1:])
 
 
 def terms_to_slots(terms, active):
@@ -155,7 +165,13 @@
     experts_count = lax.axis_size("expert")
     expert_id = lax.axis_index("expert")
     micro_count, tokens_dev, columns = hidden_in.shape
-    qkv_full = lax.all_gather(w_qkv[0], "expert", axis=0, tiled=True)
+    micro_count = hidden_in.shape[0]
+    relay_pairs = micro_count == 1 and sections == 2
+    qkv_own = w_qkv[0]
+    if relay_pairs:
+        qkv_full = layer_weights(qkv_own, section_id == 0)
+    else:
+        qkv_full = lax.all_gather(qkv_own, "expert", axis=0, tiled=True)
     out_local = w_out[0]
     shared_down_local = w_shared_down[0]
     shared_in_cols = lax.all_to_all(w_shared_in[0], "expert", split_axis=2, concat_axis=0, tiled=True)
@@ -187,6 +203,7 @@
         )
     )
     model_width, kv_local, group_cols = qkv_full.shape
+    qkv_layers = [qkv_full]
     shared_cols = shared_in_cols.shape[2]
     head_width = HD
     group = group_cols // head_width - 2
@@ -219,7 +236,9 @@
         positions = jnp.where(segments >= 0, slot_index - first_slot, 0).astype(jnp.float32)
         normed_full = norm_full_rows(incoming, attn_gain_full)
         projected = jnp.dot(
-            normed_full, qkv_full.reshape(model_width, -1), preferred_element_type=jnp.float32
+            normed_full,
+            qkv_layers[min(tick_index, len(qkv_layers) - 1)].reshape(model_width, -1),
+            preferred_element_type=jnp.float32,
         )
         projected = projected.reshape(tokens_dev, kv_local, group + 2, head_width)
         queries = rotate_heads(projected[:, :, :group], positions).astype(jnp.bfloat16)
@@ -270,6 +289,9 @@
             jax.nn.silu(shared_hidden[:, :shared_cols]) * shared_hidden[:, shared_cols:]
         ).astype(jnp.bfloat16)
         shared_act = expert_gather(shared_act.T, 0, 1)
+        if relay_pairs and tick_index == 0:
+            qkv_later, _ = lax.optimization_barrier((qkv_own, shared_act))
+            qkv_layers.append(layer_weights(qkv_later, section_id == 1))
         shared_terms = lax.dot_general(
             shared_act,
             shared_down_local,

time: 926 us -> 1020 us (1.10)
  other arithmetic: 64.5 us -> 136 us
  waiting for transfers between devices: 441 us -> 480 us
  blocking collectives: 196 us -> 161 us
  local copies, waits for them, and re-layouts: 101 us -> 123 us
    all_gather x1 -> x2, waiting for transfers between devices: 46.3 us -> 131 us  [step(): return lax.all_gather(part, 'expert', axis=0, tiled=False)]
    concatenate x4 -> x6, other arithmetic: 0.26 us -> 58.5 us  [paired_apply(): jnp.concatenate([jnp.where(active, done, theirs), jnp.where(active, their...]
    all_gather x6, waiting for transfers between devices: 273 us -> 228 us  [paired_gather(): lax.all_gather(jnp.where(active, first, second), 'expert', axis=axis, til...]
    all_gather x1, blocking collectives: 92.6 us -> 55.7 us  [local(): lax.all_gather(expert_choice[0], 'expert', axis=0, tiled=False)]
    optimization_barrier x0 -> x1, local copies, waits for them, and re-layouts: none -> 23.2 us  [local(): lax.optimization_barrier((qkv_full, shared_in_cols, choices_every, router...]
    ppermute x10, waiting for transfers between devices: 55.9 us -> 35.9 us  [swap_tensor(): lax.ppermute(value, 'tensor', [(source, (source + 1) % count) for source...]
    ppermute x28 -> x32, waiting for transfers between devices: 36.7 us -> 55.8 us  [swap_cores(): lax.ppermute(value, 'section', [(source, (source + 1) % count) for source...]
    unnamed x99 -> x109, local copies, waits for them, and re-layouts: 34.8 us -> 33.9 us
  transfers between devices with their start and end apart: 51 -> 56, of which waited for: 36 -> 37; matrix products, arithmetic and copies ran while one was open for 13% -> 16% of each run, Pallas kernels for 0% -> 0%
where the time goes in v11:
time: 1020 us; the launch traced here: 1010 us
  waiting for transfers between devices  480 us (47%)
  blocking collectives  161 us (16%)
  other arithmetic  136 us (13%)
  local copies, waits for them, and re-layouts  123 us (12%)
  matrix products  52.7 us (5%)
  starting transfers between devices  42.3 us (4%)
  between operations  15.9 us (2%)
    all_gather x6, waiting for transfers between devices, paired_gather(): lax.all_gather(jnp.where(active, first, second), 'expert', axis=axis, til...  228 us
    all_gather x2, waiting for transfers between devices, step(): return lax.all_gather(part, 'expert', axis=0, tiled=False)  131 us
    concatenate x6, other arithmetic, paired_apply(): jnp.concatenate([jnp.where(active, done, theirs), jnp.where(active, their...  58.5 us
    all_gather x2, blocking collectives, paired_gather(): lax.all_gather(jnp.where(active, first, second), 'expert', axis=axis, til...  56.1 us
    ppermute x32, waiting for transfers between devices, swap_cores(): lax.ppermute(value, 'section', [(source, (source + 1) % count) for source...  55.8 us
    all_gather x1, blocking collectives, local(): lax.all_gather(expert_choice[0], 'expert', axis=0, tiled=False)  55.7 us
    ppermute x10, waiting for transfers between devices, swap_tensor(): lax.ppermute(value, 'tensor', [(source, (source + 1) % count) for source...  35.9 us
    unnamed x109, local copies, waits for them, and re-layouts  33.9 us
  transfers between devices with their start and end apart: 56, of which 37 were waited for; matrix products, arithmetic and copies ran while one was open for 16% of the time, Pallas kernels for 0%

profile of v11, /device:TPU:0, one launch (start us, length us, event | category | flops | bytes accessed | tf_op | source)
XLA Modules:
  0.0 1010.0 jit_solution(6363471427203491483)
XLA Ops:
  7.7 2.8 collective-permute-done.1
  14.4 81.2 %all-gather.26.cloned.1.call-done = bf16[1280,2,896]{2,1,0:T(2,128)(2,1)} async-done(((bf16[160,2,896]{2,1,0:T(2,128)(2,1)}), bf16[1280,2,896]{2,1,0:T(2,128)(2,1)}) %all-gather.26.cloned.1.call-update) | async-done | bytes 4587536 | tf_op jit(solution)/shard_map/all_gather | solution.py:108
  95.6 6.1 copy.145
  101.7 3.8 all-to-all-start
  108.7 9.0 all-gather.2
  117.8 4.4 all-gather.3
  123.0 55.7 %all_gather.50 = s32[8,1,128,4]{2,3,1,0:T(4,128)S(1)} all-gather(s32[1,1,128,4]{2,3,1,0:T(4,128)S(1)} %copy-done.32), channel_id=1, replica_groups=mesh['section'=2,'expert'=8,'tensor'=2] {'expert'}, dimensions={0}, use_global_device_ids=true | all-gather | bytes 18432 | tf_op jit(solution)/shard_map/all_gather | solution.py:178
  178.7 4.7 all-gather.1
  187.4 2.7 all_to_all.70
  190.2 4.5 broadcast_select_fusion.3
  194.7 29.2 %pad_maximum_fusion = bf16[8,320,2,896]{3,2,1,0:T(2,128)(2,1)} fusion(bf16[8,160,2,896]{3,2,1,0:T(2,128)(2,1)S(1)} %bitcast.261, bf16[8,160,2,896]{3,2,1,0:T(2,128)(2,1)S(1)} %bitcast.260), kind=kLoop, calls=%fused_computation.6 | loop fusion | flops 4587520 | bytes 18350080 | tf_op jit(solution)/shard_map/concatenate | solution.py:99
  223.9 23.2 %copy.148 = bf16[2560,2,896]{0,2,1:T(8,128)(2,1)} copy(bf16[2560,2,896]{2,1,0:T(2,128)(2,1)} %bitcast.255) | data formatting | bytes 18350080 | tf_op jit(solution)/shard_map/optimization_barrier | solution.py:193
  247.1 6.2 fusion.96
  254.9 28.1 %all_gather.54 = bf16[1024,256]{0,1:T(8,128)(2,1)S(1)} all-gather(bf16[128,256]{0,1:T(8,128)(2,1)S(1)} %slice_select_fusion.13), channel_id=1, replica_groups=mesh['section'=2,'expert'=8,'tensor'=2] {'expert'}, dimensions={0}, use_global_device_ids=true | all-gather | bytes 589824 | tf_op jit(solution)/shard_map/all_gather | solution.py:51
  290.2 39.1 %all-gather.14.cloned.1.call-done = bf16[1024,640]{1,0:T(8,128)(2,1)} async-done(((bf16[128,640]{1,0:T(8,128)(2,1)}), bf16[1024,640]{1,0:T(8,128)(2,1)}) %all-gather.14.cloned.1.call-update) | async-done | bytes 1310736 | tf_op jit(solution)/shard_map/all_gather | solution.py:51
  329.3 3.2 collective-permute-done.6
  338.2 15.4 %all_to_all.92 = bf16[8,64,320]{2,1,0:T(8,128)(2,1)S(1)} all-to-all(bf16[8,64,320]{2,1,0:T(8,128)(2,1)S(1)} %copy.156), channel_id=1, replica_groups=mesh['section'=2,'expert'=8,'tensor'=2] {'expert'}, dimensions={0} | all-to-all | bytes 655360 | tf_op jit(solution)/shard_map/all_to_all | solution.py:119
  355.7 3.9 collective-permute-done.8
  362.8 8.3 collective-permute-done.10
  374.7 53.9 %all-gather.16.cloned.1.call-done = bf16[1024,1280]{1,0:T(8,128)(2,1)} async-done(((bf16[128,1280]{1,0:T(8,128)(2,1)}), bf16[1024,1280]{1,0:T(8,128)(2,1)}) %all-gather.16.cloned.1.call-update) | async-done | bytes 2621456 | tf_op jit(solution)/shard_map/all_gather | solution.py:51
  428.5 5.1 collective-permute-done.12
  441.6 2.8 collective-permute-done.23
  447.7 4.3 scatter_custom_fusion.1
  452.2 4.5 scatter_custom_fusion
  456.9 8.0 copy.202
  464.9 2.8 pad_maximum_fusion.2
  467.6 11.3 %gather_fusion = bf16[640,2560]{1,0:T(8,128)(2,1)} fusion(bf16[1024,2560]{1,0:T(8,128)(2,1)} %pad_maximum_fusion.2, s32[1024]{0:T(1024)S(1)} %pad_clamp_fusion.1), kind=kCustom, calls=%fused_computation | custom fusion | bytes 6556160 | tf_op jit(solution)/shard_map/gather | solution.py:335
  481.1 7.7 fusion.138
  488.9 4.7 convolution_convert_fusion.1
  494.1 7.9 collective-permute-done.18
  513.3 4.1 all-to-all-start.2
  517.4 49.6 %all-gather.28.cloned.1.call-done = bf16[1280,2,896]{2,1,0:T(2,128)(2,1)} async-done(((bf16[160,2,896]{2,1,0:T(2,128)(2,1)}), bf16[1280,2,896]{2,1,0:T(2,128)(2,1)}) %all-gather.28.cloned.1.call-update) | async-done | bytes 4587536 | tf_op jit(solution)/shard_map/all_gather | solution.py:108
  569.4 3.6 all-to-all-start.3
  577.4 17.3 %all-to-all-done.3 = bf16[8,40,1280]{2,1,0:T(8,128)(2,1)S(1)} async-done(((bf16[8,40,1280]{2,1,0:T(8,128)(2,1)}), bf16[8,40,1280]{2,1,0:T(8,128)(2,1)S(1)}, u32[]{:S(2)}, u32[]{:S(2)}) %all-to-all-start.3) | async-done | bytes 819232 | tf_op jit(solution)/shard_map/all_to_all | solution.py:143
  598.7 2.9 gather_fusion.1
  601.6 3.7 reshape.850
  605.3 3.4 multiply_reduce_fusion.1
  608.8 2.8 collective-permute-start.21
  611.6 4.6 broadcast_select_fusion.1
  617.4 29.1 %pad_maximum_fusion.1 = bf16[8,320,2,896]{3,2,1,0:T(2,128)(2,1)} fusion(bf16[8,160,2,896]{3,2,1,0:T(2,128)(2,1)S(1)} %bitcast.259, bf16[8,160,2,896]{3,2,1,0:T(2,128)(2,1)S(1)} %bitcast.258), kind=kLoop, calls=%fused_computation.7 | loop fusion | flops 4587520 | bytes 18350080 | tf_op jit(solution)/shard_map/concatenate | solution.py:99
  646.5 8.8 copy.203
  655.2 12.7 %copy.165 = bf16[1792,2560]{1,0:T(8,128)(2,1)} copy(bf16[1792,2560]{0,1:T(8,128)(2,1)} %bitcast.257) | data formatting | bytes 18350080 | tf_op jit(solution)/shard_map/dot_general | solution.py:238
  668.2 6.2 fusion.93
  676.0 28.0 %all_gather.60 = bf16[1024,256]{0,1:T(8,128)(2,1)S(1)} all-gather(bf16[128,256]{0,1:T(8,128)(2,1)S(1)} %slice_select_fusion.12), channel_id=1, replica_groups=mesh['section'=2,'expert'=8,'tensor'=2] {'expert'}, dimensions={0}, use_global_device_ids=true | all-gather | bytes 589824 | tf_op jit(solution)/shard_map/all_gather | solution.py:51
  711.3 38.6 %all-gather.20.cloned.1.call-done = bf16[1024,640]{1,0:T(8,128)(2,1)} async-done(((bf16[128,640]{1,0:T(8,128)(2,1)}), bf16[1024,640]{1,0:T(8,128)(2,1)}) %all-gather.20.cloned.1.call-update) | async-done | bytes 1310736 | tf_op jit(solution)/shard_map/all_gather | solution.py:51
  750.0 3.2 collective-permute-done.28
  758.8 15.4 %all_to_all.93 = bf16[8,64,320]{2,1,0:T(8,128)(2,1)S(1)} all-to-all(bf16[8,64,320]{2,1,0:T(8,128)(2,1)S(1)} %copy.174), channel_id=1, replica_groups=mesh['section'=2,'expert'=8,'tensor'=2] {'expert'}, dimensions={0} | all-to-all | bytes 655360 | tf_op jit(solution)/shard_map/all_to_all | solution.py:119
  776.3 3.8 collective-permute-done.30
  783.4 8.3 collective-permute-done.32
  795.3 53.9 %all-gather.22.cloned.1.call-done = bf16[1024,1280]{1,0:T(8,128)(2,1)} async-done(((bf16[128,1280]{1,0:T(8,128)(2,1)}), bf16[1024,1280]{1,0:T(8,128)(2,1)}) %all-gather.22.cloned.1.call-update) | async-done | bytes 2621456 | tf_op jit(solution)/shard_map/all_gather | solution.py:51
  849.1 5.1 collective-permute-done.34
  856.7 2.8 pad_maximum_fusion.3
  861.7 11.5 %gather_fusion.2 = bf16[640,2560]{1,0:T(8,128)(2,1)} fusion(bf16[1024,2560]{1,0:T(8,128)(2,1)} %pad_maximum_fusion.3, s32[1024]{0:T(1024)S(1)} %copy-done.36), kind=kCustom, calls=%fused_computation.2 | custom fusion | bytes 6556160 | tf_op jit(solution)/shard_map/gather | solution.py:335
  875.4 7.7 fusion.140
  883.5 4.7 convolution_convert_fusion
  889.6 42.9 %all-gather.24.cloned.1.call-done = bf16[1536,512]{1,0:T(8,128)(2,1)} async-done(((bf16[192,512]{1,0:T(8,128)(2,1)}), bf16[1536,512]{1,0:T(8,128)(2,1)}) %all-gather.24.cloned.1.call-update) | async-done | bytes 1572880 | tf_op jit(solution)/shard_map/all_gather | solution.py:51
  944.1 4.1 all-to-all-start.5
  948.3 11.6 %collective-permute-done.41 = bf16[8,40,1280]{2,1,0:T(8,128)(2,1)} collective-permute-done((bf16[8,40,1280]{2,1,0:T(8,128)(2,1)}, bf16[8,40,1280]{2,1,0:T(8,128)(2,1)}, u32[]{:S(2)}, u32[]{:S(2)}) %collective-permute-start.41) | collective-permute-done | bytes 819232 | tf_op jit(solution)/shard_map/ppermute | solution.py:69
  962.2 3.9 all-to-all-start.6
  969.1 2.5 broadcast_select_fusion.55
  975.3 11.3 %all-to-all-done.6 = bf16[8,40,1280]{2,1,0:T(8,128)(2,1)S(1)} async-done(((bf16[8,40,1280]{2,1,0:T(8,128)(2,1)}), bf16[8,40,1280]{2,1,0:T(8,128)(2,1)S(1)}, u32[]{:S(2)}, u32[]{:S(2)}) %all-to-all-start.6) | async-done | bytes 819232 | tf_op jit(solution)/shard_map/all_to_all | solution.py:143
  990.6 2.9 gather_fusion.3
  993.5 3.7 reshape.851
  997.2 3.4 multiply_reduce_fusion
  (375 shorter events, 131.7 us)
Async XLA Ops:
  7.2 498.8 %copy-start = (bf16[1,320,1536]{2,1,0:T(8,128)(2,1)S(1)}, bf16[1,320,1536]{2,1,0:T(8,128)(2,1)}, u32[]{:S(2)}) copy-start(bf16[1,320,1536]{2,1,0:T(8,128)(2,1)} %param.30) | copy-start | bytes 2949124
  7.2 88.4 %all-gather.26.cloned.1.call-start = ((), (), s32[]{:S(2)}) async-start(), calls=%async_computation.13 | async-start | bytes 5160960 | tf_op jit(solution)/shard_map/all_gather | solution.py:108
  7.2 3.3 collective-permute-start.1
  7.7 87.8 %copy-start.16 = (bf16[1,320,2,1536]{3,2,1,0:T(2,128)(2,1)S(1)}, bf16[1,320,2,1536]{3,2,1,0:T(2,128)(2,1)}, u32[]{:S(2)}) copy-start(bf16[1,320,2,1536]{3,2,1,0:T(2,128)(2,1)} %param.29) | copy-start | bytes 5898244
  95.6 94.6 %collective-permute-start.2 = (bf16[8,160,2,896]{3,2,1,0:T(2,128)(2,1)}, bf16[8,160,2,896]{3,2,1,0:T(2,128)(2,1)}, u32[]{:S(2)}, u32[]{:S(2)}) collective-permute-start(bf16[8,160,2,896]{3,2,1,0:T(2,128)(2,1)} %bitcast.275), channel_id=1, source_target_pairs={{0,16},{16,0},{1,17},{17,1},{2,18},{18,2},{3,19},{19,3},{4,20},{20... | collective-permute-start | bytes 13762568 | tf_op jit(solution)/shard_map/ppermute | solution.py:45
  101.7 77.0 %copy-start.34 = (f32[1,1280,8]{1,2,0:T(8,128)S(1)}, f32[1,1280,8]{1,2,0:T(8,128)}, u32[]{:S(2)}) copy-start(f32[1,1280,8]{1,2,0:T(8,128)} %param.31) | copy-start | bytes 122884
  101.7 81.7 %copy-start.43 = (s32[1,128]{1,0:T(1,128)S(1)}, s32[1,128]{1,0:T(1,128)}, u32[]{:S(2)}) copy-start(s32[1,128]{1,0:T(1,128)} %param.22) | copy-start | bytes 1540
  101.7 84.0 %all-to-all-start = ((bf16[320,2,1536]{0,1,2:T(2,128)(2,1)}), bf16[320,2,1536]{0,1,2:T(2,128)(2,1)S(1)}, u32[]{:S(2)}, u32[]{:S(2)}) async-start(bf16[320,2,1536]{0,1,2:T(2,128)(2,1)} %bitcast.264), calls=%async_computation | async-start | bytes 4718592 | tf_op jit(solution)/shard_map/all_to_all | solution.py:177
  105.5 223.8 %all-gather.14.cloned.1.call-start = ((), (), s32[]{:S(2)}) async-start(), calls=%async_computation.7 | async-start | bytes 1474560 | tf_op jit(solution)/shard_map/all_gather | solution.py:51
  107.3 76.5 %collective-permute-start = (bf16[128,1280]{1,0:T(8,128)(2,1)}, bf16[128,1280]{1,0:T(8,128)(2,1)}, u32[]{:S(2)}, u32[]{:S(2)}) collective-permute-start(bf16[128,1280]{1,0:T(8,128)(2,1)} %bitcast_select_fusion.3), channel_id=1, source_target_pairs={{0,1},{1,0},{2,3},{3,2},{4,5},{5,4},{6,7},{7,6},{8,9},{9,8},{10,11... | collective-permute-start | bytes 983048 | tf_op jit(solution)/shard_map/ppermute | solution.py:69
  122.2 249.2 %copy-start.30 = (f32[2560]{0:T(1024)}, f32[2560]{0:T(1024)S(1)}, u32[]{:S(2)}) copy-start(f32[2560]{0:T(1024)S(1)} %reduce.34) | copy-start | bytes 30724
  253.4 1.4 collective-permute-start.3
  283.0 1.9 collective-permute-start.4
  287.7 1.7 collective-permute-start.5
  290.2 44.0 %copy-start.48 = (bf16[1,320,1280]{2,1,0:T(8,128)(2,1)S(1)}, bf16[1,320,1280]{2,1,0:T(8,128)(2,1)}, u32[]{:S(2)}) copy-start(bf16[1,320,1280]{2,1,0:T(8,128)(2,1)} %param.28) | copy-start | bytes 2457604
  290.2 138.4 %all-gather.16.cloned.1.call-start = ((), (), s32[]{:S(2)}) async-start(), calls=%async_computation.8 | async-start | bytes 2949120 | tf_op jit(solution)/shard_map/all_gather | solution.py:51
  329.3 3.2 collective-permute-start.6
  335.3 2.2 collective-permute-start.7
  354.2 5.4 collective-permute-start.8
  359.6 1.5 collective-permute-start.9
  361.3 9.8 collective-permute-start.10
  371.6 2.2 collective-permute-start.11
  374.6 119.0 %all-gather.18.cloned.1.call-start = ((), (), s32[]{:S(2)}) async-start(), calls=%async_computation.9 | async-start | bytes 1769472 | tf_op jit(solution)/shard_map/all_gather | solution.py:51
  428.5 5.1 collective-permute-start.12
  438.6 1.8 collective-permute-start.13
  441.4 125.7 %all-gather.28.cloned.1.call-start = ((), (), s32[]{:S(2)}) async-start(), calls=%async_computation.14 | async-start | bytes 5160960 | tf_op jit(solution)/shard_map/all_gather | solution.py:108
  441.4 3.0 collective-permute-start.23
  493.6 8.4 collective-permute-start.18
  493.6 10.9 %collective-permute-start.14 = (bf16[1536,512]{1,0:T(8,128)(2,1)}, bf16[1536,512]{1,0:T(8,128)(2,1)S(1)}, u32[]{:S(2)}, u32[]{:S(2)}) collective-permute-start(bf16[1536,512]{1,0:T(8,128)(2,1)} %all-gather.18.cloned.1.call-done), channel_id=1, source_target_pairs={{0,16},{16,0},{1,17},{17,1},{2,18},{18,2},{3,19},{19,3},{4,20},{20... | collective-permute-start | bytes 4718600 | tf_op jit(solution)/shard_map/ppermute | solution.py:45
  507.3 2.7 collective-permute-start.15
  508.5 58.6 %collective-permute-start.19 = (bf16[8,40,1280]{2,1,0:T(8,128)(2,1)}, bf16[8,40,1280]{2,1,0:T(8,128)(2,1)}, u32[]{:S(2)}, u32[]{:S(2)}) collective-permute-start(bf16[8,40,1280]{2,1,0:T(8,128)(2,1)} %broadcast_select_fusion.27), channel_id=1, source_target_pairs={{0,1},{1,0},{2,3},{3,2},{4,5},{5,4},{6,7},{7,6},{8,9},{9,8},{10,11... | collective-permute-start | bytes 2457608 | tf_op jit(solution)/shard_map/ppermute | solution.py:69
  513.3 56.1 %all-to-all-start.2 = ((bf16[8,64,320]{2,1,0:T(8,128)(2,1)}), bf16[8,64,320]{2,1,0:T(8,128)(2,1)}, u32[]{:S(2)}, u32[]{:S(2)}) async-start(bf16[8,64,320]{2,1,0:T(8,128)(2,1)} %copy.160), calls=%async_computation.2 | async-start | bytes 786432 | tf_op jit(solution)/shard_map/all_to_all | solution.py:119
  567.0 44.6 %collective-permute-start.24 = (bf16[8,160,2,896]{3,2,1,0:T(2,128)(2,1)}, bf16[8,160,2,896]{3,2,1,0:T(2,128)(2,1)}, u32[]{:S(2)}, u32[]{:S(2)}) collective-permute-start(bf16[8,160,2,896]{3,2,1,0:T(2,128)(2,1)} %bitcast.273), channel_id=1, source_target_pairs={{0,16},{16,0},{1,17},{17,1},{2,18},{18,2},{3,19},{19,3},{4,20},{20... | collective-permute-start | bytes 13762568 | tf_op jit(solution)/shard_map/ppermute | solution.py:45
  569.4 25.3 %all-to-all-start.3 = ((bf16[8,40,1280]{2,1,0:T(8,128)(2,1)}), bf16[8,40,1280]{2,1,0:T(8,128)(2,1)S(1)}, u32[]{:S(2)}, u32[]{:S(2)}) async-start(bf16[8,40,1280]{2,1,0:T(8,128)(2,1)} %add_convert_fusion.1), calls=%async_computation.3 | async-start | bytes 1638400 | tf_op jit(solution)/shard_map/all_to_all | solution.py:143
  573.0 177.0 %all-gather.20.cloned.1.call-start = ((), (), s32[]{:S(2)}) async-start(), calls=%async_computation.10 | async-start | bytes 1474560 | tf_op jit(solution)/shard_map/all_gather | solution.py:51
  576.2 18.5 %collective-permute-start.16 = (bf16[64,1280]{1,0:T(8,128)(2,1)S(1)}, bf16[64,1280]{1,0:T(8,128)(2,1)S(1)}, u32[]{:S(2)}, u32[]{:S(2)}) collective-permute-start(bf16[64,1280]{1,0:T(8,128)(2,1)S(1)} %broadcast_select_fusion.62), channel_id=1, source_target_pairs={{0,1},{1,0},{2,3},{3,2},{4,5},{5,4},{6,7},{7,6},{8,9},{9,8},{10,11... | collective-permute-start | bytes 491528 | tf_op jit(solution)/shard_map/ppermute | solution.py:69
  594.7 2.6 collective-permute-start.20
  594.7 2.5 collective-permute-start.17
  608.8 7.4 collective-permute-start.21
  616.3 51.7 %collective-permute-start.22 = (bf16[128,1280]{1,0:T(8,128)(2,1)S(1)}, bf16[128,1280]{1,0:T(8,128)(2,1)S(1)}, u32[]{:S(2)}, u32[]{:S(2)}) collective-permute-start(bf16[128,1280]{1,0:T(8,128)(2,1)S(1)} %bitcast_select_fusion.2), channel_id=1, source_target_pairs={{0,1},{1,0},{2,3},{3,2},{4,5},{5,4},{6,7},{7,6},{8,9},{9,8},{10,11... | collective-permute-start | bytes 983048 | tf_op jit(solution)/shard_map/ppermute | solution.py:69
  674.6 31.6 %copy-start.27 = (bf16[128,2,128]{0,2,1:T(8,128)(2,1)}, bf16[128,2,128]{0,2,1:T(8,128)(2,1)S(1)}, u32[]{:S(2)}) copy-start(bf16[128,2,128]{0,2,1:T(8,128)(2,1)S(1)} %pad_maximum_fusion.20) | copy-start | bytes 196612
  674.6 1.4 collective-permute-start.25
  704.1 1.9 collective-permute-start.26
  708.8 1.7 collective-permute-start.27
  711.3 43.5 %copy-start.49 = (bf16[1,320,1280]{2,1,0:T(8,128)(2,1)S(1)}, bf16[1,320,1280]{2,1,0:T(8,128)(2,1)}, u32[]{:S(2)}) copy-start(bf16[1,320,1280]{2,1,0:T(8,128)(2,1)} %param.28) | copy-start | bytes 2457604
  711.3 137.8 %all-gather.22.cloned.1.call-start = ((), (), s32[]{:S(2)}) async-start(), calls=%async_computation.11 | async-start | bytes 2949120 | tf_op jit(solution)/shard_map/all_gather | solution.py:51
  750.0 3.2 collective-permute-start.28
  756.0 2.2 collective-permute-start.29
  774.8 5.4 collective-permute-start.30
  780.3 1.5 collective-permute-start.31
  781.8 9.8 collective-permute-start.32
  792.2 2.2 collective-permute-start.33
  795.2 137.3 %all-gather.24.cloned.1.call-start = ((), (), s32[]{:S(2)}) async-start(), calls=%async_computation.12 | async-start | bytes 1769472 | tf_op jit(solution)/shard_map/all_gather | solution.py:51
  849.1 5.1 collective-permute-start.34
  883.3 5.3 collective-permute-start.35
  888.3 44.3 %collective-permute-start.40 = (bf16[8,80,2560]{2,1,0:T(8,128)(2,1)}, bf16[8,80,2560]{2,1,0:T(8,128)(2,1)}, u32[]{:S(2)}, u32[]{:S(2)}) collective-permute-start(bf16[8,80,2560]{2,1,0:T(8,128)(2,1)} %bitcast.76), channel_id=1, source_target_pairs={{0,16},{16,0},{1,17},{17,1},{2,18},{18,2},{3,19},{19,3},{4,20},{20... | collective-permute-start | bytes 9830408 | tf_op jit(solution)/shard_map/ppermute | solution.py:45
  932.5 3.6 collective-permute-start.36
  937.8 3.0 collective-permute-start.37
  939.3 20.5 %collective-permute-start.41 = (bf16[8,40,1280]{2,1,0:T(8,128)(2,1)}, bf16[8,40,1280]{2,1,0:T(8,128)(2,1)}, u32[]{:S(2)}, u32[]{:S(2)}) collective-permute-start(bf16[8,40,1280]{2,1,0:T(8,128)(2,1)} %broadcast_select_fusion.26), channel_id=1, source_target_pairs={{0,1},{1,0},{2,3},{3,2},{4,5},{5,4},{6,7},{7,6},{8,9},{9,8},{10,11... | collective-permute-start | bytes 2457608 | tf_op jit(solution)/shard_map/ppermute | solution.py:69
  944.1 18.1 %all-to-all-start.5 = ((bf16[8,64,320]{2,1,0:T(8,128)(2,1)}), bf16[8,64,320]{2,1,0:T(8,128)(2,1)}, u32[]{:S(2)}, u32[]{:S(2)}) async-start(bf16[8,64,320]{2,1,0:T(8,128)(2,1)} %copy.178), calls=%async_computation.5 | async-start | bytes 786432 | tf_op jit(solution)/shard_map/all_to_all | solution.py:119
  962.2 24.4 %all-to-all-start.6 = ((bf16[8,40,1280]{2,1,0:T(8,128)(2,1)}), bf16[8,40,1280]{2,1,0:T(8,128)(2,1)S(1)}, u32[]{:S(2)}, u32[]{:S(2)}) async-start(bf16[8,40,1280]{2,1,0:T(8,128)(2,1)} %add_convert_fusion), calls=%async_computation.6 | async-start | bytes 1638400 | tf_op jit(solution)/shard_map/all_to_all | solution.py:143
  973.7 12.9 %collective-permute-start.38 = (bf16[64,1280]{1,0:T(8,128)(2,1)S(1)}, bf16[64,1280]{1,0:T(8,128)(2,1)S(1)}, u32[]{:S(2)}, u32[]{:S(2)}) collective-permute-start(bf16[64,1280]{1,0:T(8,128)(2,1)S(1)} %broadcast_select_fusion.60), channel_id=1, source_target_pairs={{0,1},{1,0},{2,3},{3,2},{4,5},{5,4},{6,7},{7,6},{8,9},{9,8},{10,11... | collective-permute-start | bytes 491528 | tf_op jit(solution)/shard_map/ppermute | solution.py:69
  986.6 2.6 collective-permute-start.42
  986.7 2.5 collective-permute-start.39
  (43 other events, 420.7 us)
Sparse Core Ops, SparseCore 0:
  14.5 81.0 all-gather.25
  290.3 39.0 all-gather.13
  374.7 53.7 all-gather.15
  441.5 42.7 all-gather.17
  486.3 80.6 all-gather.27
  711.4 38.5 all-gather.19
  795.3 53.7 all-gather.21
  889.7 42.7 all-gather.23

commit v12 on v11

--- a/solution.py
+++ b/solution.py
@@ -204,6 +204,8 @@
     )
     model_width, kv_local, group_cols = qkv_full.shape
     qkv_layers = [qkv_full]
+    if relay_pairs:
+        qkv_layers.append(layer_weights(qkv_own, section_id == 1))
     shared_cols = shared_in_cols.shape[2]
     head_width = HD
     group = group_cols // head_width - 2
@@ -289,9 +291,6 @@
             jax.nn.silu(shared_hidden[:, :shared_cols]) * shared_hidden[:, shared_cols:]
         ).astype(jnp.bfloat16)
         shared_act = expert_gather(shared_act.T, 0, 1)
-        if relay_pairs and tick_index == 0:
-            qkv_later, _ = lax.optimization_barrier((qkv_own, shared_act))
-            qkv_layers.append(layer_weights(qkv_later, section_id == 1))
         shared_terms = lax.dot_general(
             shared_act,
             shared_down_local,

time: 1020 us -> 1020 us (level)
    ppermute x32 -> x31, waiting for transfers between devices: 55.8 us -> 53 us  [swap_cores(): lax.ppermute(value, 'section', [(source, (source + 1) % count) for source...]
  transfers between devices with their start and end apart: 56 -> 55, of which waited for: 37 -> 36; matrix products, arithmetic and copies ran while one was open for 16% -> 16% of each run, Pallas kernels for 0% -> 0%
where the time goes in v12:
time: 1020 us; the launch traced here: 1010 us
  waiting for transfers between devices  478 us (47%)
  blocking collectives  161 us (16%)
  other arithmetic  137 us (13%)
  local copies, waits for them, and re-layouts  123 us (12%)
  matrix products  52.7 us (5%)
  starting transfers between devices  42 us (4%)
  between operations  15.9 us (2%)
    all_gather x6, waiting for transfers between devices, paired_gather(): lax.all_gather(jnp.where(active, first, second), 'expert', axis=axis, til...  228 us
    all_gather x2, waiting for transfers between devices, step(): return lax.all_gather(part, 'expert', axis=0, tiled=False)  132 us
    concatenate x6, other arithmetic, paired_apply(): jnp.concatenate([jnp.where(active, done, theirs), jnp.where(active, their...  58.5 us
    all_gather x2, blocking collectives, paired_gather(): lax.all_gather(jnp.where(active, first, second), 'expert', axis=axis, til...  56.1 us
    all_gather x1, blocking collectives, local(): lax.all_gather(expert_choice[0], 'expert', axis=0, tiled=False)  55.7 us
    ppermute x31, waiting for transfers between devices, swap_cores(): lax.ppermute(value, 'section', [(source, (source + 1) % count) for source...  53 us
    ppermute x10, waiting for transfers between devices, swap_tensor(): lax.ppermute(value, 'tensor', [(source, (source + 1) % count) for source...  35.9 us
    unnamed x109, local copies, waits for them, and re-layouts  33.9 us
  transfers between devices with their start and end apart: 55, of which 36 were waited for; matrix products, arithmetic and copies ran while one was open for 16% of the time, Pallas kernels for 0%

profile of v12, /device:TPU:0, one launch (start us, length us, event | category | flops | bytes accessed | tf_op | source)
XLA Modules:
  0.0 1009.1 jit_solution(545545021643967279)
XLA Ops:
  7.7 2.8 collective-permute-done.1
  10.5 4.5 broadcast_select_fusion.12
  16.5 81.1 %all-gather.26.cloned.1.call-done = bf16[1280,2,896]{2,1,0:T(2,128)(2,1)} async-done(((bf16[160,2,896]{2,1,0:T(2,128)(2,1)}), bf16[1280,2,896]{2,1,0:T(2,128)(2,1)}) %all-gather.26.cloned.1.call-update) | async-done | bytes 4587536 | tf_op jit(solution)/shard_map/all_gather | solution.py:108
  97.5 6.1 copy.145
  103.7 3.8 all-to-all-start
  110.7 9.0 all-gather.2
  119.8 4.4 all-gather.3
  124.9 55.7 %all_gather.50 = s32[8,1,128,4]{2,3,1,0:T(4,128)S(1)} all-gather(s32[1,1,128,4]{2,3,1,0:T(4,128)S(1)} %copy-done.32), channel_id=1, replica_groups=mesh['section'=2,'expert'=8,'tensor'=2] {'expert'}, dimensions={0}, use_global_device_ids=true | all-gather | bytes 18432 | tf_op jit(solution)/shard_map/all_gather | solution.py:178
  180.6 4.7 all-gather.1
  189.4 2.7 all_to_all.70
  192.1 4.5 broadcast_select_fusion.3
  196.6 29.2 %pad_maximum_fusion = bf16[8,320,2,896]{3,2,1,0:T(2,128)(2,1)} fusion(bf16[8,160,2,896]{3,2,1,0:T(2,128)(2,1)S(1)} %bitcast.259, bf16[8,160,2,896]{3,2,1,0:T(2,128)(2,1)S(1)} %bitcast.258), kind=kLoop, calls=%fused_computation.6 | loop fusion | flops 4587520 | bytes 18350080 | tf_op jit(solution)/shard_map/concatenate | solution.py:99
  225.9 23.2 %copy.148 = bf16[2560,2,896]{0,2,1:T(8,128)(2,1)} copy(bf16[2560,2,896]{2,1,0:T(2,128)(2,1)} %bitcast.253) | data formatting | bytes 18350080 | tf_op jit(solution)/shard_map/optimization_barrier | solution.py:193
  249.0 6.2 fusion.105
  256.8 28.1 %all_gather.54 = bf16[1024,256]{0,1:T(8,128)(2,1)S(1)} all-gather(bf16[128,256]{0,1:T(8,128)(2,1)S(1)} %slice_select_fusion.13), channel_id=1, replica_groups=mesh['section'=2,'expert'=8,'tensor'=2] {'expert'}, dimensions={0}, use_global_device_ids=true | all-gather | bytes 589824 | tf_op jit(solution)/shard_map/all_gather | solution.py:51
  292.2 39.1 %all-gather.14.cloned.1.call-done = bf16[1024,640]{1,0:T(8,128)(2,1)} async-done(((bf16[128,640]{1,0:T(8,128)(2,1)}), bf16[1024,640]{1,0:T(8,128)(2,1)}) %all-gather.14.cloned.1.call-update) | async-done | bytes 1310736 | tf_op jit(solution)/shard_map/all_gather | solution.py:51
  331.3 3.2 collective-permute-done.6
  340.2 15.4 %all_to_all.92 = bf16[8,64,320]{2,1,0:T(8,128)(2,1)S(1)} all-to-all(bf16[8,64,320]{2,1,0:T(8,128)(2,1)S(1)} %copy.156), channel_id=1, replica_groups=mesh['section'=2,'expert'=8,'tensor'=2] {'expert'}, dimensions={0} | all-to-all | bytes 655360 | tf_op jit(solution)/shard_map/all_to_all | solution.py:119
  357.7 3.9 collective-permute-done.8
  364.7 8.3 collective-permute-done.10
  376.6 53.9 %all-gather.16.cloned.1.call-done = bf16[1024,1280]{1,0:T(8,128)(2,1)} async-done(((bf16[128,1280]{1,0:T(8,128)(2,1)}), bf16[1024,1280]{1,0:T(8,128)(2,1)}) %all-gather.16.cloned.1.call-update) | async-done | bytes 2621456 | tf_op jit(solution)/shard_map/all_gather | solution.py:51
  430.5 5.1 collective-permute-done.12
  445.3 4.3 scatter_custom_fusion.1
  449.8 4.5 scatter_custom_fusion
  454.4 8.0 copy.202
  462.4 2.8 pad_maximum_fusion.2
  465.2 11.3 %gather_fusion = bf16[640,2560]{1,0:T(8,128)(2,1)} fusion(bf16[1024,2560]{1,0:T(8,128)(2,1)} %pad_maximum_fusion.2, s32[1024]{0:T(1024)S(1)} %pad_clamp_fusion.1), kind=kCustom, calls=%fused_computation | custom fusion | bytes 6556160 | tf_op jit(solution)/shard_map/gather | solution.py:334
  478.7 7.8 fusion.148
  486.5 4.7 convolution_convert_fusion.1
  491.7 7.9 collective-permute-done.18
  510.9 4.1 all-to-all-start.2
  515.0 51.1 %all-gather.28.cloned.1.call-done = bf16[1280,2,896]{2,1,0:T(2,128)(2,1)} async-done(((bf16[160,2,896]{2,1,0:T(2,128)(2,1)}), bf16[1280,2,896]{2,1,0:T(2,128)(2,1)}) %all-gather.28.cloned.1.call-update) | async-done | bytes 4587536 | tf_op jit(solution)/shard_map/all_gather | solution.py:108
  568.5 3.5 all-to-all-start.3
  576.3 17.4 %all-to-all-done.3 = bf16[8,40,1280]{2,1,0:T(8,128)(2,1)S(1)} async-done(((bf16[8,40,1280]{2,1,0:T(8,128)(2,1)}), bf16[8,40,1280]{2,1,0:T(8,128)(2,1)S(1)}, u32[]{:S(2)}, u32[]{:S(2)}) %all-to-all-start.3) | async-done | bytes 819232 | tf_op jit(solution)/shard_map/all_to_all | solution.py:143
  597.7 2.9 gather_fusion.1
  600.6 3.7 reshape.850
  604.3 3.4 multiply_reduce_fusion.1
  607.9 2.8 collective-permute-start.21
  610.7 4.6 broadcast_select_fusion.1
  616.4 29.1 %pad_maximum_fusion.1 = bf16[8,320,2,896]{3,2,1,0:T(2,128)(2,1)} fusion(bf16[8,160,2,896]{3,2,1,0:T(2,128)(2,1)S(1)} %bitcast.257, bf16[8,160,2,896]{3,2,1,0:T(2,128)(2,1)S(1)} %bitcast.256), kind=kLoop, calls=%fused_computation.7 | loop fusion | flops 4587520 | bytes 18350080 | tf_op jit(solution)/shard_map/concatenate | solution.py:99
  645.5 8.8 copy.203
  654.2 12.7 %copy.165 = bf16[1792,2560]{1,0:T(8,128)(2,1)} copy(bf16[1792,2560]{0,1:T(8,128)(2,1)} %bitcast.255) | data formatting | bytes 18350080 | tf_op jit(solution)/shard_map/dot_general | solution.py:240
  667.2 6.2 fusion.102
  675.1 28.0 %all_gather.60 = bf16[1024,256]{0,1:T(8,128)(2,1)S(1)} all-gather(bf16[128,256]{0,1:T(8,128)(2,1)S(1)} %slice_select_fusion.12), channel_id=1, replica_groups=mesh['section'=2,'expert'=8,'tensor'=2] {'expert'}, dimensions={0}, use_global_device_ids=true | all-gather | bytes 589824 | tf_op jit(solution)/shard_map/all_gather | solution.py:51
  710.3 38.7 %all-gather.20.cloned.1.call-done = bf16[1024,640]{1,0:T(8,128)(2,1)} async-done(((bf16[128,640]{1,0:T(8,128)(2,1)}), bf16[1024,640]{1,0:T(8,128)(2,1)}) %all-gather.20.cloned.1.call-update) | async-done | bytes 1310736 | tf_op jit(solution)/shard_map/all_gather | solution.py:51
  749.0 3.2 collective-permute-done.27
  757.9 15.4 %all_to_all.93 = bf16[8,64,320]{2,1,0:T(8,128)(2,1)S(1)} all-to-all(bf16[8,64,320]{2,1,0:T(8,128)(2,1)S(1)} %copy.174), channel_id=1, replica_groups=mesh['section'=2,'expert'=8,'tensor'=2] {'expert'}, dimensions={0} | all-to-all | bytes 655360 | tf_op jit(solution)/shard_map/all_to_all | solution.py:119
  775.4 3.8 collective-permute-done.29
  782.4 8.3 collective-permute-done.31
  794.3 53.9 %all-gather.22.cloned.1.call-done = bf16[1024,1280]{1,0:T(8,128)(2,1)} async-done(((bf16[128,1280]{1,0:T(8,128)(2,1)}), bf16[1024,1280]{1,0:T(8,128)(2,1)}) %all-gather.22.cloned.1.call-update) | async-done | bytes 2621456 | tf_op jit(solution)/shard_map/all_gather | solution.py:51
  848.2 5.1 collective-permute-done.33
  855.7 2.8 pad_maximum_fusion.3
  860.7 11.5 %gather_fusion.2 = bf16[640,2560]{1,0:T(8,128)(2,1)} fusion(bf16[1024,2560]{1,0:T(8,128)(2,1)} %pad_maximum_fusion.3, s32[1024]{0:T(1024)S(1)} %copy-done.36), kind=kCustom, calls=%fused_computation.2 | custom fusion | bytes 6556160 | tf_op jit(solution)/shard_map/gather | solution.py:334
  874.5 7.7 fusion.150
  882.6 4.7 convolution_convert_fusion
  888.7 42.9 %all-gather.24.cloned.1.call-done = bf16[1536,512]{1,0:T(8,128)(2,1)} async-done(((bf16[192,512]{1,0:T(8,128)(2,1)}), bf16[1536,512]{1,0:T(8,128)(2,1)}) %all-gather.24.cloned.1.call-update) | async-done | bytes 1572880 | tf_op jit(solution)/shard_map/all_gather | solution.py:51
  943.2 4.1 all-to-all-start.5
  947.3 11.6 %collective-permute-done.40 = bf16[8,40,1280]{2,1,0:T(8,128)(2,1)} collective-permute-done((bf16[8,40,1280]{2,1,0:T(8,128)(2,1)}, bf16[8,40,1280]{2,1,0:T(8,128)(2,1)}, u32[]{:S(2)}, u32[]{:S(2)}) %collective-permute-start.40) | collective-permute-done | bytes 819232 | tf_op jit(solution)/shard_map/ppermute | solution.py:69
  961.3 3.9 all-to-all-start.6
  968.2 2.5 broadcast_select_fusion.55
  974.4 11.3 %all-to-all-done.6 = bf16[8,40,1280]{2,1,0:T(8,128)(2,1)S(1)} async-done(((bf16[8,40,1280]{2,1,0:T(8,128)(2,1)}), bf16[8,40,1280]{2,1,0:T(8,128)(2,1)S(1)}, u32[]{:S(2)}, u32[]{:S(2)}) %all-to-all-start.6) | async-done | bytes 819232 | tf_op jit(solution)/shard_map/all_to_all | solution.py:143
  989.7 2.9 gather_fusion.3
  992.6 3.7 reshape.851
  996.3 3.4 multiply_reduce_fusion
  (372 shorter events, 127.5 us)
Async XLA Ops:
  7.2 496.4 %copy-start = (bf16[1,320,1536]{2,1,0:T(8,128)(2,1)S(1)}, bf16[1,320,1536]{2,1,0:T(8,128)(2,1)}, u32[]{:S(2)}) copy-start(bf16[1,320,1536]{2,1,0:T(8,128)(2,1)} %param.30) | copy-start | bytes 2949124
  7.2 90.3 %all-gather.26.cloned.1.call-start = ((), (), s32[]{:S(2)}) async-start(), calls=%async_computation.13 | async-start | bytes 5160960 | tf_op jit(solution)/shard_map/all_gather | solution.py:108
  7.2 3.3 collective-permute-start.1
  7.7 89.8 %copy-start.16 = (bf16[1,320,2,1536]{3,2,1,0:T(2,128)(2,1)S(1)}, bf16[1,320,2,1536]{3,2,1,0:T(2,128)(2,1)}, u32[]{:S(2)}) copy-start(bf16[1,320,2,1536]{3,2,1,0:T(2,128)(2,1)} %param.29) | copy-start | bytes 5898244
  97.5 94.6 %collective-permute-start.2 = (bf16[8,160,2,896]{3,2,1,0:T(2,128)(2,1)}, bf16[8,160,2,896]{3,2,1,0:T(2,128)(2,1)}, u32[]{:S(2)}, u32[]{:S(2)}) collective-permute-start(bf16[8,160,2,896]{3,2,1,0:T(2,128)(2,1)} %bitcast.269), channel_id=1, source_target_pairs={{0,16},{16,0},{1,17},{17,1},{2,18},{18,2},{3,19},{19,3},{4,20},{20... | collective-permute-start | bytes 13762568 | tf_op jit(solution)/shard_map/ppermute | solution.py:45
  103.7 77.0 %copy-start.34 = (f32[1,1280,8]{1,2,0:T(8,128)S(1)}, f32[1,1280,8]{1,2,0:T(8,128)}, u32[]{:S(2)}) copy-start(f32[1,1280,8]{1,2,0:T(8,128)} %param.31) | copy-start | bytes 122884
  103.7 81.7 %copy-start.43 = (s32[1,128]{1,0:T(1,128)S(1)}, s32[1,128]{1,0:T(1,128)}, u32[]{:S(2)}) copy-start(s32[1,128]{1,0:T(1,128)} %param.22) | copy-start | bytes 1540
  103.7 84.0 %all-to-all-start = ((bf16[320,2,1536]{0,1,2:T(2,128)(2,1)}), bf16[320,2,1536]{0,1,2:T(2,128)(2,1)S(1)}, u32[]{:S(2)}, u32[]{:S(2)}) async-start(bf16[320,2,1536]{0,1,2:T(2,128)(2,1)} %bitcast.262), calls=%async_computation | async-start | bytes 4718592 | tf_op jit(solution)/shard_map/all_to_all | solution.py:177
  107.4 223.8 %all-gather.14.cloned.1.call-start = ((), (), s32[]{:S(2)}) async-start(), calls=%async_computation.7 | async-start | bytes 1474560 | tf_op jit(solution)/shard_map/all_gather | solution.py:51
  109.2 76.5 %collective-permute-start = (bf16[128,1280]{1,0:T(8,128)(2,1)}, bf16[128,1280]{1,0:T(8,128)(2,1)}, u32[]{:S(2)}, u32[]{:S(2)}) collective-permute-start(bf16[128,1280]{1,0:T(8,128)(2,1)} %bitcast_select_fusion.3), channel_id=1, source_target_pairs={{0,1},{1,0},{2,3},{3,2},{4,5},{5,4},{6,7},{7,6},{8,9},{9,8},{10,11... | collective-permute-start | bytes 983048 | tf_op jit(solution)/shard_map/ppermute | solution.py:69
  124.1 249.2 %copy-start.30 = (f32[2560]{0:T(1024)}, f32[2560]{0:T(1024)S(1)}, u32[]{:S(2)}) copy-start(f32[2560]{0:T(1024)S(1)} %reduce.34) | copy-start | bytes 30724
  255.3 29.6 %copy-start.25 = (bf16[128,2,128]{0,2,1:T(8,128)(2,1)}, bf16[128,2,128]{0,2,1:T(8,128)(2,1)S(1)}, u32[]{:S(2)}) copy-start(bf16[128,2,128]{0,2,1:T(8,128)(2,1)S(1)} %pad_maximum_fusion.18) | copy-start | bytes 196612
  255.4 1.4 collective-permute-start.3
  284.9 1.9 collective-permute-start.4
  289.7 1.7 collective-permute-start.5
  292.1 44.0 %copy-start.48 = (bf16[1,320,1280]{2,1,0:T(8,128)(2,1)S(1)}, bf16[1,320,1280]{2,1,0:T(8,128)(2,1)}, u32[]{:S(2)}) copy-start(bf16[1,320,1280]{2,1,0:T(8,128)(2,1)} %param.28) | copy-start | bytes 2457604
  292.1 138.4 %all-gather.16.cloned.1.call-start = ((), (), s32[]{:S(2)}) async-start(), calls=%async_computation.8 | async-start | bytes 2949120 | tf_op jit(solution)/shard_map/all_gather | solution.py:51
  331.3 3.2 collective-permute-start.6
  337.3 2.2 collective-permute-start.7
  356.1 5.4 collective-permute-start.8
  361.6 1.5 collective-permute-start.9
  363.2 9.8 collective-permute-start.10
  373.6 2.2 collective-permute-start.11
  376.6 114.7 %all-gather.18.cloned.1.call-start = ((), (), s32[]{:S(2)}) async-start(), calls=%async_computation.9 | async-start | bytes 1769472 | tf_op jit(solution)/shard_map/all_gather | solution.py:51
  430.5 5.1 collective-permute-start.12
  440.6 1.8 collective-permute-start.13
  443.3 122.8 %all-gather.28.cloned.1.call-start = ((), (), s32[]{:S(2)}) async-start(), calls=%async_computation.14 | async-start | bytes 5160960 | tf_op jit(solution)/shard_map/all_gather | solution.py:108
  491.2 8.4 collective-permute-start.18
  491.3 10.8 %collective-permute-start.14 = (bf16[1536,512]{1,0:T(8,128)(2,1)}, bf16[1536,512]{1,0:T(8,128)(2,1)S(1)}, u32[]{:S(2)}, u32[]{:S(2)}) collective-permute-start(bf16[1536,512]{1,0:T(8,128)(2,1)} %all-gather.18.cloned.1.call-done), channel_id=1, source_target_pairs={{0,16},{16,0},{1,17},{17,1},{2,18},{18,2},{3,19},{19,3},{4,20},{20... | collective-permute-start | bytes 4718600 | tf_op jit(solution)/shard_map/ppermute | solution.py:45
  504.9 2.7 collective-permute-start.15
  506.1 60.1 %collective-permute-start.19 = (bf16[8,40,1280]{2,1,0:T(8,128)(2,1)}, bf16[8,40,1280]{2,1,0:T(8,128)(2,1)}, u32[]{:S(2)}, u32[]{:S(2)}) collective-permute-start(bf16[8,40,1280]{2,1,0:T(8,128)(2,1)} %broadcast_select_fusion.27), channel_id=1, source_target_pairs={{0,1},{1,0},{2,3},{3,2},{4,5},{5,4},{6,7},{7,6},{8,9},{9,8},{10,11... | collective-permute-start | bytes 2457608 | tf_op jit(solution)/shard_map/ppermute | solution.py:69
  510.9 57.6 %all-to-all-start.2 = ((bf16[8,64,320]{2,1,0:T(8,128)(2,1)}), bf16[8,64,320]{2,1,0:T(8,128)(2,1)}, u32[]{:S(2)}, u32[]{:S(2)}) async-start(bf16[8,64,320]{2,1,0:T(8,128)(2,1)} %copy.160), calls=%async_computation.2 | async-start | bytes 786432 | tf_op jit(solution)/shard_map/all_to_all | solution.py:119
  566.1 44.6 %collective-permute-start.23 = (bf16[8,160,2,896]{3,2,1,0:T(2,128)(2,1)}, bf16[8,160,2,896]{3,2,1,0:T(2,128)(2,1)}, u32[]{:S(2)}, u32[]{:S(2)}) collective-permute-start(bf16[8,160,2,896]{3,2,1,0:T(2,128)(2,1)} %bitcast.267), channel_id=1, source_target_pairs={{0,16},{16,0},{1,17},{17,1},{2,18},{18,2},{3,19},{19,3},{4,20},{20... | collective-permute-start | bytes 13762568 | tf_op jit(solution)/shard_map/ppermute | solution.py:45
  568.5 25.2 %all-to-all-start.3 = ((bf16[8,40,1280]{2,1,0:T(8,128)(2,1)}), bf16[8,40,1280]{2,1,0:T(8,128)(2,1)S(1)}, u32[]{:S(2)}, u32[]{:S(2)}) async-start(bf16[8,40,1280]{2,1,0:T(8,128)(2,1)} %add_convert_fusion.1), calls=%async_computation.3 | async-start | bytes 1638400 | tf_op jit(solution)/shard_map/all_to_all | solution.py:143
  572.1 177.0 %all-gather.20.cloned.1.call-start = ((), (), s32[]{:S(2)}) async-start(), calls=%async_computation.10 | async-start | bytes 1474560 | tf_op jit(solution)/shard_map/all_gather | solution.py:51
  575.2 18.5 %collective-permute-start.16 = (bf16[64,1280]{1,0:T(8,128)(2,1)S(1)}, bf16[64,1280]{1,0:T(8,128)(2,1)S(1)}, u32[]{:S(2)}, u32[]{:S(2)}) collective-permute-start(bf16[64,1280]{1,0:T(8,128)(2,1)S(1)} %broadcast_select_fusion.62), channel_id=1, source_target_pairs={{0,1},{1,0},{2,3},{3,2},{4,5},{5,4},{6,7},{7,6},{8,9},{9,8},{10,11... | collective-permute-start | bytes 491528 | tf_op jit(solution)/shard_map/ppermute | solution.py:69
  593.7 2.6 collective-permute-start.20
  593.8 2.5 collective-permute-start.17
  607.9 7.4 collective-permute-start.21
  615.3 51.6 %collective-permute-start.22 = (bf16[128,1280]{1,0:T(8,128)(2,1)S(1)}, bf16[128,1280]{1,0:T(8,128)(2,1)S(1)}, u32[]{:S(2)}, u32[]{:S(2)}) collective-permute-start(bf16[128,1280]{1,0:T(8,128)(2,1)S(1)} %bitcast_select_fusion.2), channel_id=1, source_target_pairs={{0,1},{1,0},{2,3},{3,2},{4,5},{5,4},{6,7},{7,6},{8,9},{9,8},{10,11... | collective-permute-start | bytes 983048 | tf_op jit(solution)/shard_map/ppermute | solution.py:69
  673.6 31.6 %copy-start.27 = (bf16[128,2,128]{0,2,1:T(8,128)(2,1)}, bf16[128,2,128]{0,2,1:T(8,128)(2,1)S(1)}, u32[]{:S(2)}) copy-start(bf16[128,2,128]{0,2,1:T(8,128)(2,1)S(1)} %pad_maximum_fusion.19) | copy-start | bytes 196612
  673.6 1.4 collective-permute-start.24
  703.1 1.9 collective-permute-start.25
  707.8 1.7 collective-permute-start.26
  710.2 43.6 %copy-start.49 = (bf16[1,320,1280]{2,1,0:T(8,128)(2,1)S(1)}, bf16[1,320,1280]{2,1,0:T(8,128)(2,1)}, u32[]{:S(2)}) copy-start(bf16[1,320,1280]{2,1,0:T(8,128)(2,1)} %param.28) | copy-start | bytes 2457604
  710.3 137.9 %all-gather.22.cloned.1.call-start = ((), (), s32[]{:S(2)}) async-start(), calls=%async_computation.11 | async-start | bytes 2949120 | tf_op jit(solution)/shard_map/all_gather | solution.py:51
  749.0 3.2 collective-permute-start.27
  755.0 2.2 collective-permute-start.28
  773.9 5.4 collective-permute-start.29
  779.3 1.5 collective-permute-start.30
  780.9 9.8 collective-permute-start.31
  791.3 2.2 collective-permute-start.32
  794.3 137.3 %all-gather.24.cloned.1.call-start = ((), (), s32[]{:S(2)}) async-start(), calls=%async_computation.12 | async-start | bytes 1769472 | tf_op jit(solution)/shard_map/all_gather | solution.py:51
  848.2 5.1 collective-permute-start.33
  882.4 5.3 collective-permute-start.34
  887.3 44.3 %collective-permute-start.39 = (bf16[8,80,2560]{2,1,0:T(8,128)(2,1)}, bf16[8,80,2560]{2,1,0:T(8,128)(2,1)}, u32[]{:S(2)}, u32[]{:S(2)}) collective-permute-start(bf16[8,80,2560]{2,1,0:T(8,128)(2,1)} %bitcast.76), channel_id=1, source_target_pairs={{0,16},{16,0},{1,17},{17,1},{2,18},{18,2},{3,19},{19,3},{4,20},{20... | collective-permute-start | bytes 9830408 | tf_op jit(solution)/shard_map/ppermute | solution.py:45
  931.6 3.6 collective-permute-start.35
  936.8 3.0 collective-permute-start.36
  938.4 20.5 %collective-permute-start.40 = (bf16[8,40,1280]{2,1,0:T(8,128)(2,1)}, bf16[8,40,1280]{2,1,0:T(8,128)(2,1)}, u32[]{:S(2)}, u32[]{:S(2)}) collective-permute-start(bf16[8,40,1280]{2,1,0:T(8,128)(2,1)} %broadcast_select_fusion.26), channel_id=1, source_target_pairs={{0,1},{1,0},{2,3},{3,2},{4,5},{5,4},{6,7},{7,6},{8,9},{9,8},{10,11... | collective-permute-start | bytes 2457608 | tf_op jit(solution)/shard_map/ppermute | solution.py:69
  943.2 18.1 %all-to-all-start.5 = ((bf16[8,64,320]{2,1,0:T(8,128)(2,1)}), bf16[8,64,320]{2,1,0:T(8,128)(2,1)}, u32[]{:S(2)}, u32[]{:S(2)}) async-start(bf16[8,64,320]{2,1,0:T(8,128)(2,1)} %copy.178), calls=%async_computation.5 | async-start | bytes 786432 | tf_op jit(solution)/shard_map/all_to_all | solution.py:119
  961.3 24.4 %all-to-all-start.6 = ((bf16[8,40,1280]{2,1,0:T(8,128)(2,1)}), bf16[8,40,1280]{2,1,0:T(8,128)(2,1)S(1)}, u32[]{:S(2)}, u32[]{:S(2)}) async-start(bf16[8,40,1280]{2,1,0:T(8,128)(2,1)} %add_convert_fusion), calls=%async_computation.6 | async-start | bytes 1638400 | tf_op jit(solution)/shard_map/all_to_all | solution.py:143
  972.8 12.9 %collective-permute-start.37 = (bf16[64,1280]{1,0:T(8,128)(2,1)S(1)}, bf16[64,1280]{1,0:T(8,128)(2,1)S(1)}, u32[]{:S(2)}, u32[]{:S(2)}) collective-permute-start(bf16[64,1280]{1,0:T(8,128)(2,1)S(1)} %broadcast_select_fusion.60), channel_id=1, source_target_pairs={{0,1},{1,0},{2,3},{3,2},{4,5},{5,4},{6,7},{7,6},{8,9},{9,8},{10,11... | collective-permute-start | bytes 491528 | tf_op jit(solution)/shard_map/ppermute | solution.py:69
  985.7 2.6 collective-permute-start.41
  985.8 2.5 collective-permute-start.38
  (42 other events, 394.1 us)
Sparse Core Ops, SparseCore 0:
  16.6 80.8 all-gather.25
  292.2 39.0 all-gather.13
  376.7 53.7 all-gather.15
  443.5 42.5 all-gather.17
  488.1 77.9 all-gather.27
  710.4 38.6 all-gather.19
  794.4 53.7 all-gather.21
  888.8 42.7 all-gather.23

commit v13 on v10

--- a/solution.py
+++ b/solution.py
@@ -155,7 +155,7 @@
     experts_count = lax.axis_size("expert")
     expert_id = lax.axis_index("expert")
     micro_count, tokens_dev, columns = hidden_in.shape
-    qkv_full = lax.all_gather(w_qkv[0], "expert", axis=0, tiled=True)
+    qkv_blocks = lax.all_gather(w_qkv[0], "expert", axis=0, tiled=False)
     out_local = w_out[0]
     shared_down_local = w_shared_down[0]
     shared_in_cols = lax.all_to_all(w_shared_in[0], "expert", split_axis=2, concat_axis=0, tiled=True)
@@ -166,7 +166,7 @@
     w_in_local = w_in[0, 0]
     w_down_local = w_down[0, 0]
     (
-        qkv_full,
+        qkv_blocks,
         shared_in_cols,
         choices_every,
         router_full,
@@ -176,7 +176,7 @@
         w_down_local,
     ) = lax.optimization_barrier(
         (
-            qkv_full,
+            qkv_blocks,
             shared_in_cols,
             choices_every,
             router_full,
@@ -186,7 +186,8 @@
             w_down_local,
         )
     )
-    model_width, kv_local, group_cols = qkv_full.shape
+    model_width = qkv_blocks.shape[0] * qkv_blocks.shape[1]
+    kv_local, group_cols = qkv_blocks.shape[2:]
     shared_cols = shared_in_cols.shape[2]
     head_width = HD
     group = group_cols // head_width - 2
@@ -218,8 +219,11 @@
         first_slot = jnp.sum(jnp.where(member, starts[None, :], 0), axis=1)
         positions = jnp.where(segments >= 0, slot_index - first_slot, 0).astype(jnp.float32)
         normed_full = norm_full_rows(incoming, attn_gain_full)
-        projected = jnp.dot(
-            normed_full, qkv_full.reshape(model_width, -1), preferred_element_type=jnp.float32
+        projected = jnp.tensordot(
+            normed_full.reshape(tokens_dev, qkv_blocks.shape[0], qkv_blocks.shape[1]),
+            qkv_blocks.reshape(qkv_blocks.shape[0], qkv_blocks.shape[1], -1),
+            axes=((1, 2), (0, 1)),
+            preferred_element_type=jnp.float32,
         )
         projected = projected.reshape(tokens_dev, kv_local, group + 2, head_width)
         queries = rotate_heads(projected[:, :, :group], positions).astype(jnp.bfloat16)

time: 926 us -> 937 us (1.012)
    unnamed x99 -> x101, local copies, waits for them, and re-layouts: 34.8 us -> 25.9 us
where the time goes in v13:
time: 937 us; the launch traced here: 926 us
  waiting for transfers between devices  434 us (46%)
  blocking collectives  197 us (21%)
  local copies, waits for them, and re-layouts  110 us (12%)
  other arithmetic  67.6 us (7%)
  matrix products  57 us (6%)
  starting transfers between devices  45.4 us (5%)
  between operations  16.1 us (2%)
    all_gather x6, waiting for transfers between devices, paired_gather(): lax.all_gather(jnp.where(active, first, second), 'expert', axis=axis, til...  273 us
    all_gather x1, blocking collectives, local(): lax.all_gather(expert_choice[0], 'expert', axis=0, tiled=False)  93.2 us
    ppermute x10, waiting for transfers between devices, swap_tensor(): lax.ppermute(value, 'tensor', [(source, (source + 1) % count) for source...  55.9 us
    all_gather x2, blocking collectives, paired_gather(): lax.all_gather(jnp.where(active, first, second), 'expert', axis=axis, til...  55.4 us
    all_gather x1, waiting for transfers between devices, local(): qkv_blocks = lax.all_gather(w_qkv[0], 'expert', axis=0, tiled=False)  40.2 us
    ppermute x28, waiting for transfers between devices, swap_cores(): lax.ppermute(value, 'section', [(source, (source + 1) % count) for source...  36.8 us
    all_to_all x2, blocking collectives, step(): lax.all_to_all(part.reshape(-1, part.shape[2]), 'expert', split_axis=0, c...  30.8 us
    all_to_all x2, waiting for transfers between devices, step(): lax.all_to_all(summed, 'expert', split_axis=0, concat_axis=0, tiled=True)  27.2 us
  transfers between devices with their start and end apart: 51, of which 36 were waited for; matrix products, arithmetic and copies ran while one was open for 13% of the time, Pallas kernels for 0%

profile of v13, /device:TPU:0, one launch (start us, length us, event | category | flops | bytes accessed | tf_op | source)
XLA Modules:
  0.0 926.4 jit_solution(13284189618699143929)
XLA Ops:
  7.2 2.6 copy.207
  9.9 6.1 copy.208
  16.0 7.4 all-to-all-start
  26.7 8.1 all-gather.1
  34.9 4.4 all-gather.2
  40.1 93.2 %all_gather.40 = s32[8,1,128,4]{2,3,1,0:T(4,128)S(1)} all-gather(s32[1,1,128,4]{2,3,1,0:T(4,128)S(1)} %copy-done.26), channel_id=1, replica_groups=mesh['section'=2,'expert'=8,'tensor'=2] {'expert'}, dimensions={0}, use_global_device_ids=true | all-gather | bytes 18432 | tf_op jit(solution)/shard_map/all_gather | solution.py:162
  133.4 4.7 all-gather
  148.2 2.7 all_to_all.70
  150.9 40.2 %all-gather.11.cloned.1.call-done = bf16[8,320,2,896]{3,1,2,0:T(8,128)(2,1)} async-done(((bf16[1,320,2,896]{3,1,2,0:T(8,128)(2,1)}), bf16[8,320,2,896]{3,1,2,0:T(8,128)(2,1)}) %all-gather.11.cloned.1.call-update) | async-done | bytes 9175056 | tf_op jit(solution)/shard_map/all_gather | solution.py:158
  191.0 7.8 copy.270
  198.9 18.1 %dot_general.67 = bf16[2,7,128,8,320]{2,1,0,4,3:T(8,128)(2,1)} reshape(bf16[1792,8,320]{0,2,1:T(8,128)(2,1)} %bitcast.240) | data formatting | bytes 18350080 | tf_op jit(solution)/shard_map/dot_general | solution.py:222
  217.1 8.4 fusion.48
  227.1 27.7 %all_gather.44 = bf16[1024,256]{0,1:T(8,128)(2,1)S(1)} all-gather(bf16[128,256]{0,1:T(8,128)(2,1)S(1)} %slice_select_fusion.13), channel_id=1, replica_groups=mesh['section'=2,'expert'=8,'tensor'=2] {'expert'}, dimensions={0}, use_global_device_ids=true | all-gather | bytes 589824 | tf_op jit(solution)/shard_map/all_gather | solution.py:51
  262.0 39.1 %all-gather.13.cloned.1.call-done = bf16[1024,640]{1,0:T(8,128)(2,1)} async-done(((bf16[128,640]{1,0:T(8,128)(2,1)}), bf16[1024,640]{1,0:T(8,128)(2,1)}) %all-gather.13.cloned.1.call-update) | async-done | bytes 1310736 | tf_op jit(solution)/shard_map/all_gather | solution.py:51
  301.1 3.2 collective-permute-done.4
  310.0 15.4 %all_to_all.92 = bf16[8,64,320]{2,1,0:T(8,128)(2,1)S(1)} all-to-all(bf16[8,64,320]{2,1,0:T(8,128)(2,1)S(1)} %copy.220), channel_id=1, replica_groups=mesh['section'=2,'expert'=8,'tensor'=2] {'expert'}, dimensions={0} | all-to-all | bytes 655360 | tf_op jit(solution)/shard_map/all_to_all | solution.py:109
  327.5 3.8 collective-permute-done.6
  334.6 8.3 collective-permute-done.8
  346.5 53.9 %all-gather.15.cloned.1.call-done = bf16[1024,1280]{1,0:T(8,128)(2,1)} async-done(((bf16[128,1280]{1,0:T(8,128)(2,1)}), bf16[1024,1280]{1,0:T(8,128)(2,1)}) %all-gather.15.cloned.1.call-update) | async-done | bytes 2621456 | tf_op jit(solution)/shard_map/all_gather | solution.py:51
  400.8 4.5 scatter_custom_fusion.1
  405.5 4.3 scatter_custom_fusion
  409.9 7.9 copy.271
  417.8 2.4 broadcast_select_fusion.7
  420.3 2.7 pad_maximum_fusion
  426.7 11.7 %gather_fusion = bf16[640,2560]{1,0:T(8,128)(2,1)} fusion(bf16[1024,2560]{1,0:T(8,128)(2,1)} %pad_maximum_fusion, s32[1024]{0:T(1024)S(1)} %pad_clamp_fusion.1), kind=kCustom, calls=%fused_computation | custom fusion | bytes 6556160 | tf_op jit(solution)/shard_map/gather | solution.py:317
  440.6 7.7 fusion.156
  448.3 4.7 convolution_convert_fusion.1
  454.1 44.1 %all-gather.17.cloned.1.call-done = bf16[1536,512]{1,0:T(8,128)(2,1)} async-done(((bf16[192,512]{1,0:T(8,128)(2,1)}), bf16[1536,512]{1,0:T(8,128)(2,1)}) %all-gather.17.cloned.1.call-update) | async-done | bytes 1572880 | tf_op jit(solution)/shard_map/all_gather | solution.py:51
  498.2 2.3 broadcast_select_fusion.3
  509.7 4.1 all-to-all-start.2
  513.8 11.6 %collective-permute-done.17 = bf16[8,40,1280]{2,1,0:T(8,128)(2,1)} collective-permute-done((bf16[8,40,1280]{2,1,0:T(8,128)(2,1)}, bf16[8,40,1280]{2,1,0:T(8,128)(2,1)}, u32[]{:S(2)}, u32[]{:S(2)}) %collective-permute-start.17) | collective-permute-done | bytes 819232 | tf_op jit(solution)/shard_map/ppermute | solution.py:69
  525.4 2.4 add_convert_fusion.1
  527.8 3.5 all-to-all-start.3
  535.9 16.0 %all-to-all-done.3 = bf16[8,40,1280]{2,1,0:T(8,128)(2,1)S(1)} async-done(((bf16[8,40,1280]{2,1,0:T(8,128)(2,1)}), bf16[8,40,1280]{2,1,0:T(8,128)(2,1)S(1)}, u32[]{:S(2)}, u32[]{:S(2)}) %all-to-all-start.3) | async-done | bytes 819232 | tf_op jit(solution)/shard_map/all_to_all | solution.py:133
  555.9 3.1 gather_fusion.1
  558.9 3.7 reshape.916
  562.6 3.4 multiply_reduce_fusion.1
  571.1 8.5 collective-permute-done.20
  580.3 8.3 fusion.51
  590.2 27.7 %all_gather.48 = bf16[1024,256]{0,1:T(8,128)(2,1)S(1)} all-gather(bf16[128,256]{0,1:T(8,128)(2,1)S(1)} %slice_select_fusion.12), channel_id=1, replica_groups=mesh['section'=2,'expert'=8,'tensor'=2] {'expert'}, dimensions={0}, use_global_device_ids=true | all-gather | bytes 589824 | tf_op jit(solution)/shard_map/all_gather | solution.py:51
  625.3 38.9 %all-gather.19.cloned.1.call-done = bf16[1024,640]{1,0:T(8,128)(2,1)} async-done(((bf16[128,640]{1,0:T(8,128)(2,1)}), bf16[1024,640]{1,0:T(8,128)(2,1)}) %all-gather.19.cloned.1.call-update) | async-done | bytes 1310736 | tf_op jit(solution)/shard_map/all_gather | solution.py:51
  664.2 3.2 collective-permute-done.24
  673.1 15.4 %all_to_all.93 = bf16[8,64,320]{2,1,0:T(8,128)(2,1)S(1)} all-to-all(bf16[8,64,320]{2,1,0:T(8,128)(2,1)S(1)} %copy.240), channel_id=1, replica_groups=mesh['section'=2,'expert'=8,'tensor'=2] {'expert'}, dimensions={0} | all-to-all | bytes 655360 | tf_op jit(solution)/shard_map/all_to_all | solution.py:109
  690.6 3.9 collective-permute-done.26
  697.6 8.3 collective-permute-done.28
  709.5 53.9 %all-gather.21.cloned.1.call-done = bf16[1024,1280]{1,0:T(8,128)(2,1)} async-done(((bf16[128,1280]{1,0:T(8,128)(2,1)}), bf16[1024,1280]{1,0:T(8,128)(2,1)}) %all-gather.21.cloned.1.call-update) | async-done | bytes 2621456 | tf_op jit(solution)/shard_map/all_gather | solution.py:51
  763.4 5.1 collective-permute-done.30
  768.5 2.4 broadcast_select_fusion.5
  773.2 2.7 pad_maximum_fusion.1
  777.0 11.6 %gather_fusion.2 = bf16[640,2560]{1,0:T(8,128)(2,1)} fusion(bf16[1024,2560]{1,0:T(8,128)(2,1)} %pad_maximum_fusion.1, s32[1024]{0:T(1024)S(1)} %copy-done.30), kind=kCustom, calls=%fused_computation.2 | custom fusion | bytes 6556160 | tf_op jit(solution)/shard_map/gather | solution.py:317
  790.8 7.7 fusion.158
  798.6 4.7 convolution_convert_fusion
  805.7 42.9 %all-gather.23.cloned.1.call-done = bf16[1536,512]{1,0:T(8,128)(2,1)} async-done(((bf16[192,512]{1,0:T(8,128)(2,1)}), bf16[1536,512]{1,0:T(8,128)(2,1)}) %all-gather.23.cloned.1.call-update) | async-done | bytes 1572880 | tf_op jit(solution)/shard_map/all_gather | solution.py:51
  848.6 2.3 broadcast_select_fusion
  860.2 4.1 all-to-all-start.5
  864.3 11.5 %collective-permute-done.37 = bf16[8,40,1280]{2,1,0:T(8,128)(2,1)} collective-permute-done((bf16[8,40,1280]{2,1,0:T(8,128)(2,1)}, bf16[8,40,1280]{2,1,0:T(8,128)(2,1)}, u32[]{:S(2)}, u32[]{:S(2)}) %collective-permute-start.37) | collective-permute-done | bytes 819232 | tf_op jit(solution)/shard_map/ppermute | solution.py:69
  875.8 2.4 add_convert_fusion
  878.2 4.0 all-to-all-start.6
  885.2 2.6 broadcast_select_fusion.47
  891.5 11.2 %all-to-all-done.6 = bf16[8,40,1280]{2,1,0:T(8,128)(2,1)S(1)} async-done(((bf16[8,40,1280]{2,1,0:T(8,128)(2,1)}), bf16[8,40,1280]{2,1,0:T(8,128)(2,1)S(1)}, u32[]{:S(2)}, u32[]{:S(2)}) %all-to-all-start.6) | async-done | bytes 819232 | tf_op jit(solution)/shard_map/all_to_all | solution.py:133
  906.7 2.9 gather_fusion.3
  909.6 3.7 reshape.917
  913.3 3.4 multiply_reduce_fusion
  916.7 2.3 fusion.125
  (353 shorter events, 119.5 us)
Async XLA Ops:
  7.2 494.9 %copy-start = (bf16[1,320,1536]{2,1,0:T(8,128)(2,1)S(1)}, bf16[1,320,1536]{2,1,0:T(8,128)(2,1)}, u32[]{:S(2)}) copy-start(bf16[1,320,1536]{2,1,0:T(8,128)(2,1)} %param.30) | copy-start | bytes 2949124
  7.2 183.8 %all-gather.11.cloned.1.call-start = ((), (), s32[]{:S(2)}) async-start(), calls=%async_computation.7 | async-start | bytes 10321920 | tf_op jit(solution)/shard_map/all_gather | solution.py:158
  16.0 117.4 %copy-start.28 = (f32[1,1280,8]{1,2,0:T(8,128)S(1)}, f32[1,1280,8]{1,2,0:T(8,128)}, u32[]{:S(2)}) copy-start(f32[1,1280,8]{1,2,0:T(8,128)} %param.31) | copy-start | bytes 122884
  16.0 122.1 %copy-start.37 = (s32[1,128]{1,0:T(1,128)S(1)}, s32[1,128]{1,0:T(1,128)}, u32[]{:S(2)}) copy-start(s32[1,128]{1,0:T(1,128)} %param.22) | copy-start | bytes 1540
  16.0 130.4 %all-to-all-start = ((bf16[320,2,1536]{0,1,2:T(2,128)(2,1)}), bf16[320,2,1536]{0,1,2:T(2,128)(2,1)S(1)}, u32[]{:S(2)}, u32[]{:S(2)}) async-start(bf16[320,2,1536]{0,1,2:T(2,128)(2,1)} %bitcast.243), calls=%async_computation | async-start | bytes 4718592 | tf_op jit(solution)/shard_map/all_to_all | solution.py:161
  23.4 277.7 %all-gather.13.cloned.1.call-start = ((), (), s32[]{:S(2)}) async-start(), calls=%async_computation.8 | async-start | bytes 1474560 | tf_op jit(solution)/shard_map/all_gather | solution.py:51
  25.2 113.7 %collective-permute-start = (bf16[128,1280]{1,0:T(8,128)(2,1)}, bf16[128,1280]{1,0:T(8,128)(2,1)}, u32[]{:S(2)}, u32[]{:S(2)}) collective-permute-start(bf16[128,1280]{1,0:T(8,128)(2,1)} %bitcast_select_fusion.3), channel_id=1, source_target_pairs={{0,1},{1,0},{2,3},{3,2},{4,5},{5,4},{6,7},{7,6},{8,9},{9,8},{10,11... | collective-permute-start | bytes 983048 | tf_op jit(solution)/shard_map/ppermute | solution.py:69
  39.3 303.9 %copy-start.24 = (f32[2560]{0:T(1024)}, f32[2560]{0:T(1024)S(1)}, u32[]{:S(2)}) copy-start(f32[2560]{0:T(1024)S(1)} %reduce.34) | copy-start | bytes 30724
  217.1 37.7 %copy-start.38 = (s32[128]{0:T(128)S(1)}, s32[128]{0:T(128)}, u32[]{:S(2)}) copy-start(s32[128]{0:T(128)} %get-tuple-element.117) | copy-start | bytes 1540
  225.5 31.3 %copy-start.15 = (bf16[128,2,1,128]{0,3,2,1:T(8,128)(2,1)}, bf16[128,2,1,128]{0,3,2,1:T(8,128)(2,1)S(1)}, u32[]{:S(2)}) copy-start(bf16[128,2,1,128]{0,3,2,1:T(8,128)(2,1)S(1)} %slice.286) | copy-start | bytes 196612
  225.6 31.2 %copy-start.17 = (bf16[128,2,128]{0,2,1:T(8,128)(2,1)}, bf16[128,2,128]{0,2,1:T(8,128)(2,1)S(1)}, u32[]{:S(2)}) copy-start(bf16[128,2,128]{0,2,1:T(8,128)(2,1)S(1)} %pad_maximum_fusion.12) | copy-start | bytes 196612
  225.6 1.4 collective-permute-start.1
  254.8 1.9 collective-permute-start.2
  259.5 1.7 collective-permute-start.3
  261.9 44.0 %copy-start.43 = (bf16[1,320,1280]{2,1,0:T(8,128)(2,1)S(1)}, bf16[1,320,1280]{2,1,0:T(8,128)(2,1)}, u32[]{:S(2)}) copy-start(bf16[1,320,1280]{2,1,0:T(8,128)(2,1)} %param.28) | copy-start | bytes 2457604
  262.0 138.4 %all-gather.15.cloned.1.call-start = ((), (), s32[]{:S(2)}) async-start(), calls=%async_computation.9 | async-start | bytes 2949120 | tf_op jit(solution)/shard_map/all_gather | solution.py:51
  301.1 3.2 collective-permute-start.4
  307.1 2.2 collective-permute-start.5
  326.0 5.4 collective-permute-start.6
  331.4 1.5 collective-permute-start.7
  333.0 9.8 %collective-permute-start.8 = (bf16[128,1280]{1,0:T(8,128)(2,1)S(1)}, bf16[128,1280]{1,0:T(8,128)(2,1)S(1)}, u32[]{:S(2)}, u32[]{:S(2)}) collective-permute-start(bf16[128,1280]{1,0:T(8,128)(2,1)S(1)} %add_convert_fusion.5), channel_id=1, source_target_pairs={{0,1},{1,0},{2,3},{3,2},{4,5},{5,4},{6,7},{7,6},{8,9},{9,8},{10,11... | collective-permute-start | bytes 983048 | tf_op jit(solution)/shard_map/ppermute | solution.py:69
  342.9 57.6 %copy-start.40 = (s32[2]{0:T(128)S(1)}, s32[2]{0:T(128)}, u32[]{:S(2)}) copy-start(s32[2]{0:T(128)} %constant.167) | copy-start | bytes 28
  342.9 57.7 %copy-start.39 = (s32[2]{0:T(128)S(1)}, s32[2]{0:T(128)}, u32[]{:S(2)}) copy-start(s32[2]{0:T(128)} %constant.170) | copy-start | bytes 28
  343.4 2.2 collective-permute-start.9
  346.4 151.7 %all-gather.17.cloned.1.call-start = ((), (), s32[]{:S(2)}) async-start(), calls=%async_computation.10 | async-start | bytes 1769472 | tf_op jit(solution)/shard_map/all_gather | solution.py:51
  400.3 17.5 %collective-permute-start.10 = (bf16[1024,1280]{1,0:T(8,128)(2,1)}, bf16[1024,1280]{1,0:T(8,128)(2,1)}, u32[]{:S(2)}, u32[]{:S(2)}) collective-permute-start(bf16[1024,1280]{1,0:T(8,128)(2,1)} %all-gather.15.cloned.1.call-done), channel_id=1, source_target_pairs={{0,16},{16,0},{1,17},{17,1},{2,18},{18,2},{3,19},{19,3},{4,20},{20... | collective-permute-start | bytes 7864328 | tf_op jit(solution)/shard_map/ppermute | solution.py:45
  409.9 28.5 %copy-start.33 = (pred[8,80]{1,0:T(8,128)(4,1)}, pred[8,80]{1,0:T(8,128)(4,1)S(1)}, u32[]{:S(2)}) copy-start(pred[8,80]{1,0:T(8,128)(4,1)S(1)} %reshape.911) | copy-start | bytes 1924
  426.2 26.9 %collective-permute-start.11 = (bf16[192,1024]{1,0:T(8,128)(2,1)}, bf16[192,1024]{1,0:T(8,128)(2,1)}, u32[]{:S(2)}, u32[]{:S(2)}) collective-permute-start(bf16[192,1024]{1,0:T(8,128)(2,1)} %fusion.123), channel_id=1, source_target_pairs={{0,16},{16,0},{1,17},{17,1},{2,18},{18,2},{3,19},{19,3},{4,20},{20... | collective-permute-start | bytes 1179656 | tf_op jit(solution)/shard_map/ppermute | solution.py:45
  453.1 45.1 %collective-permute-start.16 = (bf16[8,80,2560]{2,1,0:T(8,128)(2,1)}, bf16[8,80,2560]{2,1,0:T(8,128)(2,1)}, u32[]{:S(2)}, u32[]{:S(2)}) collective-permute-start(bf16[8,80,2560]{2,1,0:T(8,128)(2,1)} %bitcast.46), channel_id=1, source_target_pairs={{0,16},{16,0},{1,17},{17,1},{2,18},{18,2},{3,19},{19,3},{4,20},{20... | collective-permute-start | bytes 9830408 | tf_op jit(solution)/shard_map/ppermute | solution.py:45
  498.1 3.6 collective-permute-start.12
  503.4 3.0 collective-permute-start.13
  504.9 20.5 %collective-permute-start.17 = (bf16[8,40,1280]{2,1,0:T(8,128)(2,1)}, bf16[8,40,1280]{2,1,0:T(8,128)(2,1)}, u32[]{:S(2)}, u32[]{:S(2)}) collective-permute-start(bf16[8,40,1280]{2,1,0:T(8,128)(2,1)} %broadcast_select_fusion.19), channel_id=1, source_target_pairs={{0,1},{1,0},{2,3},{3,2},{4,5},{5,4},{6,7},{7,6},{8,9},{9,8},{10,11... | collective-permute-start | bytes 2457608 | tf_op jit(solution)/shard_map/ppermute | solution.py:69
  509.7 18.0 %all-to-all-start.2 = ((bf16[8,64,320]{2,1,0:T(8,128)(2,1)}), bf16[8,64,320]{2,1,0:T(8,128)(2,1)}, u32[]{:S(2)}, u32[]{:S(2)}) async-start(bf16[8,64,320]{2,1,0:T(8,128)(2,1)} %copy.224), calls=%async_computation.2 | async-start | bytes 786432 | tf_op jit(solution)/shard_map/all_to_all | solution.py:109
  527.8 24.1 %all-to-all-start.3 = ((bf16[8,40,1280]{2,1,0:T(8,128)(2,1)}), bf16[8,40,1280]{2,1,0:T(8,128)(2,1)S(1)}, u32[]{:S(2)}, u32[]{:S(2)}) async-start(bf16[8,40,1280]{2,1,0:T(8,128)(2,1)} %add_convert_fusion.1), calls=%async_computation.3 | async-start | bytes 1638400 | tf_op jit(solution)/shard_map/all_to_all | solution.py:133
  531.3 132.9 %all-gather.19.cloned.1.call-start = ((), (), s32[]{:S(2)}) async-start(), calls=%async_computation.11 | async-start | bytes 1474560 | tf_op jit(solution)/shard_map/all_gather | solution.py:51
  534.3 17.5 %collective-permute-start.14 = (bf16[64,1280]{1,0:T(8,128)(2,1)S(1)}, bf16[64,1280]{1,0:T(8,128)(2,1)S(1)}, u32[]{:S(2)}, u32[]{:S(2)}) collective-permute-start(bf16[64,1280]{1,0:T(8,128)(2,1)S(1)} %broadcast_select_fusion.54), channel_id=1, source_target_pairs={{0,1},{1,0},{2,3},{3,2},{4,5},{5,4},{6,7},{7,6},{8,9},{9,8},{10,11... | collective-permute-start | bytes 491528 | tf_op jit(solution)/shard_map/ppermute | solution.py:69
  551.9 2.6 collective-permute-start.18
  551.9 2.5 collective-permute-start.15
  566.2 3.3 collective-permute-start.19
  569.5 10.1 %collective-permute-start.20 = (bf16[128,1280]{1,0:T(8,128)(2,1)S(1)}, bf16[128,1280]{1,0:T(8,128)(2,1)S(1)}, u32[]{:S(2)}, u32[]{:S(2)}) collective-permute-start(bf16[128,1280]{1,0:T(8,128)(2,1)S(1)} %bitcast_select_fusion.2), channel_id=1, source_target_pairs={{0,1},{1,0},{2,3},{3,2},{4,5},{5,4},{6,7},{7,6},{8,9},{9,8},{10,11... | collective-permute-start | bytes 983048 | tf_op jit(solution)/shard_map/ppermute | solution.py:69
  588.7 31.3 %copy-start.19 = (bf16[128,2,128]{0,2,1:T(8,128)(2,1)}, bf16[128,2,128]{0,2,1:T(8,128)(2,1)S(1)}, u32[]{:S(2)}) copy-start(bf16[128,2,128]{0,2,1:T(8,128)(2,1)S(1)} %pad_maximum_fusion.13) | copy-start | bytes 196612
  588.7 1.4 collective-permute-start.21
  617.9 1.9 collective-permute-start.22
  622.6 1.7 collective-permute-start.23
  625.1 44.0 %copy-start.44 = (bf16[1,320,1280]{2,1,0:T(8,128)(2,1)S(1)}, bf16[1,320,1280]{2,1,0:T(8,128)(2,1)}, u32[]{:S(2)}) copy-start(bf16[1,320,1280]{2,1,0:T(8,128)(2,1)} %param.28) | copy-start | bytes 2457604
  625.1 138.3 %all-gather.21.cloned.1.call-start = ((), (), s32[]{:S(2)}) async-start(), calls=%async_computation.12 | async-start | bytes 2949120 | tf_op jit(solution)/shard_map/all_gather | solution.py:51
  664.2 3.2 collective-permute-start.24
  670.2 2.2 collective-permute-start.25
  689.1 5.4 collective-permute-start.26
  694.5 1.5 collective-permute-start.27
  696.1 9.8 %collective-permute-start.28 = (bf16[128,1280]{1,0:T(8,128)(2,1)S(1)}, bf16[128,1280]{1,0:T(8,128)(2,1)S(1)}, u32[]{:S(2)}, u32[]{:S(2)}) collective-permute-start(bf16[128,1280]{1,0:T(8,128)(2,1)S(1)} %add_convert_fusion.3), channel_id=1, source_target_pairs={{0,1},{1,0},{2,3},{3,2},{4,5},{5,4},{6,7},{7,6},{8,9},{9,8},{10,11... | collective-permute-start | bytes 983048 | tf_op jit(solution)/shard_map/ppermute | solution.py:69
  706.4 2.2 collective-permute-start.29
  709.5 139.1 %all-gather.23.cloned.1.call-start = ((), (), s32[]{:S(2)}) async-start(), calls=%async_computation.13 | async-start | bytes 1769472 | tf_op jit(solution)/shard_map/all_gather | solution.py:51
  763.4 5.1 collective-permute-start.30
  776.9 26.8 %collective-permute-start.31 = (bf16[192,1024]{1,0:T(8,128)(2,1)}, bf16[192,1024]{1,0:T(8,128)(2,1)}, u32[]{:S(2)}, u32[]{:S(2)}) collective-permute-start(bf16[192,1024]{1,0:T(8,128)(2,1)} %fusion.124), channel_id=1, source_target_pairs={{0,16},{16,0},{1,17},{17,1},{2,18},{18,2},{3,19},{19,3},{4,20},{20... | collective-permute-start | bytes 1179656 | tf_op jit(solution)/shard_map/ppermute | solution.py:45
  803.3 45.3 %collective-permute-start.36 = (bf16[8,80,2560]{2,1,0:T(8,128)(2,1)}, bf16[8,80,2560]{2,1,0:T(8,128)(2,1)}, u32[]{:S(2)}, u32[]{:S(2)}) collective-permute-start(bf16[8,80,2560]{2,1,0:T(8,128)(2,1)} %bitcast.76), channel_id=1, source_target_pairs={{0,16},{16,0},{1,17},{17,1},{2,18},{18,2},{3,19},{19,3},{4,20},{20... | collective-permute-start | bytes 9830408 | tf_op jit(solution)/shard_map/ppermute | solution.py:45
  848.6 3.6 collective-permute-start.32
  853.8 3.0 collective-permute-start.33
  855.4 20.5 %collective-permute-start.37 = (bf16[8,40,1280]{2,1,0:T(8,128)(2,1)}, bf16[8,40,1280]{2,1,0:T(8,128)(2,1)}, u32[]{:S(2)}, u32[]{:S(2)}) collective-permute-start(bf16[8,40,1280]{2,1,0:T(8,128)(2,1)} %broadcast_select_fusion.18), channel_id=1, source_target_pairs={{0,1},{1,0},{2,3},{3,2},{4,5},{5,4},{6,7},{7,6},{8,9},{9,8},{10,11... | collective-permute-start | bytes 2457608 | tf_op jit(solution)/shard_map/ppermute | solution.py:69
  860.2 18.0 %all-to-all-start.5 = ((bf16[8,64,320]{2,1,0:T(8,128)(2,1)}), bf16[8,64,320]{2,1,0:T(8,128)(2,1)}, u32[]{:S(2)}, u32[]{:S(2)}) async-start(bf16[8,64,320]{2,1,0:T(8,128)(2,1)} %copy.244), calls=%async_computation.5 | async-start | bytes 786432 | tf_op jit(solution)/shard_map/all_to_all | solution.py:109
  878.2 24.5 %all-to-all-start.6 = ((bf16[8,40,1280]{2,1,0:T(8,128)(2,1)}), bf16[8,40,1280]{2,1,0:T(8,128)(2,1)S(1)}, u32[]{:S(2)}, u32[]{:S(2)}) async-start(bf16[8,40,1280]{2,1,0:T(8,128)(2,1)} %add_convert_fusion), calls=%async_computation.6 | async-start | bytes 1638400 | tf_op jit(solution)/shard_map/all_to_all | solution.py:133
  889.9 12.8 %collective-permute-start.34 = (bf16[64,1280]{1,0:T(8,128)(2,1)S(1)}, bf16[64,1280]{1,0:T(8,128)(2,1)S(1)}, u32[]{:S(2)}, u32[]{:S(2)}) collective-permute-start(bf16[64,1280]{1,0:T(8,128)(2,1)S(1)} %broadcast_select_fusion.52), channel_id=1, source_target_pairs={{0,1},{1,0},{2,3},{3,2},{4,5},{5,4},{6,7},{7,6},{8,9},{9,8},{10,11... | collective-permute-start | bytes 491528 | tf_op jit(solution)/shard_map/ppermute | solution.py:69
  902.7 2.6 collective-permute-start.38
  902.8 2.5 collective-permute-start.35
  (34 other events, 369.6 us)
Sparse Core Ops, SparseCore 0:
  10.2 180.7 all-gather.10
  262.1 39.0 all-gather.12
  346.6 53.7 all-gather.14
  454.2 43.8 all-gather.16
  625.2 38.9 all-gather.18
  709.6 53.7 all-gather.20
  805.8 42.7 all-gather.22

commit v14 on v10

--- a/solution.py
+++ b/solution.py
@@ -98,6 +98,23 @@
     theirs = swap_cores(done)
     return jnp.concatenate(
         [jnp.where(active, done, theirs), jnp.where(active, theirs, done)], axis=out_axis
+    )
+
+
+def quad_gather(rows, active):
+    value = jnp.where(active, rows, swap_cores(rows))
+    quarters = jnp.split(value, 4, axis=1)
+    lower = lax.axis_index("tensor") == 0
+    lead = jnp.where(lower, quarters[0], quarters[2])
+    trail = jnp.where(lower, quarters[1], quarters[3])
+    gathered = lax.all_gather(jnp.where(active, lead, trail), "expert", axis=0, tiled=True)
+    sibling = swap_cores(gathered)
+    half = jnp.concatenate(
+        [jnp.where(active, gathered, sibling), jnp.where(active, sibling, gathered)], axis=1
+    )
+    other = swap_tensor(half)
+    return jnp.concatenate(
+        [jnp.where(lower, half, other), jnp.where(lower, other, half)], axis=1
     )
 
 
@@ -260,7 +277,10 @@
         attn_sum = terms_to_slots(attn_terms.astype(jnp.bfloat16), pair_active).astype(jnp.float32)
         after_attn = (incoming.astype(jnp.float32) + attn_sum).astype(jnp.bfloat16)
         moe_rows = norm_full_rows(after_attn, ffn_gain_full)
-        moe_all = expert_gather(moe_rows, 0, 1)
+        if pair_active is not None and lax.axis_size("tensor") == 2:
+            moe_all = quad_gather(moe_rows, pair_active)
+        else:
+            moe_all = expert_gather(moe_rows, 0, 1)
         shared_hidden = jnp.dot(
             moe_all,
             shared_in_cols.reshape(model_width, 2 * shared_cols),

time: 926 us -> 1010 us (1.091)
  waiting for transfers between devices: 441 us -> 514 us
    all_gather x6 -> x4, waiting for transfers between devices: 273 us -> 165 us  [paired_gather(): lax.all_gather(jnp.where(active, first, second), 'expert', axis=axis, til...]
    ppermute x10 -> x12, waiting for transfers between devices: 55.9 us -> 154 us  [swap_tensor(): lax.ppermute(value, 'tensor', [(source, (source + 1) % count) for source...]
    all_gather x0 -> x2, waiting for transfers between devices: none -> 81.8 us  [quad_gather(): lax.all_gather(jnp.where(active, lead, trail), 'expert', axis=0, tiled=True)]
    unnamed x99 -> x101, local copies, waits for them, and re-layouts: 34.8 us -> 35 us
  transfers between devices with their start and end apart: 51 -> 53, of which waited for: 36 -> 39; matrix products, arithmetic and copies ran while one was open for 13% -> 12% of each run, Pallas kernels for 0% -> 0%
where the time goes in v14:
time: 1010 us; the launch traced here: 996 us
  waiting for transfers between devices  514 us (51%)
  blocking collectives  196 us (19%)
  local copies, waits for them, and re-layouts  100 us (10%)
  other arithmetic  68.2 us (7%)
  matrix products  53.3 us (5%)
  starting transfers between devices  48.5 us (5%)
  between operations  16 us (2%)
    all_gather x4, waiting for transfers between devices, paired_gather(): lax.all_gather(jnp.where(active, first, second), 'expert', axis=axis, til...  165 us
    ppermute x12, waiting for transfers between devices, swap_tensor(): lax.ppermute(value, 'tensor', [(source, (source + 1) % count) for source...  154 us
    all_gather x1, blocking collectives, local(): lax.all_gather(expert_choice[0], 'expert', axis=0, tiled=False)  92.7 us
    all_gather x2, waiting for transfers between devices, quad_gather(): lax.all_gather(jnp.where(active, lead, trail), 'expert', axis=0, tiled=True)  81.8 us
    all_gather x2, blocking collectives, paired_gather(): lax.all_gather(jnp.where(active, first, second), 'expert', axis=axis, til...  55.4 us
    all_gather x1, waiting for transfers between devices, local(): qkv_full = lax.all_gather(w_qkv[0], 'expert', axis=0, tiled=True)  46.2 us
    ppermute x28, waiting for transfers between devices, swap_cores(): lax.ppermute(value, 'section', [(source, (source + 1) % count) for source...  38.1 us
    unnamed x101, local copies, waits for them, and re-layouts  35 us
  transfers between devices with their start and end apart: 53, of which 39 were waited for; matrix products, arithmetic and copies ran while one was open for 12% of the time, Pallas kernels for 0%

profile of v14, /device:TPU:0, one launch (start us, length us, event | category | flops | bytes accessed | tf_op | source)
XLA Modules:
  0.0 996.0 jit_solution(1176956454070067880)
XLA Ops:
  7.9 8.5 copy.144
  16.5 7.4 all-to-all-start
  27.2 8.1 all-gather.2
  35.3 4.4 all-gather.3
  40.4 92.7 %all_gather.40 = s32[8,1,128,4]{2,3,1,0:T(4,128)S(1)} all-gather(s32[1,1,128,4]{2,3,1,0:T(4,128)S(1)} %copy-done.28), channel_id=1, replica_groups=mesh['section'=2,'expert'=8,'tensor'=2] {'expert'}, dimensions={0}, use_global_device_ids=true | all-gather | bytes 18432 | tf_op jit(solution)/shard_map/all_gather | solution.py:179
  133.1 4.7 all-gather.1
  141.9 2.7 all_to_all.70
  144.6 46.2 %all-gather.24.cloned.1.call-done = bf16[1,2560,2,896]{3,2,0,1:T(2,128)(2,1)} async-done(((bf16[1,320,2,896]{3,2,0,1:T(2,128)(2,1)}), bf16[1,2560,2,896]{3,2,0,1:T(2,128)(2,1)}) %all-gather.24.cloned.1.call-update) | async-done | bytes 9175056 | tf_op jit(solution)/shard_map/all_gather | solution.py:175
  190.9 8.7 copy.200
  199.6 12.7 %copy.147 = bf16[1792,2560]{1,0:T(8,128)(2,1)} copy(bf16[1792,2560]{0,1:T(8,128)(2,1)} %bitcast.235) | data formatting | bytes 18350080 | tf_op jit(solution)/shard_map/dot_general | solution.py:238
  212.3 6.2 fusion.105
  220.1 27.5 %all_gather.44 = bf16[1024,256]{0,1:T(8,128)(2,1)S(1)} all-gather(bf16[128,256]{0,1:T(8,128)(2,1)S(1)} %slice_select_fusion.15), channel_id=1, replica_groups=mesh['section'=2,'expert'=8,'tensor'=2] {'expert'}, dimensions={0}, use_global_device_ids=true | all-gather | bytes 589824 | tf_op jit(solution)/shard_map/all_gather | solution.py:51
  255.0 39.0 %all-gather.12.cloned.1.call-done = bf16[1024,640]{1,0:T(8,128)(2,1)} async-done(((bf16[128,640]{1,0:T(8,128)(2,1)}), bf16[1024,640]{1,0:T(8,128)(2,1)}) %all-gather.12.cloned.1.call-update) | async-done | bytes 1310736 | tf_op jit(solution)/shard_map/all_gather | solution.py:51
  294.0 3.2 collective-permute-done.4
  302.9 15.4 %all_to_all.92 = bf16[8,64,320]{2,1,0:T(8,128)(2,1)S(1)} all-to-all(bf16[8,64,320]{2,1,0:T(8,128)(2,1)S(1)} %copy.155), channel_id=1, replica_groups=mesh['section'=2,'expert'=8,'tensor'=2] {'expert'}, dimensions={0} | all-to-all | bytes 655360 | tf_op jit(solution)/shard_map/all_to_all | solution.py:126
  320.4 3.9 collective-permute-done.6
  327.4 8.3 collective-permute-done.8
  339.3 41.0 %all-gather.14.cloned.1.call-done = bf16[1024,640]{1,0:T(8,128)(2,1)} async-done(((bf16[128,640]{1,0:T(8,128)(2,1)}), bf16[1024,640]{1,0:T(8,128)(2,1)}) %all-gather.14.cloned.1.call-update) | async-done | bytes 1310736 | tf_op jit(solution)/shard_map/all_gather | solution.py:110
  380.3 3.2 collective-permute-done.10
  388.8 4.3 scatter_custom_fusion.1
  393.3 4.6 scatter_custom_fusion
  398.0 7.9 copy.201
  405.8 40.3 %collective-permute-done.11 = bf16[1024,1280]{1,0:T(8,128)(2,1)} collective-permute-done((bf16[1024,1280]{1,0:T(8,128)(2,1)}, bf16[1024,1280]{1,0:T(8,128)(2,1)}, u32[]{:S(2)}, u32[]{:S(2)}) %collective-permute-start.11) | collective-permute-done | bytes 2621472 | tf_op jit(solution)/shard_map/ppermute | solution.py:69
  446.2 2.3 broadcast_select_fusion.7
  448.5 2.7 pad_maximum_fusion
  454.5 11.3 %gather_fusion = bf16[640,2560]{1,0:T(8,128)(2,1)} fusion(bf16[1024,2560]{1,0:T(8,128)(2,1)} %pad_maximum_fusion, s32[1024]{0:T(1024)S(1)} %pad_clamp_fusion.1), kind=kCustom, calls=%fused_computation | custom fusion | bytes 6556160 | tf_op jit(solution)/shard_map/gather | solution.py:333
  468.0 7.7 fusion.150
  475.7 5.1 convolution_convert_fusion.1
  482.3 43.7 %all-gather.16.cloned.1.call-done = bf16[1536,512]{1,0:T(8,128)(2,1)} async-done(((bf16[192,512]{1,0:T(8,128)(2,1)}), bf16[1536,512]{1,0:T(8,128)(2,1)}) %all-gather.16.cloned.1.call-update) | async-done | bytes 1572880 | tf_op jit(solution)/shard_map/all_gather | solution.py:51
  526.0 2.3 broadcast_select_fusion.3
  537.6 4.1 all-to-all-start.2
  541.7 11.6 %collective-permute-done.18 = bf16[8,40,1280]{2,1,0:T(8,128)(2,1)} collective-permute-done((bf16[8,40,1280]{2,1,0:T(8,128)(2,1)}, bf16[8,40,1280]{2,1,0:T(8,128)(2,1)}, u32[]{:S(2)}, u32[]{:S(2)}) %collective-permute-start.18) | collective-permute-done | bytes 819232 | tf_op jit(solution)/shard_map/ppermute | solution.py:69
  553.3 2.3 add_convert_fusion.1
  555.6 3.5 all-to-all-start.3
  563.7 16.0 %all-to-all-done.3 = bf16[8,40,1280]{2,1,0:T(8,128)(2,1)S(1)} async-done(((bf16[8,40,1280]{2,1,0:T(8,128)(2,1)}), bf16[8,40,1280]{2,1,0:T(8,128)(2,1)S(1)}, u32[]{:S(2)}, u32[]{:S(2)}) %all-to-all-start.3) | async-done | bytes 819232 | tf_op jit(solution)/shard_map/all_to_all | solution.py:150
  583.7 2.9 gather_fusion.1
  586.6 3.7 reshape.847
  590.2 3.4 multiply_reduce_fusion.1
  598.7 8.5 collective-permute-done.21
  607.5 6.2 fusion.102
  615.3 27.9 %all_gather.48 = bf16[1024,256]{0,1:T(8,128)(2,1)S(1)} all-gather(bf16[128,256]{0,1:T(8,128)(2,1)S(1)} %slice_select_fusion.14), channel_id=1, replica_groups=mesh['section'=2,'expert'=8,'tensor'=2] {'expert'}, dimensions={0}, use_global_device_ids=true | all-gather | bytes 589824 | tf_op jit(solution)/shard_map/all_gather | solution.py:51
  650.4 39.1 %all-gather.18.cloned.1.call-done = bf16[1024,640]{1,0:T(8,128)(2,1)} async-done(((bf16[128,640]{1,0:T(8,128)(2,1)}), bf16[1024,640]{1,0:T(8,128)(2,1)}) %all-gather.18.cloned.1.call-update) | async-done | bytes 1310736 | tf_op jit(solution)/shard_map/all_gather | solution.py:51
  689.5 3.2 collective-permute-done.25
  698.4 15.4 %all_to_all.93 = bf16[8,64,320]{2,1,0:T(8,128)(2,1)S(1)} all-to-all(bf16[8,64,320]{2,1,0:T(8,128)(2,1)S(1)} %copy.172), channel_id=1, replica_groups=mesh['section'=2,'expert'=8,'tensor'=2] {'expert'}, dimensions={0} | all-to-all | bytes 655360 | tf_op jit(solution)/shard_map/all_to_all | solution.py:126
  715.9 3.8 collective-permute-done.27
  722.9 8.3 collective-permute-done.29
  734.9 40.8 %all-gather.20.cloned.1.call-done = bf16[1024,640]{1,0:T(8,128)(2,1)} async-done(((bf16[128,640]{1,0:T(8,128)(2,1)}), bf16[1024,640]{1,0:T(8,128)(2,1)}) %all-gather.20.cloned.1.call-update) | async-done | bytes 1310736 | tf_op jit(solution)/shard_map/all_gather | solution.py:110
  775.7 3.2 collective-permute-done.31
  782.3 57.4 %collective-permute-done.32 = bf16[1024,1280]{1,0:T(8,128)(2,1)S(1)} collective-permute-done((bf16[1024,1280]{1,0:T(8,128)(2,1)S(1)}, bf16[1024,1280]{1,0:T(8,128)(2,1)S(1)}, u32[]{:S(2)}, u32[]{:S(2)}) %collective-permute-start.32) | collective-permute-done | bytes 2621472 | tf_op jit(solution)/shard_map/ppermute | solution.py:69
  843.0 2.8 pad_maximum_fusion.1
  846.7 11.3 %gather_fusion.2 = bf16[640,2560]{1,0:T(8,128)(2,1)} fusion(bf16[1024,2560]{1,0:T(8,128)(2,1)} %pad_maximum_fusion.1, s32[1024]{0:T(1024)S(1)} %copy-done.32), kind=kCustom, calls=%fused_computation.2 | custom fusion | bytes 6556160 | tf_op jit(solution)/shard_map/gather | solution.py:333
  860.3 7.7 fusion.152
  868.0 5.0 convolution_convert_fusion
  875.5 43.0 %all-gather.22.cloned.1.call-done = bf16[1536,512]{1,0:T(8,128)(2,1)} async-done(((bf16[192,512]{1,0:T(8,128)(2,1)}), bf16[1536,512]{1,0:T(8,128)(2,1)}) %all-gather.22.cloned.1.call-update) | async-done | bytes 1572880 | tf_op jit(solution)/shard_map/all_gather | solution.py:51
  918.5 2.3 broadcast_select_fusion
  930.2 4.1 all-to-all-start.5
  934.3 11.5 %collective-permute-done.39 = bf16[8,40,1280]{2,1,0:T(8,128)(2,1)} collective-permute-done((bf16[8,40,1280]{2,1,0:T(8,128)(2,1)}, bf16[8,40,1280]{2,1,0:T(8,128)(2,1)}, u32[]{:S(2)}, u32[]{:S(2)}) %collective-permute-start.39) | collective-permute-done | bytes 819232 | tf_op jit(solution)/shard_map/ppermute | solution.py:69
  945.8 2.4 add_convert_fusion
  948.2 3.7 all-to-all-start.6
  954.8 2.5 broadcast_select_fusion.51
  961.1 11.3 %all-to-all-done.6 = bf16[8,40,1280]{2,1,0:T(8,128)(2,1)S(1)} async-done(((bf16[8,40,1280]{2,1,0:T(8,128)(2,1)}), bf16[8,40,1280]{2,1,0:T(8,128)(2,1)S(1)}, u32[]{:S(2)}, u32[]{:S(2)}) %all-to-all-start.6) | async-done | bytes 819232 | tf_op jit(solution)/shard_map/all_to_all | solution.py:150
  976.5 2.9 gather_fusion.3
  979.3 3.7 reshape.848
  983.0 3.4 multiply_reduce_fusion
  (355 shorter events, 125.1 us)
Async XLA Ops:
  7.2 522.8 %copy-start = (bf16[1,320,1536]{2,1,0:T(8,128)(2,1)S(1)}, bf16[1,320,1536]{2,1,0:T(8,128)(2,1)}, u32[]{:S(2)}) copy-start(bf16[1,320,1536]{2,1,0:T(8,128)(2,1)} %param.30) | copy-start | bytes 2949124
  7.2 183.7 %all-gather.24.cloned.1.call-start = ((), (), s32[]{:S(2)}) async-start(), calls=%async_computation.13 | async-start | bytes 10321920 | tf_op jit(solution)/shard_map/all_gather | solution.py:175
  16.4 116.7 %copy-start.30 = (f32[1,1280,8]{1,2,0:T(8,128)S(1)}, f32[1,1280,8]{1,2,0:T(8,128)}, u32[]{:S(2)}) copy-start(f32[1,1280,8]{1,2,0:T(8,128)} %param.31) | copy-start | bytes 122884
  16.4 121.4 %copy-start.39 = (s32[1,128]{1,0:T(1,128)S(1)}, s32[1,128]{1,0:T(1,128)}, u32[]{:S(2)}) copy-start(s32[1,128]{1,0:T(1,128)} %param.22) | copy-start | bytes 1540
  16.5 123.7 %all-to-all-start = ((bf16[320,2,1536]{0,1,2:T(2,128)(2,1)}), bf16[320,2,1536]{0,1,2:T(2,128)(2,1)S(1)}, u32[]{:S(2)}, u32[]{:S(2)}) async-start(bf16[320,2,1536]{0,1,2:T(2,128)(2,1)} %bitcast.238), calls=%async_computation | async-start | bytes 4718592 | tf_op jit(solution)/shard_map/all_to_all | solution.py:178
  23.9 270.1 %all-gather.12.cloned.1.call-start = ((), (), s32[]{:S(2)}) async-start(), calls=%async_computation.7 | async-start | bytes 1474560 | tf_op jit(solution)/shard_map/all_gather | solution.py:51
  25.7 112.5 %collective-permute-start = (bf16[128,1280]{1,0:T(8,128)(2,1)}, bf16[128,1280]{1,0:T(8,128)(2,1)}, u32[]{:S(2)}, u32[]{:S(2)}) collective-permute-start(bf16[128,1280]{1,0:T(8,128)(2,1)} %bitcast_select_fusion.3), channel_id=1, source_target_pairs={{0,1},{1,0},{2,3},{3,2},{4,5},{5,4},{6,7},{7,6},{8,9},{9,8},{10,11... | collective-permute-start | bytes 983048 | tf_op jit(solution)/shard_map/ppermute | solution.py:69
  39.6 296.4 %copy-start.26 = (f32[2560]{0:T(1024)}, f32[2560]{0:T(1024)S(1)}, u32[]{:S(2)}) copy-start(f32[2560]{0:T(1024)S(1)} %reduce.34) | copy-start | bytes 30724
  218.7 1.4 collective-permute-start.1
  247.6 1.9 collective-permute-start.2
  252.3 1.7 collective-permute-start.3
  254.8 44.0 %copy-start.44 = (bf16[1,320,1280]{2,1,0:T(8,128)(2,1)S(1)}, bf16[1,320,1280]{2,1,0:T(8,128)(2,1)}, u32[]{:S(2)}) copy-start(bf16[1,320,1280]{2,1,0:T(8,128)(2,1)} %param.28) | copy-start | bytes 2457604
  254.8 125.4 %all-gather.14.cloned.1.call-start = ((), (), s32[]{:S(2)}) async-start(), calls=%async_computation.8 | async-start | bytes 1474560 | tf_op jit(solution)/shard_map/all_gather | solution.py:110
  294.0 3.2 collective-permute-start.4
  300.0 2.2 collective-permute-start.5
  318.8 5.4 collective-permute-start.6
  324.3 1.5 collective-permute-start.7
  325.9 9.8 collective-permute-start.8
  336.3 2.2 collective-permute-start.9
  339.2 186.8 %all-gather.16.cloned.1.call-start = ((), (), s32[]{:S(2)}) async-start(), calls=%async_computation.9 | async-start | bytes 1769472 | tf_op jit(solution)/shard_map/all_gather | solution.py:51
  380.3 3.2 collective-permute-start.10
  386.9 59.2 %collective-permute-start.11 = (bf16[1024,1280]{1,0:T(8,128)(2,1)}, bf16[1024,1280]{1,0:T(8,128)(2,1)}, u32[]{:S(2)}, u32[]{:S(2)}) collective-permute-start(bf16[1024,1280]{1,0:T(8,128)(2,1)} %pad_maximum_fusion.2), channel_id=1, source_target_pairs={{0,1},{1,0},{2,3},{3,2},{4,5},{5,4},{6,7},{7,6},{8,9},{9,8},{10,11... | collective-permute-start | bytes 7864328 | tf_op jit(solution)/shard_map/ppermute | solution.py:69
  398.0 67.8 %copy-start.35 = (pred[8,80]{1,0:T(8,128)(4,1)}, pred[8,80]{1,0:T(8,128)(4,1)S(1)}, u32[]{:S(2)}) copy-start(pred[8,80]{1,0:T(8,128)(4,1)S(1)} %reshape.842) | copy-start | bytes 1924
  398.0 48.2 %copy-start.2 = (bf16[1024,640]{1,0:T(8,128)(2,1)S(1)}, bf16[1024,640]{1,0:T(8,128)(2,1)}, u32[]{:S(2)}) copy-start(bf16[1024,640]{1,0:T(8,128)(2,1)} %copy-done.1) | copy-start | bytes 3932164
  405.8 48.6 %copy-start.31 = (s32[1024]{0:T(1024)}, s32[1024]{0:T(1024)S(1)}, u32[]{:S(2)}) copy-start(s32[1024]{0:T(1024)S(1)} %pad_clamp_fusion.1) | copy-start | bytes 12292
  454.4 26.9 %collective-permute-start.12 = (bf16[192,1024]{1,0:T(8,128)(2,1)}, bf16[192,1024]{1,0:T(8,128)(2,1)}, u32[]{:S(2)}, u32[]{:S(2)}) collective-permute-start(bf16[192,1024]{1,0:T(8,128)(2,1)} %fusion.115), channel_id=1, source_target_pairs={{0,16},{16,0},{1,17},{17,1},{2,18},{18,2},{3,19},{19,3},{4,20},{20... | collective-permute-start | bytes 1179656 | tf_op jit(solution)/shard_map/ppermute | solution.py:45
  480.8 45.2 %collective-permute-start.17 = (bf16[8,80,2560]{2,1,0:T(8,128)(2,1)}, bf16[8,80,2560]{2,1,0:T(8,128)(2,1)}, u32[]{:S(2)}, u32[]{:S(2)}) collective-permute-start(bf16[8,80,2560]{2,1,0:T(8,128)(2,1)} %bitcast.45), channel_id=1, source_target_pairs={{0,16},{16,0},{1,17},{17,1},{2,18},{18,2},{3,19},{19,3},{4,20},{20... | collective-permute-start | bytes 9830408 | tf_op jit(solution)/shard_map/ppermute | solution.py:45
  526.0 3.6 collective-permute-start.13
  531.2 3.0 collective-permute-start.14
  532.8 20.5 %collective-permute-start.18 = (bf16[8,40,1280]{2,1,0:T(8,128)(2,1)}, bf16[8,40,1280]{2,1,0:T(8,128)(2,1)}, u32[]{:S(2)}, u32[]{:S(2)}) collective-permute-start(bf16[8,40,1280]{2,1,0:T(8,128)(2,1)} %broadcast_select_fusion.23), channel_id=1, source_target_pairs={{0,1},{1,0},{2,3},{3,2},{4,5},{5,4},{6,7},{7,6},{8,9},{9,8},{10,11... | collective-permute-start | bytes 2457608 | tf_op jit(solution)/shard_map/ppermute | solution.py:69
  537.6 18.0 %all-to-all-start.2 = ((bf16[8,64,320]{2,1,0:T(8,128)(2,1)}), bf16[8,64,320]{2,1,0:T(8,128)(2,1)}, u32[]{:S(2)}, u32[]{:S(2)}) async-start(bf16[8,64,320]{2,1,0:T(8,128)(2,1)} %copy.159), calls=%async_computation.2 | async-start | bytes 786432 | tf_op jit(solution)/shard_map/all_to_all | solution.py:126
  555.6 24.1 %all-to-all-start.3 = ((bf16[8,40,1280]{2,1,0:T(8,128)(2,1)}), bf16[8,40,1280]{2,1,0:T(8,128)(2,1)S(1)}, u32[]{:S(2)}, u32[]{:S(2)}) async-start(bf16[8,40,1280]{2,1,0:T(8,128)(2,1)} %add_convert_fusion.1), calls=%async_computation.3 | async-start | bytes 1638400 | tf_op jit(solution)/shard_map/all_to_all | solution.py:150
  559.2 130.3 %all-gather.18.cloned.1.call-start = ((), (), s32[]{:S(2)}) async-start(), calls=%async_computation.10 | async-start | bytes 1474560 | tf_op jit(solution)/shard_map/all_gather | solution.py:51
  562.1 17.5 %collective-permute-start.15 = (bf16[64,1280]{1,0:T(8,128)(2,1)S(1)}, bf16[64,1280]{1,0:T(8,128)(2,1)S(1)}, u32[]{:S(2)}, u32[]{:S(2)}) collective-permute-start(bf16[64,1280]{1,0:T(8,128)(2,1)S(1)} %broadcast_select_fusion.58), channel_id=1, source_target_pairs={{0,1},{1,0},{2,3},{3,2},{4,5},{5,4},{6,7},{7,6},{8,9},{9,8},{10,11... | collective-permute-start | bytes 491528 | tf_op jit(solution)/shard_map/ppermute | solution.py:69
  579.7 2.6 collective-permute-start.19
  579.8 2.5 collective-permute-start.16
  593.8 3.3 collective-permute-start.20
  597.1 10.1 %collective-permute-start.21 = (bf16[128,1280]{1,0:T(8,128)(2,1)S(1)}, bf16[128,1280]{1,0:T(8,128)(2,1)S(1)}, u32[]{:S(2)}, u32[]{:S(2)}) collective-permute-start(bf16[128,1280]{1,0:T(8,128)(2,1)S(1)} %bitcast_select_fusion.2), channel_id=1, source_target_pairs={{0,1},{1,0},{2,3},{3,2},{4,5},{5,4},{6,7},{7,6},{8,9},{9,8},{10,11... | collective-permute-start | bytes 983048 | tf_op jit(solution)/shard_map/ppermute | solution.py:69
  613.8 31.4 %copy-start.23 = (bf16[128,2,128]{0,2,1:T(8,128)(2,1)}, bf16[128,2,128]{0,2,1:T(8,128)(2,1)S(1)}, u32[]{:S(2)}) copy-start(bf16[128,2,128]{0,2,1:T(8,128)(2,1)S(1)} %pad_maximum_fusion.19) | copy-start | bytes 196612
  613.8 1.4 collective-permute-start.22
  643.2 1.9 collective-permute-start.23
  647.9 1.7 collective-permute-start.24
  650.3 44.0 %copy-start.45 = (bf16[1,320,1280]{2,1,0:T(8,128)(2,1)S(1)}, bf16[1,320,1280]{2,1,0:T(8,128)(2,1)}, u32[]{:S(2)}) copy-start(bf16[1,320,1280]{2,1,0:T(8,128)(2,1)} %param.28) | copy-start | bytes 2457604
  650.3 125.4 %all-gather.20.cloned.1.call-start = ((), (), s32[]{:S(2)}) async-start(), calls=%async_computation.11 | async-start | bytes 1474560 | tf_op jit(solution)/shard_map/all_gather | solution.py:110
  689.5 3.2 collective-permute-start.25
  695.5 2.2 collective-permute-start.26
  714.3 5.4 collective-permute-start.27
  719.8 1.5 collective-permute-start.28
  721.4 9.8 collective-permute-start.29
  731.7 2.2 collective-permute-start.30
  734.7 183.9 %all-gather.22.cloned.1.call-start = ((), (), s32[]{:S(2)}) async-start(), calls=%async_computation.12 | async-start | bytes 1769472 | tf_op jit(solution)/shard_map/all_gather | solution.py:51
  775.7 3.2 collective-permute-start.31
  780.7 60.0 %copy-start.14 = (bf16[2560,2,192]{0,2,1:T(8,128)(2,1)S(1)}, bf16[2560,2,192]{0,2,1:T(8,128)(2,1)}, u32[]{:S(2)}) copy-start(bf16[2560,2,192]{0,2,1:T(8,128)(2,1)} %all_to_all.70) | copy-start | bytes 5898244
  780.7 59.0 %collective-permute-start.32 = (bf16[1024,1280]{1,0:T(8,128)(2,1)S(1)}, bf16[1024,1280]{1,0:T(8,128)(2,1)S(1)}, u32[]{:S(2)}, u32[]{:S(2)}) collective-permute-start(bf16[1024,1280]{1,0:T(8,128)(2,1)S(1)} %pad_maximum_fusion.3), channel_id=1, source_target_pairs={{0,1},{1,0},{2,3},{3,2},{4,5},{5,4},{6,7},{7,6},{8,9},{9,8},{10,11... | collective-permute-start | bytes 7864328 | tf_op jit(solution)/shard_map/ppermute | solution.py:69
  846.7 26.8 %collective-permute-start.33 = (bf16[192,1024]{1,0:T(8,128)(2,1)}, bf16[192,1024]{1,0:T(8,128)(2,1)}, u32[]{:S(2)}, u32[]{:S(2)}) collective-permute-start(bf16[192,1024]{1,0:T(8,128)(2,1)} %fusion.116), channel_id=1, source_target_pairs={{0,16},{16,0},{1,17},{17,1},{2,18},{18,2},{3,19},{19,3},{4,20},{20... | collective-permute-start | bytes 1179656 | tf_op jit(solution)/shard_map/ppermute | solution.py:45
  873.0 45.6 %collective-permute-start.38 = (bf16[8,80,2560]{2,1,0:T(8,128)(2,1)}, bf16[8,80,2560]{2,1,0:T(8,128)(2,1)}, u32[]{:S(2)}, u32[]{:S(2)}) collective-permute-start(bf16[8,80,2560]{2,1,0:T(8,128)(2,1)} %bitcast.71), channel_id=1, source_target_pairs={{0,16},{16,0},{1,17},{17,1},{2,18},{18,2},{3,19},{19,3},{4,20},{20... | collective-permute-start | bytes 9830408 | tf_op jit(solution)/shard_map/ppermute | solution.py:45
  918.5 3.6 collective-permute-start.34
  923.8 3.1 collective-permute-start.35
  925.3 20.5 %collective-permute-start.39 = (bf16[8,40,1280]{2,1,0:T(8,128)(2,1)}, bf16[8,40,1280]{2,1,0:T(8,128)(2,1)}, u32[]{:S(2)}, u32[]{:S(2)}) collective-permute-start(bf16[8,40,1280]{2,1,0:T(8,128)(2,1)} %broadcast_select_fusion.22), channel_id=1, source_target_pairs={{0,1},{1,0},{2,3},{3,2},{4,5},{5,4},{6,7},{7,6},{8,9},{9,8},{10,11... | collective-permute-start | bytes 2457608 | tf_op jit(solution)/shard_map/ppermute | solution.py:69
  930.2 18.0 %all-to-all-start.5 = ((bf16[8,64,320]{2,1,0:T(8,128)(2,1)}), bf16[8,64,320]{2,1,0:T(8,128)(2,1)}, u32[]{:S(2)}, u32[]{:S(2)}) async-start(bf16[8,64,320]{2,1,0:T(8,128)(2,1)} %copy.176), calls=%async_computation.5 | async-start | bytes 786432 | tf_op jit(solution)/shard_map/all_to_all | solution.py:126
  948.2 24.2 %all-to-all-start.6 = ((bf16[8,40,1280]{2,1,0:T(8,128)(2,1)}), bf16[8,40,1280]{2,1,0:T(8,128)(2,1)S(1)}, u32[]{:S(2)}, u32[]{:S(2)}) async-start(bf16[8,40,1280]{2,1,0:T(8,128)(2,1)} %add_convert_fusion), calls=%async_computation.6 | async-start | bytes 1638400 | tf_op jit(solution)/shard_map/all_to_all | solution.py:150
  959.6 12.9 %collective-permute-start.36 = (bf16[64,1280]{1,0:T(8,128)(2,1)S(1)}, bf16[64,1280]{1,0:T(8,128)(2,1)S(1)}, u32[]{:S(2)}, u32[]{:S(2)}) collective-permute-start(bf16[64,1280]{1,0:T(8,128)(2,1)S(1)} %broadcast_select_fusion.56), channel_id=1, source_target_pairs={{0,1},{1,0},{2,3},{3,2},{4,5},{5,4},{6,7},{7,6},{8,9},{9,8},{10,11... | collective-permute-start | bytes 491528 | tf_op jit(solution)/shard_map/ppermute | solution.py:69
  972.4 2.6 collective-permute-start.40
  972.5 2.5 collective-permute-start.37
  (36 other events, 353.0 us)
Sparse Core Ops, SparseCore 0:
  10.2 180.6 all-gather.23
  254.9 39.0 all-gather.11
  339.3 40.8 all-gather.13
  482.5 43.5 all-gather.15
  650.4 39.0 all-gather.17
  734.8 40.8 all-gather.19
  875.7 42.8 all-gather.21

commit v15 on v10

--- a/solution.py
+++ b/solution.py
@@ -310,7 +310,12 @@
             .at[source_ids, rank_at]
             .set(True, mode="drop")
         )
-        incoming_rows = jnp.where(filled[..., None], moe_all[table], jnp.zeros((), jnp.bfloat16))
+        picks = (
+            (table[..., None] == jnp.arange(moe_all.shape[0], dtype=jnp.int32)) & filled[..., None]
+        ).astype(jnp.bfloat16)
+        incoming_rows = jnp.einsum(
+            "scn,nd->scd", picks, moe_all, preferred_element_type=jnp.float32
+        ).astype(jnp.bfloat16)
         returned = expert_path(incoming_rows, w_in_local, w_down_local, pair_active)
         combined = returned.reshape(experts_count * capacity, columns)[slot_ids].astype(jnp.float32)
         combined = combined * gate_weights.reshape(-1)[:, None]

time: 926 us -> 893 us (0.964)
  local copies, waits for them, and re-layouts: 101 us -> 76.5 us
    gather x2 -> x0, local copies, waits for them, and re-layouts: 22.9 us -> none  [local(): moe_all[table]]
    unnamed x99 -> x115, local copies, waits for them, and re-layouts: 34.8 us -> 33 us
  transfers between devices with their start and end apart: 51 -> 51, of which waited for: 36 -> 36; matrix products, arithmetic and copies ran while one was open for 13% -> 10% of each run, Pallas kernels for 0% -> 0%
where the time goes in v15:
time: 893 us; the launch traced here: 883 us
  waiting for transfers between devices  434 us (49%)
  blocking collectives  196 us (22%)
  local copies, waits for them, and re-layouts  76.5 us (9%)
  other arithmetic  58.5 us (7%)
  matrix products  55.2 us (6%)
  starting transfers between devices  46.3 us (5%)
  between operations  15.8 us (2%)
    all_gather x6, waiting for transfers between devices, paired_gather(): lax.all_gather(jnp.where(active, first, second), 'expert', axis=axis, til...  271 us
    all_gather x1, blocking collectives, local(): lax.all_gather(expert_choice[0], 'expert', axis=0, tiled=False)  93 us
    ppermute x10, waiting for transfers between devices, swap_tensor(): lax.ppermute(value, 'tensor', [(source, (source + 1) % count) for source...  55.8 us
    all_gather x2, blocking collectives, paired_gather(): lax.all_gather(jnp.where(active, first, second), 'expert', axis=axis, til...  55.2 us
    all_gather x1, waiting for transfers between devices, local(): qkv_full = lax.all_gather(w_qkv[0], 'expert', axis=0, tiled=True)  44.1 us
    ppermute x28, waiting for transfers between devices, swap_cores(): lax.ppermute(value, 'section', [(source, (source + 1) % count) for source...  36.1 us
    unnamed x115, local copies, waits for them, and re-layouts  33 us
    all_to_all x2, blocking collectives, step(): lax.all_to_all(part.reshape(-1, part.shape[2]), 'expert', split_axis=0, c...  30.8 us
  transfers between devices with their start and end apart: 51, of which 36 were waited for; matrix products, arithmetic and copies ran while one was open for 10% of the time, Pallas kernels for 0%

profile of v15, /device:TPU:0, one launch (start us, length us, event | category | flops | bytes accessed | tf_op | source)
XLA Modules:
  0.0 882.8 jit_solution(13955561955774791932)
XLA Ops:
  7.9 8.5 copy.149
  16.5 7.4 all-to-all-start
  27.2 8.1 all-gather.2
  35.3 4.4 all-gather.3
  41.0 93.0 %all_gather.40 = s32[8,1,128,4]{2,3,1,0:T(4,128)} all-gather(s32[1,1,128,4]{2,3,1,0:T(4,128)S(1)} %copy-done.29), channel_id=1, replica_groups=mesh['section'=2,'expert'=8,'tensor'=2] {'expert'}, dimensions={0}, use_global_device_ids=true | all-gather | bytes 18432 | tf_op jit(solution)/shard_map/all_gather | solution.py:162
  134.0 4.7 all-gather.1
  143.9 2.8 all_to_all.70
  146.7 44.1 %all-gather.24.cloned.1.call-done = bf16[1,2560,2,896]{3,2,0,1:T(2,128)(2,1)} async-done(((bf16[1,320,2,896]{3,2,0,1:T(2,128)(2,1)}), bf16[1,2560,2,896]{3,2,0,1:T(2,128)(2,1)}) %all-gather.24.cloned.1.call-update) | async-done | bytes 9175056 | tf_op jit(solution)/shard_map/all_gather | solution.py:158
  190.8 8.7 copy.205
  199.6 12.8 %copy.152 = bf16[1792,2560]{1,0:T(8,128)(2,1)} copy(bf16[1792,2560]{0,1:T(8,128)(2,1)} %bitcast.243) | data formatting | bytes 18350080 | tf_op jit(solution)/shard_map/dot_general | solution.py:221
  212.4 6.2 fusion.124
  220.2 27.5 %all_gather.44 = bf16[1024,256]{0,1:T(8,128)(2,1)S(1)} all-gather(bf16[128,256]{0,1:T(8,128)(2,1)S(1)} %slice_select_fusion.13), channel_id=1, replica_groups=mesh['section'=2,'expert'=8,'tensor'=2] {'expert'}, dimensions={0}, use_global_device_ids=true | all-gather | bytes 589824 | tf_op jit(solution)/shard_map/all_gather | solution.py:51
  255.2 38.8 %all-gather.12.cloned.1.call-done = bf16[1024,640]{1,0:T(8,128)(2,1)} async-done(((bf16[128,640]{1,0:T(8,128)(2,1)}), bf16[1024,640]{1,0:T(8,128)(2,1)}) %all-gather.12.cloned.1.call-update) | async-done | bytes 1310736 | tf_op jit(solution)/shard_map/all_gather | solution.py:51
  294.0 3.2 collective-permute-done.4
  302.9 15.4 %all_to_all.92 = bf16[8,64,320]{2,1,0:T(8,128)(2,1)S(1)} all-to-all(bf16[8,64,320]{2,1,0:T(8,128)(2,1)S(1)} %copy.160), channel_id=1, replica_groups=mesh['section'=2,'expert'=8,'tensor'=2] {'expert'}, dimensions={0} | all-to-all | bytes 655360 | tf_op jit(solution)/shard_map/all_to_all | solution.py:109
  320.4 3.8 collective-permute-done.6
  327.5 8.3 collective-permute-done.8
  339.4 53.9 %all-gather.14.cloned.1.call-done = bf16[1024,1280]{1,0:T(8,128)(2,1)} async-done(((bf16[128,1280]{1,0:T(8,128)(2,1)}), bf16[1024,1280]{1,0:T(8,128)(2,1)}) %all-gather.14.cloned.1.call-update) | async-done | bytes 2621456 | tf_op jit(solution)/shard_map/all_gather | solution.py:51
  393.7 4.3 scatter_custom_fusion
  398.1 4.9 scatter_custom_fusion.1
  403.1 4.6 copy.206
  407.7 5.7 broadcast_select_fusion.5
  413.6 2.2 fusion.15
  416.7 3.7 fusion.4
  420.4 5.2 fusion.169
  425.6 4.9 convolution_convert_fusion.1
  431.5 43.0 %all-gather.16.cloned.1.call-done = bf16[1536,512]{1,0:T(8,128)(2,1)} async-done(((bf16[192,512]{1,0:T(8,128)(2,1)}), bf16[1536,512]{1,0:T(8,128)(2,1)}) %all-gather.16.cloned.1.call-update) | async-done | bytes 1572880 | tf_op jit(solution)/shard_map/all_gather | solution.py:51
  474.6 2.3 broadcast_select_fusion.1
  486.2 4.1 all-to-all-start.2
  490.3 11.6 %collective-permute-done.17 = bf16[8,40,1280]{2,1,0:T(8,128)(2,1)} collective-permute-done((bf16[8,40,1280]{2,1,0:T(8,128)(2,1)}, bf16[8,40,1280]{2,1,0:T(8,128)(2,1)}, u32[]{:S(2)}, u32[]{:S(2)}) %collective-permute-start.17) | collective-permute-done | bytes 819232 | tf_op jit(solution)/shard_map/ppermute | solution.py:69
  501.9 2.4 add_convert_fusion.1
  504.2 3.7 all-to-all-start.3
  514.4 14.0 %all-to-all-done.3 = bf16[8,40,1280]{2,1,0:T(8,128)(2,1)S(1)} async-done(((bf16[8,40,1280]{2,1,0:T(8,128)(2,1)}), bf16[8,40,1280]{2,1,0:T(8,128)(2,1)S(1)}, u32[]{:S(2)}, u32[]{:S(2)}) %all-to-all-start.3) | async-done | bytes 819232 | tf_op jit(solution)/shard_map/all_to_all | solution.py:133
  532.5 2.9 gather_fusion
  535.4 3.7 reshape.789
  539.1 3.4 multiply_reduce_fusion.1
  542.7 2.3 collective-permute-start.19
  547.5 8.5 collective-permute-done.20
  556.3 6.2 fusion.121
  564.1 27.7 %all_gather.48 = bf16[1024,256]{0,1:T(8,128)(2,1)S(1)} all-gather(bf16[128,256]{0,1:T(8,128)(2,1)S(1)} %slice_select_fusion.12), channel_id=1, replica_groups=mesh['section'=2,'expert'=8,'tensor'=2] {'expert'}, dimensions={0}, use_global_device_ids=true | all-gather | bytes 589824 | tf_op jit(solution)/shard_map/all_gather | solution.py:51
  599.1 39.1 %all-gather.18.cloned.1.call-done = bf16[1024,640]{1,0:T(8,128)(2,1)} async-done(((bf16[128,640]{1,0:T(8,128)(2,1)}), bf16[1024,640]{1,0:T(8,128)(2,1)}) %all-gather.18.cloned.1.call-update) | async-done | bytes 1310736 | tf_op jit(solution)/shard_map/all_gather | solution.py:51
  638.2 3.2 collective-permute-done.24
  647.1 15.4 %all_to_all.93 = bf16[8,64,320]{2,1,0:T(8,128)(2,1)S(1)} all-to-all(bf16[8,64,320]{2,1,0:T(8,128)(2,1)S(1)} %copy.177), channel_id=1, replica_groups=mesh['section'=2,'expert'=8,'tensor'=2] {'expert'}, dimensions={0} | all-to-all | bytes 655360 | tf_op jit(solution)/shard_map/all_to_all | solution.py:109
  664.6 3.9 collective-permute-done.26
  671.6 8.3 collective-permute-done.28
  683.9 53.5 %all-gather.20.cloned.1.call-done = bf16[1024,1280]{1,0:T(8,128)(2,1)} async-done(((bf16[128,1280]{1,0:T(8,128)(2,1)}), bf16[1024,1280]{1,0:T(8,128)(2,1)}) %all-gather.20.cloned.1.call-update) | async-done | bytes 2621456 | tf_op jit(solution)/shard_map/all_gather | solution.py:51
  737.4 5.1 collective-permute-done.30
  742.5 2.4 broadcast_select_fusion.3
  744.9 2.2 fusion.14
  747.2 3.7 fusion.7
  751.3 5.2 fusion.171
  756.6 4.7 convolution_convert_fusion
  762.6 42.9 %all-gather.22.cloned.1.call-done = bf16[1536,512]{1,0:T(8,128)(2,1)} async-done(((bf16[192,512]{1,0:T(8,128)(2,1)}), bf16[1536,512]{1,0:T(8,128)(2,1)}) %all-gather.22.cloned.1.call-update) | async-done | bytes 1572880 | tf_op jit(solution)/shard_map/all_gather | solution.py:51
  805.6 2.3 broadcast_select_fusion
  817.2 4.3 all-to-all-start.5
  821.5 11.4 %collective-permute-done.37 = bf16[8,40,1280]{2,1,0:T(8,128)(2,1)} collective-permute-done((bf16[8,40,1280]{2,1,0:T(8,128)(2,1)}, bf16[8,40,1280]{2,1,0:T(8,128)(2,1)}, u32[]{:S(2)}, u32[]{:S(2)}) %collective-permute-start.37) | collective-permute-done | bytes 819232 | tf_op jit(solution)/shard_map/ppermute | solution.py:69
  832.9 2.4 add_convert_fusion
  835.3 3.7 all-to-all-start.6
  841.9 2.5 broadcast_select_fusion.45
  848.1 11.4 %all-to-all-done.6 = bf16[8,40,1280]{2,1,0:T(8,128)(2,1)S(1)} async-done(((bf16[8,40,1280]{2,1,0:T(8,128)(2,1)}), bf16[8,40,1280]{2,1,0:T(8,128)(2,1)S(1)}, u32[]{:S(2)}, u32[]{:S(2)}) %all-to-all-start.6) | async-done | bytes 819232 | tf_op jit(solution)/shard_map/all_to_all | solution.py:133
  863.5 2.9 gather_fusion.1
  866.4 3.7 reshape.790
  870.1 3.4 multiply_reduce_fusion
  873.5 2.2 fusion.136
  (355 shorter events, 104.4 us)
Async XLA Ops:
  7.2 471.3 %copy-start = (bf16[1,320,1536]{2,1,0:T(8,128)(2,1)S(1)}, bf16[1,320,1536]{2,1,0:T(8,128)(2,1)}, u32[]{:S(2)}) copy-start(bf16[1,320,1536]{2,1,0:T(8,128)(2,1)} %param.30) | copy-start | bytes 2949124
  7.2 183.7 %all-gather.24.cloned.1.call-start = ((), (), s32[]{:S(2)}) async-start(), calls=%async_computation.13 | async-start | bytes 10321920 | tf_op jit(solution)/shard_map/all_gather | solution.py:158
  16.5 117.6 %copy-start.32 = (f32[1,1280,8]{1,2,0:T(8,128)S(1)}, f32[1,1280,8]{1,2,0:T(8,128)}, u32[]{:S(2)}) copy-start(f32[1,1280,8]{1,2,0:T(8,128)} %param.31) | copy-start | bytes 122884
  16.5 122.9 %copy-start.40 = (s32[1,128]{1,0:T(1,128)S(1)}, s32[1,128]{1,0:T(1,128)}, u32[]{:S(2)}) copy-start(s32[1,128]{1,0:T(1,128)} %param.22) | copy-start | bytes 1540
  16.5 125.7 %all-to-all-start = ((bf16[320,2,1536]{0,1,2:T(2,128)(2,1)}), bf16[320,2,1536]{0,1,2:T(2,128)(2,1)S(1)}, u32[]{:S(2)}, u32[]{:S(2)}) async-start(bf16[320,2,1536]{0,1,2:T(2,128)(2,1)} %bitcast.244), calls=%async_computation | async-start | bytes 4718592 | tf_op jit(solution)/shard_map/all_to_all | solution.py:161
  23.9 270.1 %all-gather.12.cloned.1.call-start = ((), (), s32[]{:S(2)}) async-start(), calls=%async_computation.7 | async-start | bytes 1474560 | tf_op jit(solution)/shard_map/all_gather | solution.py:51
  25.7 114.6 %collective-permute-start = (bf16[128,1280]{1,0:T(8,128)(2,1)}, bf16[128,1280]{1,0:T(8,128)(2,1)}, u32[]{:S(2)}, u32[]{:S(2)}) collective-permute-start(bf16[128,1280]{1,0:T(8,128)(2,1)} %bitcast_select_fusion.3), channel_id=1, source_target_pairs={{0,1},{1,0},{2,3},{3,2},{4,5},{5,4},{6,7},{7,6},{8,9},{9,8},{10,11... | collective-permute-start | bytes 983048 | tf_op jit(solution)/shard_map/ppermute | solution.py:69
  35.3 177.1 %copy-start.26 = (f32[2560]{0:T(1024)}, f32[2560]{0:T(1024)S(1)}, u32[]{:S(2)}) copy-start(f32[2560]{0:T(1024)S(1)} %reduce.33) | copy-start | bytes 30724
  212.4 35.3 %copy-start.41 = (s32[1,128]{1,0:T(1,128)S(1)}, s32[1,128]{1,0:T(1,128)}, u32[]{:S(2)}) copy-start(s32[1,128]{1,0:T(1,128)} %param.22) | copy-start | bytes 1540
  212.4 35.3 %copy-start.42 = (s32[128]{0:T(128)S(1)}, s32[128]{0:T(128)}, u32[]{:S(2)}) copy-start(s32[128]{0:T(128)} %get-tuple-element.117) | copy-start | bytes 1540
  218.7 1.4 collective-permute-start.1
  247.7 1.9 collective-permute-start.2
  252.4 1.7 collective-permute-start.3
  254.8 44.0 %copy-start.49 = (bf16[1,320,1280]{2,1,0:T(8,128)(2,1)S(1)}, bf16[1,320,1280]{2,1,0:T(8,128)(2,1)}, u32[]{:S(2)}) copy-start(bf16[1,320,1280]{2,1,0:T(8,128)(2,1)} %param.28) | copy-start | bytes 2457604
  254.9 138.4 %all-gather.14.cloned.1.call-start = ((), (), s32[]{:S(2)}) async-start(), calls=%async_computation.8 | async-start | bytes 2949120 | tf_op jit(solution)/shard_map/all_gather | solution.py:51
  294.0 3.2 collective-permute-start.4
  300.0 2.2 collective-permute-start.5
  318.9 5.4 collective-permute-start.6
  324.3 1.5 collective-permute-start.7
  326.0 9.8 %collective-permute-start.8 = (bf16[128,1280]{1,0:T(8,128)(2,1)S(1)}, bf16[128,1280]{1,0:T(8,128)(2,1)S(1)}, u32[]{:S(2)}, u32[]{:S(2)}) collective-permute-start(bf16[128,1280]{1,0:T(8,128)(2,1)S(1)} %add_convert_fusion.5), channel_id=1, source_target_pairs={{0,1},{1,0},{2,3},{3,2},{4,5},{5,4},{6,7},{7,6},{8,9},{9,8},{10,11... | collective-permute-start | bytes 983048 | tf_op jit(solution)/shard_map/ppermute | solution.py:69
  335.8 57.4 %copy-start.28 = (s32[8,1,128,4]{2,3,1,0:T(4,128)S(1)}, s32[8,1,128,4]{2,3,1,0:T(4,128)}, u32[]{:S(2)}) copy-start(s32[8,1,128,4]{2,3,1,0:T(4,128)} %all_gather.40) | copy-start | bytes 49156
  335.9 57.6 %copy-start.46 = (s32[2]{0:T(128)S(1)}, s32[2]{0:T(128)}, u32[]{:S(2)}) copy-start(s32[2]{0:T(128)} %constant.164) | copy-start | bytes 28
  335.9 57.7 %copy-start.45 = (s32[2]{0:T(128)S(1)}, s32[2]{0:T(128)}, u32[]{:S(2)}) copy-start(s32[2]{0:T(128)} %constant.167) | copy-start | bytes 28
  336.3 2.2 collective-permute-start.9
  339.4 135.2 %all-gather.16.cloned.1.call-start = ((), (), s32[]{:S(2)}) async-start(), calls=%async_computation.9 | async-start | bytes 1769472 | tf_op jit(solution)/shard_map/all_gather | solution.py:51
  393.3 14.4 %collective-permute-start.10 = (bf16[1024,1280]{1,0:T(8,128)(2,1)}, bf16[1024,1280]{1,0:T(8,128)(2,1)}, u32[]{:S(2)}, u32[]{:S(2)}) collective-permute-start(bf16[1024,1280]{1,0:T(8,128)(2,1)} %all-gather.14.cloned.1.call-done), channel_id=1, source_target_pairs={{0,16},{16,0},{1,17},{17,1},{2,18},{18,2},{3,19},{19,3},{4,20},{20... | collective-permute-start | bytes 7864328 | tf_op jit(solution)/shard_map/ppermute | solution.py:45
  416.1 14.5 %collective-permute-start.11 = (bf16[192,1024]{1,0:T(8,128)(2,1)S(1)}, bf16[192,1024]{1,0:T(8,128)(2,1)S(1)}, u32[]{:S(2)}, u32[]{:S(2)}) collective-permute-start(bf16[192,1024]{1,0:T(8,128)(2,1)S(1)} %fusion.134), channel_id=1, source_target_pairs={{0,16},{16,0},{1,17},{17,1},{2,18},{18,2},{3,19},{19,3},{4,20},{20... | collective-permute-start | bytes 1179656 | tf_op jit(solution)/shard_map/ppermute | solution.py:45
  430.5 44.1 %collective-permute-start.16 = (bf16[8,80,2560]{2,1,0:T(8,128)(2,1)}, bf16[8,80,2560]{2,1,0:T(8,128)(2,1)}, u32[]{:S(2)}, u32[]{:S(2)}) collective-permute-start(bf16[8,80,2560]{2,1,0:T(8,128)(2,1)} %bitcast.45), channel_id=1, source_target_pairs={{0,16},{16,0},{1,17},{17,1},{2,18},{18,2},{3,19},{19,3},{4,20},{20... | collective-permute-start | bytes 9830408 | tf_op jit(solution)/shard_map/ppermute | solution.py:45
  474.6 3.6 collective-permute-start.12
  479.8 3.0 collective-permute-start.13
  481.4 20.5 %collective-permute-start.17 = (bf16[8,40,1280]{2,1,0:T(8,128)(2,1)}, bf16[8,40,1280]{2,1,0:T(8,128)(2,1)}, u32[]{:S(2)}, u32[]{:S(2)}) collective-permute-start(bf16[8,40,1280]{2,1,0:T(8,128)(2,1)} %broadcast_select_fusion.17), channel_id=1, source_target_pairs={{0,1},{1,0},{2,3},{3,2},{4,5},{5,4},{6,7},{7,6},{8,9},{9,8},{10,11... | collective-permute-start | bytes 2457608 | tf_op jit(solution)/shard_map/ppermute | solution.py:69
  486.2 18.0 %all-to-all-start.2 = ((bf16[8,64,320]{2,1,0:T(8,128)(2,1)}), bf16[8,64,320]{2,1,0:T(8,128)(2,1)}, u32[]{:S(2)}, u32[]{:S(2)}) async-start(bf16[8,64,320]{2,1,0:T(8,128)(2,1)} %copy.164), calls=%async_computation.2 | async-start | bytes 786432 | tf_op jit(solution)/shard_map/all_to_all | solution.py:109
  504.2 24.2 %all-to-all-start.3 = ((bf16[8,40,1280]{2,1,0:T(8,128)(2,1)}), bf16[8,40,1280]{2,1,0:T(8,128)(2,1)S(1)}, u32[]{:S(2)}, u32[]{:S(2)}) async-start(bf16[8,40,1280]{2,1,0:T(8,128)(2,1)} %add_convert_fusion.1), calls=%async_computation.3 | async-start | bytes 1638400 | tf_op jit(solution)/shard_map/all_to_all | solution.py:133
  507.9 130.3 %all-gather.18.cloned.1.call-start = ((), (), s32[]{:S(2)}) async-start(), calls=%async_computation.10 | async-start | bytes 1474560 | tf_op jit(solution)/shard_map/all_gather | solution.py:51
  512.8 15.6 %collective-permute-start.14 = (bf16[64,1280]{1,0:T(8,128)(2,1)S(1)}, bf16[64,1280]{1,0:T(8,128)(2,1)S(1)}, u32[]{:S(2)}, u32[]{:S(2)}) collective-permute-start(bf16[64,1280]{1,0:T(8,128)(2,1)S(1)} %broadcast_select_fusion.52), channel_id=1, source_target_pairs={{0,1},{1,0},{2,3},{3,2},{4,5},{5,4},{6,7},{7,6},{8,9},{9,8},{10,11... | collective-permute-start | bytes 491528 | tf_op jit(solution)/shard_map/ppermute | solution.py:69
  528.4 2.6 collective-permute-start.18
  528.5 2.5 collective-permute-start.15
  542.7 3.3 collective-permute-start.19
  546.0 10.1 %collective-permute-start.20 = (bf16[128,1280]{1,0:T(8,128)(2,1)S(1)}, bf16[128,1280]{1,0:T(8,128)(2,1)S(1)}, u32[]{:S(2)}, u32[]{:S(2)}) collective-permute-start(bf16[128,1280]{1,0:T(8,128)(2,1)S(1)} %bitcast_select_fusion.2), channel_id=1, source_target_pairs={{0,1},{1,0},{2,3},{3,2},{4,5},{5,4},{6,7},{7,6},{8,9},{9,8},{10,11... | collective-permute-start | bytes 983048 | tf_op jit(solution)/shard_map/ppermute | solution.py:69
  562.6 31.3 %copy-start.18 = (bf16[128,2,1,128]{0,3,2,1:T(8,128)(2,1)}, bf16[128,2,1,128]{0,3,2,1:T(8,128)(2,1)S(1)}, u32[]{:S(2)}) copy-start(bf16[128,2,1,128]{0,3,2,1:T(8,128)(2,1)S(1)} %slice.281) | copy-start | bytes 196612
  562.6 31.3 %copy-start.20 = (bf16[128,2,128]{0,2,1:T(8,128)(2,1)}, bf16[128,2,128]{0,2,1:T(8,128)(2,1)S(1)}, u32[]{:S(2)}) copy-start(bf16[128,2,128]{0,2,1:T(8,128)(2,1)S(1)} %pad_maximum_fusion.21) | copy-start | bytes 196612
  562.7 1.4 collective-permute-start.21
  591.8 1.9 collective-permute-start.22
  596.6 1.7 collective-permute-start.23
  599.0 44.0 %copy-start.50 = (bf16[1,320,1280]{2,1,0:T(8,128)(2,1)S(1)}, bf16[1,320,1280]{2,1,0:T(8,128)(2,1)}, u32[]{:S(2)}) copy-start(bf16[1,320,1280]{2,1,0:T(8,128)(2,1)} %param.28) | copy-start | bytes 2457604
  599.0 138.3 %all-gather.20.cloned.1.call-start = ((), (), s32[]{:S(2)}) async-start(), calls=%async_computation.11 | async-start | bytes 2949120 | tf_op jit(solution)/shard_map/all_gather | solution.py:51
  638.2 3.2 collective-permute-start.24
  644.2 2.2 collective-permute-start.25
  663.0 5.4 collective-permute-start.26
  668.5 1.5 collective-permute-start.27
  670.1 9.8 %collective-permute-start.28 = (bf16[128,1280]{1,0:T(8,128)(2,1)S(1)}, bf16[128,1280]{1,0:T(8,128)(2,1)S(1)}, u32[]{:S(2)}, u32[]{:S(2)}) collective-permute-start(bf16[128,1280]{1,0:T(8,128)(2,1)S(1)} %add_convert_fusion.3), channel_id=1, source_target_pairs={{0,1},{1,0},{2,3},{3,2},{4,5},{5,4},{6,7},{7,6},{8,9},{9,8},{10,11... | collective-permute-start | bytes 983048 | tf_op jit(solution)/shard_map/ppermute | solution.py:69
  680.4 2.2 collective-permute-start.29
  683.4 122.1 %all-gather.22.cloned.1.call-start = ((), (), s32[]{:S(2)}) async-start(), calls=%async_computation.12 | async-start | bytes 1769472 | tf_op jit(solution)/shard_map/all_gather | solution.py:51
  737.4 5.1 collective-permute-start.30
  751.1 10.5 %collective-permute-start.31 = (bf16[192,1024]{1,0:T(8,128)(2,1)S(1)}, bf16[192,1024]{1,0:T(8,128)(2,1)S(1)}, u32[]{:S(2)}, u32[]{:S(2)}) collective-permute-start(bf16[192,1024]{1,0:T(8,128)(2,1)S(1)} %fusion.135), channel_id=1, source_target_pairs={{0,16},{16,0},{1,17},{17,1},{2,18},{18,2},{3,19},{19,3},{4,20},{20... | collective-permute-start | bytes 1179656 | tf_op jit(solution)/shard_map/ppermute | solution.py:45
  761.3 44.3 %collective-permute-start.36 = (bf16[8,80,2560]{2,1,0:T(8,128)(2,1)}, bf16[8,80,2560]{2,1,0:T(8,128)(2,1)}, u32[]{:S(2)}, u32[]{:S(2)}) collective-permute-start(bf16[8,80,2560]{2,1,0:T(8,128)(2,1)} %bitcast.71), channel_id=1, source_target_pairs={{0,16},{16,0},{1,17},{17,1},{2,18},{18,2},{3,19},{19,3},{4,20},{20... | collective-permute-start | bytes 9830408 | tf_op jit(solution)/shard_map/ppermute | solution.py:45
  805.6 3.6 collective-permute-start.32
  810.8 3.1 collective-permute-start.33
  812.4 20.5 %collective-permute-start.37 = (bf16[8,40,1280]{2,1,0:T(8,128)(2,1)}, bf16[8,40,1280]{2,1,0:T(8,128)(2,1)}, u32[]{:S(2)}, u32[]{:S(2)}) collective-permute-start(bf16[8,40,1280]{2,1,0:T(8,128)(2,1)} %broadcast_select_fusion.16), channel_id=1, source_target_pairs={{0,1},{1,0},{2,3},{3,2},{4,5},{5,4},{6,7},{7,6},{8,9},{9,8},{10,11... | collective-permute-start | bytes 2457608 | tf_op jit(solution)/shard_map/ppermute | solution.py:69
  817.2 18.1 %all-to-all-start.5 = ((bf16[8,64,320]{2,1,0:T(8,128)(2,1)}), bf16[8,64,320]{2,1,0:T(8,128)(2,1)}, u32[]{:S(2)}, u32[]{:S(2)}) async-start(bf16[8,64,320]{2,1,0:T(8,128)(2,1)} %copy.181), calls=%async_computation.5 | async-start | bytes 786432 | tf_op jit(solution)/shard_map/all_to_all | solution.py:109
  835.3 24.2 %all-to-all-start.6 = ((bf16[8,40,1280]{2,1,0:T(8,128)(2,1)}), bf16[8,40,1280]{2,1,0:T(8,128)(2,1)S(1)}, u32[]{:S(2)}, u32[]{:S(2)}) async-start(bf16[8,40,1280]{2,1,0:T(8,128)(2,1)} %add_convert_fusion), calls=%async_computation.6 | async-start | bytes 1638400 | tf_op jit(solution)/shard_map/all_to_all | solution.py:133
  846.5 13.0 %collective-permute-start.34 = (bf16[64,1280]{1,0:T(8,128)(2,1)S(1)}, bf16[64,1280]{1,0:T(8,128)(2,1)S(1)}, u32[]{:S(2)}, u32[]{:S(2)}) collective-permute-start(bf16[64,1280]{1,0:T(8,128)(2,1)S(1)} %broadcast_select_fusion.50), channel_id=1, source_target_pairs={{0,1},{1,0},{2,3},{3,2},{4,5},{5,4},{6,7},{7,6},{8,9},{9,8},{10,11... | collective-permute-start | bytes 491528 | tf_op jit(solution)/shard_map/ppermute | solution.py:69
  859.5 2.6 collective-permute-start.38
  859.6 2.5 collective-permute-start.35
  (41 other events, 376.4 us)
Sparse Core Ops, SparseCore 0:
  10.2 180.5 all-gather.23
  255.0 39.0 all-gather.11
  339.5 53.7 all-gather.13
  431.7 42.8 all-gather.15
  599.1 39.0 all-gather.17
  683.6 53.7 all-gather.19
  762.8 42.7 all-gather.21
